TPU v7x, 32 devices: a whole 2x2x4 slice. The times are simulated.
32 devices in a mesh: section: 4 (over y, core), seq: 8 (over z, x).
Axes of the slice: x: 2, y: 2, z: 4, core: 2. Of those that a mesh axis runs over, the one named last changes fastest.
Arguments:
- queries: bfloat16 [4, 2048, 4096], P('section', 'seq'), may hold values from -42 to 42
- keys: bfloat16 [4, 2048, 512], P('section', 'seq'), may hold values from -6 to 6
- values: bfloat16 [4, 2048, 512], P('section', 'seq'), may hold values from -6 to 6
- out_grads: bfloat16 [4, 2048, 4096], P('section', 'seq'), may hold values from -6 to 6
- random_blocks: int32 [4, 32, 3], P('section'), may hold values from 0 to 31, as said below
- global_blocks: int32 [4, 2], P('section'), may hold values from 0 to 31, as said below
- pad_lengths: int32 [4, 8], P('section'), may hold values from 0 to 63, as said below
Outputs:
- passed_query_grad: bfloat16 [4, 2048, 4096], P('section', 'seq')
- passed_key_grad: bfloat16 [4, 2048, 512], P('section', 'seq')
- passed_value_grad: bfloat16 [4, 2048, 512], P('section', 'seq')
Inputs may be any that keep to these rules, and one draw needn't show every extreme that they name: `random_blocks`: over the 12 random blocks named by one shard's query blocks, the blocks of any one shard are named at most 2 times, and on every shard some shard's blocks exactly 2 times; within one random slot (one column) at most 1 times, and exactly 1 times for some shard. `global_blocks`: the 2 global blocks of a section are distinct. `pad_lengths`: every section has a shard with exactly 63 padding tokens.
All inputs are finite; a program needn't handle non-finite values.
Results may differ from a plain program's by a relative error of at most 0.007.
Values may be sent and summed in bfloat16 or wider, within the bound.
No kernel may reach another device: no remote copies, remote signals or barrier semaphores. Data moves between devices by JAX's collectives and lax.ppermute only.
A program may use at most 128 MiB of HBM per device.

v0:
```python
import math

import jax
import jax.numpy as jnp
from jax import lax
from jax.sharding import PartitionSpec as P

HDIM = 128
BLK = 64
GLOB = 2
RAND = 3


def extended_2(array, sides, width):
    for axis, dim in sides:
        devices, length = (lax.axis_size(axis), array.shape[dim])
        up = [(i, (i + 1) % devices) for i in range(devices - 1)]
        down = [(j, i) for i, j in up]
        last = lax.slice_in_dim(array, length - width, length, axis=dim)
        leading = lax.slice_in_dim(array, 0, width, axis=dim)
        before = lax.ppermute(last, axis, up)
        after = lax.ppermute(leading, axis, down)
        array = jnp.concatenate([before, array, after], axis=dim)
    return array


def broadcast(array, axis, root):
    mine = lax.axis_index(axis) == root
    return lax.psum(jnp.where(mine, array, jnp.zeros_like(array)), axis)


def from_behind(block, axis, distance):
    devices = range(lax.axis_size(axis))
    route = [((i - distance) % len(devices), i) for i in devices]
    return lax.ppermute(block, axis, route)


def block_backward(query_rows, grad_rows, key_tiles, value_tiles, key_live):
    nblocks, block_len, qwidth = query_rows.shape
    ntiles = key_tiles.shape[1]
    kwidth = key_tiles.shape[-1]
    heads_kv = kwidth // HDIM
    group = qwidth // kwidth
    score_scale = 1.0 / math.sqrt(HDIM)
    query_heads = jnp.moveaxis(query_rows.reshape(nblocks, block_len, heads_kv, group, HDIM), 2, 0)
    grad_heads = jnp.moveaxis(grad_rows.reshape(nblocks, block_len, heads_kv, group, HDIM), 2, 0)
    key_heads = jnp.moveaxis(key_tiles.reshape(nblocks, ntiles, block_len, heads_kv, HDIM), 3, 0)
    value_heads = jnp.moveaxis(
        value_tiles.reshape(nblocks, ntiles, block_len, heads_kv, HDIM), 3, 0
    )
    live_mask = key_live[:, None, None, :, :]

    def one_head(inputs):
        query_one, grad_one, key_one, value_one = inputs
        scores = (
            jnp.einsum("bqgd,btkd->bgqtk", query_one, key_one, preferred_element_type=jnp.float32)
            * score_scale
        )
        scores = jnp.where(live_mask, scores, -1e30)
        row_max = jnp.max(scores, axis=(3, 4), keepdims=True)
        log_total = row_max + jnp.log(
            jnp.sum(jnp.exp(scores - row_max), axis=(3, 4), keepdims=True)
        )
        probs = jnp.exp(scores - log_total)
        probs_low = probs.astype(jnp.bfloat16)
        output = jnp.einsum(
            "bgqtk,btkd->bqgd", probs_low, value_one, preferred_element_type=jnp.float32
        )
        row_dot = jnp.sum(grad_one * output, axis=-1)
        prob_grad = jnp.einsum(
            "bqgd,btkd->bgqtk", grad_one, value_one, preferred_element_type=jnp.float32
        )
        score_grad = (
            probs * (prob_grad - jnp.transpose(row_dot, (0, 2, 1))[:, :, :, None, None])
        ).astype(jnp.bfloat16)
        query_grad = (
            jnp.einsum("bgqtk,btkd->bqgd", score_grad, key_one, preferred_element_type=jnp.float32)
            * score_scale
        )
        key_grad = (
            jnp.einsum(
                "bgqtk,bqgd->btkd", score_grad, query_one, preferred_element_type=jnp.float32
            )
            * score_scale
        )
        value_grad = jnp.einsum(
            "bgqtk,bqgd->btkd", probs_low, grad_one, preferred_element_type=jnp.float32
        )
        return (query_grad, key_grad, value_grad)

    query_grad, key_grad, value_grad = lax.map(
        one_head, (query_heads, grad_heads, key_heads, value_heads)
    )
    return (
        jnp.moveaxis(query_grad, 0, 2).reshape(nblocks, block_len, qwidth),
        jnp.moveaxis(key_grad, 0, 3).reshape(nblocks, ntiles, block_len, kwidth),
        jnp.moveaxis(value_grad, 0, 3).reshape(nblocks, ntiles, block_len, kwidth),
    )


def request_plan(request_lists, this_shard, query_blocks):
    shards, count = request_lists.shape
    capacity = -(-count // shards)
    owner_ids = request_lists // query_blocks
    local_ids = request_lists % query_blocks
    order = jnp.arange(count, dtype=jnp.int32)
    earlier = order[None, :] < order[:, None]
    same_owner = owner_ids[:, :, None] == owner_ids[:, None, :]
    slot_rank = jnp.sum(same_owner & earlier[None], axis=2)
    slot_ids = jnp.arange(capacity, dtype=jnp.int32)
    chosen = (owner_ids[:, None, :] == this_shard) & (
        slot_rank[:, None, :] == slot_ids[None, :, None]
    )
    serve_block = jnp.sum(jnp.where(chosen, local_ids[:, None, :], 0), axis=2)
    slot_used = jnp.any(chosen, axis=2)
    owner_mine = lax.dynamic_index_in_dim(owner_ids, this_shard, 0, keepdims=False)
    rank_mine = lax.dynamic_index_in_dim(slot_rank, this_shard, 0, keepdims=False)
    return (serve_block, slot_used, owner_mine, rank_mine)


def serve_tiles(own_blocks, request_info):
    serve_block, slot_used = (request_info[0], request_info[1])
    shards, capacity = serve_block.shape
    gathered = jnp.take(own_blocks, serve_block.reshape(-1), axis=1)
    gathered = gathered.reshape(2, shards, capacity, own_blocks.shape[2], own_blocks.shape[3])
    return jnp.where(slot_used[None, :, :, None, None], gathered, jnp.zeros((), own_blocks.dtype))


def pick_tiles(received, request_info):
    return received[:, request_info[2], request_info[3]]


def place_terms(terms, request_info):
    serve_block = request_info[0]
    shards, capacity = serve_block.shape
    holder = jnp.zeros((2, shards, capacity, terms.shape[2], terms.shape[3]), terms.dtype)
    return holder.at[:, request_info[2], request_info[3]].set(terms)


def absorb_terms(received, request_info, query_blocks):
    serve_block, slot_used = (request_info[0], request_info[1])
    onehot = (
        slot_used[:, :, None]
        & (serve_block[:, :, None] == jnp.arange(query_blocks, dtype=jnp.int32)[None, None, :])
    ).astype(jnp.bfloat16)
    return jnp.einsum("ncq,xncsk->xqsk", onehot, received, preferred_element_type=jnp.float32)


def token_live(tile_ids, pad_sizes, query_blocks, shard_tokens, total_blocks):
    valid = (tile_ids >= 0) & (tile_ids < total_blocks)
    safe_ids = jnp.clip(tile_ids, 0, total_blocks - 1)
    owner_shard = safe_ids // query_blocks
    shards = pad_sizes.shape[0]
    pad_of = jnp.sum(
        jnp.where(owner_shard[..., None] == jnp.arange(shards, dtype=jnp.int32), pad_sizes, 0),
        axis=-1,
    )
    within = (safe_ids % query_blocks)[..., None] * BLK + jnp.arange(BLK, dtype=jnp.int32)
    return valid[..., None] & (within < (shard_tokens - pad_of)[..., None])


def body(queries, keys, values, out_grads, random_blocks, global_blocks, pad_lengths):
    query_rows = queries[0]
    key_rows = keys[0]
    value_rows = values[0]
    grad_rows = out_grads[0]
    random_table = random_blocks[0]
    global_ids = global_blocks[0]
    pad_sizes = pad_lengths[0]
    shards = lax.axis_size("seq")
    this_shard = lax.axis_index("seq")
    shard_tokens, qwidth = query_rows.shape
    kwidth = key_rows.shape[1]
    query_blocks = shard_tokens // BLK
    total_blocks = query_blocks * shards
    near = 3 + GLOB
    kvpair = jnp.stack([key_rows, value_rows])
    extended = extended_2(kvpair, (("seq", 1),), BLK)
    ext_blocks = extended.reshape(2, query_blocks + 2, BLK, kwidth)
    window = jnp.stack(
        [ext_blocks[:, offset : offset + query_blocks] for offset in range(3)], axis=2
    )
    own_blocks = kvpair.reshape(2, query_blocks, BLK, kwidth)
    global_list = []
    for glob_num in range(GLOB):
        owner_dev = global_ids[glob_num] // query_blocks
        local_tile = lax.dynamic_index_in_dim(
            own_blocks, global_ids[glob_num] % query_blocks, 1, keepdims=False
        )
        global_list.append(broadcast(local_tile, "seq", owner_dev))
    global_tiles = jnp.stack(global_list, axis=1)
    random_three = random_table.reshape(shards, query_blocks, RAND)
    slot_plans = []
    pieces = []
    for slot_num in range(RAND):
        slot_plan = request_plan(random_three[:, :, slot_num], this_shard, query_blocks)
        received = lax.all_to_all(
            serve_tiles(own_blocks, slot_plan), "seq", split_axis=1, concat_axis=1, tiled=True
        )
        pieces.append(pick_tiles(received, slot_plan))
        slot_plans.append(slot_plan)
    fetched = jnp.stack(pieces, axis=2)
    spread_global = jnp.broadcast_to(global_tiles[:, None], (2, query_blocks, GLOB, BLK, kwidth))
    all_tiles = jnp.concatenate([window, spread_global, fetched], axis=2)
    base_ids = this_shard * query_blocks + jnp.arange(query_blocks, dtype=jnp.int32)
    window_ids = base_ids[:, None] + jnp.arange(-1, 2, dtype=jnp.int32)[None, :]
    my_random = lax.dynamic_index_in_dim(random_three, this_shard, 0, keepdims=False)
    tile_ids = jnp.concatenate(
        [window_ids, jnp.broadcast_to(global_ids[None, :], (query_blocks, GLOB)), my_random], axis=1
    )
    key_live = token_live(tile_ids, pad_sizes, query_blocks, shard_tokens, total_blocks)
    query_grad, key_terms, value_terms = block_backward(
        query_rows.reshape(query_blocks, BLK, qwidth),
        grad_rows.reshape(query_blocks, BLK, qwidth),
        all_tiles[0],
        all_tiles[1],
        key_live,
    )
    contrib = jnp.stack([key_terms, value_terms])
    local_sum = contrib[:, :, 1]
    local_sum = local_sum + jnp.pad(contrib[:, 1:, 0], ((0, 0), (0, 1), (0, 0), (0, 0)))
    local_sum = local_sum + jnp.pad(contrib[:, :-1, 2], ((0, 0), (1, 0), (0, 0), (0, 0)))
    edge_out = jnp.concatenate([contrib[:, 0, 0], contrib[:, query_blocks - 1, 2]], axis=1)
    edge_in = extended_2(edge_out.astype(jnp.bfloat16), (("seq", 1),), BLK).astype(edge_out.dtype)
    local_sum = local_sum.at[:, 0].add(edge_in[:, :BLK])
    local_sum = local_sum.at[:, query_blocks - 1].add(edge_in[:, 3 * BLK :])
    global_part = jnp.sum(contrib[:, :, 3:near], axis=1)
    global_total = lax.psum(global_part, "seq")
    global_pick = (
        (global_ids[:, None] // query_blocks == this_shard)
        & (global_ids[:, None] % query_blocks == jnp.arange(query_blocks, dtype=jnp.int32)[None, :])
    ).astype(jnp.float32)
    local_sum = local_sum + jnp.einsum(
        "gq,xgsk->xqsk", global_pick, global_total, precision=lax.Precision.HIGHEST
    )
    random_terms = contrib[:, :, near:].astype(jnp.bfloat16)
    for slot_num in range(RAND):
        returned = lax.all_to_all(
            place_terms(random_terms[:, :, slot_num], slot_plans[slot_num]),
            "seq",
            split_axis=1,
            concat_axis=1,
            tiled=True,
        )
        local_sum = local_sum + absorb_terms(returned, slot_plans[slot_num], query_blocks)
    key_grad = local_sum[0].reshape(shard_tokens, kwidth).astype(jnp.bfloat16)
    value_grad = local_sum[1].reshape(shard_tokens, kwidth).astype(jnp.bfloat16)
    query_low = query_grad.reshape(shard_tokens, qwidth).astype(jnp.bfloat16)
    packed = jnp.concatenate([query_low, key_grad, value_grad], axis=-1)
    handed = from_behind(packed, "section", -1)
    return (
        handed[None, :, :qwidth],
        handed[None, :, qwidth : qwidth + kwidth],
        handed[None, :, qwidth + kwidth :],
    )


def solution(mesh):
    in_specs = (
        P("section", "seq", None),
        P("section", "seq", None),
        P("section", "seq", None),
        P("section", "seq", None),
        P("section", None, None),
        P("section", None),
        P("section", None),
    )
    out_specs = (P("section", "seq", None), P("section", "seq", None), P("section", "seq", None))
    return jax.shard_map(body, mesh=mesh, in_specs=in_specs, out_specs=out_specs, check_vma=False)
```

profile of v0, /device:TPU:1, one launch (start us, length us, event | category | flops | bytes accessed | tf_op | source)
XLA Modules:
  0.0 463.5 jit_solution(16679181156214838141)
XLA Ops:
  9.2 4.0 collective-permute-start
  17.7 6.4 %all-to-all-start = ((bf16[2,8,1,64,512]{4,3,0,2,1:T(8,128)(2,1)}), bf16[2,8,1,64,512]{4,3,0,2,1:T(8,128)(2,1)S(1)}, u32[]{:S(2)}, u32[]{:S(2)}) async-start(bf16[2,8,1,64,512]{4,3,0,2,1:T(8,128)(2,1)} %fusion.54), calls=%async_computation | async-start | bytes 2097152 | tf_op jit(solution)/shard_map/all_to_all | solution.py:197
  35.6 15.4 %all-to-all-done = bf16[2,8,1,64,512]{4,3,0,2,1:T(8,128)(2,1)S(1)} async-done(((bf16[2,8,1,64,512]{4,3,0,2,1:T(8,128)(2,1)}), bf16[2,8,1,64,512]{4,3,0,2,1:T(8,128)(2,1)S(1)}, u32[]{:S(2)}, u32[]{:S(2)}) %all-to-all-start) | async-done | bytes 1048608 | tf_op jit(solution)/shard_map/all_to_all | solution.py:197
  51.1 5.3 %all-to-all-start.1 = ((bf16[2,8,1,64,512]{4,3,0,2,1:T(8,128)(2,1)}), bf16[2,8,1,64,512]{4,3,0,2,1:T(8,128)(2,1)S(1)}, u32[]{:S(2)}, u32[]{:S(2)}) async-start(bf16[2,8,1,64,512]{4,3,0,2,1:T(8,128)(2,1)} %fusion.53), calls=%async_computation.1 | async-start | bytes 2097152 | tf_op jit(solution)/shard_map/all_to_all | solution.py:197
  57.9 2.4 fusion.52
  60.3 21.6 %all-to-all-done.1 = bf16[2,8,1,64,512]{4,3,0,2,1:T(8,128)(2,1)S(1)} async-done(((bf16[2,8,1,64,512]{4,3,0,2,1:T(8,128)(2,1)}), bf16[2,8,1,64,512]{4,3,0,2,1:T(8,128)(2,1)S(1)}, u32[]{:S(2)}, u32[]{:S(2)}) %all-to-all-start.1) | async-done | bytes 1048608 | tf_op jit(solution)/shard_map/all_to_all | solution.py:197
  82.0 4.8 %all-to-all-start.2 = ((bf16[2,8,1,64,512]{4,3,0,2,1:T(8,128)(2,1)}), bf16[2,8,1,64,512]{4,3,0,2,1:T(8,128)(2,1)}, u32[]{:S(2)}, u32[]{:S(2)}) async-start(bf16[2,8,1,64,512]{4,3,0,2,1:T(8,128)(2,1)} %fusion.52), calls=%async_computation.2 | async-start | bytes 2097152 | tf_op jit(solution)/shard_map/all_to_all | solution.py:197
  87.4 3.6 copy.201
  95.4 21.6 %all-reduce.8.cloned.1.call-done = (bf16[2,1,64,512]{3,2,1,0:T(8,128)(2,1)}, bf16[2,1,64,512]{3,2,1,0:T(8,128)(2,1)}) async-done(((bf16[2,1,64,512]{3,2,1,0:T(8,128)(2,1)}, bf16[2,1,64,512]{3,2,1,0:T(8,128)(2,1)}), (bf16[2,1,64,512]{3,2,1,0:T(8,128)(2,1)}, bf16[2,1,64,512]{3,2,1,0:T(8,128)(2,1)})) %all-reduce.8.cloned.1.call-update) | async-done | bytes 262160 | tf_op jit(solution)/shard_map/psum | solution.py:29
  127.2 4.0 fusion.130
  135.4 4.0 reshape_squeeze.13
  139.4 3.5 copy.160
  142.8 77.5 %while.17 = (s32[]{:T(128)}, bf16[4,4,64,8,128]{4,2,3,1,0:T(8,128)(2,1)}, f32[4,4,8,64,128]{4,3,2,1,0:T(8,128)}, f32[4,4,8,64,128]{4,3,2,1,0:T(8,128)}, bf16[4,4...) while((s32[]{:T(128)}, ...), condition=%wide.region_16.18_spmd.clone, body=%wide.region_12.17_spmd.clone.sunk | while | flops 1633945600 | bytes 56234432 | solution.py:91
  148.6 3.6 fusion.171
  152.2 2.9 fusion.167
  155.1 3.0 fusion.168
  168.0 3.5 fusion.171
  171.5 2.9 fusion.167
  174.4 3.0 fusion.168
  187.4 3.6 fusion.171
  190.9 2.9 fusion.167
  193.9 3.0 fusion.168
  206.7 3.6 fusion.171
  210.3 2.9 fusion.167
  213.2 3.0 fusion.168
  220.3 7.8 %copy.163 = f32[4,8,64,4,128]{4,3,2,0,1:T(4,128)} copy(f32[4,8,64,4,128]{4,2,1,0,3:T(8,128)} %bitcast.563) | data formatting | bytes 8388608 | tf_op jit(solution)/shard_map/transpose | solution.py:96
  228.1 5.5 %stack_reshape.6 = f32[1,4,8,64,512]{4,3,0,1,2:T(8,128)} reshape(f32[4,8,64,4,128]{4,3,2,0,1:T(4,128)} %copy.163) | data formatting | bytes 8388608 | tf_op jit(solution)/shard_map/stack;reshape | solution.py:219
  233.6 5.0 %constant_dynamic-update-slice_fusion.3 = f32[2,4,8,64,512]{4,3,0,1,2:T(8,128)} fusion(f32[1,4,8,64,512]{4,3,0,1,2:T(8,128)} %stack_reshape.6), kind=kLoop, calls=%fused_computation.124 | loop fusion | bytes 8388608
  238.6 5.6 %copy.164 = f32[4,8,64,4,128]{4,3,2,0,1:T(4,128)} copy(f32[4,8,64,4,128]{4,2,1,0,3:T(8,128)S(1)} %bitcast.564) | data formatting | bytes 8388608 | tf_op jit(solution)/shard_map/transpose | solution.py:97
  244.1 5.5 %stack_reshape.7 = f32[1,4,8,64,512]{4,3,0,1,2:T(8,128)} reshape(f32[4,8,64,4,128]{4,3,2,0,1:T(4,128)} %copy.164) | data formatting | bytes 8388608 | tf_op jit(solution)/shard_map/stack;reshape | solution.py:219
  249.6 4.8 %constant_dynamic-update-slice_fusion.2 = f32[2,4,8,64,512]{4,3,0,1,2:T(8,128)} fusion(f32[2,4,8,64,512]{4,3,0,1,2:T(8,128)} %constant_dynamic-update-slice_fusion.3, f32[1,4,8,64,512]{4,3,0,1,2:T(8,128)} %stack_reshape.7), kind=kLoop, calls=%fused_computation.123 | loop fusion | bytes 8388608 | tf_op jit(solution)/shard_map/stack | solution.py:219
  254.4 4.0 convert.13
  262.9 3.7 all-to-all-start.3
  268.6 22.3 %all-to-all-done.3 = bf16[2,8,1,64,512]{4,3,0,2,1:T(8,128)(2,1)S(1)} async-done(((bf16[2,8,1,64,512]{4,3,0,2,1:T(8,128)(2,1)}), bf16[2,8,1,64,512]{4,3,0,2,1:T(8,128)(2,1)S(1)}, u32[]{:S(2)}, u32[]{:S(2)}) %all-to-all-start.3) | async-done | bytes 1048608 | tf_op jit(solution)/shard_map/all_to_all | solution.py:238
  290.9 5.1 %all-to-all-start.4 = ((bf16[2,8,1,64,512]{4,3,0,2,1:T(8,128)(2,1)}), bf16[2,8,1,64,512]{4,3,0,2,1:T(8,128)(2,1)}, u32[]{:S(2)}, u32[]{:S(2)}) async-start(bf16[2,8,1,64,512]{4,3,0,2,1:T(8,128)(2,1)} %copy.173), calls=%async_computation.4 | async-start | bytes 2097152 | tf_op jit(solution)/shard_map/all_to_all | solution.py:238
  301.3 19.4 %all-to-all-done.4 = bf16[2,8,1,64,512]{4,3,0,2,1:T(8,128)(2,1)} async-done(((bf16[2,8,1,64,512]{4,3,0,2,1:T(8,128)(2,1)}), bf16[2,8,1,64,512]{4,3,0,2,1:T(8,128)(2,1)}, u32[]{:S(2)}, u32[]{:S(2)}) %all-to-all-start.4) | async-done | bytes 1048608 | tf_op jit(solution)/shard_map/all_to_all | solution.py:238
  320.6 5.1 %all-to-all-start.5 = ((bf16[2,8,1,64,512]{4,3,0,2,1:T(8,128)(2,1)}), bf16[2,8,1,64,512]{4,3,0,2,1:T(8,128)(2,1)}, u32[]{:S(2)}, u32[]{:S(2)}) async-start(bf16[2,8,1,64,512]{4,3,0,2,1:T(8,128)(2,1)} %copy.176), calls=%async_computation.5 | async-start | bytes 2097152 | tf_op jit(solution)/shard_map/all_to_all | solution.py:238
  327.9 3.7 collective-permute-start.2
  334.1 2.5 fusion.48
  336.6 4.3 copy.162
  340.9 2.8 convert_element_type.53
  346.5 2.9 copy.167
  350.6 6.1 %scatter-add.9 = f32[2,4,64,512]{3,1,2,0:T(4,128)} dynamic-update-slice(f32[2,4,64,512]{3,1,2,0:T(4,128)} %copy.167, f32[2,1,64,512]{3,1,2,0:T(1,128)S(1)} %copy_add_fusion, s32[]{:T(128)} %constant.241.clone.1, s32[]{:T(128)} %constant.245.clone.1, s32[]{:T(128)} %constant.241.clone.1, s32[]{:T(128)} %constant.241.clone.1) | dynamic-update-slice | bytes 524292 | tf_op jit(solution)/shard_map/scatter-add | solution.py:226
  356.8 54.0 %all-reduce.6.cloned.1.call-done = f32[2,2,64,512]{3,1,2,0:T(2,128)} async-done(((f32[2,2,64,512]{3,1,2,0:T(2,128)}), f32[2,2,64,512]{3,1,2,0:T(2,128)}) %all-reduce.6.cloned.1.call-update) | async-done | bytes 524304 | tf_op jit(solution)/shard_map/psum | solution.py:228
  410.8 2.6 fusion.45
  415.5 3.0 fusion.43
  421.4 2.5 collective-permute-start.4
  424.0 30.4 %collective-permute-done.4 = bf16[256,5120]{1,0:T(8,128)(2,1)S(1)} collective-permute-done((bf16[256,5120]{1,0:T(8,128)(2,1)S(1)}, bf16[256,5120]{1,0:T(8,128)(2,1)S(1)}, u32[]{:S(2)}, u32[]{:S(2)}) %collective-permute-start.4) | collective-permute-done | bytes 2621472 | tf_op jit(solution)/shard_map/ppermute | solution.py:35
  (198 shorter events, 100.1 us)
Async XLA Ops:
  7.2 17.0 %copy-start.20 = (s32[1,2]{1,0:T(1,128)S(1)}, s32[1,2]{1,0:T(1,128)}, u32[]{:S(2)}) copy-start(s32[1,2]{1,0:T(1,128)} %param.20) | copy-start | bytes 28
  9.2 83.6 %collective-permute-start = (bf16[2,64,512]{2,1,0:T(8,128)(2,1)S(1)}, bf16[2,64,512]{2,1,0:T(8,128)(2,1)S(1)}, u32[]{:S(2)}, u32[]{:S(2)}) collective-permute-start(bf16[2,64,512]{2,1,0:T(8,128)(2,1)S(1)} %get-tuple-element.194), channel_id=1, source_target_pairs={{0,1},{1,2},{2,3},{3,4},{4,5},{5,6},{6,7},{8,9},{9,10},{10,11},{11... | collective-permute-start | bytes 393224 | tf_op jit(solution)/shard_map/ppermute | solution.py:21
  13.1 79.7 %collective-permute-start.1 = (bf16[2,64,512]{2,1,0:T(8,128)(2,1)S(1)}, bf16[2,64,512]{2,1,0:T(8,128)(2,1)S(1)}, u32[]{:S(2)}, u32[]{:S(2)}) collective-permute-start(bf16[2,64,512]{2,1,0:T(8,128)(2,1)S(1)} %get-tuple-element.195), channel_id=1, source_target_pairs={{1,0},{2,1},{3,2},{4,3},{5,4},{6,5},{7,6},{9,8},{10,9},{11,10},{12... | collective-permute-start | bytes 393224 | tf_op jit(solution)/shard_map/ppermute | solution.py:22
  15.9 15.9 %copy-start.5 = (pred[8]{0:T(512)(128)(4,1)}, pred[8]{0:T(512)(128)(4,1)S(1)}, u32[]{:S(2)}) copy-start(pred[8]{0:T(512)(128)(4,1)S(1)} %get-tuple-element.173) | copy-start | bytes 28
  15.9 15.9 %copy-start.11 = (s32[8]{0:T(128)}, s32[8]{0:T(128)S(1)}, u32[]{:S(2)}) copy-start(s32[8]{0:T(128)S(1)} %fusion.79) | copy-start | bytes 100
  17.7 33.3 %all-to-all-start = ((bf16[2,8,1,64,512]{4,3,0,2,1:T(8,128)(2,1)}), bf16[2,8,1,64,512]{4,3,0,2,1:T(8,128)(2,1)S(1)}, u32[]{:S(2)}, u32[]{:S(2)}) async-start(bf16[2,8,1,64,512]{4,3,0,2,1:T(8,128)(2,1)} %fusion.54), calls=%async_computation | async-start | bytes 2097152 | tf_op jit(solution)/shard_map/all_to_all | solution.py:197
  24.1 92.9 %all-reduce.8.cloned.1.call-start = ((), (), s32[]{:S(2)}) async-start(), calls=%async_computation.7 | async-start | bytes 524288 | tf_op jit(solution)/shard_map/psum | solution.py:29
  30.8 20.3 %copy-start.7 = (pred[8]{0:T(512)(128)(4,1)}, pred[8]{0:T(512)(128)(4,1)S(1)}, u32[]{:S(2)}) copy-start(pred[8]{0:T(512)(128)(4,1)S(1)} %get-tuple-element.171) | copy-start | bytes 28
  30.8 20.2 %copy-start.13 = (s32[8]{0:T(128)}, s32[8]{0:T(128)S(1)}, u32[]{:S(2)}) copy-start(s32[8]{0:T(128)S(1)} %fusion.83) | copy-start | bytes 100
  31.8 24.8 %copy-start.22 = (s32[1,8]{1,0:T(1,128)S(1)}, s32[1,8]{1,0:T(1,128)}, u32[]{:S(2)}) copy-start(s32[1,8]{1,0:T(1,128)} %param.21) | copy-start | bytes 100
  32.6 27.7 %copy-start.9 = (pred[8]{0:T(512)(128)(4,1)}, pred[8]{0:T(512)(128)(4,1)S(1)}, u32[]{:S(2)}) copy-start(pred[8]{0:T(512)(128)(4,1)S(1)} %get-tuple-element.169) | copy-start | bytes 28
  32.7 27.7 %copy-start.15 = (s32[8]{0:T(128)}, s32[8]{0:T(128)S(1)}, u32[]{:S(2)}) copy-start(s32[8]{0:T(128)S(1)} %fusion.87) | copy-start | bytes 100
  51.1 30.9 %all-to-all-start.1 = ((bf16[2,8,1,64,512]{4,3,0,2,1:T(8,128)(2,1)}), bf16[2,8,1,64,512]{4,3,0,2,1:T(8,128)(2,1)S(1)}, u32[]{:S(2)}, u32[]{:S(2)}) async-start(bf16[2,8,1,64,512]{4,3,0,2,1:T(8,128)(2,1)} %fusion.53), calls=%async_computation.1 | async-start | bytes 2097152 | tf_op jit(solution)/shard_map/all_to_all | solution.py:197
  82.0 42.5 %all-to-all-start.2 = ((bf16[2,8,1,64,512]{4,3,0,2,1:T(8,128)(2,1)}), bf16[2,8,1,64,512]{4,3,0,2,1:T(8,128)(2,1)}, u32[]{:S(2)}, u32[]{:S(2)}) async-start(bf16[2,8,1,64,512]{4,3,0,2,1:T(8,128)(2,1)} %fusion.52), calls=%async_computation.2 | async-start | bytes 2097152 | tf_op jit(solution)/shard_map/all_to_all | solution.py:197
  87.4 3.6 copy-start.3
  148.6 3.6 copy-start.4
  168.0 3.6 copy-start.4
  187.3 3.6 copy-start.4
  206.7 3.6 copy-start.4
  233.6 5.0 %copy-start.1 = (f32[4,4,8,64,128]{4,3,2,1,0:T(8,128)S(1)}, f32[4,4,8,64,128]{4,3,2,1,0:T(8,128)}, u32[]{:S(2)}) copy-start(f32[4,4,8,64,128]{4,3,2,1,0:T(8,128)} %get-tuple-element.79) | copy-start | bytes 12582916
  258.4 2.0 copy-start
  260.4 0.6 copy-start.19
  260.5 6.2 %copy-start.18 = (s32[4]{0:T(128)S(1)}, s32[4]{0:T(128)}, u32[]{:S(2)}) copy-start(s32[4]{0:T(128)} %get-tuple-element.206) | copy-start | bytes 52
  262.9 33.1 %copy-start.21 = (s32[1,2]{1,0:T(1,128)S(1)}, s32[1,2]{1,0:T(1,128)}, u32[]{:S(2)}) copy-start(s32[1,2]{1,0:T(1,128)} %param.20) | copy-start | bytes 28
  262.9 28.0 %all-to-all-start.3 = ((bf16[2,8,1,64,512]{4,3,0,2,1:T(8,128)(2,1)}), bf16[2,8,1,64,512]{4,3,0,2,1:T(8,128)(2,1)S(1)}, u32[]{:S(2)}, u32[]{:S(2)}) async-start(bf16[2,8,1,64,512]{4,3,0,2,1:T(8,128)(2,1)} %copy.170), calls=%async_computation.3 | async-start | bytes 2097152 | tf_op jit(solution)/shard_map/all_to_all | solution.py:238
  266.6 29.6 %copy-start.17 = (s32[4]{0:T(128)S(1)}, s32[4]{0:T(128)}, u32[]{:S(2)}) copy-start(s32[4]{0:T(128)} %get-tuple-element.204) | copy-start | bytes 52
  290.9 10.3 %copy-start.2 = (bf16[2,8,1,64,512]{4,3,0,2,1:T(8,128)(2,1)}, bf16[2,8,1,64,512]{4,3,0,2,1:T(8,128)(2,1)S(1)}, u32[]{:S(2)}) copy-start(bf16[2,8,1,64,512]{4,3,0,2,1:T(8,128)(2,1)S(1)} %all-to-all-done.3) | copy-start | bytes 3145732
  290.9 29.7 %all-to-all-start.4 = ((bf16[2,8,1,64,512]{4,3,0,2,1:T(8,128)(2,1)}), bf16[2,8,1,64,512]{4,3,0,2,1:T(8,128)(2,1)}, u32[]{:S(2)}, u32[]{:S(2)}) async-start(bf16[2,8,1,64,512]{4,3,0,2,1:T(8,128)(2,1)} %copy.173), calls=%async_computation.4 | async-start | bytes 2097152 | tf_op jit(solution)/shard_map/all_to_all | solution.py:238
  320.6 97.9 %all-to-all-start.5 = ((bf16[2,8,1,64,512]{4,3,0,2,1:T(8,128)(2,1)}), bf16[2,8,1,64,512]{4,3,0,2,1:T(8,128)(2,1)}, u32[]{:S(2)}, u32[]{:S(2)}) async-start(bf16[2,8,1,64,512]{4,3,0,2,1:T(8,128)(2,1)} %copy.176), calls=%async_computation.5 | async-start | bytes 2097152 | tf_op jit(solution)/shard_map/all_to_all | solution.py:238
  325.7 85.0 %all-reduce.6.cloned.1.call-start = ((), (), s32[]{:S(2)}) async-start(), calls=%async_computation.6 | async-start | bytes 1048576 | tf_op jit(solution)/shard_map/psum | solution.py:228
  327.9 15.9 %collective-permute-start.2 = (bf16[2,64,512]{2,1,0:T(8,128)(2,1)S(1)}, bf16[2,64,512]{2,1,0:T(8,128)(2,1)}, u32[]{:S(2)}, u32[]{:S(2)}) collective-permute-start(bf16[2,64,512]{2,1,0:T(8,128)(2,1)S(1)} %get-tuple-element.184), channel_id=1, source_target_pairs={{0,1},{1,2},{2,3},{3,4},{4,5},{5,6},{6,7},{8,9},{9,10},{10,11},{11... | collective-permute-start | bytes 393224 | tf_op jit(solution)/shard_map/ppermute | solution.py:21
  331.6 12.2 %collective-permute-start.3 = (bf16[2,64,512]{2,1,0:T(8,128)(2,1)}, bf16[2,64,512]{2,1,0:T(8,128)(2,1)}, u32[]{:S(2)}, u32[]{:S(2)}) collective-permute-start(bf16[2,64,512]{2,1,0:T(8,128)(2,1)} %get-tuple-element.185), channel_id=1, source_target_pairs={{1,0},{2,1},{3,2},{4,3},{5,4},{6,5},{7,6},{9,8},{10,9},{11,10},{12... | collective-permute-start | bytes 393224 | tf_op jit(solution)/shard_map/ppermute | solution.py:22
  343.7 69.7 %copy-start.6 = (pred[8]{0:T(512)(128)(4,1)S(1)}, pred[8]{0:T(512)(128)(4,1)}, u32[]{:S(2)}) copy-start(pred[8]{0:T(512)(128)(4,1)} %copy-done.5) | copy-start | bytes 28
  343.8 69.7 %copy-start.12 = (s32[8]{0:T(128)S(1)}, s32[8]{0:T(128)}, u32[]{:S(2)}) copy-start(s32[8]{0:T(128)} %copy-done.11) | copy-start | bytes 100
  349.3 66.1 %copy-start.8 = (pred[8]{0:T(512)(128)(4,1)S(1)}, pred[8]{0:T(512)(128)(4,1)}, u32[]{:S(2)}) copy-start(pred[8]{0:T(512)(128)(4,1)} %copy-done.7) | copy-start | bytes 28
  349.4 66.1 %copy-start.14 = (s32[8]{0:T(128)S(1)}, s32[8]{0:T(128)}, u32[]{:S(2)}) copy-start(s32[8]{0:T(128)} %copy-done.13) | copy-start | bytes 100
  356.8 61.8 %copy-start.10 = (pred[8]{0:T(512)(128)(4,1)S(1)}, pred[8]{0:T(512)(128)(4,1)}, u32[]{:S(2)}) copy-start(pred[8]{0:T(512)(128)(4,1)} %copy-done.9) | copy-start | bytes 28
  356.8 61.8 %copy-start.16 = (s32[8]{0:T(128)S(1)}, s32[8]{0:T(128)}, u32[]{:S(2)}) copy-start(s32[8]{0:T(128)} %copy-done.15) | copy-start | bytes 100
  421.4 33.0 %collective-permute-start.4 = (bf16[256,5120]{1,0:T(8,128)(2,1)S(1)}, bf16[256,5120]{1,0:T(8,128)(2,1)S(1)}, u32[]{:S(2)}, u32[]{:S(2)}) collective-permute-start(bf16[256,5120]{1,0:T(8,128)(2,1)S(1)} %pad_maximum_fusion), channel_id=1, source_target_pairs={{8,0},{16,8},{24,16},{0,24},{9,1},{17,9},{25,17},{1,25},{10,2},{18... | collective-permute-start | bytes 7864328 | tf_op jit(solution)/shard_map/ppermute | solution.py:35
Sparse Core Ops, SparseCore 0:
  30.9 86.1 all-reduce.7
  334.3 76.4 all-reduce.5
where the time goes:
time: 465 us; the launch traced here: 463 us
  waiting for transfers between devices  185 us (40%)
  local copies, waits for them, and re-layouts  112 us (24%)
  matrix products  73.1 us (16%)
  starting transfers between devices  43.5 us (9%)
  other arithmetic  30.4 us (7%)
  between operations  19.9 us (4%)
    psum x1, waiting for transfers between devices, body(): global_total = lax.psum(global_part, 'seq')  54 us
    all_to_all x3, waiting for transfers between devices, body(): lax.all_to_all(place_terms(random_terms[:, :, slot_num], slot_plans[slot_...  41.7 us
    all_to_all x3, waiting for transfers between devices, body(): lax.all_to_all(serve_tiles(own_blocks, slot_plan), 'seq', split_axis=1, c...  37.1 us
    ppermute x1, waiting for transfers between devices, from_behind(): return lax.ppermute(block, axis, route)  30.4 us
    unnamed x56, local copies, waits for them, and re-layouts  24.8 us
    psum x1, waiting for transfers between devices, broadcast(): return lax.psum(jnp.where(mine, array, jnp.zeros_like(array)), axis)  21.6 us
    all_to_all x3, starting transfers between devices, body(): lax.all_to_all(serve_tiles(own_blocks, slot_plan), 'seq', split_axis=1, c...  16.5 us
    another operation x3, local copies, waits for them, and re-layouts, body(): contrib = jnp.stack([key_terms, value_terms])  15.8 us
  transfers between devices with their start and end apart: 13, of which 7 were waited for; matrix products, arithmetic and copies ran while one was open for 15% of the time, Pallas kernels for 0%

commit v1 on v0

--- a/solution.py
+++ b/solution.py
@@ -3,6 +3,7 @@
 import jax
 import jax.numpy as jnp
 from jax import lax
+from jax.experimental import pallas as pl
 from jax.sharding import PartitionSpec as P
 
 HDIM = 128
@@ -35,67 +36,88 @@
     return lax.ppermute(block, axis, route)
 
 
+def attention_kernel(q_ref, g_ref, k_ref, v_ref, live_ref, dq_ref, dk_ref, dv_ref):
+    block_len, width = q_ref.shape
+    group = width // HDIM
+    ntiles = k_ref.shape[0]
+    score_scale = 1.0 / math.sqrt(HDIM)
+    query = q_ref[...]
+    grad = g_ref[...]
+    query_rows = jnp.concatenate(
+        [query[:, g * HDIM : (g + 1) * HDIM] for g in range(group)], axis=0
+    )
+    grad_rows = jnp.concatenate([grad[:, g * HDIM : (g + 1) * HDIM] for g in range(group)], axis=0)
+    key_rows = k_ref[...].reshape(ntiles * block_len, HDIM)
+    value_rows = v_ref[...].reshape(ntiles * block_len, HDIM)
+    live = live_ref[...] > 0.5
+    contract_last = (((1,), (1,)), ((), ()))
+    contract_first = (((0,), (0,)), ((), ()))
+    scores = (
+        lax.dot_general(query_rows, key_rows, contract_last, preferred_element_type=jnp.float32)
+        * score_scale
+    )
+    scores = jnp.where(live, scores, -1e30)
+    row_max = jnp.max(scores, axis=1, keepdims=True)
+    shifted = jnp.exp(scores - row_max)
+    total = jnp.sum(shifted, axis=1, keepdims=True)
+    probs = shifted * (1.0 / total)
+    probs_low = probs.astype(jnp.bfloat16)
+    output = jnp.dot(probs_low, value_rows, preferred_element_type=jnp.float32)
+    row_dot = jnp.sum(grad_rows.astype(jnp.float32) * output, axis=1, keepdims=True)
+    prob_grad = lax.dot_general(
+        grad_rows, value_rows, contract_last, preferred_element_type=jnp.float32
+    )
+    score_grad = (probs * (prob_grad - row_dot)).astype(jnp.bfloat16)
+    query_grad = jnp.dot(score_grad, key_rows, preferred_element_type=jnp.float32) * score_scale
+    key_grad = (
+        lax.dot_general(score_grad, query_rows, contract_first, preferred_element_type=jnp.float32)
+        * score_scale
+    )
+    value_grad = lax.dot_general(
+        probs_low, grad_rows, contract_first, preferred_element_type=jnp.float32
+    )
+    for g in range(group):
+        dq_ref[:, g * HDIM : (g + 1) * HDIM] = query_grad[g * block_len : (g + 1) * block_len].astype(
+            dq_ref.dtype
+        )
+    dk_ref[...] = key_grad.reshape(ntiles, block_len, HDIM)
+    dv_ref[...] = value_grad.reshape(ntiles, block_len, HDIM)
+
+
 def block_backward(query_rows, grad_rows, key_tiles, value_tiles, key_live):
     nblocks, block_len, qwidth = query_rows.shape
     ntiles = key_tiles.shape[1]
     kwidth = key_tiles.shape[-1]
     heads_kv = kwidth // HDIM
-    group = qwidth // kwidth
-    score_scale = 1.0 / math.sqrt(HDIM)
-    query_heads = jnp.moveaxis(query_rows.reshape(nblocks, block_len, heads_kv, group, HDIM), 2, 0)
-    grad_heads = jnp.moveaxis(grad_rows.reshape(nblocks, block_len, heads_kv, group, HDIM), 2, 0)
-    key_heads = jnp.moveaxis(key_tiles.reshape(nblocks, ntiles, block_len, heads_kv, HDIM), 3, 0)
-    value_heads = jnp.moveaxis(
-        value_tiles.reshape(nblocks, ntiles, block_len, heads_kv, HDIM), 3, 0
-    )
-    live_mask = key_live[:, None, None, :, :]
-
-    def one_head(inputs):
-        query_one, grad_one, key_one, value_one = inputs
-        scores = (
-            jnp.einsum("bqgd,btkd->bgqtk", query_one, key_one, preferred_element_type=jnp.float32)
-            * score_scale
-        )
-        scores = jnp.where(live_mask, scores, -1e30)
-        row_max = jnp.max(scores, axis=(3, 4), keepdims=True)
-        log_total = row_max + jnp.log(
-            jnp.sum(jnp.exp(scores - row_max), axis=(3, 4), keepdims=True)
-        )
-        probs = jnp.exp(scores - log_total)
-        probs_low = probs.astype(jnp.bfloat16)
-        output = jnp.einsum(
-            "bgqtk,btkd->bqgd", probs_low, value_one, preferred_element_type=jnp.float32
-        )
-        row_dot = jnp.sum(grad_one * output, axis=-1)
-        prob_grad = jnp.einsum(
-            "bqgd,btkd->bgqtk", grad_one, value_one, preferred_element_type=jnp.float32
-        )
-        score_grad = (
-            probs * (prob_grad - jnp.transpose(row_dot, (0, 2, 1))[:, :, :, None, None])
-        ).astype(jnp.bfloat16)
-        query_grad = (
-            jnp.einsum("bgqtk,btkd->bqgd", score_grad, key_one, preferred_element_type=jnp.float32)
-            * score_scale
-        )
-        key_grad = (
-            jnp.einsum(
-                "bgqtk,bqgd->btkd", score_grad, query_one, preferred_element_type=jnp.float32
-            )
-            * score_scale
-        )
-        value_grad = jnp.einsum(
-            "bgqtk,bqgd->btkd", probs_low, grad_one, preferred_element_type=jnp.float32
-        )
-        return (query_grad, key_grad, value_grad)
-
-    query_grad, key_grad, value_grad = lax.map(
-        one_head, (query_heads, grad_heads, key_heads, value_heads)
-    )
-    return (
-        jnp.moveaxis(query_grad, 0, 2).reshape(nblocks, block_len, qwidth),
-        jnp.moveaxis(key_grad, 0, 3).reshape(nblocks, ntiles, block_len, kwidth),
-        jnp.moveaxis(value_grad, 0, 3).reshape(nblocks, ntiles, block_len, kwidth),
-    )
+    group_width = qwidth // heads_kv
+    live = key_live.reshape(nblocks, 1, ntiles * block_len).astype(jnp.float32)
+    row_spec = pl.BlockSpec((block_len, group_width), lambda b, h: (b, h))
+    tile_spec = pl.BlockSpec((None, ntiles, block_len, HDIM), lambda b, h: (b, 0, 0, h))
+    live_spec = pl.BlockSpec((None, 1, ntiles * block_len), lambda b, h: (b, 0, 0))
+    flops = 12 * nblocks * heads_kv * (group_width // HDIM) * block_len * ntiles * block_len * HDIM
+    query_grad, key_grad, value_grad = pl.pallas_call(
+        attention_kernel,
+        grid=(nblocks, heads_kv),
+        in_specs=[row_spec, row_spec, tile_spec, tile_spec, live_spec],
+        out_specs=[row_spec, tile_spec, tile_spec],
+        out_shape=[
+            jax.ShapeDtypeStruct((nblocks * block_len, qwidth), jnp.bfloat16),
+            jax.ShapeDtypeStruct((nblocks, ntiles, block_len, kwidth), jnp.float32),
+            jax.ShapeDtypeStruct((nblocks, ntiles, block_len, kwidth), jnp.float32),
+        ],
+        cost_estimate=pl.CostEstimate(
+            flops=flops,
+            transcendentals=nblocks * qwidth // HDIM * block_len * ntiles * block_len,
+            bytes_accessed=nblocks * block_len * qwidth * 6 + nblocks * ntiles * block_len * kwidth * 12,
+        ),
+    )(
+        query_rows.reshape(nblocks * block_len, qwidth),
+        grad_rows.reshape(nblocks * block_len, qwidth),
+        key_tiles,
+        value_tiles,
+        live,
+    )
+    return (query_grad, key_grad, value_grad)
 
 
 def request_plan(request_lists, this_shard, query_blocks):
@@ -245,7 +267,7 @@
         local_sum = local_sum + absorb_terms(returned, slot_plans[slot_num], query_blocks)
     key_grad = local_sum[0].reshape(shard_tokens, kwidth).astype(jnp.bfloat16)
     value_grad = local_sum[1].reshape(shard_tokens, kwidth).astype(jnp.bfloat16)
-    query_low = query_grad.reshape(shard_tokens, qwidth).astype(jnp.bfloat16)
+    query_low = query_grad
     packed = jnp.concatenate([query_low, key_grad, value_grad], axis=-1)
     handed = from_behind(packed, "section", -1)
     return (

time: 465 us -> 373 us (0.80)
  local copies, waits for them, and re-layouts: 112 us -> 38.9 us
  matrix products: 73.1 us -> 10.1 us
  Pallas kernels: 0 us -> 27.5 us
  waiting for transfers between devices: 185 us -> 209 us
  other arithmetic: 30.4 us -> 22.4 us
    dot_general x24 -> x0, matrix products: 63 us -> none  [the longest x4 14.3 us: one_head(): jnp.einsum('bgqtk,bqgd->btkd', probs_low, grad_one, preferred_element_typ...]
    pallas_call x0 -> x1, Pallas kernels: none -> 27.5 us  [block_backward(): pl.pallas_call(attention_kernel, grid=(nblocks, heads_kv), in_specs=[row_...]
    another operation x6 -> x0, local copies, waits for them, and re-layouts: 22.8 us -> none  [the longest x3 15.8 us: body(): contrib = jnp.stack([key_terms, value_terms])]
    psum x1, waiting for transfers between devices: 54 us -> 70.7 us  [body(): global_total = lax.psum(global_part, 'seq')]
    unnamed x56 -> x35, local copies, waits for them, and re-layouts: 24.8 us -> 9.36 us
    transpose x2 -> x0, local copies, waits for them, and re-layouts: 13.3 us -> none  [the longest x1 7.75 us: block_backward(): jnp.moveaxis(key_grad, 0, 3).reshape(nblocks, ntiles, block_len, kwidth)]
    scatter-add x2 -> x0, local copies, waits for them, and re-layouts: 9.02 us -> none  [the longest x1 6.14 us: body(): local_sum = local_sum.at[:, query_blocks - 1].add(edge_in[:, 3 * BLK:])]
    reduce_sum x4 -> x0, other arithmetic: 8.8 us -> none  [one_head(): jnp.sum(jnp.exp(scores - row_max), axis=(3, 4), keepdims=True)]
  transfers between devices with their start and end apart: 13 -> 13, of which waited for: 7 -> 7; matrix products, arithmetic and copies ran while one was open for 15% -> 12% of each run, Pallas kernels for 0% -> 0%
where the time goes in v1:
time: 373 us; the launch traced here: 372 us
  waiting for transfers between devices  209 us (56%)
  starting transfers between devices  43.9 us (12%)
  local copies, waits for them, and re-layouts  38.9 us (10%)
  Pallas kernels  27.5 us (7%)
  other arithmetic  22.4 us (6%)
  between operations  19.8 us (5%)
  matrix products  10.1 us (3%)
    psum x1, waiting for transfers between devices, body(): global_total = lax.psum(global_part, 'seq')  70.7 us
    all_to_all x3, waiting for transfers between devices, body(): lax.all_to_all(place_terms(random_terms[:, :, slot_num], slot_plans[slot_...  43.7 us
    all_to_all x3, waiting for transfers between devices, body(): lax.all_to_all(serve_tiles(own_blocks, slot_plan), 'seq', split_axis=1, c...  37.1 us
    ppermute x1, waiting for transfers between devices, from_behind(): return lax.ppermute(block, axis, route)  30.4 us
    psum x1, waiting for transfers between devices, broadcast(): return lax.psum(jnp.where(mine, array, jnp.zeros_like(array)), axis)  27.5 us
    pallas_call x1, Pallas kernels, block_backward(): pl.pallas_call(attention_kernel, grid=(nblocks, heads_kv), in_specs=[row_...  27.5 us
    all_to_all x3, starting transfers between devices, body(): lax.all_to_all(serve_tiles(own_blocks, slot_plan), 'seq', split_axis=1, c...  15.7 us
    all_to_all x3, starting transfers between devices, body(): lax.all_to_all(place_terms(random_terms[:, :, slot_num], slot_plans[slot_...  13.8 us
  transfers between devices with their start and end apart: 13, of which 7 were waited for; matrix products, arithmetic and copies ran while one was open for 12% of the time, Pallas kernels for 0%

profile of v1, /device:TPU:1, one launch (start us, length us, event | category | flops | bytes accessed | tf_op | source)
XLA Modules:
  0.0 372.2 jit_solution(13965432448529210250)
XLA Ops:
  7.2 1.0 constant_dynamic-update-slice_fusion.1
  8.2 1.0 constant_dynamic-update-slice_fusion
  9.2 1.3 collective-permute-start.1
  10.5 4.6 %collective-permute-start = (bf16[2,64,512]{2,1,0:T(8,128)(2,1)S(1)}, bf16[2,64,512]{2,1,0:T(8,128)(2,1)S(1)}, u32[]{:S(2)}, u32[]{:S(2)}) collective-permute-start(bf16[2,64,512]{2,1,0:T(8,128)(2,1)S(1)} %get-tuple-element.62), channel_id=1, source_target_pairs={{0,1},{1,2},{2,3},{3,4},{4,5},{5,6},{6,7},{8,9},{9,10},{10,11},{11... | collective-permute-start | bytes 393224 | tf_op jit(solution)/shard_map/ppermute | solution.py:22
  17.2 1.2 fusion.15
  18.3 5.7 %all-to-all-start = ((bf16[2,8,1,64,512]{4,3,0,2,1:T(8,128)(2,1)}), bf16[2,8,1,64,512]{4,3,0,2,1:T(8,128)(2,1)S(1)}, u32[]{:S(2)}, u32[]{:S(2)}) async-start(bf16[2,8,1,64,512]{4,3,0,2,1:T(8,128)(2,1)} %fusion.15), calls=%async_computation | async-start | bytes 2097152 | tf_op jit(solution)/shard_map/all_to_all | solution.py:219
  32.9 1.2 fusion.14
  34.1 16.8 %all-to-all-done = bf16[2,8,1,64,512]{4,3,0,2,1:T(8,128)(2,1)S(1)} async-done(((bf16[2,8,1,64,512]{4,3,0,2,1:T(8,128)(2,1)}), bf16[2,8,1,64,512]{4,3,0,2,1:T(8,128)(2,1)S(1)}, u32[]{:S(2)}, u32[]{:S(2)}) %all-to-all-start) | async-done | bytes 1048608 | tf_op jit(solution)/shard_map/all_to_all | solution.py:219
  50.9 5.3 %all-to-all-start.1 = ((bf16[2,8,1,64,512]{4,3,0,2,1:T(8,128)(2,1)}), bf16[2,8,1,64,512]{4,3,0,2,1:T(8,128)(2,1)S(1)}, u32[]{:S(2)}, u32[]{:S(2)}) async-start(bf16[2,8,1,64,512]{4,3,0,2,1:T(8,128)(2,1)} %fusion.14), calls=%async_computation.1 | async-start | bytes 2097152 | tf_op jit(solution)/shard_map/all_to_all | solution.py:219
  56.2 1.6 gather_fusion.5
  59.2 2.4 fusion.13
  61.6 20.2 %all-to-all-done.1 = bf16[2,8,1,64,512]{4,3,0,2,1:T(8,128)(2,1)S(1)} async-done(((bf16[2,8,1,64,512]{4,3,0,2,1:T(8,128)(2,1)}), bf16[2,8,1,64,512]{4,3,0,2,1:T(8,128)(2,1)S(1)}, u32[]{:S(2)}, u32[]{:S(2)}) %all-to-all-start.1) | async-done | bytes 1048608 | tf_op jit(solution)/shard_map/all_to_all | solution.py:219
  81.8 4.8 %all-to-all-start.2 = ((bf16[2,8,1,64,512]{4,3,0,2,1:T(8,128)(2,1)}), bf16[2,8,1,64,512]{4,3,0,2,1:T(8,128)(2,1)}, u32[]{:S(2)}, u32[]{:S(2)}) async-start(bf16[2,8,1,64,512]{4,3,0,2,1:T(8,128)(2,1)} %fusion.13), calls=%async_computation.2 | async-start | bytes 2097152 | tf_op jit(solution)/shard_map/all_to_all | solution.py:219
  89.3 27.5 %all-reduce.8.cloned.1.call-done = (bf16[2,1,64,512]{3,2,1,0:T(8,128)(2,1)}, bf16[2,1,64,512]{3,2,1,0:T(8,128)(2,1)}) async-done(((bf16[2,1,64,512]{3,2,1,0:T(8,128)(2,1)}, bf16[2,1,64,512]{3,2,1,0:T(8,128)(2,1)}), (bf16[2,1,64,512]{3,2,1,0:T(8,128)(2,1)}, bf16[2,1,64,512]{3,2,1,0:T(8,128)(2,1)})) %all-reduce.8.cloned.1.call-update) | async-done | bytes 262160 | tf_op jit(solution)/shard_map/psum | solution.py:30
  116.8 1.0 pad_maximum_fusion.3
  117.8 1.1 broadcast_dynamic-update-slice_fusion
  118.9 1.1 copy.131
  120.0 1.8 gather_fusion
  124.2 1.3 copy.143
  127.0 4.8 %slice_bitcast_fusion.1 = (bf16[4,8,64,512]{3,2,1,0:T(8,128)(2,1)}, bf16[4,8,64,512]{3,2,1,0:T(8,128)(2,1)}) fusion(bf16[2,4,8,64,512]{4,3,2,1,0:T(8,128)(2,1)} %bitcast_dynamic-update-slice_fusion), kind=kLoop, calls=%fused_computation.23 | loop fusion | bytes 8388608 | tf_op jit(solution)/shard_map/squeeze | solution.py:238
  131.8 27.5 %shard_map.97 = (bf16[256,4096]{1,0:T(8,128)(2,1)}, f32[4,8,64,512]{3,2,1,0:T(8,128)}, f32[4,8,64,512]{3,2,1,0:T(8,128)}) custom-call(bf16[256,4096]{1,0:T(8,128)(2,1)} %bitcast.387, bf16[256,4096]{1,0:T(8,128)(2,1)} %bitcast.388, bf16[4,8,64,512]{3,2,1,0:T(8,128)(2,1)} %get-tuple-element.55.k_ref, bf16[4,8,64,512]{3,2,1,0:T(8,128)(2,1)} %get-tuple-element.54.v_ref, ...), custom_call_target="tpu_custom_call" | custom-call | flops 6442450944 | bytes 18874368 | tf_op jit(solution)/shard_map/pallas_call | solution.py:98
  159.3 4.2 %fusion = bf16[2,4,8,64,512]{4,3,2,1,0:T(8,128)(2,1)S(1)} fusion(f32[1,4,8,64,512]{4,3,2,1,0:T(8,128)} %bitcast.363, f32[1,4,8,64,512]{4,3,2,1,0:T(8,128)} %bitcast.359), kind=kLoop, calls=%fused_computation.18 | loop fusion | flops 2097152 | bytes 12582912 | tf_op jit(solution)/shard_map/convert.6
  163.4 2.0 copy-done.2
  166.4 1.1 copy.167
  167.5 3.6 all-to-all-start.5
  171.9 1.1 copy.162
  173.0 22.3 %all-to-all-done.5 = bf16[2,8,1,64,512]{4,3,0,2,1:T(8,128)(2,1)S(1)} async-done(((bf16[2,8,1,64,512]{4,3,0,2,1:T(8,128)(2,1)}), bf16[2,8,1,64,512]{4,3,0,2,1:T(8,128)(2,1)S(1)}, u32[]{:S(2)}, u32[]{:S(2)}) %all-to-all-start.5) | async-done | bytes 1048608 | tf_op jit(solution)/shard_map/all_to_all | solution.py:260
  195.3 5.2 %all-to-all-start.4 = ((bf16[2,8,1,64,512]{4,3,0,2,1:T(8,128)(2,1)}), bf16[2,8,1,64,512]{4,3,0,2,1:T(8,128)(2,1)}, u32[]{:S(2)}, u32[]{:S(2)}) async-start(bf16[2,8,1,64,512]{4,3,0,2,1:T(8,128)(2,1)} %copy.162), calls=%async_computation.4 | async-start | bytes 2097152 | tf_op jit(solution)/shard_map/all_to_all | solution.py:260
  202.5 1.1 copy.157
  203.6 21.5 %all-to-all-done.4 = bf16[2,8,1,64,512]{4,3,0,2,1:T(8,128)(2,1)} async-done(((bf16[2,8,1,64,512]{4,3,0,2,1:T(8,128)(2,1)}), bf16[2,8,1,64,512]{4,3,0,2,1:T(8,128)(2,1)}, u32[]{:S(2)}, u32[]{:S(2)}) %all-to-all-start.4) | async-done | bytes 1048608 | tf_op jit(solution)/shard_map/all_to_all | solution.py:260
  225.1 5.1 %all-to-all-start.3 = ((bf16[2,8,1,64,512]{4,3,0,2,1:T(8,128)(2,1)}), bf16[2,8,1,64,512]{4,3,0,2,1:T(8,128)(2,1)}, u32[]{:S(2)}, u32[]{:S(2)}) async-start(bf16[2,8,1,64,512]{4,3,0,2,1:T(8,128)(2,1)} %copy.157), calls=%async_computation.3 | async-start | bytes 2097152 | tf_op jit(solution)/shard_map/all_to_all | solution.py:260
  230.2 1.7 fusion.19
  232.9 2.1 slice_bitcast_fusion.12
  235.0 1.3 collective-permute-start.3
  236.3 4.6 %collective-permute-start.2 = (bf16[2,64,512]{2,1,0:T(8,128)(2,1)S(1)}, bf16[2,64,512]{2,1,0:T(8,128)(2,1)}, u32[]{:S(2)}, u32[]{:S(2)}) collective-permute-start(bf16[2,64,512]{2,1,0:T(8,128)(2,1)S(1)} %get-tuple-element.52), channel_id=1, source_target_pairs={{0,1},{1,2},{2,3},{3,4},{4,5},{5,6},{6,7},{8,9},{9,10},{10,11},{11... | collective-permute-start | bytes 393224 | tf_op jit(solution)/shard_map/ppermute | solution.py:22
  241.2 1.3 copy.153
  242.5 1.7 fusion.5
  244.3 1.0 fusion.26
  245.2 1.0 fusion.24
  246.2 70.7 %all-reduce.6.cloned.1.call-done = f32[2,2,64,512]{3,1,2,0:T(2,128)} async-done(((f32[2,2,64,512]{3,1,2,0:T(2,128)}), f32[2,2,64,512]{3,1,2,0:T(2,128)}) %all-reduce.6.cloned.1.call-update) | async-done | bytes 524304 | tf_op jit(solution)/shard_map/psum | solution.py:250
  316.9 3.2 fusion.74
  320.1 1.7 fusion.7
  321.9 3.1 fusion.9
  324.9 2.1 fusion.11
  327.1 2.7 fusion.6
  330.1 2.5 collective-permute-start.4
  332.6 30.4 %collective-permute-done.4 = bf16[256,5120]{1,0:T(8,128)(2,1)S(1)} collective-permute-done((bf16[256,5120]{1,0:T(8,128)(2,1)S(1)}, bf16[256,5120]{1,0:T(8,128)(2,1)S(1)}, u32[]{:S(2)}, u32[]{:S(2)}) %collective-permute-start.4) | collective-permute-done | bytes 2621472 | tf_op jit(solution)/shard_map/ppermute | solution.py:36
  363.1 1.5 slice_bitcast_fusion
  (125 shorter events, 19.8 us)
Async XLA Ops:
  7.2 16.9 %copy-start.5 = (s32[1,2]{1,0:T(1,128)S(1)}, s32[1,2]{1,0:T(1,128)}, u32[]{:S(2)}) copy-start(s32[1,2]{1,0:T(1,128)} %param.18) | copy-start | bytes 28
  9.2 77.5 %collective-permute-start.1 = (bf16[2,64,512]{2,1,0:T(8,128)(2,1)S(1)}, bf16[2,64,512]{2,1,0:T(8,128)(2,1)S(1)}, u32[]{:S(2)}, u32[]{:S(2)}) collective-permute-start(bf16[2,64,512]{2,1,0:T(8,128)(2,1)S(1)} %get-tuple-element.63), channel_id=1, source_target_pairs={{1,0},{2,1},{3,2},{4,3},{5,4},{6,5},{7,6},{9,8},{10,9},{11,10},{12... | collective-permute-start | bytes 393224 | tf_op jit(solution)/shard_map/ppermute | solution.py:23
  10.5 76.2 %collective-permute-start = (bf16[2,64,512]{2,1,0:T(8,128)(2,1)S(1)}, bf16[2,64,512]{2,1,0:T(8,128)(2,1)S(1)}, u32[]{:S(2)}, u32[]{:S(2)}) collective-permute-start(bf16[2,64,512]{2,1,0:T(8,128)(2,1)S(1)} %get-tuple-element.62), channel_id=1, source_target_pairs={{0,1},{1,2},{2,3},{3,4},{4,5},{5,6},{6,7},{8,9},{9,10},{10,11},{11... | collective-permute-start | bytes 393224 | tf_op jit(solution)/shard_map/ppermute | solution.py:22
  18.3 32.6 %all-to-all-start = ((bf16[2,8,1,64,512]{4,3,0,2,1:T(8,128)(2,1)}), bf16[2,8,1,64,512]{4,3,0,2,1:T(8,128)(2,1)S(1)}, u32[]{:S(2)}, u32[]{:S(2)}) async-start(bf16[2,8,1,64,512]{4,3,0,2,1:T(8,128)(2,1)} %fusion.15), calls=%async_computation | async-start | bytes 2097152 | tf_op jit(solution)/shard_map/all_to_all | solution.py:219
  24.0 92.8 %all-reduce.8.cloned.1.call-start = ((), (), s32[]{:S(2)}) async-start(), calls=%async_computation.7 | async-start | bytes 524288 | tf_op jit(solution)/shard_map/psum | solution.py:30
  31.6 26.1 %copy-start.6 = (s32[8]{0:T(128)}, s32[8]{0:T(128)S(1)}, u32[]{:S(2)}) copy-start(s32[8]{0:T(128)S(1)} %fusion.46) | copy-start | bytes 100
  31.7 26.3 %copy-start.12 = (s32[1,8]{1,0:T(1,128)S(1)}, s32[1,8]{1,0:T(1,128)}, u32[]{:S(2)}) copy-start(s32[1,8]{1,0:T(1,128)} %param.19) | copy-start | bytes 100
  32.7 28.9 %copy-start.8 = (s32[8]{0:T(128)}, s32[8]{0:T(128)S(1)}, u32[]{:S(2)}) copy-start(s32[8]{0:T(128)S(1)} %fusion.50) | copy-start | bytes 100
  50.9 30.9 %all-to-all-start.1 = ((bf16[2,8,1,64,512]{4,3,0,2,1:T(8,128)(2,1)}), bf16[2,8,1,64,512]{4,3,0,2,1:T(8,128)(2,1)S(1)}, u32[]{:S(2)}, u32[]{:S(2)}) async-start(bf16[2,8,1,64,512]{4,3,0,2,1:T(8,128)(2,1)} %fusion.14), calls=%async_computation.1 | async-start | bytes 2097152 | tf_op jit(solution)/shard_map/all_to_all | solution.py:219
  81.8 42.4 %all-to-all-start.2 = ((bf16[2,8,1,64,512]{4,3,0,2,1:T(8,128)(2,1)}), bf16[2,8,1,64,512]{4,3,0,2,1:T(8,128)(2,1)}, u32[]{:S(2)}, u32[]{:S(2)}) async-start(bf16[2,8,1,64,512]{4,3,0,2,1:T(8,128)(2,1)} %fusion.13), calls=%async_computation.2 | async-start | bytes 2097152 | tf_op jit(solution)/shard_map/all_to_all | solution.py:219
  163.4 2.0 copy-start.2
  167.5 27.8 %all-to-all-start.5 = ((bf16[2,8,1,64,512]{4,3,0,2,1:T(8,128)(2,1)}), bf16[2,8,1,64,512]{4,3,0,2,1:T(8,128)(2,1)S(1)}, u32[]{:S(2)}, u32[]{:S(2)}) async-start(bf16[2,8,1,64,512]{4,3,0,2,1:T(8,128)(2,1)} %copy.167), calls=%async_computation.5 | async-start | bytes 2097152 | tf_op jit(solution)/shard_map/all_to_all | solution.py:260
  195.3 29.8 %all-to-all-start.4 = ((bf16[2,8,1,64,512]{4,3,0,2,1:T(8,128)(2,1)}), bf16[2,8,1,64,512]{4,3,0,2,1:T(8,128)(2,1)}, u32[]{:S(2)}, u32[]{:S(2)}) async-start(bf16[2,8,1,64,512]{4,3,0,2,1:T(8,128)(2,1)} %copy.162), calls=%async_computation.4 | async-start | bytes 2097152 | tf_op jit(solution)/shard_map/all_to_all | solution.py:260
  225.1 99.9 %all-to-all-start.3 = ((bf16[2,8,1,64,512]{4,3,0,2,1:T(8,128)(2,1)}), bf16[2,8,1,64,512]{4,3,0,2,1:T(8,128)(2,1)}, u32[]{:S(2)}, u32[]{:S(2)}) async-start(bf16[2,8,1,64,512]{4,3,0,2,1:T(8,128)(2,1)} %copy.157), calls=%async_computation.3 | async-start | bytes 2097152 | tf_op jit(solution)/shard_map/all_to_all | solution.py:260
  230.1 86.8 %all-reduce.6.cloned.1.call-start = ((), (), s32[]{:S(2)}) async-start(), calls=%async_computation.6 | async-start | bytes 1048576 | tf_op jit(solution)/shard_map/psum | solution.py:250
  230.2 10.8 %copy-start = (f32[4,8,64,512]{3,2,1,0:T(8,128)S(1)}, f32[4,8,64,512]{3,2,1,0:T(8,128)}, u32[]{:S(2)}) copy-start(f32[4,8,64,512]{3,2,1,0:T(8,128)} %get-tuple-element.32) | copy-start | bytes 12582916
  230.2 10.8 %copy-start.1 = (f32[4,8,64,512]{3,2,1,0:T(8,128)S(1)}, f32[4,8,64,512]{3,2,1,0:T(8,128)}, u32[]{:S(2)}) copy-start(f32[4,8,64,512]{3,2,1,0:T(8,128)} %get-tuple-element.33) | copy-start | bytes 12582916
  235.0 9.2 %collective-permute-start.3 = (bf16[2,64,512]{2,1,0:T(8,128)(2,1)}, bf16[2,64,512]{2,1,0:T(8,128)(2,1)}, u32[]{:S(2)}, u32[]{:S(2)}) collective-permute-start(bf16[2,64,512]{2,1,0:T(8,128)(2,1)} %get-tuple-element.53), channel_id=1, source_target_pairs={{1,0},{2,1},{3,2},{4,3},{5,4},{6,5},{7,6},{9,8},{10,9},{11,10},{12... | collective-permute-start | bytes 393224 | tf_op jit(solution)/shard_map/ppermute | solution.py:23
  236.3 8.0 %collective-permute-start.2 = (bf16[2,64,512]{2,1,0:T(8,128)(2,1)S(1)}, bf16[2,64,512]{2,1,0:T(8,128)(2,1)}, u32[]{:S(2)}, u32[]{:S(2)}) collective-permute-start(bf16[2,64,512]{2,1,0:T(8,128)(2,1)S(1)} %get-tuple-element.52), channel_id=1, source_target_pairs={{0,1},{1,2},{2,3},{3,4},{4,5},{5,6},{6,7},{8,9},{9,10},{10,11},{11... | collective-permute-start | bytes 393224 | tf_op jit(solution)/shard_map/ppermute | solution.py:22
  242.5 74.4 %copy-start.10 = (pred[2]{0:T(512)(128)(4,1)S(1)}, pred[2]{0:T(512)(128)(4,1)}, u32[]{:S(2)}) copy-start(pred[2]{0:T(512)(128)(4,1)} %fusion.90) | copy-start | bytes 10
  242.5 74.4 %copy-start.11 = (s32[2]{0:T(128)S(1)}, s32[2]{0:T(128)}, u32[]{:S(2)}) copy-start(s32[2]{0:T(128)} %and_select_fusion) | copy-start | bytes 28
  242.5 77.6 %copy-start.9 = (s32[8]{0:T(128)S(1)}, s32[8]{0:T(128)}, u32[]{:S(2)}) copy-start(s32[8]{0:T(128)} %copy-done.8) | copy-start | bytes 100
  244.2 77.6 %copy-start.7 = (s32[8]{0:T(128)S(1)}, s32[8]{0:T(128)}, u32[]{:S(2)}) copy-start(s32[8]{0:T(128)} %copy-done.6) | copy-start | bytes 100
  321.9 5.2 %copy-start.3 = (f32[2,64,512,4]{2,3,1,0:T(4,128)S(1)}, f32[2,64,512,4]{2,3,1,0:T(4,128)}, u32[]{:S(2)}) copy-start(f32[2,64,512,4]{2,3,1,0:T(4,128)} %fusion.74) | copy-start | bytes 3145732
  324.9 4.9 %copy-start.4 = (bf16[256,4096]{1,0:T(8,128)(2,1)S(1)}, bf16[256,4096]{1,0:T(8,128)(2,1)}, u32[]{:S(2)}) copy-start(bf16[256,4096]{1,0:T(8,128)(2,1)} %get-tuple-element.31) | copy-start | bytes 6291460
  330.1 33.0 %collective-permute-start.4 = (bf16[256,5120]{1,0:T(8,128)(2,1)S(1)}, bf16[256,5120]{1,0:T(8,128)(2,1)S(1)}, u32[]{:S(2)}, u32[]{:S(2)}) collective-permute-start(bf16[256,5120]{1,0:T(8,128)(2,1)S(1)} %pad_maximum_fusion.1), channel_id=1, source_target_pairs={{8,0},{16,8},{24,16},{0,24},{9,1},{17,9},{25,17},{1,25},{10,2},{18... | collective-permute-start | bytes 7864328 | tf_op jit(solution)/shard_map/ppermute | solution.py:36
Sparse Core Ops, SparseCore 0:
  30.7 86.0 all-reduce.7
  242.6 74.2 all-reduce.5

commit v2 on v1

--- a/solution.py
+++ b/solution.py
@@ -36,7 +36,7 @@
     return lax.ppermute(block, axis, route)
 
 
-def attention_kernel(q_ref, g_ref, k_ref, v_ref, live_ref, dq_ref, dk_ref, dv_ref):
+def attention_kernel(q_ref, g_ref, k_ref, v_ref, live_ref, dq_ref, dkv_ref):
     block_len, width = q_ref.shape
     group = width // HDIM
     ntiles = k_ref.shape[0]
@@ -80,44 +80,38 @@
         dq_ref[:, g * HDIM : (g + 1) * HDIM] = query_grad[g * block_len : (g + 1) * block_len].astype(
             dq_ref.dtype
         )
-    dk_ref[...] = key_grad.reshape(ntiles, block_len, HDIM)
-    dv_ref[...] = value_grad.reshape(ntiles, block_len, HDIM)
-
-
-def block_backward(query_rows, grad_rows, key_tiles, value_tiles, key_live):
-    nblocks, block_len, qwidth = query_rows.shape
-    ntiles = key_tiles.shape[1]
-    kwidth = key_tiles.shape[-1]
+    dkv_ref[:, 0] = key_grad.reshape(ntiles, block_len, HDIM)
+    dkv_ref[:, 1] = value_grad.reshape(ntiles, block_len, HDIM)
+
+
+def block_backward(query_rows, grad_rows, kv_tiles, key_live):
+    shard_tokens, qwidth = query_rows.shape
+    nblocks, ntiles, _, block_len, kwidth = kv_tiles.shape
     heads_kv = kwidth // HDIM
     group_width = qwidth // heads_kv
     live = key_live.reshape(nblocks, 1, ntiles * block_len).astype(jnp.float32)
     row_spec = pl.BlockSpec((block_len, group_width), lambda b, h: (b, h))
-    tile_spec = pl.BlockSpec((None, ntiles, block_len, HDIM), lambda b, h: (b, 0, 0, h))
+    key_spec = pl.BlockSpec((None, ntiles, None, block_len, HDIM), lambda b, h: (b, 0, 0, 0, h))
+    value_spec = pl.BlockSpec((None, ntiles, None, block_len, HDIM), lambda b, h: (b, 0, 1, 0, h))
+    term_spec = pl.BlockSpec((None, ntiles, 2, block_len, HDIM), lambda b, h: (b, 0, 0, 0, h))
     live_spec = pl.BlockSpec((None, 1, ntiles * block_len), lambda b, h: (b, 0, 0))
     flops = 12 * nblocks * heads_kv * (group_width // HDIM) * block_len * ntiles * block_len * HDIM
-    query_grad, key_grad, value_grad = pl.pallas_call(
+    query_grad, terms = pl.pallas_call(
         attention_kernel,
         grid=(nblocks, heads_kv),
-        in_specs=[row_spec, row_spec, tile_spec, tile_spec, live_spec],
-        out_specs=[row_spec, tile_spec, tile_spec],
+        in_specs=[row_spec, row_spec, key_spec, value_spec, live_spec],
+        out_specs=[row_spec, term_spec],
         out_shape=[
-            jax.ShapeDtypeStruct((nblocks * block_len, qwidth), jnp.bfloat16),
-            jax.ShapeDtypeStruct((nblocks, ntiles, block_len, kwidth), jnp.float32),
-            jax.ShapeDtypeStruct((nblocks, ntiles, block_len, kwidth), jnp.float32),
+            jax.ShapeDtypeStruct((shard_tokens, qwidth), jnp.bfloat16),
+            jax.ShapeDtypeStruct((nblocks, ntiles, 2, block_len, kwidth), jnp.float32),
         ],
         cost_estimate=pl.CostEstimate(
             flops=flops,
             transcendentals=nblocks * qwidth // HDIM * block_len * ntiles * block_len,
-            bytes_accessed=nblocks * block_len * qwidth * 6 + nblocks * ntiles * block_len * kwidth * 12,
+            bytes_accessed=shard_tokens * qwidth * 6 + nblocks * ntiles * block_len * kwidth * 12,
         ),
-    )(
-        query_rows.reshape(nblocks * block_len, qwidth),
-        grad_rows.reshape(nblocks * block_len, qwidth),
-        key_tiles,
-        value_tiles,
-        live,
-    )
-    return (query_grad, key_grad, value_grad)
+    )(query_rows, grad_rows, kv_tiles, kv_tiles, live)
+    return (query_grad, terms)
 
 
 def request_plan(request_lists, this_shard, query_blocks):
@@ -196,84 +190,65 @@
     query_blocks = shard_tokens // BLK
     total_blocks = query_blocks * shards
     near = 3 + GLOB
-    kvpair = jnp.stack([key_rows, value_rows])
-    extended = extended_2(kvpair, (("seq", 1),), BLK)
-    ext_blocks = extended.reshape(2, query_blocks + 2, BLK, kwidth)
-    window = jnp.stack(
-        [ext_blocks[:, offset : offset + query_blocks] for offset in range(3)], axis=2
-    )
-    own_blocks = kvpair.reshape(2, query_blocks, BLK, kwidth)
-    global_list = []
-    for glob_num in range(GLOB):
-        owner_dev = global_ids[glob_num] // query_blocks
-        local_tile = lax.dynamic_index_in_dim(
-            own_blocks, global_ids[glob_num] % query_blocks, 1, keepdims=False
-        )
-        global_list.append(broadcast(local_tile, "seq", owner_dev))
-    global_tiles = jnp.stack(global_list, axis=1)
+    kvpair = jnp.stack(
+        [key_rows.reshape(query_blocks, BLK, kwidth), value_rows.reshape(query_blocks, BLK, kwidth)],
+        axis=1,
+    )
+    all_blocks = lax.all_gather(kvpair, "seq", axis=0, tiled=True)
     random_three = random_table.reshape(shards, query_blocks, RAND)
-    slot_plans = []
-    pieces = []
-    for slot_num in range(RAND):
-        slot_plan = request_plan(random_three[:, :, slot_num], this_shard, query_blocks)
-        received = lax.all_to_all(
-            serve_tiles(own_blocks, slot_plan), "seq", split_axis=1, concat_axis=1, tiled=True
-        )
-        pieces.append(pick_tiles(received, slot_plan))
-        slot_plans.append(slot_plan)
-    fetched = jnp.stack(pieces, axis=2)
-    spread_global = jnp.broadcast_to(global_tiles[:, None], (2, query_blocks, GLOB, BLK, kwidth))
-    all_tiles = jnp.concatenate([window, spread_global, fetched], axis=2)
     base_ids = this_shard * query_blocks + jnp.arange(query_blocks, dtype=jnp.int32)
     window_ids = base_ids[:, None] + jnp.arange(-1, 2, dtype=jnp.int32)[None, :]
     my_random = lax.dynamic_index_in_dim(random_three, this_shard, 0, keepdims=False)
     tile_ids = jnp.concatenate(
         [window_ids, jnp.broadcast_to(global_ids[None, :], (query_blocks, GLOB)), my_random], axis=1
     )
+    ntiles = tile_ids.shape[1]
+    safe_ids = jnp.clip(tile_ids, 0, total_blocks - 1)
+    kv_tiles = jnp.take(all_blocks, safe_ids.reshape(-1), axis=0).reshape(
+        query_blocks, ntiles, 2, BLK, kwidth
+    )
     key_live = token_live(tile_ids, pad_sizes, query_blocks, shard_tokens, total_blocks)
-    query_grad, key_terms, value_terms = block_backward(
-        query_rows.reshape(query_blocks, BLK, qwidth),
-        grad_rows.reshape(query_blocks, BLK, qwidth),
-        all_tiles[0],
-        all_tiles[1],
-        key_live,
-    )
-    contrib = jnp.stack([key_terms, value_terms])
-    local_sum = contrib[:, :, 1]
-    local_sum = local_sum + jnp.pad(contrib[:, 1:, 0], ((0, 0), (0, 1), (0, 0), (0, 0)))
-    local_sum = local_sum + jnp.pad(contrib[:, :-1, 2], ((0, 0), (1, 0), (0, 0), (0, 0)))
-    edge_out = jnp.concatenate([contrib[:, 0, 0], contrib[:, query_blocks - 1, 2]], axis=1)
-    edge_in = extended_2(edge_out.astype(jnp.bfloat16), (("seq", 1),), BLK).astype(edge_out.dtype)
-    local_sum = local_sum.at[:, 0].add(edge_in[:, :BLK])
-    local_sum = local_sum.at[:, query_blocks - 1].add(edge_in[:, 3 * BLK :])
-    global_part = jnp.sum(contrib[:, :, 3:near], axis=1)
-    global_total = lax.psum(global_part, "seq")
-    global_pick = (
-        (global_ids[:, None] // query_blocks == this_shard)
-        & (global_ids[:, None] % query_blocks == jnp.arange(query_blocks, dtype=jnp.int32)[None, :])
-    ).astype(jnp.float32)
-    local_sum = local_sum + jnp.einsum(
-        "gq,xgsk->xqsk", global_pick, global_total, precision=lax.Precision.HIGHEST
-    )
-    random_terms = contrib[:, :, near:].astype(jnp.bfloat16)
-    for slot_num in range(RAND):
-        returned = lax.all_to_all(
-            place_terms(random_terms[:, :, slot_num], slot_plans[slot_num]),
-            "seq",
-            split_axis=1,
-            concat_axis=1,
-            tiled=True,
-        )
-        local_sum = local_sum + absorb_terms(returned, slot_plans[slot_num], query_blocks)
-    key_grad = local_sum[0].reshape(shard_tokens, kwidth).astype(jnp.bfloat16)
-    value_grad = local_sum[1].reshape(shard_tokens, kwidth).astype(jnp.bfloat16)
-    query_low = query_grad
-    packed = jnp.concatenate([query_low, key_grad, value_grad], axis=-1)
-    handed = from_behind(packed, "section", -1)
+    query_grad, terms = block_backward(query_rows, grad_rows, kv_tiles, key_live)
+    handed_query = from_behind(query_grad, "section", -1)
+    local_sum = terms[:, 1]
+    local_sum = local_sum + jnp.pad(terms[1:, 0], ((0, 1), (0, 0), (0, 0), (0, 0)))
+    local_sum = local_sum + jnp.pad(terms[:-1, 2], ((1, 0), (0, 0), (0, 0), (0, 0)))
+    global_part = jnp.sum(terms[:, 3:near], axis=0)
+    random_part = terms[:, near:].astype(jnp.bfloat16).astype(jnp.float32)
+    foreign = jnp.concatenate(
+        [
+            terms[0:1, 0],
+            terms[query_blocks - 1 : query_blocks, 2],
+            global_part,
+            random_part.reshape(query_blocks * RAND, 2, BLK, kwidth),
+        ],
+        axis=0,
+    )
+    foreign_ids = jnp.concatenate(
+        [
+            safe_ids[0:1, 0],
+            safe_ids[query_blocks - 1 : query_blocks, 2],
+            global_ids,
+            my_random.reshape(-1),
+        ]
+    )
+    partial = jnp.zeros((total_blocks, 2, BLK, kwidth), jnp.float32).at[foreign_ids].add(foreign)
+    returned = lax.psum_scatter(
+        partial.astype(jnp.bfloat16), "seq", scatter_dimension=0, tiled=True
+    )
+    kv_sum = local_sum + returned.astype(jnp.float32)
+    kv_grad = jnp.concatenate(
+        [
+            kv_sum[:, 0].reshape(shard_tokens, kwidth).astype(jnp.bfloat16),
+            kv_sum[:, 1].reshape(shard_tokens, kwidth).astype(jnp.bfloat16),
+        ],
+        axis=-1,
+    )
+    handed_kv = from_behind(kv_grad, "section", -1)
     return (
-        handed[None, :, :qwidth],
-        handed[None, :, qwidth : qwidth + kwidth],
-        handed[None, :, qwidth + kwidth :],
+        handed_query[None],
+        handed_kv[None, :, :kwidth],
+        handed_kv[None, :, kwidth:],
     )
 
 

time: 373 us -> 260 us (0.70)
  waiting for transfers between devices: 209 us -> 161 us
  starting transfers between devices: 43.9 us -> 2.61 us
  local copies, waits for them, and re-layouts: 38.9 us -> 21 us
  other arithmetic: 22.4 us -> 33.2 us
  matrix products: 10.1 us -> 0 us
  between operations: 19.8 us -> 14.1 us
    psum x2 -> x0, waiting for transfers between devices: 98.2 us -> none  [the longest x1 70.7 us: body(): global_total = lax.psum(global_part, 'seq')]
    reduce_scatter x0 -> x1, waiting for transfers between devices: none -> 83.4 us  [body(): lax.psum_scatter(partial.astype(jnp.bfloat16), 'seq', scatter_dimension=0...]
    all_to_all x6 -> x0, waiting for transfers between devices: 80.8 us -> none  [the longest x3 43.7 us: body(): lax.all_to_all(place_terms(random_terms[:, :, slot_num], slot_plans[slot_...]
    all_gather x0 -> x1, waiting for transfers between devices: none -> 69.2 us  [body(): all_blocks = lax.all_gather(kvpair, 'seq', axis=0, tiled=True)]
    all_to_all x6 -> x0, starting transfers between devices: 29.5 us -> none  [the longest x3 15.7 us: body(): lax.all_to_all(serve_tiles(own_blocks, slot_plan), 'seq', split_axis=1, c...]
    ppermute x1 -> x2, waiting for transfers between devices: 30.4 us -> 7.98 us  [from_behind(): return lax.ppermute(block, axis, route)]
    ppermute x4 -> x0, starting transfers between devices: 11.8 us -> none  [the longest x2 9.22 us: extended_2(): before = lax.ppermute(last, axis, up)]
    dot_general x4 -> x0, matrix products: 10.1 us -> none  [the longest x3 6.91 us: absorb_terms(): jnp.einsum('ncq,xncsk->xqsk', onehot, received, preferred_element_type=jn...]
  transfers between devices with their start and end apart: 13 -> 4, of which waited for: 7 -> 3; matrix products, arithmetic and copies ran while one was open for 12% -> 4% of each run, Pallas kernels for 0% -> 0%
where the time goes in v2:
time: 260 us; the launch traced here: 259 us
  waiting for transfers between devices  161 us (62%)
  other arithmetic  33.2 us (13%)
  Pallas kernels  27.7 us (11%)
  local copies, waits for them, and re-layouts  21 us (8%)
  between operations  14.1 us (5%)
  starting transfers between devices  2.61 us (1%)
    reduce_scatter x1, waiting for transfers between devices, body(): lax.psum_scatter(partial.astype(jnp.bfloat16), 'seq', scatter_dimension=0...  83.4 us
    all_gather x1, waiting for transfers between devices, body(): all_blocks = lax.all_gather(kvpair, 'seq', axis=0, tiled=True)  69.2 us
    pallas_call x1, Pallas kernels, block_backward(): pl.pallas_call(attention_kernel, grid=(nblocks, heads_kv), in_specs=[row_...  27.7 us
    scatter-add x1, other arithmetic, body(): jnp.zeros((total_blocks, 2, BLK, kwidth), jnp.float32).at[foreign_ids]  9.62 us
    ppermute x2, waiting for transfers between devices, from_behind(): return lax.ppermute(block, axis, route)  7.98 us
    convert_element_type x1, other arithmetic, body(): partial.astype(jnp.bfloat16)  5.95 us
  transfers between devices with their start and end apart: 4, of which 3 were waited for; matrix products, arithmetic and copies ran while one was open for 4% of the time, Pallas kernels for 0%

profile of v2, /device:TPU:1, one launch (start us, length us, event | category | flops | bytes accessed | tf_op | source)
XLA Modules:
  0.0 259.2 jit_solution(6068928609720046767)
XLA Ops:
  7.2 0.0 all-gather.2.cloned.1.call-start
  7.2 1.9 pad_maximum_fusion.1
  9.1 0.0 all-gather.2.cloned.1.call-update
  9.1 0.0 reduce-scatter.2.cloned.1.call-start
  9.2 0.7 reduce
  9.9 0.1 reshape_squeeze.2
  10.0 0.1 copy.23
  10.0 0.7 pad.23.clone
  10.8 0.1 concatenate.51
  10.9 0.1 broadcast_add_fusion
  10.9 0.1 fusion.4
  11.0 0.1 min.14
  11.1 0.1 compare_and_fusion
  11.2 0.1 and.61
  11.3 0.1 and.66
  11.4 0.9 select_reduce_fusion
  12.3 0.1 lt.69
  12.3 0.1 lt.70
  12.4 0.1 add.141
  12.5 0.1 add.142
  12.6 0.1 add.144
  12.7 0.6 fusion.9
  13.2 2.0 fusion.7
  15.3 0.6 and_convert_fusion.live_ref
  15.9 69.2 %all-gather.2.cloned.1.call-done = bf16[32,2,64,512]{3,2,0,1:T(8,128)(2,1)} async-done(((bf16[4,2,64,512]{3,2,0,1:T(8,128)(2,1)}), bf16[32,2,64,512]{3,2,0,1:T(8,128)(2,1)}) %all-gather.2.cloned.1.call-update) | async-done | bytes 4194320 | tf_op jit(solution)/shard_map/all_gather | solution.py:197
  85.1 4.9 %gather_fusion = bf16[32,2,64,512]{3,2,1,0:T(8,128)(2,1)} fusion(bf16[32,2,64,512]{3,2,0,1:T(8,128)(2,1)} %all-gather.2.cloned.1.call-done, s32[1024]{0:T(1024)S(1)} %pad_clamp_fusion), kind=kCustom, calls=%fused_computation | custom fusion | bytes 8388736 | tf_op jit(solution)/shard_map/jit(_take)/gather | solution.py:207
  90.0 4.6 %broadcast_select_fusion.k_ref.v_ref = bf16[4,8,2,64,512]{4,3,2,1,0:T(8,128)(2,1)} fusion(bf16[4,8,2,64,512]{4,3,2,1,0:T(8,128)(2,1)} %bitcast.45, pred[4,8]{1,0:T(4,128)(4,1)S(1)} %compare_and_fusion.1), kind=kLoop, calls=%fused_computation.3 | loop fusion | flops 2097152 | bytes 8388640 | tf_op jit(solution)/shard_map/jit(_take)/select_n | solution.py:207
  94.6 27.7 %shard_map.94 = (bf16[256,4096]{1,0:T(8,128)(2,1)}, f32[4,8,2,64,512]{4,3,2,1,0:T(8,128)}) custom-call(bf16[256,4096]{1,0:T(8,128)(2,1)} %bitcast.55, bf16[256,4096]{1,0:T(8,128)(2,1)} %bitcast.56, bf16[4,8,2,64,512]{4,3,2,1,0:T(8,128)(2,1)} %broadcast_select_fusion.k_ref.v_ref, bf16[4,8,2,64,512]{4,3,2,1,0:T(8,128)(2,1)} %broadcast_select_fusion.k_ref.v_ref, ...), custom_call_target="tpu_custom_call" | custom-call | flops 6442450944 | bytes 18874368 | tf_op jit(solution)/shard_map/pallas_call | solution.py:99
  122.3 2.1 slice.81
  124.5 1.9 slice_reduce_fusion
  126.4 1.1 slice_bitcast_fusion.6
  127.4 0.5 bitcast_convert_fusion
  128.0 2.4 pad_maximum_fusion
  130.4 4.3 %broadcast_in_dim.53 = f32[32,2,64,512]{3,2,1,0:T(8,128)} broadcast(f32[]{:T(128)} %constant.66.clone.1), dimensions={} | broadcast | bytes 8388612 | tf_op jit(solution)/shard_map/broadcast_in_dim | solution.py:235
  134.7 9.6 %scatter_fusion = f32[32,2,64,512]{3,2,1,0:T(8,128)} fusion(f32[32,2,64,512]{3,2,1,0:T(8,128)} %broadcast_in_dim.53, s32[16]{0:T(128)S(1)} %fusion.7, f32[16,2,64,512]{3,2,1,0:T(8,128)} %pad_maximum_fusion), kind=kCustom, calls=%fused_computation.1 | custom fusion | flops 1048576 | bytes 12582976 | tf_op jit(solution)/shard_map/scatter-add | solution.py:235
  144.3 6.0 %convert_element_type.24 = bf16[32,2,64,512]{3,2,1,0:T(8,128)(2,1)} convert(f32[32,2,64,512]{3,2,1,0:T(8,128)} %scatter_fusion) | non-fusion elementwise | flops 2097152 | bytes 12582912 | tf_op jit(solution)/shard_map/convert_element_type | solution.py:237
  150.2 0.0 reduce-scatter.2.cloned.1.call-update
  150.3 1.9 collective-permute-start
  152.1 1.2 slice_bitcast_fusion.2
  153.3 1.2 slice_bitcast_fusion.1
  154.5 83.4 %reduce-scatter.2.cloned.1.call-done = bf16[4,2,64,512]{3,2,1,0:T(8,128)(2,1)} async-done(((bf16[32,2,64,512]{3,2,1,0:T(8,128)(2,1)}), bf16[4,2,64,512]{3,2,1,0:T(8,128)(2,1)}) %reduce-scatter.2.cloned.1.call-update) | async-done | bytes 524304 | tf_op jit(solution)/shard_map/reduce_scatter | solution.py:236
  237.9 1.7 fusion.3
  239.7 0.1 pad_maximum_fusion.2
  239.7 0.7 collective-permute-start.1
  240.4 0.0 collective-permute-done
  240.4 8.0 %collective-permute-done.1 = bf16[256,1024]{1,0:T(8,128)(2,1)S(1)} collective-permute-done((bf16[256,1024]{1,0:T(8,128)(2,1)S(1)}, bf16[256,1024]{1,0:T(8,128)(2,1)S(1)}, u32[]{:S(2)}, u32[]{:S(2)}) %collective-permute-start.1) | collective-permute-done | bytes 524320 | tf_op jit(solution)/shard_map/ppermute | solution.py:36
  248.4 0.8 slice_bitcast_fusion.3
  249.2 3.1 %copy.36 = bf16[1,256,4096]{2,1,0:T(8,128)(2,1)} copy(bf16[1,256,4096]{2,1,0:T(8,128)(2,1)} %bitcast.9) | data formatting | bytes 4194304
  (10 shorter events, 0.1 us)
Async XLA Ops:
  7.2 77.9 %all-gather.2.cloned.1.call-start = ((), (), s32[]{:S(2)}) async-start(), calls=%async_computation.1 | async-start | bytes 4718592 | tf_op jit(solution)/shard_map/all_gather | solution.py:197
  9.1 228.8 %reduce-scatter.2.cloned.1.call-start = ((), (), s32[]{:S(2)}) async-start(), calls=%async_computation.2 | async-start | bytes 4718592 | tf_op jit(solution)/shard_map/reduce_scatter | solution.py:236
  150.3 90.2 %collective-permute-start = (bf16[256,4096]{1,0:T(8,128)(2,1)}, bf16[256,4096]{1,0:T(8,128)(2,1)}, u32[]{:S(2)}, u32[]{:S(2)}) collective-permute-start(bf16[256,4096]{1,0:T(8,128)(2,1)} %get-tuple-element.5), channel_id=1, source_target_pairs={{8,0},{16,8},{24,16},{0,24},{9,1},{17,9},{25,17},{1,25},{10,2},{18... | collective-permute-start | bytes 6291464 | tf_op jit(solution)/shard_map/ppermute | solution.py:36
  239.7 8.7 %collective-permute-start.1 = (bf16[256,1024]{1,0:T(8,128)(2,1)S(1)}, bf16[256,1024]{1,0:T(8,128)(2,1)S(1)}, u32[]{:S(2)}, u32[]{:S(2)}) collective-permute-start(bf16[256,1024]{1,0:T(8,128)(2,1)S(1)} %pad_maximum_fusion.2), channel_id=1, source_target_pairs={{8,0},{16,8},{24,16},{0,24},{9,1},{17,9},{25,17},{1,25},{10,2},{18... | collective-permute-start | bytes 1572872 | tf_op jit(solution)/shard_map/ppermute | solution.py:36
Sparse Core Ops, SparseCore 0:
  10.8 74.2 all-gather.1
  150.4 87.4 reduce-scatter.1

commit v3 on v2

--- a/solution.py
+++ b/solution.py
@@ -4,6 +4,7 @@
 import jax.numpy as jnp
 from jax import lax
 from jax.experimental import pallas as pl
+from jax.experimental.pallas import tpu as pltpu
 from jax.sharding import PartitionSpec as P
 
 HDIM = 128
@@ -36,10 +37,17 @@
     return lax.ppermute(block, axis, route)
 
 
-def attention_kernel(q_ref, g_ref, k_ref, v_ref, live_ref, dq_ref, dkv_ref):
+def attention_kernel(ids_ref, q_ref, g_ref, *refs):
+    del ids_ref
+    ntiles = len(refs) - 6
+    tile_refs = refs[:ntiles]
+    live_ref = refs[ntiles]
+    dq_ref, own_ref, edge_ref, glob_ref, rand_ref = refs[ntiles + 1 :]
+    nblocks = own_ref.shape[0]
     block_len, width = q_ref.shape
     group = width // HDIM
-    ntiles = k_ref.shape[0]
+    near = 3 + GLOB
+    b = pl.program_id(1)
     score_scale = 1.0 / math.sqrt(HDIM)
     query = q_ref[...]
     grad = g_ref[...]
@@ -47,8 +55,8 @@
         [query[:, g * HDIM : (g + 1) * HDIM] for g in range(group)], axis=0
     )
     grad_rows = jnp.concatenate([grad[:, g * HDIM : (g + 1) * HDIM] for g in range(group)], axis=0)
-    key_rows = k_ref[...].reshape(ntiles * block_len, HDIM)
-    value_rows = v_ref[...].reshape(ntiles * block_len, HDIM)
+    key_rows = jnp.concatenate([tile_refs[t][0] for t in range(ntiles)], axis=0)
+    value_rows = jnp.concatenate([tile_refs[t][1] for t in range(ntiles)], axis=0)
     live = live_ref[...] > 0.5
     contract_last = (((1,), (1,)), ((), ()))
     contract_first = (((0,), (0,)), ((), ()))
@@ -80,38 +88,85 @@
         dq_ref[:, g * HDIM : (g + 1) * HDIM] = query_grad[g * block_len : (g + 1) * block_len].astype(
             dq_ref.dtype
         )
-    dkv_ref[:, 0] = key_grad.reshape(ntiles, block_len, HDIM)
-    dkv_ref[:, 1] = value_grad.reshape(ntiles, block_len, HDIM)
-
-
-def block_backward(query_rows, grad_rows, kv_tiles, key_live):
+    terms = jnp.stack(
+        [key_grad.reshape(ntiles, block_len, HDIM), value_grad.reshape(ntiles, block_len, HDIM)],
+        axis=1,
+    )
+
+    @pl.when(b == 0)
+    def _():
+        own_ref[...] = jnp.zeros_like(own_ref)
+        glob_ref[...] = jnp.zeros_like(glob_ref)
+        edge_ref[0] = terms[0]
+
+    @pl.when(b > 0)
+    def _():
+        before = jnp.maximum(b - 1, 0)
+        own_ref[before] = own_ref[before] + terms[0]
+
+    own_ref[b] = own_ref[b] + terms[1]
+
+    @pl.when(b < nblocks - 1)
+    def _():
+        after = jnp.minimum(b + 1, nblocks - 1)
+        own_ref[after] = own_ref[after] + terms[2]
+
+    @pl.when(b == nblocks - 1)
+    def _():
+        edge_ref[1] = terms[2]
+
+    glob_ref[...] = glob_ref[...] + terms[3:near]
+    rand_ref[...] = terms[near:].astype(rand_ref.dtype)
+
+
+def block_backward(query_rows, grad_rows, all_blocks, tile_ids, key_live):
     shard_tokens, qwidth = query_rows.shape
-    nblocks, ntiles, _, block_len, kwidth = kv_tiles.shape
+    _, _, block_len, kwidth = all_blocks.shape
+    nblocks, ntiles = tile_ids.shape
     heads_kv = kwidth // HDIM
     group_width = qwidth // heads_kv
+    near = 3 + GLOB
+    nrand = ntiles - near
     live = key_live.reshape(nblocks, 1, ntiles * block_len).astype(jnp.float32)
-    row_spec = pl.BlockSpec((block_len, group_width), lambda b, h: (b, h))
-    key_spec = pl.BlockSpec((None, ntiles, None, block_len, HDIM), lambda b, h: (b, 0, 0, 0, h))
-    value_spec = pl.BlockSpec((None, ntiles, None, block_len, HDIM), lambda b, h: (b, 0, 1, 0, h))
-    term_spec = pl.BlockSpec((None, ntiles, 2, block_len, HDIM), lambda b, h: (b, 0, 0, 0, h))
-    live_spec = pl.BlockSpec((None, 1, ntiles * block_len), lambda b, h: (b, 0, 0))
+    row_spec = pl.BlockSpec((block_len, group_width), lambda h, b, ids: (b, h))
+    tile_specs = [
+        pl.BlockSpec(
+            (None, 2, block_len, HDIM), lambda h, b, ids, t=t: (ids[b * ntiles + t], 0, 0, h)
+        )
+        for t in range(ntiles)
+    ]
+    live_spec = pl.BlockSpec((None, 1, ntiles * block_len), lambda h, b, ids: (b, 0, 0))
+    own_spec = pl.BlockSpec((nblocks, 2, block_len, HDIM), lambda h, b, ids: (0, 0, 0, h))
+    edge_spec = pl.BlockSpec((2, 2, block_len, HDIM), lambda h, b, ids: (0, 0, 0, h))
+    glob_spec = pl.BlockSpec((GLOB, 2, block_len, HDIM), lambda h, b, ids: (0, 0, 0, h))
+    rand_spec = pl.BlockSpec((None, nrand, 2, block_len, HDIM), lambda h, b, ids: (b, 0, 0, 0, h))
     flops = 12 * nblocks * heads_kv * (group_width // HDIM) * block_len * ntiles * block_len * HDIM
-    query_grad, terms = pl.pallas_call(
+    grid_spec = pltpu.PrefetchScalarGridSpec(
+        num_scalar_prefetch=1,
+        grid=(heads_kv, nblocks),
+        in_specs=[row_spec, row_spec, *tile_specs, live_spec],
+        out_specs=[row_spec, own_spec, edge_spec, glob_spec, rand_spec],
+    )
+    outs = pl.pallas_call(
         attention_kernel,
-        grid=(nblocks, heads_kv),
-        in_specs=[row_spec, row_spec, key_spec, value_spec, live_spec],
-        out_specs=[row_spec, term_spec],
+        grid_spec=grid_spec,
         out_shape=[
             jax.ShapeDtypeStruct((shard_tokens, qwidth), jnp.bfloat16),
-            jax.ShapeDtypeStruct((nblocks, ntiles, 2, block_len, kwidth), jnp.float32),
+            jax.ShapeDtypeStruct((nblocks, 2, block_len, kwidth), jnp.float32),
+            jax.ShapeDtypeStruct((2, 2, block_len, kwidth), jnp.float32),
+            jax.ShapeDtypeStruct((GLOB, 2, block_len, kwidth), jnp.float32),
+            jax.ShapeDtypeStruct((nblocks, nrand, 2, block_len, kwidth), jnp.bfloat16),
         ],
+        compiler_params=pltpu.CompilerParams(
+            dimension_semantics=("arbitrary", "arbitrary")
+        ),
         cost_estimate=pl.CostEstimate(
             flops=flops,
             transcendentals=nblocks * qwidth // HDIM * block_len * ntiles * block_len,
-            bytes_accessed=shard_tokens * qwidth * 6 + nblocks * ntiles * block_len * kwidth * 12,
+            bytes_accessed=shard_tokens * qwidth * 6 + nblocks * ntiles * block_len * kwidth * 6,
         ),
-    )(query_rows, grad_rows, kv_tiles, kv_tiles, live)
-    return (query_grad, terms)
+    )(tile_ids.reshape(-1), query_rows, grad_rows, *([all_blocks] * ntiles), live)
+    return outs
 
 
 def request_plan(request_lists, this_shard, query_blocks):
@@ -202,24 +257,16 @@
     tile_ids = jnp.concatenate(
         [window_ids, jnp.broadcast_to(global_ids[None, :], (query_blocks, GLOB)), my_random], axis=1
     )
-    ntiles = tile_ids.shape[1]
     safe_ids = jnp.clip(tile_ids, 0, total_blocks - 1)
-    kv_tiles = jnp.take(all_blocks, safe_ids.reshape(-1), axis=0).reshape(
-        query_blocks, ntiles, 2, BLK, kwidth
-    )
     key_live = token_live(tile_ids, pad_sizes, query_blocks, shard_tokens, total_blocks)
-    query_grad, terms = block_backward(query_rows, grad_rows, kv_tiles, key_live)
+    query_grad, local_sum, edge_terms, global_part, random_part = block_backward(
+        query_rows, grad_rows, all_blocks, safe_ids, key_live
+    )
     handed_query = from_behind(query_grad, "section", -1)
-    local_sum = terms[:, 1]
-    local_sum = local_sum + jnp.pad(terms[1:, 0], ((0, 1), (0, 0), (0, 0), (0, 0)))
-    local_sum = local_sum + jnp.pad(terms[:-1, 2], ((1, 0), (0, 0), (0, 0), (0, 0)))
-    global_part = jnp.sum(terms[:, 3:near], axis=0)
-    random_part = terms[:, near:].astype(jnp.bfloat16).astype(jnp.float32)
     foreign = jnp.concatenate(
         [
-            terms[0:1, 0],
-            terms[query_blocks - 1 : query_blocks, 2],
-            global_part,
+            edge_terms.astype(jnp.bfloat16),
+            global_part.astype(jnp.bfloat16),
             random_part.reshape(query_blocks * RAND, 2, BLK, kwidth),
         ],
         axis=0,
@@ -232,9 +279,14 @@
             my_random.reshape(-1),
         ]
     )
-    partial = jnp.zeros((total_blocks, 2, BLK, kwidth), jnp.float32).at[foreign_ids].add(foreign)
+    onehot = (
+        foreign_ids[None, :] == jnp.arange(total_blocks, dtype=jnp.int32)[:, None]
+    ).astype(jnp.bfloat16)
+    partial = jnp.einsum(
+        "nf,fxsk->nxsk", onehot, foreign, preferred_element_type=jnp.float32
+    ).astype(jnp.bfloat16)
     returned = lax.psum_scatter(
-        partial.astype(jnp.bfloat16), "seq", scatter_dimension=0, tiled=True
+        partial, "seq", scatter_dimension=0, tiled=True
     )
     kv_sum = local_sum + returned.astype(jnp.float32)
     kv_grad = jnp.concatenate(

time: 260 us -> 234 us (0.900)
  other arithmetic: 33.2 us -> 9.84 us
  local copies, waits for them, and re-layouts: 21 us -> 10.7 us
  Pallas kernels: 27.7 us -> 32.1 us
    scatter-add x1 -> x0, other arithmetic: 9.62 us -> none  [body(): jnp.zeros((total_blocks, 2, BLK, kwidth), jnp.float32).at[foreign_ids]]
    select_n x3 -> x0, other arithmetic: 6.66 us -> none  [the longest x2 4.63 us: body(): jnp.take(all_blocks, safe_ids.reshape(-1), axis=0)]
    gather x1 -> x0, local copies, waits for them, and re-layouts: 4.93 us -> none  [body(): jnp.take(all_blocks, safe_ids.reshape(-1), axis=0)]
    pallas_call x1, Pallas kernels: 27.7 us -> 32.1 us  [block_backward(): pl.pallas_call(attention_kernel, grid_spec=grid_spec, out_shape=[jax.Shap...]
    dot_general x0 -> x1, local copies, waits for them, and re-layouts: none -> 4.34 us  [body(): jnp.einsum('nf,fxsk->nxsk', onehot, foreign, preferred_element_type=jnp.f...]
    broadcast_in_dim x1 -> x0, local copies, waits for them, and re-layouts: 4.28 us -> none  [body(): jnp.zeros((total_blocks, 2, BLK, kwidth), jnp.float32).at[foreign_ids]]
    convert_element_type x1 -> x2, other arithmetic: 5.95 us -> 2.27 us  [the longest x1 1.19 us: body(): edge_terms.astype(jnp.bfloat16)]
    squeeze x3 -> x0, local copies, waits for them, and re-layouts: 3.44 us -> none  [the longest x1 1.19 us: body(): terms[1:, 0]]
where the time goes in v3:
time: 234 us
  waiting for transfers between devices  162 us (69%)
  Pallas kernels  32.1 us (14%)
  between operations  14.1 us (6%)
  local copies, waits for them, and re-layouts  10.7 us (5%)
  other arithmetic  9.84 us (4%)
  starting transfers between devices  2.67 us (1%)
    reduce_scatter x1, waiting for transfers between devices, body(): returned = lax.psum_scatter(partial, 'seq', scatter_dimension=0, tiled=True)  85.8 us
    all_gather x1, waiting for transfers between devices, body(): all_blocks = lax.all_gather(kvpair, 'seq', axis=0, tiled=True)  68.7 us
    pallas_call x1, Pallas kernels, block_backward(): pl.pallas_call(attention_kernel, grid_spec=grid_spec, out_shape=[jax.Shap...  32.1 us
    ppermute x2, waiting for transfers between devices, from_behind(): return lax.ppermute(block, axis, route)  7.98 us
  transfers between devices with their start and end apart: 4, of which 3 were waited for; matrix products, arithmetic and copies ran while one was open for 4% of the time, Pallas kernels for 0%

profile of v3, /device:TPU:1, one launch (start us, length us, event | category | flops | bytes accessed | tf_op | source)
XLA Modules:
  0.0 233.6 jit_solution(15284736381499196749)
XLA Ops:
  7.2 0.0 all-gather.2.cloned.1.call-start
  7.2 1.9 pad_maximum_fusion
  9.1 0.0 all-gather.2.cloned.1.call-update
  9.1 0.0 reduce-scatter.2.cloned.1.call-start
  9.2 0.7 pad.12.clone
  9.9 0.7 reduce
  10.6 0.1 add.96
  10.7 0.1 reshape_squeeze.2
  10.8 0.1 copy.30
  10.9 0.1 reshape.249
  11.0 0.1 broadcast_add_fusion
  11.0 0.1 fusion.9
  11.1 0.6 min.14.ids_ref
  11.7 0.1 compare_and_fusion
  11.8 0.1 and.52
  11.9 0.1 and.57
  12.0 0.9 select_reduce_fusion
  12.9 0.1 lt.42
  12.9 0.1 lt.43
  13.0 0.1 add.93
  13.1 0.1 add.94
  13.2 0.6 fusion.13
  13.8 2.0 pad_add_fusion.1
  15.8 0.6 and_convert_fusion.refs_8_
  16.4 68.7 %all-gather.2.cloned.1.call-done.refs_0_.refs_1_.refs_2_.refs_3_.refs_4_.refs_5_.refs_6_.refs_7_ = bf16[32,2,64,512]{3,2,1,0:T(8,128)(2,1)} async-done(((bf16[4,2,64,512]{3,2,1,0:T(8,128)(2,1)}), bf16[32,2,64,512]{3,2,1,0:T(8,128)(2,1)}) %all-gather.2.cloned.1.call-update) | async-done | bytes 4194320 | tf_op jit(solution)/shard_map/all_gather | solution.py:252
  85.0 32.1 %shard_map.94 = (bf16[256,4096]{1,0:T(8,128)(2,1)}, f32[4,2,64,512]{3,2,1,0:T(8,128)}, f32[2,2,64,512]{3,2,1,0:T(8,128)}, f32[2,2,64,512]{3,2,1,0:T(8,128)}, bf16[4,3,2,64,512]{4,3,2,1,0:T(8,128)(2,1)}) custom-call(s32[32]{0:T(128)} %min.14.ids_ref, bf16[256,4096]{1,0:T(8,128)(2,1)} %bitcast.24, bf16[256,4096]{1,0:T(8,128)(2,1)} %bitcast.25, ...), custom_call_target="tpu_custom_call" | custom-call | flops 6442450944 | bytes 12582912 | tf_op jit(solution)/shard_map/pallas_call | solution.py:150
  117.1 0.0 copy-start
  117.1 1.2 convert_element_type.25
  118.3 0.3 copy.33
  118.6 1.1 convert_element_type.26
  119.7 0.3 copy.34
  119.9 0.0 copy-done
  120.0 0.9 copy.35
  120.9 1.6 fusion
  122.5 4.3 %copy.39 = bf16[32,2,64,512]{3,2,1,0:T(8,128)(2,1)} copy(bf16[32,2,64,512]{3,0,2,1:T(8,128)(2,1)S(1)} %fusion) | data formatting | bytes 8388608 | tf_op jit(solution)/shard_map/nf,fxsk->nxsk/dot_general | solution.py:285
  126.9 0.0 copy-start.1
  126.9 0.0 reduce-scatter.2.cloned.1.call-update
  126.9 1.9 collective-permute-start
  128.8 85.8 %reduce-scatter.2.cloned.1.call-done = bf16[4,2,64,512]{3,2,1,0:T(8,128)(2,1)} async-done(((bf16[32,2,64,512]{3,2,1,0:T(8,128)(2,1)}), bf16[4,2,64,512]{3,2,1,0:T(8,128)(2,1)}) %reduce-scatter.2.cloned.1.call-update) | async-done | bytes 524304 | tf_op jit(solution)/shard_map/reduce_scatter | solution.py:288
  214.6 0.0 copy-done.1
  214.6 1.2 add_convert_fusion
  215.9 0.1 pad_maximum_fusion.1
  215.9 0.7 collective-permute-start.1
  216.6 0.0 collective-permute-done
  216.6 8.0 %collective-permute-done.1 = bf16[256,1024]{1,0:T(8,128)(2,1)S(1)} collective-permute-done((bf16[256,1024]{1,0:T(8,128)(2,1)S(1)}, bf16[256,1024]{1,0:T(8,128)(2,1)S(1)}, u32[]{:S(2)}, u32[]{:S(2)}) %collective-permute-start.1) | collective-permute-done | bytes 524320 | tf_op jit(solution)/shard_map/ppermute | solution.py:37
  224.6 0.8 slice_bitcast_fusion
  225.4 1.3 copy.41
  (7 shorter events, 0.1 us)
Async XLA Ops:
  7.2 77.9 %all-gather.2.cloned.1.call-start = ((), (), s32[]{:S(2)}) async-start(), calls=%async_computation.1 | async-start | bytes 4718592 | tf_op jit(solution)/shard_map/all_gather | solution.py:252
  9.1 205.5 %reduce-scatter.2.cloned.1.call-start = ((), (), s32[]{:S(2)}) async-start(), calls=%async_computation.2 | async-start | bytes 4718592 | tf_op jit(solution)/shard_map/reduce_scatter | solution.py:288
  117.1 2.8 %copy-start = (bf16[4,3,2,64,512]{4,3,2,1,0:T(8,128)(2,1)S(1)}, bf16[4,3,2,64,512]{4,3,2,1,0:T(8,128)(2,1)}, u32[]{:S(2)}) copy-start(bf16[4,3,2,64,512]{4,3,2,1,0:T(8,128)(2,1)} %get-tuple-element.12) | copy-start | bytes 4718596
  126.9 87.7 %copy-start.1 = (f32[4,2,64,512]{3,2,1,0:T(8,128)S(1)}, f32[4,2,64,512]{3,2,1,0:T(8,128)}, u32[]{:S(2)}) copy-start(f32[4,2,64,512]{3,2,1,0:T(8,128)} %get-tuple-element.9) | copy-start | bytes 3145732
  126.9 89.7 %collective-permute-start = (bf16[256,4096]{1,0:T(8,128)(2,1)}, bf16[256,4096]{1,0:T(8,128)(2,1)S(1)}, u32[]{:S(2)}, u32[]{:S(2)}) collective-permute-start(bf16[256,4096]{1,0:T(8,128)(2,1)} %get-tuple-element.8), channel_id=1, source_target_pairs={{8,0},{16,8},{24,16},{0,24},{9,1},{17,9},{25,17},{1,25},{10,2},{18... | collective-permute-start | bytes 6291464 | tf_op jit(solution)/shard_map/ppermute | solution.py:37
  215.9 8.7 %collective-permute-start.1 = (bf16[256,1024]{1,0:T(8,128)(2,1)S(1)}, bf16[256,1024]{1,0:T(8,128)(2,1)S(1)}, u32[]{:S(2)}, u32[]{:S(2)}) collective-permute-start(bf16[256,1024]{1,0:T(8,128)(2,1)S(1)} %pad_maximum_fusion.1), channel_id=1, source_target_pairs={{8,0},{16,8},{24,16},{0,24},{9,1},{17,9},{25,17},{1,25},{10,2},{18... | collective-permute-start | bytes 1572872 | tf_op jit(solution)/shard_map/ppermute | solution.py:37
Sparse Core Ops, SparseCore 0:
  10.7 74.2 all-gather.1
  127.0 87.5 reduce-scatter.1

commit v4 on v3

--- a/solution.py
+++ b/solution.py
@@ -35,6 +35,17 @@
     devices = range(lax.axis_size(axis))
     route = [((i - distance) % len(devices), i) for i in devices]
     return lax.ppermute(block, axis, route)
+
+
+def tree_sum(array, axis):
+    devices = lax.axis_size(axis)
+    if devices & (devices - 1):
+        return lax.psum(array, axis)
+    step = 1
+    while step < devices:
+        array = array + lax.ppermute(array, axis, [(i, i ^ step) for i in range(devices)])
+        step *= 2
+    return array
 
 
 def attention_kernel(ids_ref, q_ref, g_ref, *refs):
@@ -244,51 +255,82 @@
     kwidth = key_rows.shape[1]
     query_blocks = shard_tokens // BLK
     total_blocks = query_blocks * shards
-    near = 3 + GLOB
-    kvpair = jnp.stack(
+    own_blocks = jnp.stack(
         [key_rows.reshape(query_blocks, BLK, kwidth), value_rows.reshape(query_blocks, BLK, kwidth)],
         axis=1,
     )
-    all_blocks = lax.all_gather(kvpair, "seq", axis=0, tiled=True)
+    up = [(i, (i + 1) % shards) for i in range(shards - 1)]
+    down = [(j, i) for i, j in up]
+    edge_before = lax.ppermute(own_blocks[query_blocks - 1 :], "seq", up)
+    edge_after = lax.ppermute(own_blocks[:1], "seq", down)
+    global_mine = [
+        jnp.where(
+            global_ids[g] // query_blocks == this_shard,
+            lax.dynamic_index_in_dim(own_blocks, global_ids[g] % query_blocks, 0, keepdims=True),
+            jnp.zeros((), own_blocks.dtype),
+        )
+        for g in range(GLOB)
+    ]
+    global_tiles = tree_sum(jnp.concatenate(global_mine, axis=0), "seq")
+    requests = random_table.reshape(shards, query_blocks * RAND)
+    plan = request_plan(requests, this_shard, query_blocks)
+    serve_block, slot_used, owner_mine, rank_mine = plan
+    capacity = serve_block.shape[1]
+    served = jnp.take(own_blocks, serve_block.reshape(-1), axis=0)
+    received = lax.all_to_all(served, "seq", 0, 0, tiled=True)
+    sources = jnp.concatenate([own_blocks, edge_before, edge_after, global_tiles, received], axis=0)
+    nb = query_blocks
+    block_range = jnp.arange(nb, dtype=jnp.int32)
+    source_ids = jnp.concatenate(
+        [
+            jnp.where(block_range == 0, nb, block_range - 1)[:, None],
+            block_range[:, None],
+            jnp.where(block_range == nb - 1, nb + 1, block_range + 1)[:, None],
+            jnp.broadcast_to(nb + 2 + jnp.arange(GLOB, dtype=jnp.int32)[None, :], (nb, GLOB)),
+            (nb + 2 + GLOB + owner_mine * capacity + rank_mine).reshape(nb, RAND),
+        ],
+        axis=1,
+    )
+    source_ids = jnp.clip(source_ids, 0, sources.shape[0] - 1)
     random_three = random_table.reshape(shards, query_blocks, RAND)
-    base_ids = this_shard * query_blocks + jnp.arange(query_blocks, dtype=jnp.int32)
+    base_ids = this_shard * query_blocks + block_range
     window_ids = base_ids[:, None] + jnp.arange(-1, 2, dtype=jnp.int32)[None, :]
     my_random = lax.dynamic_index_in_dim(random_three, this_shard, 0, keepdims=False)
     tile_ids = jnp.concatenate(
         [window_ids, jnp.broadcast_to(global_ids[None, :], (query_blocks, GLOB)), my_random], axis=1
     )
-    safe_ids = jnp.clip(tile_ids, 0, total_blocks - 1)
     key_live = token_live(tile_ids, pad_sizes, query_blocks, shard_tokens, total_blocks)
     query_grad, local_sum, edge_terms, global_part, random_part = block_backward(
-        query_rows, grad_rows, all_blocks, safe_ids, key_live
+        query_rows, grad_rows, sources, source_ids, key_live
     )
     handed_query = from_behind(query_grad, "section", -1)
-    foreign = jnp.concatenate(
-        [
-            edge_terms.astype(jnp.bfloat16),
-            global_part.astype(jnp.bfloat16),
-            random_part.reshape(query_blocks * RAND, 2, BLK, kwidth),
-        ],
-        axis=0,
-    )
-    foreign_ids = jnp.concatenate(
-        [
-            safe_ids[0:1, 0],
-            safe_ids[query_blocks - 1 : query_blocks, 2],
-            global_ids,
-            my_random.reshape(-1),
-        ]
+    edge_low = edge_terms.astype(jnp.bfloat16)
+    from_after = lax.ppermute(edge_low[:1], "seq", down)
+    from_before = lax.ppermute(edge_low[1:], "seq", up)
+    holder = jnp.zeros((shards, capacity, 2, BLK, kwidth), random_part.dtype)
+    holder = holder.at[owner_mine, rank_mine].set(
+        random_part.reshape(query_blocks * RAND, 2, BLK, kwidth)
+    )
+    returned = lax.all_to_all(
+        holder.reshape(shards * capacity, 2, BLK, kwidth), "seq", 0, 0, tiled=True
     )
     onehot = (
-        foreign_ids[None, :] == jnp.arange(total_blocks, dtype=jnp.int32)[:, None]
+        slot_used.reshape(-1)[None, :]
+        & (serve_block.reshape(-1)[None, :] == block_range[:, None])
     ).astype(jnp.bfloat16)
-    partial = jnp.einsum(
-        "nf,fxsk->nxsk", onehot, foreign, preferred_element_type=jnp.float32
-    ).astype(jnp.bfloat16)
-    returned = lax.psum_scatter(
-        partial, "seq", scatter_dimension=0, tiled=True
-    )
-    kv_sum = local_sum + returned.astype(jnp.float32)
+    kv_sum = local_sum + jnp.einsum(
+        "qf,fxsk->qxsk", onehot, returned, preferred_element_type=jnp.float32
+    )
+    kv_sum = kv_sum.at[nb - 1].add(from_after[0].astype(jnp.float32))
+    kv_sum = kv_sum.at[0].add(from_before[0].astype(jnp.float32))
+    global_total = tree_sum(global_part, "seq")
+    global_pick = (
+        (global_ids[:, None] // query_blocks == this_shard)
+        & (global_ids[:, None] % query_blocks == block_range[None, :])
+    ).astype(jnp.float32)
+    kv_sum = kv_sum + jnp.einsum(
+        "gq,gxsk->qxsk", global_pick, global_total, precision=lax.Precision.HIGHEST
+    )
     kv_grad = jnp.concatenate(
         [
             kv_sum[:, 0].reshape(shard_tokens, kwidth).astype(jnp.bfloat16),

time: 234 us -> 242 us (1.034)
  waiting for transfers between devices: 162 us -> 103 us
  starting transfers between devices: 2.67 us -> 34 us
  local copies, waits for them, and re-layouts: 10.7 us -> 35.9 us
  other arithmetic: 9.84 us -> 25.3 us
  between operations: 14.1 us -> 6.15 us
    ppermute x0 -> x10, waiting for transfers between devices: none -> 95.1 us  [the longest x6 95.1 us: tree_sum(): lax.ppermute(array, axis, [(i, i ^ step) for i in range(devices)])]
    reduce_scatter x1 -> x0, waiting for transfers between devices: 85.8 us -> none  [body(): returned = lax.psum_scatter(partial, 'seq', scatter_dimension=0, tiled=True)]
    all_gather x1 -> x0, waiting for transfers between devices: 68.7 us -> none  [body(): all_blocks = lax.all_gather(kvpair, 'seq', axis=0, tiled=True)]
    ppermute x0 -> x10, starting transfers between devices: none -> 18.4 us  [the longest x6 7.88 us: tree_sum(): lax.ppermute(array, axis, [(i, i ^ step) for i in range(devices)])]
    all_to_all x0 -> x2, starting transfers between devices: none -> 12.7 us  [the longest x1 6.49 us: body(): received = lax.all_to_all(served, 'seq', 0, 0, tiled=True)]
    add x1 -> x9, other arithmetic: 0.01 us -> 6.98 us  [the longest x5 4.74 us: tree_sum(): array + lax.ppermute(array, axis, [(i, i ^ step) for i in range(devices)])]
    select_n x0 -> x6, other arithmetic: none -> 5.6 us  [the longest x2 3.18 us: body(): served = jnp.take(own_blocks, serve_block.reshape(-1), axis=0)]
    unnamed x5 -> x22, local copies, waits for them, and re-layouts: 1.33 us -> 6.85 us
  transfers between devices with their start and end apart: 4 -> 14, of which waited for: 3 -> 7; matrix products, arithmetic and copies ran while one was open for 4% -> 17% of each run, Pallas kernels for 0% -> 0%
where the time goes in v4:
time: 242 us; the launch traced here: 240 us
  waiting for transfers between devices  103 us (43%)
  local copies, waits for them, and re-layouts  35.9 us (15%)
  starting transfers between devices  34 us (14%)
  Pallas kernels  32.1 us (13%)
  other arithmetic  25.3 us (10%)
  between operations  6.15 us (3%)
  matrix products  3.83 us (2%)
    ppermute x6, waiting for transfers between devices, tree_sum(): lax.ppermute(array, axis, [(i, i ^ step) for i in range(devices)])  95.1 us
    pallas_call x1, Pallas kernels, block_backward(): pl.pallas_call(attention_kernel, grid_spec=grid_spec, out_shape=[jax.Shap...  32.1 us
    ppermute x2, waiting for transfers between devices, from_behind(): return lax.ppermute(block, axis, route)  7.97 us
    ppermute x6, starting transfers between devices, tree_sum(): lax.ppermute(array, axis, [(i, i ^ step) for i in range(devices)])  7.88 us
    unnamed x22, local copies, waits for them, and re-layouts  6.85 us
    all_to_all x1, starting transfers between devices, body(): received = lax.all_to_all(served, 'seq', 0, 0, tiled=True)  6.49 us
    all_to_all x1, starting transfers between devices, body(): lax.all_to_all(holder.reshape(shards * capacity, 2, BLK, kwidth), 'seq',...  6.26 us
    scatter x1, local copies, waits for them, and re-layouts, body(): holder.at[owner_mine, rank_mine]  5.1 us
  transfers between devices with their start and end apart: 14, of which 7 were waited for; matrix products, arithmetic and copies ran while one was open for 17% of the time, Pallas kernels for 0%

profile of v4, /device:TPU:1, one launch (start us, length us, event | category | flops | bytes accessed | tf_op | source)
XLA Modules:
  0.0 240.4 jit_solution(15391628746396909280)
XLA Ops:
  2.5 1.9 pad_maximum_fusion
  4.4 3.0 %gather_fusion = bf16[16,2,64,512]{3,2,1,0:T(8,128)(2,1)} fusion(bf16[4,2,64,512]{3,2,1,0:T(8,128)(2,1)} %get-tuple-element.45, s32[1024]{0:T(1024)S(1)} %pad_clamp_fusion), kind=kCustom, calls=%fused_computation | custom fusion | bytes 4194368 | tf_op jit(solution)/shard_map/jit(_take)/gather | solution.py:279
  7.5 3.2 %broadcast_select_fusion = bf16[16,2,64,512]{3,2,1,0:T(8,128)(2,1)} fusion(bf16[16,2,64,512]{3,2,1,0:T(8,128)(2,1)} %gather_fusion, pred[16]{0:T(512)(128)(4,1)S(1)} %compare_and_fusion.1), kind=kLoop, calls=%fused_computation.4 | loop fusion | flops 1048576 | bytes 4194320 | tf_op jit(solution)/shard_map/jit(_take)/select_n | solution.py:279
  10.6 6.5 %all-to-all-start = ((bf16[16,2,64,512]{3,2,1,0:T(8,128)(2,1)}), bf16[16,2,64,512]{3,2,1,0:T(8,128)(2,1)}, u32[]{:S(2)}, u32[]{:S(2)}) async-start(bf16[16,2,64,512]{3,2,1,0:T(8,128)(2,1)} %broadcast_select_fusion), calls=%async_computation | async-start | bytes 4194304 | tf_op jit(solution)/shard_map/all_to_all | solution.py:280
  22.9 1.8 fusion.10
  24.7 4.0 %collective-permute-start = (bf16[1,2,64,512]{3,2,1,0:T(8,128)(2,1)}, bf16[1,2,64,512]{3,2,1,0:T(8,128)(2,1)}, u32[]{:S(2)}, u32[]{:S(2)}) collective-permute-start(bf16[1,2,64,512]{3,2,1,0:T(8,128)(2,1)} %get-tuple-element.48), channel_id=1, source_target_pairs={{0,1},{1,2},{2,3},{3,4},{4,5},{5,6},{6,7},{8,9},{9,10},{10,11},{11... | collective-permute-start | bytes 393224 | tf_op jit(solution)/shard_map/ppermute | solution.py:264
  28.8 1.3 collective-permute-start.1
  30.8 2.1 collective-permute-start.2
  34.1 1.3 add.254
  37.4 1.2 pad.7.clone
  39.8 1.4 concatenate.40
  41.3 1.3 broadcast_clamp_fusion
  42.5 1.3 fusion.19
  45.4 4.7 %collective-permute-done.2 = bf16[2,2,64,512]{3,2,1,0:T(8,128)(2,1)} collective-permute-done((bf16[2,2,64,512]{3,2,1,0:T(8,128)(2,1)}, bf16[2,2,64,512]{3,2,1,0:T(8,128)(2,1)}, u32[]{:S(2)}, u32[]{:S(2)}) %collective-permute-start.2) | collective-permute-done | bytes 262176 | tf_op jit(solution)/shard_map/ppermute | solution.py:46
  50.1 1.7 fusion.36
  52.5 1.3 lt.136
  53.9 1.4 lt.137
  55.2 1.3 add.272
  56.6 1.4 add.273
  58.6 1.3 and_convert_fusion.refs_8_
  60.0 8.8 %collective-permute-done.3 = bf16[2,2,64,512]{3,2,1,0:T(8,128)(2,1)} collective-permute-done((bf16[2,2,64,512]{3,2,1,0:T(8,128)(2,1)}, bf16[2,2,64,512]{3,2,1,0:T(8,128)(2,1)}, u32[]{:S(2)}, u32[]{:S(2)}) %collective-permute-start.3) | collective-permute-done | bytes 262176 | tf_op jit(solution)/shard_map/ppermute | solution.py:46
  68.8 1.8 fusion.40
  70.6 3.1 %collective-permute-start.4 = (bf16[2,2,64,512]{3,2,1,0:T(8,128)(2,1)}, bf16[2,2,64,512]{3,2,1,0:T(8,128)(2,1)S(1)}, u32[]{:S(2)}, u32[]{:S(2)}) collective-permute-start(bf16[2,2,64,512]{3,2,1,0:T(8,128)(2,1)} %fusion.40), channel_id=1, source_target_pairs={{0,4},{1,5},{2,6},{3,7},{4,0},{5,1},{6,2},{7,3},{8,12},{9,13},{10,... | collective-permute-start | bytes 786440 | tf_op jit(solution)/shard_map/ppermute | solution.py:46
  73.7 1.3 min.18.ids_ref
  75.1 0.9 constant_dynamic-update-slice_fusion.2
  76.0 8.7 %collective-permute-done.4 = bf16[2,2,64,512]{3,2,1,0:T(8,128)(2,1)S(1)} collective-permute-done((bf16[2,2,64,512]{3,2,1,0:T(8,128)(2,1)}, bf16[2,2,64,512]{3,2,1,0:T(8,128)(2,1)S(1)}, u32[]{:S(2)}, u32[]{:S(2)}) %collective-permute-start.4) | collective-permute-done | bytes 262176 | tf_op jit(solution)/shard_map/ppermute | solution.py:46
  84.7 1.0 add_dynamic-update-slice_fusion
  85.8 1.8 constant_dynamic-update-slice_fusion.refs_0_.refs_1_.refs_2_.refs_3_.refs_4_.refs_5_.refs_6_.refs_7_
  87.6 1.6 copy-done
  89.2 32.1 %shard_map.97 = (bf16[256,4096]{1,0:T(8,128)(2,1)}, f32[4,2,64,512]{3,2,1,0:T(8,128)}, f32[2,2,64,512]{3,2,1,0:T(8,128)}, f32[2,2,64,512]{3,2,1,0:T(8,128)}, bf16[4,3,2,64,512]{4,3,2,1,0:T(8,128)(2,1)}) custom-call(s32[32]{0:T(128)} %min.18.ids_ref, bf16[256,4096]{1,0:T(8,128)(2,1)} %bitcast.48, bf16[256,4096]{1,0:T(8,128)(2,1)} %bitcast.49, ...), custom_call_target="tpu_custom_call" | custom-call | flops 6442450944 | bytes 12582912 | tf_op jit(solution)/shard_map/pallas_call | solution.py:161
  121.3 1.6 broadcast_in_dim.98
  123.2 5.1 %scatter_fusion = bf16[8,2,2,64,512]{4,3,2,1,0:T(8,128)(2,1)} fusion(bf16[8,2,2,64,512]{4,3,2,1,0:T(8,128)(2,1)} %broadcast_in_dim.98, s32[12]{0:T(128)S(1)} %fusion.34, bf16[12,2,64,512]{3,2,1,0:T(8,128)(2,1)S(1)} %bitcast.50), kind=kCustom, calls=%fused_computation.1 | custom fusion | bytes 4718688 | tf_op jit(solution)/shard_map/scatter | solution.py:311
  128.3 6.3 %all-to-all-start.1 = ((bf16[16,2,64,512]{3,2,1,0:T(8,128)(2,1)}), bf16[16,2,64,512]{3,2,1,0:T(8,128)(2,1)S(1)}, u32[]{:S(2)}, u32[]{:S(2)}) async-start(bf16[16,2,64,512]{3,2,1,0:T(8,128)(2,1)} %bitcast.17), calls=%async_computation.1 | async-start | bytes 4194304 | tf_op jit(solution)/shard_map/all_to_all | solution.py:314
  134.6 1.5 collective-permute-start.8
  136.1 33.9 %collective-permute-done.8 = f32[2,2,64,512]{3,2,1,0:T(8,128)S(1)} collective-permute-done((f32[2,2,64,512]{3,2,1,0:T(8,128)S(1)}, f32[2,2,64,512]{3,2,1,0:T(8,128)S(1)}, u32[]{:S(2)}, u32[]{:S(2)}) %collective-permute-start.8) | collective-permute-done | bytes 524320 | tf_op jit(solution)/shard_map/ppermute | solution.py:46
  170.7 22.9 %collective-permute-done.9 = f32[2,2,64,512]{3,2,1,0:T(8,128)S(1)} collective-permute-done((f32[2,2,64,512]{3,2,1,0:T(8,128)S(1)}, f32[2,2,64,512]{3,2,1,0:T(8,128)S(1)}, u32[]{:S(2)}, u32[]{:S(2)}) %collective-permute-start.9) | collective-permute-done | bytes 524320 | tf_op jit(solution)/shard_map/ppermute | solution.py:46
  193.6 1.1 collective-permute-start.10
  195.9 1.1 convert_element_type.29
  197.7 1.3 collective-permute-start.6
  199.0 4.0 %collective-permute-start.7 = (bf16[1,2,64,512]{3,2,1,0:T(8,128)(2,1)S(1)}, bf16[1,2,64,512]{3,2,1,0:T(8,128)(2,1)S(1)}, u32[]{:S(2)}, u32[]{:S(2)}) collective-permute-start(bf16[1,2,64,512]{3,2,1,0:T(8,128)(2,1)S(1)} %get-tuple-element.51), channel_id=1, source_target_pairs={{0,1},{1,2},{2,3},{3,4},{4,5},{5,6},{6,7},{8,9},{9,10},{10,11},{11... | collective-permute-start | bytes 393224 | tf_op jit(solution)/shard_map/ppermute | solution.py:309
  203.0 16.1 %collective-permute-done.10 = f32[2,2,64,512]{3,2,1,0:T(8,128)} collective-permute-done((f32[2,2,64,512]{3,2,1,0:T(8,128)S(1)}, f32[2,2,64,512]{3,2,1,0:T(8,128)}, u32[]{:S(2)}, u32[]{:S(2)}) %collective-permute-start.10) | collective-permute-done | bytes 524320 | tf_op jit(solution)/shard_map/ppermute | solution.py:46
  219.1 1.1 add.286
  220.2 2.5 %fusion.3 = f32[4,2,64,512]{3,0,2,1:T(4,128)} fusion(f32[2,2,64,512]{3,2,1,0:T(8,128)S(1)} %add.286, pred[2]{0:T(512)(128)(4,1)S(1)} %copy-done.8, s32[2]{0:T(128)S(1)} %and_select_fusion), kind=kOutput, calls=%fused_computation.18 | convolution fusion | flops 6291472 | bytes 1572874 | tf_op jit(solution)/shard_map/gq,gxsk->qxsk/dot_general | solution.py:331
  222.8 1.3 fusion
  224.1 1.7 copy_add_fusion.1
  226.4 2.0 collective-permute-start.11
  228.4 8.0 %collective-permute-done.11 = bf16[256,1024]{1,0:T(8,128)(2,1)S(1)} collective-permute-done((bf16[256,1024]{1,0:T(8,128)(2,1)S(1)}, bf16[256,1024]{1,0:T(8,128)(2,1)S(1)}, u32[]{:S(2)}, u32[]{:S(2)}) %collective-permute-start.11) | collective-permute-done | bytes 524320 | tf_op jit(solution)/shard_map/ppermute | solution.py:37
  237.2 3.1 %copy.96 = bf16[1,256,4096]{2,1,0:T(8,128)(2,1)} copy(bf16[1,256,4096]{2,1,0:T(8,128)(2,1)} %bitcast.10) | data formatting | bytes 4194304
  (80 shorter events, 15.0 us)
Async XLA Ops:
  2.4 5.0 %copy-start.4 = (s32[16]{0:T(128)}, s32[16]{0:T(128)S(1)}, u32[]{:S(2)}) copy-start(s32[16]{0:T(128)S(1)} %reshape.651) | copy-start | bytes 196
  10.6 6.5 %copy-start.6 = (s32[1,2]{1,0:T(1,128)S(1)}, s32[1,2]{1,0:T(1,128)}, u32[]{:S(2)}) copy-start(s32[1,2]{1,0:T(1,128)} %param.16) | copy-start | bytes 28
  10.6 75.1 %all-to-all-start = ((bf16[16,2,64,512]{3,2,1,0:T(8,128)(2,1)}), bf16[16,2,64,512]{3,2,1,0:T(8,128)(2,1)}, u32[]{:S(2)}, u32[]{:S(2)}) async-start(bf16[16,2,64,512]{3,2,1,0:T(8,128)(2,1)} %broadcast_select_fusion), calls=%async_computation | async-start | bytes 4194304 | tf_op jit(solution)/shard_map/all_to_all | solution.py:280
  24.7 50.3 %collective-permute-start = (bf16[1,2,64,512]{3,2,1,0:T(8,128)(2,1)}, bf16[1,2,64,512]{3,2,1,0:T(8,128)(2,1)}, u32[]{:S(2)}, u32[]{:S(2)}) collective-permute-start(bf16[1,2,64,512]{3,2,1,0:T(8,128)(2,1)} %get-tuple-element.48), channel_id=1, source_target_pairs={{0,1},{1,2},{2,3},{3,4},{4,5},{5,6},{6,7},{8,9},{9,10},{10,11},{11... | collective-permute-start | bytes 393224 | tf_op jit(solution)/shard_map/ppermute | solution.py:264
  28.8 47.2 %collective-permute-start.1 = (bf16[1,2,64,512]{3,2,1,0:T(8,128)(2,1)}, bf16[1,2,64,512]{3,2,1,0:T(8,128)(2,1)S(1)}, u32[]{:S(2)}, u32[]{:S(2)}) collective-permute-start(bf16[1,2,64,512]{3,2,1,0:T(8,128)(2,1)} %get-tuple-element.49), channel_id=1, source_target_pairs={{1,0},{2,1},{3,2},{4,3},{5,4},{6,5},{7,6},{9,8},{10,9},{11,10},{12... | collective-permute-start | bytes 393224 | tf_op jit(solution)/shard_map/ppermute | solution.py:265
  30.8 19.3 %collective-permute-start.2 = (bf16[2,2,64,512]{3,2,1,0:T(8,128)(2,1)}, bf16[2,2,64,512]{3,2,1,0:T(8,128)(2,1)}, u32[]{:S(2)}, u32[]{:S(2)}) collective-permute-start(bf16[2,2,64,512]{3,2,1,0:T(8,128)(2,1)} %pad_maximum_fusion.2), channel_id=1, source_target_pairs={{0,1},{1,0},{2,3},{3,2},{4,5},{5,4},{6,7},{7,6},{8,9},{9,8},{10,11... | collective-permute-start | bytes 786440 | tf_op jit(solution)/shard_map/ppermute | solution.py:46
  51.7 17.0 %collective-permute-start.3 = (bf16[2,2,64,512]{3,2,1,0:T(8,128)(2,1)}, bf16[2,2,64,512]{3,2,1,0:T(8,128)(2,1)}, u32[]{:S(2)}, u32[]{:S(2)}) collective-permute-start(bf16[2,2,64,512]{3,2,1,0:T(8,128)(2,1)} %fusion.36), channel_id=1, source_target_pairs={{0,2},{1,3},{2,0},{3,1},{4,6},{5,7},{6,4},{7,5},{8,10},{9,11},{10,... | collective-permute-start | bytes 786440 | tf_op jit(solution)/shard_map/ppermute | solution.py:46
  70.6 14.2 %collective-permute-start.4 = (bf16[2,2,64,512]{3,2,1,0:T(8,128)(2,1)}, bf16[2,2,64,512]{3,2,1,0:T(8,128)(2,1)S(1)}, u32[]{:S(2)}, u32[]{:S(2)}) collective-permute-start(bf16[2,2,64,512]{3,2,1,0:T(8,128)(2,1)} %fusion.40), channel_id=1, source_target_pairs={{0,4},{1,5},{2,6},{3,7},{4,0},{5,1},{6,2},{7,3},{8,12},{9,13},{10,... | collective-permute-start | bytes 786440 | tf_op jit(solution)/shard_map/ppermute | solution.py:46
  87.6 1.6 copy-start
  121.3 1.9 copy-start.2
  128.3 6.3 %copy-start.3 = (f32[2,2,64,512]{3,2,1,0:T(8,128)S(1)}, f32[2,2,64,512]{3,2,1,0:T(8,128)}, u32[]{:S(2)}) copy-start(f32[2,2,64,512]{3,2,1,0:T(8,128)} %get-tuple-element.36) | copy-start | bytes 1572868
  128.3 41.8 %copy-start.7 = (s32[1,2]{1,0:T(1,128)S(1)}, s32[1,2]{1,0:T(1,128)}, u32[]{:S(2)}) copy-start(s32[1,2]{1,0:T(1,128)} %param.16) | copy-start | bytes 28
  128.3 94.4 %all-to-all-start.1 = ((bf16[16,2,64,512]{3,2,1,0:T(8,128)(2,1)}), bf16[16,2,64,512]{3,2,1,0:T(8,128)(2,1)S(1)}, u32[]{:S(2)}, u32[]{:S(2)}) async-start(bf16[16,2,64,512]{3,2,1,0:T(8,128)(2,1)} %bitcast.17), calls=%async_computation.1 | async-start | bytes 4194304 | tf_op jit(solution)/shard_map/all_to_all | solution.py:314
  134.6 35.4 %collective-permute-start.8 = (f32[2,2,64,512]{3,2,1,0:T(8,128)S(1)}, f32[2,2,64,512]{3,2,1,0:T(8,128)S(1)}, u32[]{:S(2)}, u32[]{:S(2)}) collective-permute-start(f32[2,2,64,512]{3,2,1,0:T(8,128)S(1)} %copy-done.3), channel_id=1, source_target_pairs={{0,1},{1,0},{2,3},{3,2},{4,5},{5,4},{6,7},{7,6},{8,9},{9,8},{10,11... | collective-permute-start | bytes 1572872 | tf_op jit(solution)/shard_map/ppermute | solution.py:46
  170.1 23.5 %collective-permute-start.9 = (f32[2,2,64,512]{3,2,1,0:T(8,128)S(1)}, f32[2,2,64,512]{3,2,1,0:T(8,128)S(1)}, u32[]{:S(2)}, u32[]{:S(2)}) collective-permute-start(f32[2,2,64,512]{3,2,1,0:T(8,128)S(1)} %add.284), channel_id=1, source_target_pairs={{0,2},{1,3},{2,0},{3,1},{4,6},{5,7},{6,4},{7,5},{8,10},{9,11},{10,... | collective-permute-start | bytes 1572872 | tf_op jit(solution)/shard_map/ppermute | solution.py:46
  193.6 25.5 %collective-permute-start.10 = (f32[2,2,64,512]{3,2,1,0:T(8,128)S(1)}, f32[2,2,64,512]{3,2,1,0:T(8,128)}, u32[]{:S(2)}, u32[]{:S(2)}) collective-permute-start(f32[2,2,64,512]{3,2,1,0:T(8,128)S(1)} %add.285), channel_id=1, source_target_pairs={{0,4},{1,5},{2,6},{3,7},{4,0},{5,1},{6,2},{7,3},{8,12},{9,13},{10,... | collective-permute-start | bytes 1572872 | tf_op jit(solution)/shard_map/ppermute | solution.py:46
  194.9 25.3 %copy-start.8 = (pred[2]{0:T(512)(128)(4,1)S(1)}, pred[2]{0:T(512)(128)(4,1)}, u32[]{:S(2)}) copy-start(pred[2]{0:T(512)(128)(4,1)} %fusion.35) | copy-start | bytes 10
  195.1 33.3 %collective-permute-start.5 = (bf16[256,4096]{1,0:T(8,128)(2,1)}, bf16[256,4096]{1,0:T(8,128)(2,1)}, u32[]{:S(2)}, u32[]{:S(2)}) collective-permute-start(bf16[256,4096]{1,0:T(8,128)(2,1)} %get-tuple-element.32), channel_id=1, source_target_pairs={{8,0},{16,8},{24,16},{0,24},{9,1},{17,9},{25,17},{1,25},{10,2},{18... | collective-permute-start | bytes 6291464 | tf_op jit(solution)/shard_map/ppermute | solution.py:37
  195.9 26.9 %copy-start.5 = (s32[16]{0:T(128)S(1)}, s32[16]{0:T(128)}, u32[]{:S(2)}) copy-start(s32[16]{0:T(128)} %copy-done.4) | copy-start | bytes 196
  197.7 28.1 %collective-permute-start.6 = (bf16[1,2,64,512]{3,2,1,0:T(8,128)(2,1)}, bf16[1,2,64,512]{3,2,1,0:T(8,128)(2,1)S(1)}, u32[]{:S(2)}, u32[]{:S(2)}) collective-permute-start(bf16[1,2,64,512]{3,2,1,0:T(8,128)(2,1)} %get-tuple-element.52), channel_id=1, source_target_pairs={{1,0},{2,1},{3,2},{4,3},{5,4},{6,5},{7,6},{9,8},{10,9},{11,10},{12... | collective-permute-start | bytes 393224 | tf_op jit(solution)/shard_map/ppermute | solution.py:308
  199.0 26.9 %collective-permute-start.7 = (bf16[1,2,64,512]{3,2,1,0:T(8,128)(2,1)S(1)}, bf16[1,2,64,512]{3,2,1,0:T(8,128)(2,1)S(1)}, u32[]{:S(2)}, u32[]{:S(2)}) collective-permute-start(bf16[1,2,64,512]{3,2,1,0:T(8,128)(2,1)S(1)} %get-tuple-element.51), channel_id=1, source_target_pairs={{0,1},{1,2},{2,3},{3,4},{4,5},{5,6},{6,7},{8,9},{9,10},{10,11},{11... | collective-permute-start | bytes 393224 | tf_op jit(solution)/shard_map/ppermute | solution.py:309
  224.1 1.9 copy-start.1
  226.4 10.0 %collective-permute-start.11 = (bf16[256,1024]{1,0:T(8,128)(2,1)S(1)}, bf16[256,1024]{1,0:T(8,128)(2,1)S(1)}, u32[]{:S(2)}, u32[]{:S(2)}) collective-permute-start(bf16[256,1024]{1,0:T(8,128)(2,1)S(1)} %pad_maximum_fusion.1), channel_id=1, source_target_pairs={{8,0},{16,8},{24,16},{0,24},{9,1},{17,9},{25,17},{1,25},{10,2},{18... | collective-permute-start | bytes 1572872 | tf_op jit(solution)/shard_map/ppermute | solution.py:37

commit v5 on v4

--- a/solution.py
+++ b/solution.py
@@ -39,13 +39,26 @@
 
 def tree_sum(array, axis):
     devices = lax.axis_size(axis)
-    if devices & (devices - 1):
+    rows = array.size // array.shape[-1]
+    if devices & (devices - 1) or rows % devices:
         return lax.psum(array, axis)
+    me = lax.axis_index(axis)
+    pieces = array.reshape(rows, array.shape[-1])
     step = 1
     while step < devices:
-        array = array + lax.ppermute(array, axis, [(i, i ^ step) for i in range(devices)])
+        half = pieces.shape[0] // 2
+        bit = (me // step) % 2
+        keep = lax.dynamic_slice_in_dim(pieces, bit * half, half)
+        send = lax.dynamic_slice_in_dim(pieces, (1 - bit) * half, half)
+        pieces = keep + lax.ppermute(send, axis, [(i, i ^ step) for i in range(devices)])
         step *= 2
-    return array
+    while step > 1:
+        step //= 2
+        bit = (me // step) % 2
+        other = lax.ppermute(pieces, axis, [(i, i ^ step) for i in range(devices)])
+        both = jnp.concatenate([pieces, other], axis=0)
+        pieces = jnp.where(bit == 0, both, jnp.concatenate([other, pieces], axis=0))
+    return pieces.reshape(array.shape)
 
 
 def attention_kernel(ids_ref, q_ref, g_ref, *refs):

time: 242 us -> 245 us (1.012)
  starting transfers between devices: 34 us -> 48.1 us
  local copies, waits for them, and re-layouts: 35.9 us -> 28.5 us
  other arithmetic: 25.3 us -> 19.3 us
  waiting for transfers between devices: 103 us -> 106 us
    ppermute x6 -> x12, starting transfers between devices: 7.88 us -> 22.5 us  [the longest x6 14.3 us: tree_sum(): lax.ppermute(send, axis, [(i, i ^ step) for i in range(devices)])]
    ppermute x2, waiting for transfers between devices: 7.97 us -> 18.9 us  [from_behind(): return lax.ppermute(block, axis, route)]
    ppermute x6 -> x12, waiting for transfers between devices: 95.1 us -> 86.2 us  [the longest x6 73.1 us: tree_sum(): lax.ppermute(send, axis, [(i, i ^ step) for i in range(devices)])]
    add x5 -> x6, other arithmetic: 4.74 us -> 1.04 us  [tree_sum(): keep + lax.ppermute(send, axis, [(i, i ^ step) for i in range(devices)])]
    unnamed x22 -> x31, local copies, waits for them, and re-layouts: 6.85 us -> 6.88 us
  transfers between devices with their start and end apart: 14 -> 20, of which waited for: 7 -> 13; matrix products, arithmetic and copies ran while one was open for 17% -> 14% of each run, Pallas kernels for 0% -> 0%
where the time goes in v5:
time: 245 us; the launch traced here: 244 us
  waiting for transfers between devices  106 us (43%)
  starting transfers between devices  48.1 us (20%)
  Pallas kernels  32.1 us (13%)
  local copies, waits for them, and re-layouts  28.5 us (12%)
  other arithmetic  19.3 us (8%)
  between operations  6.43 us (3%)
  matrix products  2.86 us (1%)
    ppermute x6, waiting for transfers between devices, tree_sum(): lax.ppermute(send, axis, [(i, i ^ step) for i in range(devices)])  73.1 us
    pallas_call x1, Pallas kernels, block_backward(): pl.pallas_call(attention_kernel, grid_spec=grid_spec, out_shape=[jax.Shap...  32.1 us
    ppermute x2, waiting for transfers between devices, from_behind(): return lax.ppermute(block, axis, route)  18.9 us
    ppermute x6, starting transfers between devices, tree_sum(): lax.ppermute(send, axis, [(i, i ^ step) for i in range(devices)])  14.3 us
    ppermute x6, waiting for transfers between devices, tree_sum(): other = lax.ppermute(pieces, axis, [(i, i ^ step) for i in range(devices)])  13.1 us
    ppermute x6, starting transfers between devices, tree_sum(): other = lax.ppermute(pieces, axis, [(i, i ^ step) for i in range(devices)])  8.2 us
    unnamed x31, local copies, waits for them, and re-layouts  6.88 us
    ppermute x2, starting transfers between devices, from_behind(): return lax.ppermute(block, axis, route)  5.17 us
  transfers between devices with their start and end apart: 20, of which 13 were waited for; matrix products, arithmetic and copies ran while one was open for 14% of the time, Pallas kernels for 0%

profile of v5, /device:TPU:1, one launch (start us, length us, event | category | flops | bytes accessed | tf_op | source)
XLA Modules:
  0.0 243.6 jit_solution(1354248913474525294)
XLA Ops:
  0.6 1.3 fusion.38
  7.2 1.8 fusion.10
  9.0 4.6 %collective-permute-start = (bf16[1,2,64,512]{3,2,1,0:T(8,128)(2,1)}, bf16[1,2,64,512]{3,2,1,0:T(8,128)(2,1)}, u32[]{:S(2)}, u32[]{:S(2)}) collective-permute-start(bf16[1,2,64,512]{3,2,1,0:T(8,128)(2,1)} %get-tuple-element.48), channel_id=1, source_target_pairs={{0,1},{1,2},{2,3},{3,4},{4,5},{5,6},{6,7},{8,9},{9,10},{10,11},{11... | collective-permute-start | bytes 393224 | tf_op jit(solution)/shard_map/ppermute | solution.py:277
  13.6 1.3 collective-permute-start.1
  15.6 2.1 collective-permute-start.2
  18.3 1.9 pad_maximum_fusion
  21.6 1.2 broadcast_compare_fusion
  24.3 1.0 convert_reduce_fusion
  26.5 3.0 %gather_fusion = bf16[16,2,64,512]{3,2,1,0:T(8,128)(2,1)} fusion(bf16[4,2,64,512]{3,2,1,0:T(8,128)(2,1)} %get-tuple-element.45, s32[1024]{0:T(1024)S(1)} %pad_clamp_fusion), kind=kCustom, calls=%fused_computation | custom fusion | bytes 4194368 | tf_op jit(solution)/shard_map/jit(_take)/gather | solution.py:292
  29.5 3.2 %broadcast_select_fusion = bf16[16,2,64,512]{3,2,1,0:T(8,128)(2,1)} fusion(bf16[16,2,64,512]{3,2,1,0:T(8,128)(2,1)} %gather_fusion, pred[16]{0:T(512)(128)(4,1)S(1)} %compare_and_fusion.1), kind=kLoop, calls=%fused_computation.4 | loop fusion | flops 1048576 | bytes 4194320 | tf_op jit(solution)/shard_map/jit(_take)/select_n | solution.py:292
  32.7 5.0 %all-to-all-start = ((bf16[16,2,64,512]{3,2,1,0:T(8,128)(2,1)}), bf16[16,2,64,512]{3,2,1,0:T(8,128)(2,1)}, u32[]{:S(2)}, u32[]{:S(2)}) async-start(bf16[16,2,64,512]{3,2,1,0:T(8,128)(2,1)} %broadcast_select_fusion), calls=%async_computation | async-start | bytes 4194304 | tf_op jit(solution)/shard_map/all_to_all | solution.py:293
  41.4 0.9 select_reduce_fusion
  44.6 1.3 and_convert_fusion.refs_8_
  45.9 0.9 dynamic-slice_add_fusion.2
  46.9 1.5 collective-permute-start.3
  48.4 23.3 %collective-permute-done.3 = bf16[64,512]{1,0:T(8,128)(2,1)S(1)} collective-permute-done((bf16[64,512]{1,0:T(8,128)(2,1)S(1)}, bf16[64,512]{1,0:T(8,128)(2,1)S(1)}, u32[]{:S(2)}, u32[]{:S(2)}) %collective-permute-start.3) | collective-permute-done | bytes 65568 | tf_op jit(solution)/shard_map/ppermute | solution.py:53
  71.7 4.1 %collective-permute-start.4 = (bf16[32,512]{1,0:T(8,128)(2,1)S(1)}, bf16[32,512]{1,0:T(8,128)(2,1)S(1)}, u32[]{:S(2)}, u32[]{:S(2)}) collective-permute-start(bf16[32,512]{1,0:T(8,128)(2,1)S(1)} %constant_dynamic-slice_fusion.4), channel_id=1, source_target_pairs={{0,4},{1,5},{2,6},{3,7},{4,0},{5,1},{6,2},{7,3},{8,12},{9,13},{10,... | collective-permute-start | bytes 98312 | tf_op jit(solution)/shard_map/ppermute | solution.py:53
  76.7 8.9 %collective-permute-done.4 = bf16[32,512]{1,0:T(8,128)(2,1)S(1)} collective-permute-done((bf16[32,512]{1,0:T(8,128)(2,1)S(1)}, bf16[32,512]{1,0:T(8,128)(2,1)S(1)}, u32[]{:S(2)}, u32[]{:S(2)}) %collective-permute-start.4) | collective-permute-done | bytes 32800 | tf_op jit(solution)/shard_map/ppermute | solution.py:53
  85.8 3.6 %collective-permute-done.5 = bf16[32,512]{1,0:T(8,128)(2,1)S(1)} collective-permute-done((bf16[32,512]{1,0:T(8,128)(2,1)S(1)}, bf16[32,512]{1,0:T(8,128)(2,1)S(1)}, u32[]{:S(2)}, u32[]{:S(2)}) %collective-permute-start.5) | collective-permute-done | bytes 32800 | tf_op jit(solution)/shard_map/ppermute | solution.py:58
  89.4 1.4 collective-permute-start.6
  93.0 2.5 %collective-permute-start.7 = (bf16[128,512]{1,0:T(8,128)(2,1)S(1)}, bf16[128,512]{1,0:T(8,128)(2,1)S(1)}, u32[]{:S(2)}, u32[]{:S(2)}) collective-permute-start(bf16[128,512]{1,0:T(8,128)(2,1)S(1)} %maximum_select_fusion.3), channel_id=1, source_target_pairs={{0,1},{1,0},{2,3},{3,2},{4,5},{5,4},{6,7},{7,6},{8,9},{9,8},{10,11... | collective-permute-start | bytes 393224 | tf_op jit(solution)/shard_map/ppermute | solution.py:58
  95.5 0.9 constant_dynamic-update-slice_fusion.3
  96.5 1.4 collective-permute-done.7
  98.0 1.8 constant_dynamic-update-slice_fusion.refs_0_.refs_1_.refs_2_.refs_3_.refs_4_.refs_5_.refs_6_.refs_7_
  99.7 1.6 copy-done
  101.4 32.1 %shard_map.97 = (bf16[256,4096]{1,0:T(8,128)(2,1)}, f32[4,2,64,512]{3,2,1,0:T(8,128)}, f32[2,2,64,512]{3,2,1,0:T(8,128)}, f32[2,2,64,512]{3,2,1,0:T(8,128)}, bf16[4,3,2,64,512]{4,3,2,1,0:T(8,128)(2,1)}) custom-call(s32[32]{0:T(128)} %min.18.ids_ref, bf16[256,4096]{1,0:T(8,128)(2,1)} %bitcast.52, bf16[256,4096]{1,0:T(8,128)(2,1)} %bitcast.53, ...), custom_call_target="tpu_custom_call" | custom-call | flops 6442450944 | bytes 12582912 | tf_op jit(solution)/shard_map/pallas_call | solution.py:174
  133.4 1.5 broadcast_in_dim.98
  135.4 5.1 %scatter_fusion = bf16[8,2,2,64,512]{4,3,2,1,0:T(8,128)(2,1)} fusion(bf16[8,2,2,64,512]{4,3,2,1,0:T(8,128)(2,1)} %broadcast_in_dim.98, s32[12]{0:T(128)S(1)} %fusion.34, bf16[12,2,64,512]{3,2,1,0:T(8,128)(2,1)S(1)} %bitcast.55), kind=kCustom, calls=%fused_computation.1 | custom fusion | bytes 4718688 | tf_op jit(solution)/shard_map/scatter | solution.py:324
  140.5 4.3 %all-to-all-start.1 = ((bf16[16,2,64,512]{3,2,1,0:T(8,128)(2,1)}), bf16[16,2,64,512]{3,2,1,0:T(8,128)(2,1)S(1)}, u32[]{:S(2)}, u32[]{:S(2)}) async-start(bf16[16,2,64,512]{3,2,1,0:T(8,128)(2,1)} %bitcast.19), calls=%async_computation.1 | async-start | bytes 4194304 | tf_op jit(solution)/shard_map/all_to_all | solution.py:327
  144.8 1.5 collective-permute-start.11
  146.3 21.6 %collective-permute-done.11 = f32[128,512]{1,0:T(8,128)S(1)} collective-permute-done((f32[128,512]{1,0:T(8,128)S(1)}, f32[128,512]{1,0:T(8,128)S(1)}, u32[]{:S(2)}, u32[]{:S(2)}) %collective-permute-start.11) | collective-permute-done | bytes 262176 | tf_op jit(solution)/shard_map/ppermute | solution.py:53
  168.0 1.3 collective-permute-start.12
  169.2 9.1 %collective-permute-done.12 = f32[64,512]{1,0:T(8,128)S(1)} collective-permute-done((f32[64,512]{1,0:T(8,128)S(1)}, f32[64,512]{1,0:T(8,128)S(1)}, u32[]{:S(2)}, u32[]{:S(2)}) %collective-permute-start.12) | collective-permute-done | bytes 131104 | tf_op jit(solution)/shard_map/ppermute | solution.py:53
  178.4 3.9 %collective-permute-start.13 = (f32[32,512]{1,0:T(8,128)S(1)}, f32[32,512]{1,0:T(8,128)S(1)}, u32[]{:S(2)}, u32[]{:S(2)}) collective-permute-start(f32[32,512]{1,0:T(8,128)S(1)} %constant_dynamic-slice_fusion), channel_id=1, source_target_pairs={{0,4},{1,5},{2,6},{3,7},{4,0},{5,1},{6,2},{7,3},{8,12},{9,13},{10,... | collective-permute-start | bytes 196616 | tf_op jit(solution)/shard_map/ppermute | solution.py:53
  182.2 10.2 %collective-permute-done.13 = f32[32,512]{1,0:T(8,128)S(1)} collective-permute-done((f32[32,512]{1,0:T(8,128)S(1)}, f32[32,512]{1,0:T(8,128)S(1)}, u32[]{:S(2)}, u32[]{:S(2)}) %collective-permute-start.13) | collective-permute-done | bytes 65568 | tf_op jit(solution)/shard_map/ppermute | solution.py:53
  192.6 4.4 %collective-permute-done.14 = f32[32,512]{1,0:T(8,128)S(1)} collective-permute-done((f32[32,512]{1,0:T(8,128)S(1)}, f32[32,512]{1,0:T(8,128)S(1)}, u32[]{:S(2)}, u32[]{:S(2)}) %collective-permute-start.14) | collective-permute-done | bytes 65568 | tf_op jit(solution)/shard_map/ppermute | solution.py:58
  197.0 1.0 collective-permute-start.15
  198.1 2.8 %collective-permute-done.15 = f32[64,512]{1,0:T(8,128)S(1)} collective-permute-done((f32[64,512]{1,0:T(8,128)S(1)}, f32[64,512]{1,0:T(8,128)S(1)}, u32[]{:S(2)}, u32[]{:S(2)}) %collective-permute-start.15) | collective-permute-done | bytes 131104 | tf_op jit(solution)/shard_map/ppermute | solution.py:58
  200.9 3.1 %collective-permute-start.16 = (f32[128,512]{1,0:T(8,128)S(1)}, f32[128,512]{1,0:T(8,128)S(1)}, u32[]{:S(2)}, u32[]{:S(2)}) collective-permute-start(f32[128,512]{1,0:T(8,128)S(1)} %maximum_select_fusion.2), channel_id=1, source_target_pairs={{0,1},{1,0},{2,3},{3,2},{4,5},{5,4},{6,7},{7,6},{8,9},{9,8},{10,11... | collective-permute-start | bytes 786440 | tf_op jit(solution)/shard_map/ppermute | solution.py:58
  204.4 4.7 %collective-permute-start.8 = (bf16[256,4096]{1,0:T(8,128)(2,1)}, bf16[256,4096]{1,0:T(8,128)(2,1)}, u32[]{:S(2)}, u32[]{:S(2)}) collective-permute-start(bf16[256,4096]{1,0:T(8,128)(2,1)} %get-tuple-element.32), channel_id=1, source_target_pairs={{8,0},{16,8},{24,16},{0,24},{9,1},{17,9},{25,17},{1,25},{10,2},{18... | collective-permute-start | bytes 6291464 | tf_op jit(solution)/shard_map/ppermute | solution.py:37
  209.7 1.3 collective-permute-start.9
  211.0 4.0 %collective-permute-start.10 = (bf16[1,2,64,512]{3,2,1,0:T(8,128)(2,1)S(1)}, bf16[1,2,64,512]{3,2,1,0:T(8,128)(2,1)S(1)}, u32[]{:S(2)}, u32[]{:S(2)}) collective-permute-start(bf16[1,2,64,512]{3,2,1,0:T(8,128)(2,1)S(1)} %get-tuple-element.51), channel_id=1, source_target_pairs={{0,1},{1,2},{2,3},{3,4},{4,5},{5,6},{6,7},{8,9},{9,10},{10,11},{11... | collective-permute-start | bytes 393224 | tf_op jit(solution)/shard_map/ppermute | solution.py:322
  215.1 1.6 fusion.3
  216.7 1.3 fusion
  218.4 1.2 collective-permute-done.10
  220.7 13.4 %collective-permute-done.8 = bf16[256,4096]{1,0:T(8,128)(2,1)} collective-permute-done((bf16[256,4096]{1,0:T(8,128)(2,1)}, bf16[256,4096]{1,0:T(8,128)(2,1)}, u32[]{:S(2)}, u32[]{:S(2)}) %collective-permute-start.8) | collective-permute-done | bytes 2097184 | tf_op jit(solution)/shard_map/ppermute | solution.py:37
  234.1 5.5 %collective-permute-done.17 = bf16[256,1024]{1,0:T(8,128)(2,1)S(1)} collective-permute-done((bf16[256,1024]{1,0:T(8,128)(2,1)S(1)}, bf16[256,1024]{1,0:T(8,128)(2,1)S(1)}, u32[]{:S(2)}, u32[]{:S(2)}) %collective-permute-start.17) | collective-permute-done | bytes 524320 | tf_op jit(solution)/shard_map/ppermute | solution.py:37
  240.5 3.1 %copy.95 = bf16[1,256,4096]{2,1,0:T(8,128)(2,1)} copy(bf16[1,256,4096]{2,1,0:T(8,128)(2,1)} %bitcast.12) | data formatting | bytes 4194304
  (113 shorter events, 18.5 us)
Async XLA Ops:
  9.0 86.5 %collective-permute-start = (bf16[1,2,64,512]{3,2,1,0:T(8,128)(2,1)}, bf16[1,2,64,512]{3,2,1,0:T(8,128)(2,1)}, u32[]{:S(2)}, u32[]{:S(2)}) collective-permute-start(bf16[1,2,64,512]{3,2,1,0:T(8,128)(2,1)} %get-tuple-element.48), channel_id=1, source_target_pairs={{0,1},{1,2},{2,3},{3,4},{4,5},{5,6},{6,7},{8,9},{9,10},{10,11},{11... | collective-permute-start | bytes 393224 | tf_op jit(solution)/shard_map/ppermute | solution.py:277
  13.6 82.8 %collective-permute-start.1 = (bf16[1,2,64,512]{3,2,1,0:T(8,128)(2,1)}, bf16[1,2,64,512]{3,2,1,0:T(8,128)(2,1)S(1)}, u32[]{:S(2)}, u32[]{:S(2)}) collective-permute-start(bf16[1,2,64,512]{3,2,1,0:T(8,128)(2,1)} %get-tuple-element.49), channel_id=1, source_target_pairs={{1,0},{2,1},{3,2},{4,3},{5,4},{6,5},{7,6},{9,8},{10,9},{11,10},{12... | collective-permute-start | bytes 393224 | tf_op jit(solution)/shard_map/ppermute | solution.py:278
  15.6 30.3 %collective-permute-start.2 = (bf16[128,512]{1,0:T(8,128)(2,1)}, bf16[128,512]{1,0:T(8,128)(2,1)}, u32[]{:S(2)}, u32[]{:S(2)}) collective-permute-start(bf16[128,512]{1,0:T(8,128)(2,1)} %constant_dynamic-slice_fusion.6), channel_id=1, source_target_pairs={{0,1},{1,0},{2,3},{3,2},{4,5},{5,4},{6,7},{7,6},{8,9},{9,8},{10,11... | collective-permute-start | bytes 393224 | tf_op jit(solution)/shard_map/ppermute | solution.py:53
  22.9 1.4 copy-start.7
  25.4 4.1 %copy-start.5 = (s32[8,12]{1,0:T(8,128)}, s32[8,12]{1,0:T(8,128)S(1)}, u32[]{:S(2)}) copy-start(s32[8,12]{1,0:T(8,128)S(1)} %copy.66) | copy-start | bytes 1156
  26.4 3.1 %copy-start.10 = (s32[16]{0:T(128)}, s32[16]{0:T(128)S(1)}, u32[]{:S(2)}) copy-start(s32[16]{0:T(128)S(1)} %reshape.668) | copy-start | bytes 196
  32.7 5.0 %copy-start.9 = (s32[1,32,3]{1,0,2:T(1,128)S(1)}, s32[1,32,3]{1,0,2:T(1,128)}, u32[]{:S(2)}) copy-start(s32[1,32,3]{1,0,2:T(1,128)} %param.15) | copy-start | bytes 1156
  32.7 65.3 %all-to-all-start = ((bf16[16,2,64,512]{3,2,1,0:T(8,128)(2,1)}), bf16[16,2,64,512]{3,2,1,0:T(8,128)(2,1)}, u32[]{:S(2)}, u32[]{:S(2)}) async-start(bf16[16,2,64,512]{3,2,1,0:T(8,128)(2,1)} %broadcast_select_fusion), calls=%async_computation | async-start | bytes 4194304 | tf_op jit(solution)/shard_map/all_to_all | solution.py:293
  46.9 24.8 %collective-permute-start.3 = (bf16[64,512]{1,0:T(8,128)(2,1)S(1)}, bf16[64,512]{1,0:T(8,128)(2,1)S(1)}, u32[]{:S(2)}, u32[]{:S(2)}) collective-permute-start(bf16[64,512]{1,0:T(8,128)(2,1)S(1)} %constant_dynamic-slice_fusion.5), channel_id=1, source_target_pairs={{0,2},{1,3},{2,0},{3,1},{4,6},{5,7},{6,4},{7,5},{8,10},{9,11},{10,... | collective-permute-start | bytes 196616 | tf_op jit(solution)/shard_map/ppermute | solution.py:53
  71.7 13.9 %collective-permute-start.4 = (bf16[32,512]{1,0:T(8,128)(2,1)S(1)}, bf16[32,512]{1,0:T(8,128)(2,1)S(1)}, u32[]{:S(2)}, u32[]{:S(2)}) collective-permute-start(bf16[32,512]{1,0:T(8,128)(2,1)S(1)} %constant_dynamic-slice_fusion.4), channel_id=1, source_target_pairs={{0,4},{1,5},{2,6},{3,7},{4,0},{5,1},{6,2},{7,3},{8,12},{9,13},{10,... | collective-permute-start | bytes 98312 | tf_op jit(solution)/shard_map/ppermute | solution.py:53
  85.7 3.7 %collective-permute-start.5 = (bf16[32,512]{1,0:T(8,128)(2,1)S(1)}, bf16[32,512]{1,0:T(8,128)(2,1)S(1)}, u32[]{:S(2)}, u32[]{:S(2)}) collective-permute-start(bf16[32,512]{1,0:T(8,128)(2,1)S(1)} %dynamic-slice_add_fusion.5), channel_id=1, source_target_pairs={{0,4},{1,5},{2,6},{3,7},{4,0},{5,1},{6,2},{7,3},{8,12},{9,13},{10,... | collective-permute-start | bytes 98312 | tf_op jit(solution)/shard_map/ppermute | solution.py:58
  89.4 3.5 %collective-permute-start.6 = (bf16[64,512]{1,0:T(8,128)(2,1)S(1)}, bf16[64,512]{1,0:T(8,128)(2,1)S(1)}, u32[]{:S(2)}, u32[]{:S(2)}) collective-permute-start(bf16[64,512]{1,0:T(8,128)(2,1)S(1)} %maximum_select_fusion.5), channel_id=1, source_target_pairs={{0,2},{1,3},{2,0},{3,1},{4,6},{5,7},{6,4},{7,5},{8,10},{9,11},{10,... | collective-permute-start | bytes 196616 | tf_op jit(solution)/shard_map/ppermute | solution.py:58
  93.0 4.9 %collective-permute-start.7 = (bf16[128,512]{1,0:T(8,128)(2,1)S(1)}, bf16[128,512]{1,0:T(8,128)(2,1)S(1)}, u32[]{:S(2)}, u32[]{:S(2)}) collective-permute-start(bf16[128,512]{1,0:T(8,128)(2,1)S(1)} %maximum_select_fusion.3), channel_id=1, source_target_pairs={{0,1},{1,0},{2,3},{3,2},{4,5},{5,4},{6,7},{7,6},{8,9},{9,8},{10,11... | collective-permute-start | bytes 393224 | tf_op jit(solution)/shard_map/ppermute | solution.py:58
  99.7 1.6 copy-start
  133.4 1.9 copy-start.1
  140.5 4.3 %copy-start.4 = (f32[2,2,64,512]{3,2,1,0:T(8,128)S(1)}, f32[2,2,64,512]{3,2,1,0:T(8,128)}, u32[]{:S(2)}) copy-start(f32[2,2,64,512]{3,2,1,0:T(8,128)} %get-tuple-element.36) | copy-start | bytes 1572868
  140.5 76.2 %all-to-all-start.1 = ((bf16[16,2,64,512]{3,2,1,0:T(8,128)(2,1)}), bf16[16,2,64,512]{3,2,1,0:T(8,128)(2,1)S(1)}, u32[]{:S(2)}, u32[]{:S(2)}) async-start(bf16[16,2,64,512]{3,2,1,0:T(8,128)(2,1)} %bitcast.19), calls=%async_computation.1 | async-start | bytes 4194304 | tf_op jit(solution)/shard_map/all_to_all | solution.py:327
  144.8 47.8 %copy-start.12 = (s32[1,2]{1,0:T(1,128)S(1)}, s32[1,2]{1,0:T(1,128)}, u32[]{:S(2)}) copy-start(s32[1,2]{1,0:T(1,128)} %param.16) | copy-start | bytes 28
  144.8 59.3 %copy-start.6 = (s32[8,12]{1,0:T(8,128)S(1)}, s32[8,12]{1,0:T(8,128)}, u32[]{:S(2)}) copy-start(s32[8,12]{1,0:T(8,128)} %copy-done.5) | copy-start | bytes 1156
  144.8 59.3 %copy-start.8 = (pred[8,12]{1,0:T(8,128)(4,1)S(1)}, pred[8,12]{1,0:T(8,128)(4,1)}, u32[]{:S(2)}) copy-start(pred[8,12]{1,0:T(8,128)(4,1)} %get-tuple-element.39) | copy-start | bytes 292
  144.8 64.2 %copy-start.3 = (f32[2,2,64,512]{3,2,1,0:T(8,128)S(1)}, f32[2,2,64,512]{3,2,1,0:T(8,128)}, u32[]{:S(2)}) copy-start(f32[2,2,64,512]{3,2,1,0:T(8,128)} %get-tuple-element.35) | copy-start | bytes 1572868
  144.8 23.1 %collective-permute-start.11 = (f32[128,512]{1,0:T(8,128)S(1)}, f32[128,512]{1,0:T(8,128)S(1)}, u32[]{:S(2)}, u32[]{:S(2)}) collective-permute-start(f32[128,512]{1,0:T(8,128)S(1)} %constant_dynamic-slice_fusion.2), channel_id=1, source_target_pairs={{0,1},{1,0},{2,3},{3,2},{4,5},{5,4},{6,7},{7,6},{8,9},{9,8},{10,11... | collective-permute-start | bytes 786440 | tf_op jit(solution)/shard_map/ppermute | solution.py:53
  168.0 10.4 %collective-permute-start.12 = (f32[64,512]{1,0:T(8,128)S(1)}, f32[64,512]{1,0:T(8,128)S(1)}, u32[]{:S(2)}, u32[]{:S(2)}) collective-permute-start(f32[64,512]{1,0:T(8,128)S(1)} %constant_dynamic-slice_fusion.1), channel_id=1, source_target_pairs={{0,2},{1,3},{2,0},{3,1},{4,6},{5,7},{6,4},{7,5},{8,10},{9,11},{10,... | collective-permute-start | bytes 393224 | tf_op jit(solution)/shard_map/ppermute | solution.py:53
  178.4 14.1 %collective-permute-start.13 = (f32[32,512]{1,0:T(8,128)S(1)}, f32[32,512]{1,0:T(8,128)S(1)}, u32[]{:S(2)}, u32[]{:S(2)}) collective-permute-start(f32[32,512]{1,0:T(8,128)S(1)} %constant_dynamic-slice_fusion), channel_id=1, source_target_pairs={{0,4},{1,5},{2,6},{3,7},{4,0},{5,1},{6,2},{7,3},{8,12},{9,13},{10,... | collective-permute-start | bytes 196616 | tf_op jit(solution)/shard_map/ppermute | solution.py:53
  192.5 4.5 %collective-permute-start.14 = (f32[32,512]{1,0:T(8,128)S(1)}, f32[32,512]{1,0:T(8,128)S(1)}, u32[]{:S(2)}, u32[]{:S(2)}) collective-permute-start(f32[32,512]{1,0:T(8,128)S(1)} %dynamic-slice_add_fusion.3), channel_id=1, source_target_pairs={{0,4},{1,5},{2,6},{3,7},{4,0},{5,1},{6,2},{7,3},{8,12},{9,13},{10,... | collective-permute-start | bytes 196616 | tf_op jit(solution)/shard_map/ppermute | solution.py:58
  197.0 3.9 %collective-permute-start.15 = (f32[64,512]{1,0:T(8,128)S(1)}, f32[64,512]{1,0:T(8,128)S(1)}, u32[]{:S(2)}, u32[]{:S(2)}) collective-permute-start(f32[64,512]{1,0:T(8,128)S(1)} %maximum_select_fusion.4), channel_id=1, source_target_pairs={{0,2},{1,3},{2,0},{3,1},{4,6},{5,7},{6,4},{7,5},{8,10},{9,11},{10,... | collective-permute-start | bytes 393224 | tf_op jit(solution)/shard_map/ppermute | solution.py:58
  200.9 15.7 %copy-start.11 = (s32[16]{0:T(128)S(1)}, s32[16]{0:T(128)}, u32[]{:S(2)}) copy-start(s32[16]{0:T(128)} %copy-done.10) | copy-start | bytes 196
  200.9 14.1 %collective-permute-start.16 = (f32[128,512]{1,0:T(8,128)S(1)}, f32[128,512]{1,0:T(8,128)S(1)}, u32[]{:S(2)}, u32[]{:S(2)}) collective-permute-start(f32[128,512]{1,0:T(8,128)S(1)} %maximum_select_fusion.2), channel_id=1, source_target_pairs={{0,1},{1,0},{2,3},{3,2},{4,5},{5,4},{6,7},{7,6},{8,9},{9,8},{10,11... | collective-permute-start | bytes 786440 | tf_op jit(solution)/shard_map/ppermute | solution.py:58
  204.4 29.8 %collective-permute-start.8 = (bf16[256,4096]{1,0:T(8,128)(2,1)}, bf16[256,4096]{1,0:T(8,128)(2,1)}, u32[]{:S(2)}, u32[]{:S(2)}) collective-permute-start(bf16[256,4096]{1,0:T(8,128)(2,1)} %get-tuple-element.32), channel_id=1, source_target_pairs={{8,0},{16,8},{24,16},{0,24},{9,1},{17,9},{25,17},{1,25},{10,2},{18... | collective-permute-start | bytes 6291464 | tf_op jit(solution)/shard_map/ppermute | solution.py:37
  209.7 8.6 %collective-permute-start.9 = (bf16[1,2,64,512]{3,2,1,0:T(8,128)(2,1)}, bf16[1,2,64,512]{3,2,1,0:T(8,128)(2,1)S(1)}, u32[]{:S(2)}, u32[]{:S(2)}) collective-permute-start(bf16[1,2,64,512]{3,2,1,0:T(8,128)(2,1)} %get-tuple-element.52), channel_id=1, source_target_pairs={{1,0},{2,1},{3,2},{4,3},{5,4},{6,5},{7,6},{9,8},{10,9},{11,10},{12... | collective-permute-start | bytes 393224 | tf_op jit(solution)/shard_map/ppermute | solution.py:321
  211.0 8.6 %collective-permute-start.10 = (bf16[1,2,64,512]{3,2,1,0:T(8,128)(2,1)S(1)}, bf16[1,2,64,512]{3,2,1,0:T(8,128)(2,1)S(1)}, u32[]{:S(2)}, u32[]{:S(2)}) collective-permute-start(bf16[1,2,64,512]{3,2,1,0:T(8,128)(2,1)S(1)} %get-tuple-element.51), channel_id=1, source_target_pairs={{0,1},{1,2},{2,3},{3,4},{4,5},{5,6},{6,7},{8,9},{9,10},{10,11},{11... | collective-permute-start | bytes 393224 | tf_op jit(solution)/shard_map/ppermute | solution.py:322
  216.7 1.3 copy-start.2
  220.2 19.5 %collective-permute-start.17 = (bf16[256,1024]{1,0:T(8,128)(2,1)S(1)}, bf16[256,1024]{1,0:T(8,128)(2,1)S(1)}, u32[]{:S(2)}, u32[]{:S(2)}) collective-permute-start(bf16[256,1024]{1,0:T(8,128)(2,1)S(1)} %pad_maximum_fusion.1), channel_id=1, source_target_pairs={{8,0},{16,8},{24,16},{0,24},{9,1},{17,9},{25,17},{1,25},{10,2},{18... | collective-permute-start | bytes 1572872 | tf_op jit(solution)/shard_map/ppermute | solution.py:37

commit v6 on v4

--- a/solution.py
+++ b/solution.py
@@ -72,29 +72,30 @@
     contract_last = (((1,), (1,)), ((), ()))
     contract_first = (((0,), (0,)), ((), ()))
     scores = (
-        lax.dot_general(query_rows, key_rows, contract_last, preferred_element_type=jnp.float32)
+        lax.dot_general(key_rows, query_rows, contract_last, preferred_element_type=jnp.float32)
         * score_scale
     )
     scores = jnp.where(live, scores, -1e30)
-    row_max = jnp.max(scores, axis=1, keepdims=True)
+    row_max = jnp.max(scores, axis=0, keepdims=True)
     shifted = jnp.exp(scores - row_max)
-    total = jnp.sum(shifted, axis=1, keepdims=True)
+    total = jnp.sum(shifted, axis=0, keepdims=True)
     probs = shifted * (1.0 / total)
     probs_low = probs.astype(jnp.bfloat16)
-    output = jnp.dot(probs_low, value_rows, preferred_element_type=jnp.float32)
-    row_dot = jnp.sum(grad_rows.astype(jnp.float32) * output, axis=1, keepdims=True)
+    output = lax.dot_general(
+        value_rows, probs_low, contract_first, preferred_element_type=jnp.float32
+    )
+    grad_cols = grad_rows.astype(jnp.float32).T
+    row_dot = jnp.sum(grad_cols * output, axis=0, keepdims=True)
     prob_grad = lax.dot_general(
-        grad_rows, value_rows, contract_last, preferred_element_type=jnp.float32
+        value_rows, grad_rows, contract_last, preferred_element_type=jnp.float32
     )
     score_grad = (probs * (prob_grad - row_dot)).astype(jnp.bfloat16)
-    query_grad = jnp.dot(score_grad, key_rows, preferred_element_type=jnp.float32) * score_scale
-    key_grad = (
-        lax.dot_general(score_grad, query_rows, contract_first, preferred_element_type=jnp.float32)
+    query_grad = (
+        lax.dot_general(key_rows, score_grad, contract_first, preferred_element_type=jnp.float32)
         * score_scale
-    )
-    value_grad = lax.dot_general(
-        probs_low, grad_rows, contract_first, preferred_element_type=jnp.float32
-    )
+    ).T
+    key_grad = jnp.dot(score_grad, query_rows, preferred_element_type=jnp.float32) * score_scale
+    value_grad = jnp.dot(probs_low, grad_rows, preferred_element_type=jnp.float32)
     for g in range(group):
         dq_ref[:, g * HDIM : (g + 1) * HDIM] = query_grad[g * block_len : (g + 1) * block_len].astype(
             dq_ref.dtype
@@ -138,7 +139,7 @@
     group_width = qwidth // heads_kv
     near = 3 + GLOB
     nrand = ntiles - near
-    live = key_live.reshape(nblocks, 1, ntiles * block_len).astype(jnp.float32)
+    live = key_live.reshape(nblocks, ntiles * block_len, 1).astype(jnp.float32)
     row_spec = pl.BlockSpec((block_len, group_width), lambda h, b, ids: (b, h))
     tile_specs = [
         pl.BlockSpec(
@@ -146,7 +147,7 @@
         )
         for t in range(ntiles)
     ]
-    live_spec = pl.BlockSpec((None, 1, ntiles * block_len), lambda h, b, ids: (b, 0, 0))
+    live_spec = pl.BlockSpec((None, ntiles * block_len, 1), lambda h, b, ids: (b, 0, 0))
     own_spec = pl.BlockSpec((nblocks, 2, block_len, HDIM), lambda h, b, ids: (0, 0, 0, h))
     edge_spec = pl.BlockSpec((2, 2, block_len, HDIM), lambda h, b, ids: (0, 0, 0, h))
     glob_spec = pl.BlockSpec((GLOB, 2, block_len, HDIM), lambda h, b, ids: (0, 0, 0, h))

time: 242 us -> 238 us (0.983)
  Pallas kernels: 32.1 us -> 28.4 us
    pallas_call x1, Pallas kernels: 32.1 us -> 28.4 us  [block_backward(): pl.pallas_call(attention_kernel, grid_spec=grid_spec, out_shape=[jax.Shap...]
    unnamed x22 -> x26, local copies, waits for them, and re-layouts: 6.85 us -> 6.85 us
where the time goes in v6:
time: 238 us; the launch traced here: 237 us
  waiting for transfers between devices  103 us (43%)
  local copies, waits for them, and re-layouts  36.1 us (15%)
  starting transfers between devices  35 us (15%)
  Pallas kernels  28.4 us (12%)
  other arithmetic  23.8 us (10%)
  between operations  6.16 us (3%)
  matrix products  3.84 us (2%)
    ppermute x6, waiting for transfers between devices, tree_sum(): lax.ppermute(array, axis, [(i, i ^ step) for i in range(devices)])  95.3 us
    pallas_call x1, Pallas kernels, block_backward(): pl.pallas_call(attention_kernel, grid_spec=grid_spec, out_shape=[jax.Shap...  28.4 us
    ppermute x2, waiting for transfers between devices, from_behind(): return lax.ppermute(block, axis, route)  8.09 us
    ppermute x6, starting transfers between devices, tree_sum(): lax.ppermute(array, axis, [(i, i ^ step) for i in range(devices)])  8.01 us
    unnamed x26, local copies, waits for them, and re-layouts  6.85 us
    all_to_all x1, starting transfers between devices, body(): lax.all_to_all(holder.reshape(shards * capacity, 2, BLK, kwidth), 'seq',...  6.73 us
    all_to_all x1, starting transfers between devices, body(): received = lax.all_to_all(served, 'seq', 0, 0, tiled=True)  6.49 us
    scatter x1, local copies, waits for them, and re-layouts, body(): holder.at[owner_mine, rank_mine]  5.14 us
  transfers between devices with their start and end apart: 14, of which 7 were waited for; matrix products, arithmetic and copies ran while one was open for 17% of the time, Pallas kernels for 0%

profile of v6, /device:TPU:1, one launch (start us, length us, event | category | flops | bytes accessed | tf_op | source)
XLA Modules:
  0.0 236.7 jit_solution(10790011535326838328)
XLA Ops:
  0.7 0.8 copy.73
  2.5 1.9 pad_maximum_fusion
  4.4 3.0 %gather_fusion = bf16[16,2,64,512]{3,2,1,0:T(8,128)(2,1)} fusion(bf16[4,2,64,512]{3,2,1,0:T(8,128)(2,1)} %get-tuple-element.45, s32[1024]{0:T(1024)S(1)} %pad_clamp_fusion), kind=kCustom, calls=%fused_computation | custom fusion | bytes 4194368 | tf_op jit(solution)/shard_map/jit(_take)/gather | solution.py:280
  7.5 3.2 %broadcast_select_fusion = bf16[16,2,64,512]{3,2,1,0:T(8,128)(2,1)} fusion(bf16[16,2,64,512]{3,2,1,0:T(8,128)(2,1)} %gather_fusion, pred[16]{0:T(512)(128)(4,1)S(1)} %compare_and_fusion.1), kind=kLoop, calls=%fused_computation.4 | loop fusion | flops 1048576 | bytes 4194320 | tf_op jit(solution)/shard_map/jit(_take)/select_n | solution.py:280
  10.6 6.5 %all-to-all-start = ((bf16[16,2,64,512]{3,2,1,0:T(8,128)(2,1)}), bf16[16,2,64,512]{3,2,1,0:T(8,128)(2,1)}, u32[]{:S(2)}, u32[]{:S(2)}) async-start(bf16[16,2,64,512]{3,2,1,0:T(8,128)(2,1)} %broadcast_select_fusion), calls=%async_computation | async-start | bytes 4194304 | tf_op jit(solution)/shard_map/all_to_all | solution.py:281
  22.9 1.8 fusion.12
  24.8 4.0 %collective-permute-start = (bf16[1,2,64,512]{3,2,1,0:T(8,128)(2,1)}, bf16[1,2,64,512]{3,2,1,0:T(8,128)(2,1)}, u32[]{:S(2)}, u32[]{:S(2)}) collective-permute-start(bf16[1,2,64,512]{3,2,1,0:T(8,128)(2,1)} %get-tuple-element.48), channel_id=1, source_target_pairs={{0,1},{1,2},{2,3},{3,4},{4,5},{5,6},{6,7},{8,9},{9,10},{10,11},{11... | collective-permute-start | bytes 393224 | tf_op jit(solution)/shard_map/ppermute | solution.py:265
  28.8 1.3 collective-permute-start.1
  30.1 0.7 pad_maximum_fusion.2
  30.8 2.1 collective-permute-start.2
  34.4 0.7 pad.7.clone
  35.9 1.8 and.211
  37.8 0.9 select_reduce_fusion
  39.4 2.7 %lt.142 = s32[4,512,1]{2,1,0:T(8,128)} reshape(s32[4,8,64]{2,1,0:T(8,128)} %lt.136) | data formatting | bytes 16384 | tf_op jit(solution)/shard_map/lt | solution.py:242
  42.1 1.3 add.272
  43.4 2.7 %add.288 = s32[4,512,1]{2,1,0:T(8,128)} reshape(s32[4,8,64]{2,1,0:T(8,128)} %add.272) | data formatting | bytes 16384 | tf_op jit(solution)/shard_map/add | solution.py:241
  46.8 2.9 %fusion.4.refs_8_ = f32[4,512,1]{2,1,0:T(8,128)} fusion(pred[4,512,1]{2,1,0:T(8,128)(4,1)} %and.211, s32[4,512,1]{2,1,0:T(8,128)} %lt.142, s32[4,512,1]{2,1,0:T(8,128)} %add.288, s32[512]{0:T(512)S(1)} %add.275), kind=kLoop, calls=%fused_computation.10 | loop fusion | flops 8192 | bytes 28672 | tf_op jit(solution)/shard_map/convert_element_type | solution.py:142
  50.1 1.7 fusion.38
  53.7 1.4 concatenate.40
  55.8 13.0 %collective-permute-done.3 = bf16[2,2,64,512]{3,2,1,0:T(8,128)(2,1)} collective-permute-done((bf16[2,2,64,512]{3,2,1,0:T(8,128)(2,1)}, bf16[2,2,64,512]{3,2,1,0:T(8,128)(2,1)}, u32[]{:S(2)}, u32[]{:S(2)}) %collective-permute-start.3) | collective-permute-done | bytes 262176 | tf_op jit(solution)/shard_map/ppermute | solution.py:46
  68.8 1.8 fusion.42
  70.6 2.8 %collective-permute-start.4 = (bf16[2,2,64,512]{3,2,1,0:T(8,128)(2,1)}, bf16[2,2,64,512]{3,2,1,0:T(8,128)(2,1)S(1)}, u32[]{:S(2)}, u32[]{:S(2)}) collective-permute-start(bf16[2,2,64,512]{3,2,1,0:T(8,128)(2,1)} %fusion.42), channel_id=1, source_target_pairs={{0,4},{1,5},{2,6},{3,7},{4,0},{5,1},{6,2},{7,3},{8,12},{9,13},{10,... | collective-permute-start | bytes 786440 | tf_op jit(solution)/shard_map/ppermute | solution.py:46
  74.0 0.9 constant_dynamic-update-slice_fusion.2
  75.0 9.2 %collective-permute-done.4 = bf16[2,2,64,512]{3,2,1,0:T(8,128)(2,1)S(1)} collective-permute-done((bf16[2,2,64,512]{3,2,1,0:T(8,128)(2,1)}, bf16[2,2,64,512]{3,2,1,0:T(8,128)(2,1)S(1)}, u32[]{:S(2)}, u32[]{:S(2)}) %collective-permute-start.4) | collective-permute-done | bytes 262176 | tf_op jit(solution)/shard_map/ppermute | solution.py:46
  84.1 1.0 add_dynamic-update-slice_fusion
  85.2 1.8 constant_dynamic-update-slice_fusion.refs_0_.refs_1_.refs_2_.refs_3_.refs_4_.refs_5_.refs_6_.refs_7_
  87.0 1.6 copy-done
  88.6 28.4 %shard_map.97 = (bf16[256,4096]{1,0:T(8,128)(2,1)}, f32[4,2,64,512]{3,2,1,0:T(8,128)}, f32[2,2,64,512]{3,2,1,0:T(8,128)}, f32[2,2,64,512]{3,2,1,0:T(8,128)}, bf16[4,3,2,64,512]{4,3,2,1,0:T(8,128)(2,1)}) custom-call(s32[32]{0:T(128)} %min.18.ids_ref, bf16[256,4096]{1,0:T(8,128)(2,1)} %bitcast.48, bf16[256,4096]{1,0:T(8,128)(2,1)} %bitcast.49, ...), custom_call_target="tpu_custom_call" | custom-call | flops 6442450944 | bytes 12582912 | tf_op jit(solution)/shard_map/pallas_call | solution.py:162
  117.0 1.6 broadcast_in_dim.98
  119.0 5.1 %scatter_fusion = bf16[8,2,2,64,512]{4,3,2,1,0:T(8,128)(2,1)} fusion(bf16[8,2,2,64,512]{4,3,2,1,0:T(8,128)(2,1)} %broadcast_in_dim.98, s32[12]{0:T(128)S(1)} %fusion.36, bf16[12,2,64,512]{3,2,1,0:T(8,128)(2,1)S(1)} %bitcast.50), kind=kCustom, calls=%fused_computation.1 | custom fusion | bytes 4718688 | tf_op jit(solution)/shard_map/scatter | solution.py:312
  124.1 6.7 %all-to-all-start.1 = ((bf16[16,2,64,512]{3,2,1,0:T(8,128)(2,1)}), bf16[16,2,64,512]{3,2,1,0:T(8,128)(2,1)S(1)}, u32[]{:S(2)}, u32[]{:S(2)}) async-start(bf16[16,2,64,512]{3,2,1,0:T(8,128)(2,1)} %bitcast.17), calls=%async_computation.1 | async-start | bytes 4194304 | tf_op jit(solution)/shard_map/all_to_all | solution.py:315
  130.9 1.5 collective-permute-start.8
  132.4 33.8 %collective-permute-done.8 = f32[2,2,64,512]{3,2,1,0:T(8,128)S(1)} collective-permute-done((f32[2,2,64,512]{3,2,1,0:T(8,128)S(1)}, f32[2,2,64,512]{3,2,1,0:T(8,128)S(1)}, u32[]{:S(2)}, u32[]{:S(2)}) %collective-permute-start.8) | collective-permute-done | bytes 524320 | tf_op jit(solution)/shard_map/ppermute | solution.py:46
  166.3 23.2 %collective-permute-done.9 = f32[2,2,64,512]{3,2,1,0:T(8,128)S(1)} collective-permute-done((f32[2,2,64,512]{3,2,1,0:T(8,128)S(1)}, f32[2,2,64,512]{3,2,1,0:T(8,128)S(1)}, u32[]{:S(2)}, u32[]{:S(2)}) %collective-permute-start.9) | collective-permute-done | bytes 524320 | tf_op jit(solution)/shard_map/ppermute | solution.py:46
  189.7 1.3 collective-permute-start.10
  191.4 0.8 collective-permute-start.5
  192.2 1.1 convert_element_type.29
  193.9 1.3 collective-permute-start.6
  195.2 4.0 %collective-permute-start.7 = (bf16[1,2,64,512]{3,2,1,0:T(8,128)(2,1)S(1)}, bf16[1,2,64,512]{3,2,1,0:T(8,128)(2,1)S(1)}, u32[]{:S(2)}, u32[]{:S(2)}) collective-permute-start(bf16[1,2,64,512]{3,2,1,0:T(8,128)(2,1)S(1)} %get-tuple-element.51), channel_id=1, source_target_pairs={{0,1},{1,2},{2,3},{3,4},{4,5},{5,6},{6,7},{8,9},{9,10},{10,11},{11... | collective-permute-start | bytes 393224 | tf_op jit(solution)/shard_map/ppermute | solution.py:310
  199.2 15.7 %collective-permute-done.10 = f32[2,2,64,512]{3,2,1,0:T(8,128)} collective-permute-done((f32[2,2,64,512]{3,2,1,0:T(8,128)S(1)}, f32[2,2,64,512]{3,2,1,0:T(8,128)}, u32[]{:S(2)}, u32[]{:S(2)}) %collective-permute-start.10) | collective-permute-done | bytes 524320 | tf_op jit(solution)/shard_map/ppermute | solution.py:46
  214.9 1.1 add.286
  216.0 2.5 %fusion.5 = f32[4,2,64,512]{3,0,2,1:T(4,128)} fusion(f32[2,2,64,512]{3,2,1,0:T(8,128)S(1)} %add.286, pred[2]{0:T(512)(128)(4,1)S(1)} %fusion.37, s32[2]{0:T(128)S(1)} %and_select_fusion), kind=kOutput, calls=%fused_computation.21 | convolution fusion | flops 6291472 | bytes 1572874 | tf_op jit(solution)/shard_map/gq,gxsk->qxsk/dot_general | solution.py:332
  218.6 1.3 fusion
  219.9 1.7 copy_add_fusion.1
  222.2 2.4 %collective-permute-start.11 = (bf16[256,1024]{1,0:T(8,128)(2,1)S(1)}, bf16[256,1024]{1,0:T(8,128)(2,1)S(1)}, u32[]{:S(2)}, u32[]{:S(2)}) collective-permute-start(bf16[256,1024]{1,0:T(8,128)(2,1)S(1)} %pad_maximum_fusion.1), channel_id=1, source_target_pairs={{8,0},{16,8},{24,16},{0,24},{9,1},{17,9},{25,17},{1,25},{10,2},{18... | collective-permute-start | bytes 1572872 | tf_op jit(solution)/shard_map/ppermute | solution.py:37
  224.7 8.1 %collective-permute-done.11 = bf16[256,1024]{1,0:T(8,128)(2,1)S(1)} collective-permute-done((bf16[256,1024]{1,0:T(8,128)(2,1)S(1)}, bf16[256,1024]{1,0:T(8,128)(2,1)S(1)}, u32[]{:S(2)}, u32[]{:S(2)}) %collective-permute-start.11) | collective-permute-done | bytes 524320 | tf_op jit(solution)/shard_map/ppermute | solution.py:37
  232.8 0.8 slice_bitcast_fusion
  233.6 3.1 %copy.107 = bf16[1,256,4096]{2,1,0:T(8,128)(2,1)} copy(bf16[1,256,4096]{2,1,0:T(8,128)(2,1)} %bitcast.10) | data formatting | bytes 4194304
  (84 shorter events, 11.2 us)
Async XLA Ops:
  1.5 5.9 %copy-start.4 = (pred[8,12]{1,0:T(8,128)(4,1)}, pred[8,12]{1,0:T(8,128)(4,1)S(1)}, u32[]{:S(2)}) copy-start(pred[8,12]{1,0:T(8,128)(4,1)S(1)} %get-tuple-element.39) | copy-start | bytes 292
  2.4 5.0 %copy-start.7 = (s32[16]{0:T(128)}, s32[16]{0:T(128)S(1)}, u32[]{:S(2)}) copy-start(s32[16]{0:T(128)S(1)} %reshape.651) | copy-start | bytes 196
  10.6 6.5 %copy-start.9 = (s32[1,2]{1,0:T(1,128)S(1)}, s32[1,2]{1,0:T(1,128)}, u32[]{:S(2)}) copy-start(s32[1,2]{1,0:T(1,128)} %param.16) | copy-start | bytes 28
  10.6 22.2 %copy-start.6 = (s32[1,32,3]{1,0,2:T(1,128)S(1)}, s32[1,32,3]{1,0,2:T(1,128)}, u32[]{:S(2)}) copy-start(s32[1,32,3]{1,0,2:T(1,128)} %param.15) | copy-start | bytes 1156
  10.6 74.5 %all-to-all-start = ((bf16[16,2,64,512]{3,2,1,0:T(8,128)(2,1)}), bf16[16,2,64,512]{3,2,1,0:T(8,128)(2,1)}, u32[]{:S(2)}, u32[]{:S(2)}) async-start(bf16[16,2,64,512]{3,2,1,0:T(8,128)(2,1)} %broadcast_select_fusion), calls=%async_computation | async-start | bytes 4194304 | tf_op jit(solution)/shard_map/all_to_all | solution.py:281
  24.8 49.2 %collective-permute-start = (bf16[1,2,64,512]{3,2,1,0:T(8,128)(2,1)}, bf16[1,2,64,512]{3,2,1,0:T(8,128)(2,1)}, u32[]{:S(2)}, u32[]{:S(2)}) collective-permute-start(bf16[1,2,64,512]{3,2,1,0:T(8,128)(2,1)} %get-tuple-element.48), channel_id=1, source_target_pairs={{0,1},{1,2},{2,3},{3,4},{4,5},{5,6},{6,7},{8,9},{9,10},{10,11},{11... | collective-permute-start | bytes 393224 | tf_op jit(solution)/shard_map/ppermute | solution.py:265
  28.8 46.2 %collective-permute-start.1 = (bf16[1,2,64,512]{3,2,1,0:T(8,128)(2,1)}, bf16[1,2,64,512]{3,2,1,0:T(8,128)(2,1)S(1)}, u32[]{:S(2)}, u32[]{:S(2)}) collective-permute-start(bf16[1,2,64,512]{3,2,1,0:T(8,128)(2,1)} %get-tuple-element.49), channel_id=1, source_target_pairs={{1,0},{2,1},{3,2},{4,3},{5,4},{6,5},{7,6},{9,8},{10,9},{11,10},{12... | collective-permute-start | bytes 393224 | tf_op jit(solution)/shard_map/ppermute | solution.py:266
  30.8 19.3 %collective-permute-start.2 = (bf16[2,2,64,512]{3,2,1,0:T(8,128)(2,1)}, bf16[2,2,64,512]{3,2,1,0:T(8,128)(2,1)}, u32[]{:S(2)}, u32[]{:S(2)}) collective-permute-start(bf16[2,2,64,512]{3,2,1,0:T(8,128)(2,1)} %pad_maximum_fusion.2), channel_id=1, source_target_pairs={{0,1},{1,0},{2,3},{3,2},{4,5},{5,4},{6,7},{7,6},{8,9},{9,8},{10,11... | collective-permute-start | bytes 786440 | tf_op jit(solution)/shard_map/ppermute | solution.py:46
  51.8 17.0 %collective-permute-start.3 = (bf16[2,2,64,512]{3,2,1,0:T(8,128)(2,1)}, bf16[2,2,64,512]{3,2,1,0:T(8,128)(2,1)}, u32[]{:S(2)}, u32[]{:S(2)}) collective-permute-start(bf16[2,2,64,512]{3,2,1,0:T(8,128)(2,1)} %fusion.38), channel_id=1, source_target_pairs={{0,2},{1,3},{2,0},{3,1},{4,6},{5,7},{6,4},{7,5},{8,10},{9,11},{10,... | collective-permute-start | bytes 786440 | tf_op jit(solution)/shard_map/ppermute | solution.py:46
  70.6 13.6 %collective-permute-start.4 = (bf16[2,2,64,512]{3,2,1,0:T(8,128)(2,1)}, bf16[2,2,64,512]{3,2,1,0:T(8,128)(2,1)S(1)}, u32[]{:S(2)}, u32[]{:S(2)}) collective-permute-start(bf16[2,2,64,512]{3,2,1,0:T(8,128)(2,1)} %fusion.42), channel_id=1, source_target_pairs={{0,4},{1,5},{2,6},{3,7},{4,0},{5,1},{6,2},{7,3},{8,12},{9,13},{10,... | collective-permute-start | bytes 786440 | tf_op jit(solution)/shard_map/ppermute | solution.py:46
  87.0 1.7 copy-start
  117.0 1.9 copy-start.2
  124.1 6.7 %copy-start.3 = (f32[2,2,64,512]{3,2,1,0:T(8,128)S(1)}, f32[2,2,64,512]{3,2,1,0:T(8,128)}, u32[]{:S(2)}) copy-start(f32[2,2,64,512]{3,2,1,0:T(8,128)} %get-tuple-element.36) | copy-start | bytes 1572868
  124.1 42.2 %copy-start.10 = (s32[1,2]{1,0:T(1,128)S(1)}, s32[1,2]{1,0:T(1,128)}, u32[]{:S(2)}) copy-start(s32[1,2]{1,0:T(1,128)} %param.16) | copy-start | bytes 28
  124.1 94.5 %all-to-all-start.1 = ((bf16[16,2,64,512]{3,2,1,0:T(8,128)(2,1)}), bf16[16,2,64,512]{3,2,1,0:T(8,128)(2,1)S(1)}, u32[]{:S(2)}, u32[]{:S(2)}) async-start(bf16[16,2,64,512]{3,2,1,0:T(8,128)(2,1)} %bitcast.17), calls=%async_computation.1 | async-start | bytes 4194304 | tf_op jit(solution)/shard_map/all_to_all | solution.py:315
  130.8 60.2 %copy-start.5 = (pred[8,12]{1,0:T(8,128)(4,1)S(1)}, pred[8,12]{1,0:T(8,128)(4,1)}, u32[]{:S(2)}) copy-start(pred[8,12]{1,0:T(8,128)(4,1)} %copy-done.4) | copy-start | bytes 292
  130.9 35.3 %collective-permute-start.8 = (f32[2,2,64,512]{3,2,1,0:T(8,128)S(1)}, f32[2,2,64,512]{3,2,1,0:T(8,128)S(1)}, u32[]{:S(2)}, u32[]{:S(2)}) collective-permute-start(f32[2,2,64,512]{3,2,1,0:T(8,128)S(1)} %copy-done.3), channel_id=1, source_target_pairs={{0,1},{1,0},{2,3},{3,2},{4,5},{5,4},{6,7},{7,6},{8,9},{9,8},{10,11... | collective-permute-start | bytes 1572872 | tf_op jit(solution)/shard_map/ppermute | solution.py:46
  166.2 23.3 %collective-permute-start.9 = (f32[2,2,64,512]{3,2,1,0:T(8,128)S(1)}, f32[2,2,64,512]{3,2,1,0:T(8,128)S(1)}, u32[]{:S(2)}, u32[]{:S(2)}) collective-permute-start(f32[2,2,64,512]{3,2,1,0:T(8,128)S(1)} %add.284), channel_id=1, source_target_pairs={{0,2},{1,3},{2,0},{3,1},{4,6},{5,7},{6,4},{7,5},{8,10},{9,11},{10,... | collective-permute-start | bytes 1572872 | tf_op jit(solution)/shard_map/ppermute | solution.py:46
  189.7 25.3 %collective-permute-start.10 = (f32[2,2,64,512]{3,2,1,0:T(8,128)S(1)}, f32[2,2,64,512]{3,2,1,0:T(8,128)}, u32[]{:S(2)}, u32[]{:S(2)}) collective-permute-start(f32[2,2,64,512]{3,2,1,0:T(8,128)S(1)} %add.285), channel_id=1, source_target_pairs={{0,4},{1,5},{2,6},{3,7},{4,0},{5,1},{6,2},{7,3},{8,12},{9,13},{10,... | collective-permute-start | bytes 1572872 | tf_op jit(solution)/shard_map/ppermute | solution.py:46
  191.4 33.3 %collective-permute-start.5 = (bf16[256,4096]{1,0:T(8,128)(2,1)}, bf16[256,4096]{1,0:T(8,128)(2,1)}, u32[]{:S(2)}, u32[]{:S(2)}) collective-permute-start(bf16[256,4096]{1,0:T(8,128)(2,1)} %get-tuple-element.32), channel_id=1, source_target_pairs={{8,0},{16,8},{24,16},{0,24},{9,1},{17,9},{25,17},{1,25},{10,2},{18... | collective-permute-start | bytes 6291464 | tf_op jit(solution)/shard_map/ppermute | solution.py:37
  192.2 26.4 %copy-start.8 = (s32[16]{0:T(128)S(1)}, s32[16]{0:T(128)}, u32[]{:S(2)}) copy-start(s32[16]{0:T(128)} %copy-done.7) | copy-start | bytes 196
  193.9 27.6 %collective-permute-start.6 = (bf16[1,2,64,512]{3,2,1,0:T(8,128)(2,1)}, bf16[1,2,64,512]{3,2,1,0:T(8,128)(2,1)S(1)}, u32[]{:S(2)}, u32[]{:S(2)}) collective-permute-start(bf16[1,2,64,512]{3,2,1,0:T(8,128)(2,1)} %get-tuple-element.52), channel_id=1, source_target_pairs={{1,0},{2,1},{3,2},{4,3},{5,4},{6,5},{7,6},{9,8},{10,9},{11,10},{12... | collective-permute-start | bytes 393224 | tf_op jit(solution)/shard_map/ppermute | solution.py:309
  195.2 26.4 %collective-permute-start.7 = (bf16[1,2,64,512]{3,2,1,0:T(8,128)(2,1)S(1)}, bf16[1,2,64,512]{3,2,1,0:T(8,128)(2,1)S(1)}, u32[]{:S(2)}, u32[]{:S(2)}) collective-permute-start(bf16[1,2,64,512]{3,2,1,0:T(8,128)(2,1)S(1)} %get-tuple-element.51), channel_id=1, source_target_pairs={{0,1},{1,2},{2,3},{3,4},{4,5},{5,6},{6,7},{8,9},{9,10},{10,11},{11... | collective-permute-start | bytes 393224 | tf_op jit(solution)/shard_map/ppermute | solution.py:310
  219.9 1.9 copy-start.1
  222.2 10.5 %collective-permute-start.11 = (bf16[256,1024]{1,0:T(8,128)(2,1)S(1)}, bf16[256,1024]{1,0:T(8,128)(2,1)S(1)}, u32[]{:S(2)}, u32[]{:S(2)}) collective-permute-start(bf16[256,1024]{1,0:T(8,128)(2,1)S(1)} %pad_maximum_fusion.1), channel_id=1, source_target_pairs={{8,0},{16,8},{24,16},{0,24},{9,1},{17,9},{25,17},{1,25},{10,2},{18... | collective-permute-start | bytes 1572872 | tf_op jit(solution)/shard_map/ppermute | solution.py:37

commit v7 on v6

--- a/solution.py
+++ b/solution.py
@@ -278,6 +278,7 @@
     serve_block, slot_used, owner_mine, rank_mine = plan
     capacity = serve_block.shape[1]
     served = jnp.take(own_blocks, serve_block.reshape(-1), axis=0)
+    served, global_tiles = lax.optimization_barrier((served, global_tiles))
     received = lax.all_to_all(served, "seq", 0, 0, tiled=True)
     sources = jnp.concatenate([own_blocks, edge_before, edge_after, global_tiles, received], axis=0)
     nb = query_blocks
@@ -312,6 +313,8 @@
     holder = holder.at[owner_mine, rank_mine].set(
         random_part.reshape(query_blocks * RAND, 2, BLK, kwidth)
     )
+    global_total = tree_sum(global_part, "seq")
+    holder, global_total = lax.optimization_barrier((holder, global_total))
     returned = lax.all_to_all(
         holder.reshape(shards * capacity, 2, BLK, kwidth), "seq", 0, 0, tiled=True
     )
@@ -324,7 +327,6 @@
     )
     kv_sum = kv_sum.at[nb - 1].add(from_after[0].astype(jnp.float32))
     kv_sum = kv_sum.at[0].add(from_before[0].astype(jnp.float32))
-    global_total = tree_sum(global_part, "seq")
     global_pick = (
         (global_ids[:, None] // query_blocks == this_shard)
         & (global_ids[:, None] % query_blocks == block_range[None, :])

time: 238 us -> 254 us (1.067)
  waiting for transfers between devices: 103 us -> 120 us
  starting transfers between devices: 35 us -> 41.9 us
  local copies, waits for them, and re-layouts: 36.1 us -> 31.3 us
    ppermute x6, waiting for transfers between devices: 95.3 us -> 51 us  [tree_sum(): lax.ppermute(array, axis, [(i, i ^ step) for i in range(devices)])]
    all_to_all x1, waiting for transfers between devices: 0.01 us -> 35.8 us  [body(): lax.all_to_all(holder.reshape(shards * capacity, 2, BLK, kwidth), 'seq',...]
    all_to_all x1, waiting for transfers between devices: 0.01 us -> 25 us  [body(): received = lax.all_to_all(served, 'seq', 0, 0, tiled=True)]
    ppermute x6, starting transfers between devices: 8.01 us -> 16.1 us  [tree_sum(): lax.ppermute(array, axis, [(i, i ^ step) for i in range(devices)])]
    all_to_all x1, starting transfers between devices: 6.73 us -> 3.73 us  [body(): lax.all_to_all(holder.reshape(shards * capacity, 2, BLK, kwidth), 'seq',...]
    ppermute x2, starting transfers between devices: 3.26 us -> 5.81 us  [from_behind(): return lax.ppermute(block, axis, route)]
    unnamed x26 -> x33, local copies, waits for them, and re-layouts: 6.85 us -> 6.53 us
  transfers between devices with their start and end apart: 14 -> 14, of which waited for: 7 -> 9; matrix products, arithmetic and copies ran while one was open for 17% -> 16% of each run, Pallas kernels for 0% -> 0%
where the time goes in v7:
time: 254 us; the launch traced here: 253 us
  waiting for transfers between devices  120 us (47%)
  starting transfers between devices  41.9 us (16%)
  local copies, waits for them, and re-layouts  31.3 us (12%)
  Pallas kernels  28.4 us (11%)
  other arithmetic  21.5 us (8%)
  between operations  6.21 us (2%)
  matrix products  3.87 us (2%)
    ppermute x6, waiting for transfers between devices, tree_sum(): lax.ppermute(array, axis, [(i, i ^ step) for i in range(devices)])  51 us
    all_to_all x1, waiting for transfers between devices, body(): lax.all_to_all(holder.reshape(shards * capacity, 2, BLK, kwidth), 'seq',...  35.8 us
    pallas_call x1, Pallas kernels, block_backward(): pl.pallas_call(attention_kernel, grid_spec=grid_spec, out_shape=[jax.Shap...  28.4 us
    all_to_all x1, waiting for transfers between devices, body(): received = lax.all_to_all(served, 'seq', 0, 0, tiled=True)  25 us
    ppermute x6, starting transfers between devices, tree_sum(): lax.ppermute(array, axis, [(i, i ^ step) for i in range(devices)])  16.1 us
    ppermute x2, waiting for transfers between devices, from_behind(): return lax.ppermute(block, axis, route)  7.99 us
    unnamed x33, local copies, waits for them, and re-layouts  6.53 us
    ppermute x2, starting transfers between devices, from_behind(): return lax.ppermute(block, axis, route)  5.81 us
  transfers between devices with their start and end apart: 14, of which 9 were waited for; matrix products, arithmetic and copies ran while one was open for 16% of the time, Pallas kernels for 0%

profile of v7, /device:TPU:1, one launch (start us, length us, event | category | flops | bytes accessed | tf_op | source)
XLA Modules:
  0.0 252.9 jit_solution(11733148028507605877)
XLA Ops:
  0.6 1.3 fusion.41
  7.2 1.8 fusion.12
  9.7 2.0 collective-permute-start.2
  11.8 0.8 copy.73
  12.7 1.9 pad_maximum_fusion
  15.4 2.7 %collective-permute-done.2 = bf16[2,2,64,512]{3,2,1,0:T(8,128)(2,1)} collective-permute-done((bf16[2,2,64,512]{3,2,1,0:T(8,128)(2,1)}, bf16[2,2,64,512]{3,2,1,0:T(8,128)(2,1)}, u32[]{:S(2)}, u32[]{:S(2)}) %collective-permute-start.2) | collective-permute-done | bytes 262176 | tf_op jit(solution)/shard_map/ppermute | solution.py:46
  18.1 1.7 fusion.38
  19.8 1.2 collective-permute-start.3
  21.1 3.0 %gather_fusion = bf16[16,2,64,512]{3,2,1,0:T(8,128)(2,1)} fusion(bf16[4,2,64,512]{3,2,1,0:T(8,128)(2,1)} %get-tuple-element.57, s32[1024]{0:T(1024)S(1)} %pad_clamp_fusion), kind=kCustom, calls=%fused_computation | custom fusion | bytes 4194368 | tf_op jit(solution)/shard_map/jit(_take)/gather | solution.py:280
  24.2 2.5 collective-permute-done.3
  26.7 1.1 fusion.42
  27.8 2.0 collective-permute-start.4
  29.7 3.2 %broadcast_select_fusion = bf16[16,2,64,512]{3,2,1,0:T(8,128)(2,1)} fusion(bf16[16,2,64,512]{3,2,1,0:T(8,128)(2,1)} %gather_fusion, pred[16]{0:T(512)(128)(4,1)S(1)} %compare_and_fusion.1), kind=kLoop, calls=%fused_computation.4 | loop fusion | flops 1048576 | bytes 4194320 | tf_op jit(solution)/shard_map/jit(_take)/select_n | solution.py:280
  32.9 8.9 %collective-permute-done.4 = bf16[2,2,64,512]{3,2,1,0:T(8,128)(2,1)S(1)} collective-permute-done((bf16[2,2,64,512]{3,2,1,0:T(8,128)(2,1)S(1)}, bf16[2,2,64,512]{3,2,1,0:T(8,128)(2,1)S(1)}, u32[]{:S(2)}, u32[]{:S(2)}) %collective-permute-start.4) | collective-permute-done | bytes 262176 | tf_op jit(solution)/shard_map/ppermute | solution.py:46
  41.9 5.7 %all-to-all-start = ((bf16[16,2,64,512]{3,2,1,0:T(8,128)(2,1)}), bf16[16,2,64,512]{3,2,1,0:T(8,128)(2,1)}, u32[]{:S(2)}, u32[]{:S(2)}) async-start(bf16[16,2,64,512]{3,2,1,0:T(8,128)(2,1)} %broadcast_select_fusion), calls=%async_computation | async-start | bytes 4194304 | tf_op jit(solution)/shard_map/all_to_all | solution.py:282
  47.7 4.0 %collective-permute-start = (bf16[1,2,64,512]{3,2,1,0:T(8,128)(2,1)}, bf16[1,2,64,512]{3,2,1,0:T(8,128)(2,1)}, u32[]{:S(2)}, u32[]{:S(2)}) collective-permute-start(bf16[1,2,64,512]{3,2,1,0:T(8,128)(2,1)} %get-tuple-element.54), channel_id=1, source_target_pairs={{0,1},{1,2},{2,3},{3,4},{4,5},{5,6},{6,7},{8,9},{9,10},{10,11},{11... | collective-permute-start | bytes 393224 | tf_op jit(solution)/shard_map/ppermute | solution.py:265
  51.7 1.3 collective-permute-start.1
  54.7 0.9 select_reduce_fusion
  55.7 2.0 lt.142
  58.4 1.8 and.211
  61.0 2.0 add.288
  65.8 2.9 %fusion.4.refs_8_ = f32[4,512,1]{2,1,0:T(8,128)} fusion(pred[4,512,1]{2,1,0:T(8,128)(4,1)} %and.211, s32[4,512,1]{2,1,0:T(8,128)} %lt.142, s32[4,512,1]{2,1,0:T(8,128)} %add.288, s32[512]{0:T(512)S(1)} %add.275), kind=kLoop, calls=%fused_computation.10 | loop fusion | flops 8192 | bytes 28672 | tf_op jit(solution)/shard_map/convert_element_type | solution.py:142
  69.3 0.9 constant_dynamic-update-slice_fusion.3
  70.3 25.0 %all-to-all-done = bf16[16,2,64,512]{3,2,1,0:T(8,128)(2,1)} async-done(((bf16[16,2,64,512]{3,2,1,0:T(8,128)(2,1)}), bf16[16,2,64,512]{3,2,1,0:T(8,128)(2,1)}, u32[]{:S(2)}, u32[]{:S(2)}) %all-to-all-start) | async-done | bytes 2097184 | tf_op jit(solution)/shard_map/all_to_all | solution.py:282
  95.3 1.8 constant_dynamic-update-slice_fusion.refs_0_.refs_1_.refs_2_.refs_3_.refs_4_.refs_5_.refs_6_.refs_7_
  97.1 1.6 copy-done
  98.7 28.4 %shard_map.97 = (bf16[256,4096]{1,0:T(8,128)(2,1)}, f32[4,2,64,512]{3,2,1,0:T(8,128)}, f32[2,2,64,512]{3,2,1,0:T(8,128)}, f32[2,2,64,512]{3,2,1,0:T(8,128)}, bf16[4,3,2,64,512]{4,3,2,1,0:T(8,128)(2,1)}) custom-call(s32[32]{0:T(128)} %min.18.ids_ref, bf16[256,4096]{1,0:T(8,128)(2,1)} %bitcast.48, bf16[256,4096]{1,0:T(8,128)(2,1)} %bitcast.49, ...), custom_call_target="tpu_custom_call" | custom-call | flops 6442450944 | bytes 12582912 | tf_op jit(solution)/shard_map/pallas_call | solution.py:162
  127.2 2.8 %collective-permute-start.6 = (f32[2,2,64,512]{3,2,1,0:T(8,128)}, f32[2,2,64,512]{3,2,1,0:T(8,128)S(1)}, u32[]{:S(2)}, u32[]{:S(2)}) collective-permute-start(f32[2,2,64,512]{3,2,1,0:T(8,128)} %get-tuple-element.41), channel_id=1, source_target_pairs={{0,1},{1,0},{2,3},{3,2},{4,5},{5,4},{6,7},{7,6},{8,9},{9,8},{10,11... | collective-permute-start | bytes 1572872 | tf_op jit(solution)/shard_map/ppermute | solution.py:46
  130.0 10.6 %collective-permute-done.6 = f32[2,2,64,512]{3,2,1,0:T(8,128)S(1)} collective-permute-done((f32[2,2,64,512]{3,2,1,0:T(8,128)}, f32[2,2,64,512]{3,2,1,0:T(8,128)S(1)}, u32[]{:S(2)}, u32[]{:S(2)}) %collective-permute-start.6) | collective-permute-done | bytes 524320 | tf_op jit(solution)/shard_map/ppermute | solution.py:46
  140.6 1.1 add.280
  141.7 2.3 collective-permute-start.7
  144.0 10.2 %collective-permute-done.7 = f32[2,2,64,512]{3,2,1,0:T(8,128)S(1)} collective-permute-done((f32[2,2,64,512]{3,2,1,0:T(8,128)S(1)}, f32[2,2,64,512]{3,2,1,0:T(8,128)S(1)}, u32[]{:S(2)}, u32[]{:S(2)}) %collective-permute-start.7) | collective-permute-done | bytes 524320 | tf_op jit(solution)/shard_map/ppermute | solution.py:46
  154.3 5.7 %collective-permute-start.8 = (f32[2,2,64,512]{3,2,1,0:T(8,128)S(1)}, f32[2,2,64,512]{3,2,1,0:T(8,128)S(1)}, u32[]{:S(2)}, u32[]{:S(2)}) collective-permute-start(f32[2,2,64,512]{3,2,1,0:T(8,128)S(1)} %add.281), channel_id=1, source_target_pairs={{0,4},{1,5},{2,6},{3,7},{4,0},{5,1},{6,2},{7,3},{8,12},{9,13},{10,... | collective-permute-start | bytes 1572872 | tf_op jit(solution)/shard_map/ppermute | solution.py:46
  160.7 1.5 broadcast_in_dim.98
  162.2 5.1 %scatter_fusion = bf16[8,2,2,64,512]{4,3,2,1,0:T(8,128)(2,1)} fusion(bf16[8,2,2,64,512]{4,3,2,1,0:T(8,128)(2,1)} %broadcast_in_dim.98, s32[12]{0:T(128)S(1)} %fusion.36, bf16[12,2,64,512]{3,2,1,0:T(8,128)(2,1)S(1)} %bitcast.50), kind=kCustom, calls=%fused_computation.1 | custom fusion | bytes 4718688 | tf_op jit(solution)/shard_map/scatter | solution.py:313
  167.3 16.1 %collective-permute-done.8 = f32[2,2,64,512]{3,2,1,0:T(8,128)S(1)} collective-permute-done((f32[2,2,64,512]{3,2,1,0:T(8,128)S(1)}, f32[2,2,64,512]{3,2,1,0:T(8,128)S(1)}, u32[]{:S(2)}, u32[]{:S(2)}) %collective-permute-start.8) | collective-permute-done | bytes 524320 | tf_op jit(solution)/shard_map/ppermute | solution.py:46
  183.4 0.9 add.282
  184.3 3.7 %all-to-all-start.1 = ((bf16[16,2,64,512]{3,2,1,0:T(8,128)(2,1)}), bf16[16,2,64,512]{3,2,1,0:T(8,128)(2,1)S(1)}, u32[]{:S(2)}, u32[]{:S(2)}) async-start(bf16[16,2,64,512]{3,2,1,0:T(8,128)(2,1)} %bitcast.17), calls=%async_computation.1 | async-start | bytes 4194304 | tf_op jit(solution)/shard_map/all_to_all | solution.py:318
  189.2 1.3 collective-permute-start.9
  190.4 4.0 %collective-permute-start.10 = (bf16[1,2,64,512]{3,2,1,0:T(8,128)(2,1)S(1)}, bf16[1,2,64,512]{3,2,1,0:T(8,128)(2,1)S(1)}, u32[]{:S(2)}, u32[]{:S(2)}) collective-permute-start(bf16[1,2,64,512]{3,2,1,0:T(8,128)(2,1)S(1)} %get-tuple-element.59), channel_id=1, source_target_pairs={{0,1},{1,2},{2,3},{3,4},{4,5},{5,6},{6,7},{8,9},{9,10},{10,11},{11... | collective-permute-start | bytes 393224 | tf_op jit(solution)/shard_map/ppermute | solution.py:311
  194.4 2.0 collective-permute-start.5
  196.4 2.6 %fusion.5 = f32[4,2,64,512]{3,0,2,1:T(4,128)S(1)} fusion(f32[2,2,64,512]{3,2,1,0:T(8,128)} %add.282, pred[2]{0:T(512)(128)(4,1)S(1)} %fusion.37, s32[2]{0:T(128)S(1)} %and_select_fusion), kind=kOutput, calls=%fused_computation.21 | convolution fusion | flops 6291472 | bytes 1572874 | tf_op jit(solution)/shard_map/gq,gxsk->qxsk/dot_general | solution.py:334
  199.0 35.8 %all-to-all-done.1 = bf16[16,2,64,512]{3,2,1,0:T(8,128)(2,1)S(1)} async-done(((bf16[16,2,64,512]{3,2,1,0:T(8,128)(2,1)}), bf16[16,2,64,512]{3,2,1,0:T(8,128)(2,1)S(1)}, u32[]{:S(2)}, u32[]{:S(2)}) %all-to-all-start.1) | async-done | bytes 2097184 | tf_op jit(solution)/shard_map/all_to_all | solution.py:318
  234.8 1.3 fusion
  237.1 3.8 %collective-permute-start.11 = (bf16[256,1024]{1,0:T(8,128)(2,1)S(1)}, bf16[256,1024]{1,0:T(8,128)(2,1)S(1)}, u32[]{:S(2)}, u32[]{:S(2)}) collective-permute-start(bf16[256,1024]{1,0:T(8,128)(2,1)S(1)} %pad_maximum_fusion.1), channel_id=1, source_target_pairs={{8,0},{16,8},{24,16},{0,24},{9,1},{17,9},{25,17},{1,25},{10,2},{18... | collective-permute-start | bytes 1572872 | tf_op jit(solution)/shard_map/ppermute | solution.py:37
  240.9 8.0 %collective-permute-done.11 = bf16[256,1024]{1,0:T(8,128)(2,1)S(1)} collective-permute-done((bf16[256,1024]{1,0:T(8,128)(2,1)S(1)}, bf16[256,1024]{1,0:T(8,128)(2,1)S(1)}, u32[]{:S(2)}, u32[]{:S(2)}) %collective-permute-start.11) | collective-permute-done | bytes 524320 | tf_op jit(solution)/shard_map/ppermute | solution.py:37
  248.9 0.8 slice_bitcast_fusion
  249.8 3.1 %copy.107 = bf16[1,256,4096]{2,1,0:T(8,128)(2,1)} copy(bf16[1,256,4096]{2,1,0:T(8,128)(2,1)} %bitcast.10) | data formatting | bytes 4194304
  (91 shorter events, 11.4 us)
Async XLA Ops:
  9.7 8.4 %collective-permute-start.2 = (bf16[2,2,64,512]{3,2,1,0:T(8,128)(2,1)}, bf16[2,2,64,512]{3,2,1,0:T(8,128)(2,1)}, u32[]{:S(2)}, u32[]{:S(2)}) collective-permute-start(bf16[2,2,64,512]{3,2,1,0:T(8,128)(2,1)} %pad_maximum_fusion.2), channel_id=1, source_target_pairs={{0,1},{1,0},{2,3},{3,2},{4,5},{5,4},{6,7},{7,6},{8,9},{9,8},{10,11... | collective-permute-start | bytes 786440 | tf_op jit(solution)/shard_map/ppermute | solution.py:46
  12.6 2.1 copy-start.6
  12.6 11.5 %copy-start.8 = (pred[8,12]{1,0:T(8,128)(4,1)}, pred[8,12]{1,0:T(8,128)(4,1)S(1)}, u32[]{:S(2)}) copy-start(pred[8,12]{1,0:T(8,128)(4,1)S(1)} %get-tuple-element.47) | copy-start | bytes 292
  15.1 9.1 %copy-start.4 = (s32[8,12]{1,0:T(8,128)}, s32[8,12]{1,0:T(8,128)S(1)}, u32[]{:S(2)}) copy-start(s32[8,12]{1,0:T(8,128)S(1)} %copy.75) | copy-start | bytes 1156
  19.8 6.9 %collective-permute-start.3 = (bf16[2,2,64,512]{3,2,1,0:T(8,128)(2,1)}, bf16[2,2,64,512]{3,2,1,0:T(8,128)(2,1)}, u32[]{:S(2)}, u32[]{:S(2)}) collective-permute-start(bf16[2,2,64,512]{3,2,1,0:T(8,128)(2,1)} %fusion.38), channel_id=1, source_target_pairs={{0,2},{1,3},{2,0},{3,1},{4,6},{5,7},{6,4},{7,5},{8,10},{9,11},{10,... | collective-permute-start | bytes 786440 | tf_op jit(solution)/shard_map/ppermute | solution.py:46
  21.1 3.1 %copy-start.11 = (s32[16]{0:T(128)}, s32[16]{0:T(128)S(1)}, u32[]{:S(2)}) copy-start(s32[16]{0:T(128)S(1)} %reshape.651) | copy-start | bytes 196
  27.8 14.1 %collective-permute-start.4 = (bf16[2,2,64,512]{3,2,1,0:T(8,128)(2,1)S(1)}, bf16[2,2,64,512]{3,2,1,0:T(8,128)(2,1)S(1)}, u32[]{:S(2)}, u32[]{:S(2)}) collective-permute-start(bf16[2,2,64,512]{3,2,1,0:T(8,128)(2,1)S(1)} %fusion.42), channel_id=1, source_target_pairs={{0,4},{1,5},{2,6},{3,7},{4,0},{5,1},{6,2},{7,3},{8,12},{9,13},{10,... | collective-permute-start | bytes 786440 | tf_op jit(solution)/shard_map/ppermute | solution.py:46
  41.9 11.0 %copy-start.10 = (s32[1,32,3]{1,0,2:T(1,128)S(1)}, s32[1,32,3]{1,0,2:T(1,128)}, u32[]{:S(2)}) copy-start(s32[1,32,3]{1,0,2:T(1,128)} %param.15) | copy-start | bytes 1156
  41.9 53.4 %all-to-all-start = ((bf16[16,2,64,512]{3,2,1,0:T(8,128)(2,1)}), bf16[16,2,64,512]{3,2,1,0:T(8,128)(2,1)}, u32[]{:S(2)}, u32[]{:S(2)}) async-start(bf16[16,2,64,512]{3,2,1,0:T(8,128)(2,1)} %broadcast_select_fusion), calls=%async_computation | async-start | bytes 4194304 | tf_op jit(solution)/shard_map/all_to_all | solution.py:282
  47.7 21.6 %collective-permute-start = (bf16[1,2,64,512]{3,2,1,0:T(8,128)(2,1)}, bf16[1,2,64,512]{3,2,1,0:T(8,128)(2,1)}, u32[]{:S(2)}, u32[]{:S(2)}) collective-permute-start(bf16[1,2,64,512]{3,2,1,0:T(8,128)(2,1)} %get-tuple-element.54), channel_id=1, source_target_pairs={{0,1},{1,2},{2,3},{3,4},{4,5},{5,6},{6,7},{8,9},{9,10},{10,11},{11... | collective-permute-start | bytes 393224 | tf_op jit(solution)/shard_map/ppermute | solution.py:265
  51.7 18.5 %collective-permute-start.1 = (bf16[1,2,64,512]{3,2,1,0:T(8,128)(2,1)}, bf16[1,2,64,512]{3,2,1,0:T(8,128)(2,1)S(1)}, u32[]{:S(2)}, u32[]{:S(2)}) collective-permute-start(bf16[1,2,64,512]{3,2,1,0:T(8,128)(2,1)} %get-tuple-element.55), channel_id=1, source_target_pairs={{1,0},{2,1},{3,2},{4,3},{5,4},{6,5},{7,6},{9,8},{10,9},{11,10},{12... | collective-permute-start | bytes 393224 | tf_op jit(solution)/shard_map/ppermute | solution.py:266
  54.7 0.9 copy-start.7
  97.1 1.7 copy-start
  127.2 32.8 %copy-start.5 = (s32[8,12]{1,0:T(8,128)S(1)}, s32[8,12]{1,0:T(8,128)}, u32[]{:S(2)}) copy-start(s32[8,12]{1,0:T(8,128)} %copy-done.4) | copy-start | bytes 1156
  127.2 13.4 %collective-permute-start.6 = (f32[2,2,64,512]{3,2,1,0:T(8,128)}, f32[2,2,64,512]{3,2,1,0:T(8,128)S(1)}, u32[]{:S(2)}, u32[]{:S(2)}) collective-permute-start(f32[2,2,64,512]{3,2,1,0:T(8,128)} %get-tuple-element.41), channel_id=1, source_target_pairs={{0,1},{1,0},{2,3},{3,2},{4,5},{5,4},{6,7},{7,6},{8,9},{9,8},{10,11... | collective-permute-start | bytes 1572872 | tf_op jit(solution)/shard_map/ppermute | solution.py:46
  141.7 20.5 %copy-start.1 = (bf16[4,3,2,64,512]{4,3,2,1,0:T(8,128)(2,1)S(1)}, bf16[4,3,2,64,512]{4,3,2,1,0:T(8,128)(2,1)}, u32[]{:S(2)}) copy-start(bf16[4,3,2,64,512]{4,3,2,1,0:T(8,128)(2,1)} %get-tuple-element.40) | copy-start | bytes 4718596
  141.7 12.5 %collective-permute-start.7 = (f32[2,2,64,512]{3,2,1,0:T(8,128)S(1)}, f32[2,2,64,512]{3,2,1,0:T(8,128)S(1)}, u32[]{:S(2)}, u32[]{:S(2)}) collective-permute-start(f32[2,2,64,512]{3,2,1,0:T(8,128)S(1)} %add.280), channel_id=1, source_target_pairs={{0,2},{1,3},{2,0},{3,1},{4,6},{5,7},{6,4},{7,5},{8,10},{9,11},{10,... | collective-permute-start | bytes 1572872 | tf_op jit(solution)/shard_map/ppermute | solution.py:46
  154.3 29.1 %collective-permute-start.8 = (f32[2,2,64,512]{3,2,1,0:T(8,128)S(1)}, f32[2,2,64,512]{3,2,1,0:T(8,128)S(1)}, u32[]{:S(2)}, u32[]{:S(2)}) collective-permute-start(f32[2,2,64,512]{3,2,1,0:T(8,128)S(1)} %add.281), channel_id=1, source_target_pairs={{0,4},{1,5},{2,6},{3,7},{4,0},{5,1},{6,2},{7,3},{8,12},{9,13},{10,... | collective-permute-start | bytes 1572872 | tf_op jit(solution)/shard_map/ppermute | solution.py:46
  184.3 3.8 %copy-start.9 = (pred[8,12]{1,0:T(8,128)(4,1)S(1)}, pred[8,12]{1,0:T(8,128)(4,1)}, u32[]{:S(2)}) copy-start(pred[8,12]{1,0:T(8,128)(4,1)} %copy-done.8) | copy-start | bytes 292
  184.3 4.1 %copy-start.13 = (s32[1,2]{1,0:T(1,128)S(1)}, s32[1,2]{1,0:T(1,128)}, u32[]{:S(2)}) copy-start(s32[1,2]{1,0:T(1,128)} %param.16) | copy-start | bytes 28
  184.3 4.1 %copy-start.3 = (f32[2,2,64,512]{3,2,1,0:T(8,128)S(1)}, f32[2,2,64,512]{3,2,1,0:T(8,128)}, u32[]{:S(2)}) copy-start(f32[2,2,64,512]{3,2,1,0:T(8,128)} %get-tuple-element.43) | copy-start | bytes 1572868
  184.3 50.5 %all-to-all-start.1 = ((bf16[16,2,64,512]{3,2,1,0:T(8,128)(2,1)}), bf16[16,2,64,512]{3,2,1,0:T(8,128)(2,1)S(1)}, u32[]{:S(2)}, u32[]{:S(2)}) async-start(bf16[16,2,64,512]{3,2,1,0:T(8,128)(2,1)} %bitcast.17), calls=%async_computation.1 | async-start | bytes 4194304 | tf_op jit(solution)/shard_map/all_to_all | solution.py:318
  188.0 46.7 %copy-start.12 = (s32[16]{0:T(128)S(1)}, s32[16]{0:T(128)}, u32[]{:S(2)}) copy-start(s32[16]{0:T(128)} %copy-done.11) | copy-start | bytes 196
  189.2 47.3 %collective-permute-start.9 = (bf16[1,2,64,512]{3,2,1,0:T(8,128)(2,1)}, bf16[1,2,64,512]{3,2,1,0:T(8,128)(2,1)S(1)}, u32[]{:S(2)}, u32[]{:S(2)}) collective-permute-start(bf16[1,2,64,512]{3,2,1,0:T(8,128)(2,1)} %get-tuple-element.60), channel_id=1, source_target_pairs={{1,0},{2,1},{3,2},{4,3},{5,4},{6,5},{7,6},{9,8},{10,9},{11,10},{12... | collective-permute-start | bytes 393224 | tf_op jit(solution)/shard_map/ppermute | solution.py:310
  190.4 46.1 %collective-permute-start.10 = (bf16[1,2,64,512]{3,2,1,0:T(8,128)(2,1)S(1)}, bf16[1,2,64,512]{3,2,1,0:T(8,128)(2,1)S(1)}, u32[]{:S(2)}, u32[]{:S(2)}) collective-permute-start(bf16[1,2,64,512]{3,2,1,0:T(8,128)(2,1)S(1)} %get-tuple-element.59), channel_id=1, source_target_pairs={{0,1},{1,2},{2,3},{3,4},{4,5},{5,6},{6,7},{8,9},{9,10},{10,11},{11... | collective-permute-start | bytes 393224 | tf_op jit(solution)/shard_map/ppermute | solution.py:311
  194.4 46.5 %collective-permute-start.5 = (bf16[256,4096]{1,0:T(8,128)(2,1)}, bf16[256,4096]{1,0:T(8,128)(2,1)}, u32[]{:S(2)}, u32[]{:S(2)}) collective-permute-start(bf16[256,4096]{1,0:T(8,128)(2,1)} %get-tuple-element.38), channel_id=1, source_target_pairs={{8,0},{16,8},{24,16},{0,24},{9,1},{17,9},{25,17},{1,25},{10,2},{18... | collective-permute-start | bytes 6291464 | tf_op jit(solution)/shard_map/ppermute | solution.py:37
  234.8 1.3 copy-start.2
  237.1 11.8 %collective-permute-start.11 = (bf16[256,1024]{1,0:T(8,128)(2,1)S(1)}, bf16[256,1024]{1,0:T(8,128)(2,1)S(1)}, u32[]{:S(2)}, u32[]{:S(2)}) collective-permute-start(bf16[256,1024]{1,0:T(8,128)(2,1)S(1)} %pad_maximum_fusion.1), channel_id=1, source_target_pairs={{8,0},{16,8},{24,16},{0,24},{9,1},{17,9},{25,17},{1,25},{10,2},{18... | collective-permute-start | bytes 1572872 | tf_op jit(solution)/shard_map/ppermute | solution.py:37

commit v8 on v3

--- a/solution.py
+++ b/solution.py
@@ -61,29 +61,30 @@
     contract_last = (((1,), (1,)), ((), ()))
     contract_first = (((0,), (0,)), ((), ()))
     scores = (
-        lax.dot_general(query_rows, key_rows, contract_last, preferred_element_type=jnp.float32)
+        lax.dot_general(key_rows, query_rows, contract_last, preferred_element_type=jnp.float32)
         * score_scale
     )
     scores = jnp.where(live, scores, -1e30)
-    row_max = jnp.max(scores, axis=1, keepdims=True)
+    row_max = jnp.max(scores, axis=0, keepdims=True)
     shifted = jnp.exp(scores - row_max)
-    total = jnp.sum(shifted, axis=1, keepdims=True)
+    total = jnp.sum(shifted, axis=0, keepdims=True)
     probs = shifted * (1.0 / total)
     probs_low = probs.astype(jnp.bfloat16)
-    output = jnp.dot(probs_low, value_rows, preferred_element_type=jnp.float32)
-    row_dot = jnp.sum(grad_rows.astype(jnp.float32) * output, axis=1, keepdims=True)
+    output = lax.dot_general(
+        value_rows, probs_low, contract_first, preferred_element_type=jnp.float32
+    )
+    grad_cols = grad_rows.astype(jnp.float32).T
+    row_dot = jnp.sum(grad_cols * output, axis=0, keepdims=True)
     prob_grad = lax.dot_general(
-        grad_rows, value_rows, contract_last, preferred_element_type=jnp.float32
+        value_rows, grad_rows, contract_last, preferred_element_type=jnp.float32
     )
     score_grad = (probs * (prob_grad - row_dot)).astype(jnp.bfloat16)
-    query_grad = jnp.dot(score_grad, key_rows, preferred_element_type=jnp.float32) * score_scale
-    key_grad = (
-        lax.dot_general(score_grad, query_rows, contract_first, preferred_element_type=jnp.float32)
+    query_grad = (
+        lax.dot_general(key_rows, score_grad, contract_first, preferred_element_type=jnp.float32)
         * score_scale
-    )
-    value_grad = lax.dot_general(
-        probs_low, grad_rows, contract_first, preferred_element_type=jnp.float32
-    )
+    ).T
+    key_grad = jnp.dot(score_grad, query_rows, preferred_element_type=jnp.float32) * score_scale
+    value_grad = jnp.dot(probs_low, grad_rows, preferred_element_type=jnp.float32)
     for g in range(group):
         dq_ref[:, g * HDIM : (g + 1) * HDIM] = query_grad[g * block_len : (g + 1) * block_len].astype(
             dq_ref.dtype
@@ -127,7 +128,7 @@
     group_width = qwidth // heads_kv
     near = 3 + GLOB
     nrand = ntiles - near
-    live = key_live.reshape(nblocks, 1, ntiles * block_len).astype(jnp.float32)
+    live = key_live.reshape(nblocks, ntiles * block_len, 1).astype(jnp.float32)
     row_spec = pl.BlockSpec((block_len, group_width), lambda h, b, ids: (b, h))
     tile_specs = [
         pl.BlockSpec(
@@ -135,7 +136,7 @@
         )
         for t in range(ntiles)
     ]
-    live_spec = pl.BlockSpec((None, 1, ntiles * block_len), lambda h, b, ids: (b, 0, 0))
+    live_spec = pl.BlockSpec((None, ntiles * block_len, 1), lambda h, b, ids: (b, 0, 0))
     own_spec = pl.BlockSpec((nblocks, 2, block_len, HDIM), lambda h, b, ids: (0, 0, 0, h))
     edge_spec = pl.BlockSpec((2, 2, block_len, HDIM), lambda h, b, ids: (0, 0, 0, h))
     glob_spec = pl.BlockSpec((GLOB, 2, block_len, HDIM), lambda h, b, ids: (0, 0, 0, h))

time: 234 us -> 230 us (0.983)
  Pallas kernels: 32.1 us -> 28.4 us
  local copies, waits for them, and re-layouts: 10.7 us -> 13.6 us
    pallas_call x1, Pallas kernels: 32.1 us -> 28.4 us  [block_backward(): pl.pallas_call(attention_kernel, grid_spec=grid_spec, out_shape=[jax.Shap...]
  transfers between devices with their start and end apart: 4 -> 4, of which waited for: 3 -> 3; matrix products, arithmetic and copies ran while one was open for 4% -> 5% of each run, Pallas kernels for 0% -> 0%
where the time goes in v8:
time: 230 us
  waiting for transfers between devices  160 us (70%)
  Pallas kernels  28.4 us (12%)
  between operations  14.2 us (6%)
  local copies, waits for them, and re-layouts  13.6 us (6%)
  other arithmetic  9.18 us (4%)
  starting transfers between devices  2.67 us (1%)
    reduce_scatter x1, waiting for transfers between devices, body(): returned = lax.psum_scatter(partial, 'seq', scatter_dimension=0, tiled=True)  85.7 us
    all_gather x1, waiting for transfers between devices, body(): all_blocks = lax.all_gather(kvpair, 'seq', axis=0, tiled=True)  66.4 us
    pallas_call x1, Pallas kernels, block_backward(): pl.pallas_call(attention_kernel, grid_spec=grid_spec, out_shape=[jax.Shap...  28.4 us
    ppermute x2, waiting for transfers between devices, from_behind(): return lax.ppermute(block, axis, route)  7.98 us
  transfers between devices with their start and end apart: 4, of which 3 were waited for; matrix products, arithmetic and copies ran while one was open for 5% of the time, Pallas kernels for 0%

profile of v8, /device:TPU:1, one launch (start us, length us, event | category | flops | bytes accessed | tf_op | source)
XLA Modules:
  0.0 229.8 jit_solution(3228949526348614156)
XLA Ops:
  7.2 0.0 copy-start.3
  7.2 0.0 copy-start.2
  7.2 0.0 all-gather.2.cloned.1.call-start
  7.2 1.9 pad_maximum_fusion
  9.1 0.0 all-gather.2.cloned.1.call-update
  9.1 0.0 reduce-scatter.2.cloned.1.call-start
  9.2 0.7 pad.12.clone
  9.9 0.7 reduce
  10.6 0.1 add.96
  10.7 0.1 reshape_squeeze.2
  10.8 0.1 copy.43
  10.9 0.1 reshape.249
  11.0 0.1 broadcast_add_fusion
  11.1 0.1 fusion.11
  11.1 0.6 min.14.ids_ref
  11.7 0.1 compare_and_fusion
  11.8 0.1 and.52
  11.9 1.1 and.57
  13.0 0.1 add.93
  13.1 1.0 add.100
  14.1 0.0 copy-done.2
  14.1 0.2 select_reduce_fusion
  14.4 0.1 lt.42
  14.4 1.0 lt.45
  15.5 0.6 fusion.15
  16.1 0.0 copy-done.3
  16.1 1.3 pad_add_fusion.1
  17.4 1.3 fusion.7.refs_8_
  18.7 66.4 %all-gather.2.cloned.1.call-done.refs_0_.refs_1_.refs_2_.refs_3_.refs_4_.refs_5_.refs_6_.refs_7_ = bf16[32,2,64,512]{3,2,1,0:T(8,128)(2,1)} async-done(((bf16[4,2,64,512]{3,2,1,0:T(8,128)(2,1)}), bf16[32,2,64,512]{3,2,1,0:T(8,128)(2,1)}) %all-gather.2.cloned.1.call-update) | async-done | bytes 4194320 | tf_op jit(solution)/shard_map/all_gather | solution.py:253
  85.0 28.4 %shard_map.94 = (bf16[256,4096]{1,0:T(8,128)(2,1)}, f32[4,2,64,512]{3,2,1,0:T(8,128)}, f32[2,2,64,512]{3,2,1,0:T(8,128)}, f32[2,2,64,512]{3,2,1,0:T(8,128)}, bf16[4,3,2,64,512]{4,3,2,1,0:T(8,128)(2,1)}) custom-call(s32[32]{0:T(128)} %min.14.ids_ref, bf16[256,4096]{1,0:T(8,128)(2,1)} %bitcast.24, bf16[256,4096]{1,0:T(8,128)(2,1)} %bitcast.25, ...), custom_call_target="tpu_custom_call" | custom-call | flops 6442450944 | bytes 12582912 | tf_op jit(solution)/shard_map/pallas_call | solution.py:151
  113.5 0.0 copy-start
  113.5 1.2 convert_element_type.25
  114.7 0.3 copy.49
  114.9 1.1 convert_element_type.26
  116.0 0.3 copy.50
  116.3 0.9 copy.51
  117.2 1.6 fusion
  118.9 4.3 %copy.55 = bf16[32,2,64,512]{3,2,1,0:T(8,128)(2,1)} copy(bf16[32,2,64,512]{3,0,2,1:T(8,128)(2,1)S(1)} %fusion) | data formatting | bytes 8388608 | tf_op jit(solution)/shard_map/nf,fxsk->nxsk/dot_general | solution.py:286
  123.2 0.0 reduce-scatter.2.cloned.1.call-update
  123.2 1.9 collective-permute-start
  125.1 85.7 %reduce-scatter.2.cloned.1.call-done = bf16[4,2,64,512]{3,2,1,0:T(8,128)(2,1)} async-done(((bf16[32,2,64,512]{3,2,1,0:T(8,128)(2,1)}), bf16[4,2,64,512]{3,2,1,0:T(8,128)(2,1)}) %reduce-scatter.2.cloned.1.call-update) | async-done | bytes 524304 | tf_op jit(solution)/shard_map/reduce_scatter | solution.py:289
  210.8 1.2 add_convert_fusion
  212.1 0.1 pad_maximum_fusion.1
  212.1 0.7 collective-permute-start.1
  212.8 0.0 collective-permute-done
  212.8 8.0 %collective-permute-done.1 = bf16[256,1024]{1,0:T(8,128)(2,1)S(1)} collective-permute-done((bf16[256,1024]{1,0:T(8,128)(2,1)S(1)}, bf16[256,1024]{1,0:T(8,128)(2,1)S(1)}, u32[]{:S(2)}, u32[]{:S(2)}) %collective-permute-start.1) | collective-permute-done | bytes 524320 | tf_op jit(solution)/shard_map/ppermute | solution.py:37
  220.8 0.8 slice_bitcast_fusion
  221.6 1.3 copy.57
  (10 shorter events, 0.1 us)
Async XLA Ops:
  7.2 8.9 %copy-start.3 = (s32[1,2]{1,0:T(1,128)S(1)}, s32[1,2]{1,0:T(1,128)}, u32[]{:S(2)}) copy-start(s32[1,2]{1,0:T(1,128)} %param.12) | copy-start | bytes 28
  7.2 7.0 %copy-start.2 = (s32[1,8]{1,0:T(1,128)S(1)}, s32[1,8]{1,0:T(1,128)}, u32[]{:S(2)}) copy-start(s32[1,8]{1,0:T(1,128)} %param.13) | copy-start | bytes 100
  7.2 77.9 %all-gather.2.cloned.1.call-start = ((), (), s32[]{:S(2)}) async-start(), calls=%async_computation.1 | async-start | bytes 4718592 | tf_op jit(solution)/shard_map/all_gather | solution.py:253
  9.1 201.7 %reduce-scatter.2.cloned.1.call-start = ((), (), s32[]{:S(2)}) async-start(), calls=%async_computation.2 | async-start | bytes 4718592 | tf_op jit(solution)/shard_map/reduce_scatter | solution.py:289
  113.5 2.8 %copy-start = (bf16[4,3,2,64,512]{4,3,2,1,0:T(8,128)(2,1)S(1)}, bf16[4,3,2,64,512]{4,3,2,1,0:T(8,128)(2,1)}, u32[]{:S(2)}) copy-start(bf16[4,3,2,64,512]{4,3,2,1,0:T(8,128)(2,1)} %get-tuple-element.12) | copy-start | bytes 4718596
  123.2 87.6 %copy-start.1 = (f32[4,2,64,512]{3,2,1,0:T(8,128)S(1)}, f32[4,2,64,512]{3,2,1,0:T(8,128)}, u32[]{:S(2)}) copy-start(f32[4,2,64,512]{3,2,1,0:T(8,128)} %get-tuple-element.9) | copy-start | bytes 3145732
  123.2 89.6 %collective-permute-start = (bf16[256,4096]{1,0:T(8,128)(2,1)}, bf16[256,4096]{1,0:T(8,128)(2,1)S(1)}, u32[]{:S(2)}, u32[]{:S(2)}) collective-permute-start(bf16[256,4096]{1,0:T(8,128)(2,1)} %get-tuple-element.8), channel_id=1, source_target_pairs={{8,0},{16,8},{24,16},{0,24},{9,1},{17,9},{25,17},{1,25},{10,2},{18... | collective-permute-start | bytes 6291464 | tf_op jit(solution)/shard_map/ppermute | solution.py:37
  212.1 8.7 %collective-permute-start.1 = (bf16[256,1024]{1,0:T(8,128)(2,1)S(1)}, bf16[256,1024]{1,0:T(8,128)(2,1)S(1)}, u32[]{:S(2)}, u32[]{:S(2)}) collective-permute-start(bf16[256,1024]{1,0:T(8,128)(2,1)S(1)} %pad_maximum_fusion.1), channel_id=1, source_target_pairs={{8,0},{16,8},{24,16},{0,24},{9,1},{17,9},{25,17},{1,25},{10,2},{18... | collective-permute-start | bytes 1572872 | tf_op jit(solution)/shard_map/ppermute | solution.py:37
Sparse Core Ops, SparseCore 0:
  10.7 74.2 all-gather.1
  123.3 87.4 reduce-scatter.1

commit v9 on v6

--- a/solution.py
+++ b/solution.py
@@ -35,17 +35,6 @@
     devices = range(lax.axis_size(axis))
     route = [((i - distance) % len(devices), i) for i in devices]
     return lax.ppermute(block, axis, route)
-
-
-def tree_sum(array, axis):
-    devices = lax.axis_size(axis)
-    if devices & (devices - 1):
-        return lax.psum(array, axis)
-    step = 1
-    while step < devices:
-        array = array + lax.ppermute(array, axis, [(i, i ^ step) for i in range(devices)])
-        step *= 2
-    return array
 
 
 def attention_kernel(ids_ref, q_ref, g_ref, *refs):
@@ -201,34 +190,6 @@
     return (serve_block, slot_used, owner_mine, rank_mine)
 
 
-def serve_tiles(own_blocks, request_info):
-    serve_block, slot_used = (request_info[0], request_info[1])
-    shards, capacity = serve_block.shape
-    gathered = jnp.take(own_blocks, serve_block.reshape(-1), axis=1)
-    gathered = gathered.reshape(2, shards, capacity, own_blocks.shape[2], own_blocks.shape[3])
-    return jnp.where(slot_used[None, :, :, None, None], gathered, jnp.zeros((), own_blocks.dtype))
-
-
-def pick_tiles(received, request_info):
-    return received[:, request_info[2], request_info[3]]
-
-
-def place_terms(terms, request_info):
-    serve_block = request_info[0]
-    shards, capacity = serve_block.shape
-    holder = jnp.zeros((2, shards, capacity, terms.shape[2], terms.shape[3]), terms.dtype)
-    return holder.at[:, request_info[2], request_info[3]].set(terms)
-
-
-def absorb_terms(received, request_info, query_blocks):
-    serve_block, slot_used = (request_info[0], request_info[1])
-    onehot = (
-        slot_used[:, :, None]
-        & (serve_block[:, :, None] == jnp.arange(query_blocks, dtype=jnp.int32)[None, None, :])
-    ).astype(jnp.bfloat16)
-    return jnp.einsum("ncq,xncsk->xqsk", onehot, received, preferred_element_type=jnp.float32)
-
-
 def token_live(tile_ids, pad_sizes, query_blocks, shard_tokens, total_blocks):
     valid = (tile_ids >= 0) & (tile_ids < total_blocks)
     safe_ids = jnp.clip(tile_ids, 0, total_blocks - 1)
@@ -272,13 +233,24 @@
         )
         for g in range(GLOB)
     ]
-    global_tiles = tree_sum(jnp.concatenate(global_mine, axis=0), "seq")
     requests = random_table.reshape(shards, query_blocks * RAND)
     plan = request_plan(requests, this_shard, query_blocks)
     serve_block, slot_used, owner_mine, rank_mine = plan
     capacity = serve_block.shape[1]
-    served = jnp.take(own_blocks, serve_block.reshape(-1), axis=0)
-    received = lax.all_to_all(served, "seq", 0, 0, tiled=True)
+    block_rows = 2 * BLK
+    served = jnp.take(own_blocks, serve_block.reshape(-1), axis=0).reshape(
+        shards, capacity * block_rows, kwidth
+    )
+    global_chunks = jnp.concatenate(global_mine, axis=0).reshape(shards, -1, kwidth)
+    received = lax.all_to_all(
+        jnp.concatenate([served, global_chunks], axis=1), "seq", 0, 0, tiled=True
+    )
+    random_tiles = received[:, : capacity * block_rows].reshape(shards * capacity, 2, BLK, kwidth)
+    global_piece = jnp.sum(received[:, capacity * block_rows :], axis=0, dtype=own_blocks.dtype)
+    global_tiles = lax.all_to_all(
+        jnp.broadcast_to(global_piece[None], (shards,) + global_piece.shape), "seq", 0, 0, tiled=True
+    ).reshape(GLOB, 2, BLK, kwidth)
+    received = random_tiles
     sources = jnp.concatenate([own_blocks, edge_before, edge_after, global_tiles, received], axis=0)
     nb = query_blocks
     block_range = jnp.arange(nb, dtype=jnp.int32)
@@ -312,19 +284,28 @@
     holder = holder.at[owner_mine, rank_mine].set(
         random_part.reshape(query_blocks * RAND, 2, BLK, kwidth)
     )
+    global_low = global_part.astype(jnp.bfloat16).reshape(shards, -1, kwidth)
     returned = lax.all_to_all(
-        holder.reshape(shards * capacity, 2, BLK, kwidth), "seq", 0, 0, tiled=True
-    )
+        jnp.concatenate([holder.reshape(shards, capacity * block_rows, kwidth), global_low], axis=1),
+        "seq",
+        0,
+        0,
+        tiled=True,
+    )
+    random_back = returned[:, : capacity * block_rows].reshape(shards * capacity, 2, BLK, kwidth)
+    global_sum = jnp.sum(returned[:, capacity * block_rows :].astype(jnp.float32), axis=0)
+    global_total = lax.all_to_all(
+        jnp.broadcast_to(global_sum[None], (shards,) + global_sum.shape), "seq", 0, 0, tiled=True
+    ).reshape(GLOB, 2, BLK, kwidth)
     onehot = (
         slot_used.reshape(-1)[None, :]
         & (serve_block.reshape(-1)[None, :] == block_range[:, None])
     ).astype(jnp.bfloat16)
     kv_sum = local_sum + jnp.einsum(
-        "qf,fxsk->qxsk", onehot, returned, preferred_element_type=jnp.float32
+        "qf,fxsk->qxsk", onehot, random_back, preferred_element_type=jnp.float32
     )
     kv_sum = kv_sum.at[nb - 1].add(from_after[0].astype(jnp.float32))
     kv_sum = kv_sum.at[0].add(from_before[0].astype(jnp.float32))
-    global_total = tree_sum(global_part, "seq")
     global_pick = (
         (global_ids[:, None] // query_blocks == this_shard)
         & (global_ids[:, None] % query_blocks == block_range[None, :])

time: 238 us -> 225 us (0.945)
  waiting for transfers between devices: 103 us -> 94.7 us
  other arithmetic: 23.8 us -> 18.2 us
    ppermute x6 -> x0, waiting for transfers between devices: 95.3 us -> none  [tree_sum(): lax.ppermute(array, axis, [(i, i ^ step) for i in range(devices)])]
    all_to_all x2 -> x4, waiting for transfers between devices: 0.01 us -> 86.7 us  [the longest x1 43.6 us: body(): lax.all_to_all(jnp.concatenate([holder.reshape(shards, capacity * block_r...]
    all_to_all x2 -> x4, starting transfers between devices: 13.2 us -> 21.7 us  [the longest x1 6.49 us: body(): lax.all_to_all(jnp.concatenate([served, global_chunks], axis=1), 'seq', 0...]
    ppermute x6 -> x0, starting transfers between devices: 8.01 us -> none  [tree_sum(): lax.ppermute(array, axis, [(i, i ^ step) for i in range(devices)])]
    add x6 -> x1, other arithmetic: 6.43 us -> 0.44 us  [body(): local_sum + jnp.einsum('qf,fxsk->qxsk', onehot, random_back, preferred_el...]
    slice x0 -> x2, local copies, waits for them, and re-layouts: none -> 3.27 us  [the longest x1 3.05 us: body(): received[:, :capacity * block_rows]]
    concatenate x1 -> x3, other arithmetic: 0.73 us -> 3.29 us  [the longest x1 1.68 us: body(): jnp.concatenate([holder.reshape(shards, capacity * block_rows, kwidth), g...]
    unnamed x26 -> x25, local copies, waits for them, and re-layouts: 6.85 us -> 6.94 us
  transfers between devices with their start and end apart: 14 -> 10, of which waited for: 7 -> 5; matrix products, arithmetic and copies ran while one was open for 17% -> 13% of each run, Pallas kernels for 0% -> 0%
where the time goes in v9:
time: 225 us; the launch traced here: 224 us
  waiting for transfers between devices  94.7 us (42%)
  starting transfers between devices  37.1 us (16%)
  local copies, waits for them, and re-layouts  36.1 us (16%)
  Pallas kernels  28.4 us (13%)
  other arithmetic  18.2 us (8%)
  between operations  6.21 us (3%)
  matrix products  2.85 us (1%)
    all_to_all x1, waiting for transfers between devices, body(): lax.all_to_all(jnp.concatenate([holder.reshape(shards, capacity * block_r...  43.6 us
    all_to_all x1, waiting for transfers between devices, body(): lax.all_to_all(jnp.concatenate([served, global_chunks], axis=1), 'seq', 0...  31.3 us
    pallas_call x1, Pallas kernels, block_backward(): pl.pallas_call(attention_kernel, grid_spec=grid_spec, out_shape=[jax.Shap...  28.4 us
    all_to_all x1, waiting for transfers between devices, body(): lax.all_to_all(jnp.broadcast_to(global_sum[None], (shards,) + global_sum....  10.7 us
    ppermute x2, waiting for transfers between devices, from_behind(): return lax.ppermute(block, axis, route)  8 us
    unnamed x25, local copies, waits for them, and re-layouts  6.94 us
    all_to_all x1, starting transfers between devices, body(): lax.all_to_all(jnp.concatenate([served, global_chunks], axis=1), 'seq', 0...  6.49 us
    all_to_all x1, starting transfers between devices, body(): lax.all_to_all(jnp.broadcast_to(global_sum[None], (shards,) + global_sum....  5.74 us
  transfers between devices with their start and end apart: 10, of which 5 were waited for; matrix products, arithmetic and copies ran while one was open for 13% of the time, Pallas kernels for 0%

profile of v9, /device:TPU:1, one launch (start us, length us, event | category | flops | bytes accessed | tf_op | source)
XLA Modules:
  0.0 223.6 jit_solution(7163499957520388940)
XLA Ops:
  0.6 1.3 fusion.40
  7.2 0.8 copy.63
  9.2 1.9 pad_maximum_fusion.2
  11.1 1.8 fusion.12
  13.0 3.0 %gather_fusion = bf16[16,2,64,512]{3,2,1,0:T(8,128)(2,1)} fusion(bf16[4,2,64,512]{3,2,1,0:T(8,128)(2,1)} %get-tuple-element.45, s32[1024]{0:T(1024)S(1)} %pad_clamp_fusion), kind=kCustom, calls=%fused_computation | custom fusion | bytes 4194368 | tf_op jit(solution)/shard_map/jit(_take)/gather | solution.py:241
  16.0 1.8 broadcast_select_fusion
  17.8 1.6 pad_maximum_fusion
  19.4 6.5 %all-to-all-start = ((bf16[8,288,512]{2,1,0:T(8,128)(2,1)}), bf16[8,288,512]{2,1,0:T(8,128)(2,1)}, u32[]{:S(2)}, u32[]{:S(2)}) async-start(bf16[8,288,512]{2,1,0:T(8,128)(2,1)} %pad_maximum_fusion), calls=%async_computation | async-start | bytes 4718592 | tf_op jit(solution)/shard_map/all_to_all | solution.py:245
  25.9 4.0 %collective-permute-start = (bf16[1,2,64,512]{3,2,1,0:T(8,128)(2,1)}, bf16[1,2,64,512]{3,2,1,0:T(8,128)(2,1)}, u32[]{:S(2)}, u32[]{:S(2)}) collective-permute-start(bf16[1,2,64,512]{3,2,1,0:T(8,128)(2,1)} %get-tuple-element.48), channel_id=1, source_target_pairs={{0,1},{1,2},{2,3},{3,4},{4,5},{5,6},{6,7},{8,9},{9,10},{10,11},{11... | collective-permute-start | bytes 393224 | tf_op jit(solution)/shard_map/ppermute | solution.py:226
  29.9 1.3 collective-permute-start.1
  31.6 0.7 fusion.21
  32.5 2.0 lt.142
  34.6 1.1 and.211
  35.8 1.3 add.251
  37.1 2.7 %add.264 = s32[4,512,1]{2,1,0:T(8,128)} reshape(s32[4,8,64]{2,1,0:T(8,128)} %add.251) | data formatting | bytes 16384 | tf_op jit(solution)/shard_map/add | solution.py:202
  39.8 0.7 add.254
  41.0 0.7 add.236
  41.8 0.6 fusion.19
  43.5 1.4 concatenate.46
  44.9 2.8 %fusion.4.refs_8_ = f32[4,512,1]{2,1,0:T(8,128)} fusion(pred[4,512,1]{2,1,0:T(8,128)(4,1)S(1)} %and.211, s32[4,512,1]{2,1,0:T(8,128)} %lt.142, s32[4,512,1]{2,1,0:T(8,128)} %add.264, s32[512]{0:T(512)} %add.254), kind=kLoop, calls=%fused_computation.12 | loop fusion | flops 8192 | bytes 28672 | tf_op jit(solution)/shard_map/convert_element_type | solution.py:131
  47.7 31.3 %all-to-all-done = bf16[8,288,512]{2,1,0:T(8,128)(2,1)} async-done(((bf16[8,288,512]{2,1,0:T(8,128)(2,1)}), bf16[8,288,512]{2,1,0:T(8,128)(2,1)}, u32[]{:S(2)}, u32[]{:S(2)}) %all-to-all-start) | async-done | bytes 2359328 | tf_op jit(solution)/shard_map/all_to_all | solution.py:245
  79.0 1.0 slice_reduce_fusion
  80.0 0.7 broadcast_in_dim.113
  80.7 4.7 %all-to-all-start.1 = ((bf16[8,32,512]{2,1,0:T(8,128)(2,1)}), bf16[8,32,512]{2,1,0:T(8,128)(2,1)S(1)}, u32[]{:S(2)}, u32[]{:S(2)}) async-start(bf16[8,32,512]{2,1,0:T(8,128)(2,1)} %broadcast_in_dim.113), calls=%async_computation.1 | async-start | bytes 524288 | tf_op jit(solution)/shard_map/all_to_all | solution.py:250
  86.0 1.3 min.18.ids_ref
  87.3 0.9 constant_dynamic-update-slice_fusion.3
  88.2 3.0 %slice.127 = bf16[8,256,512]{2,1,0:T(8,128)(2,1)} slice(bf16[8,288,512]{2,1,0:T(8,128)(2,1)} %all-to-all-done), slice={[0:8], [0:256], [0:512]} | slice | bytes 4194304 | tf_op jit(solution)/shard_map/slice | solution.py:248
  91.3 1.2 all-to-all-done.1
  92.5 1.8 constant_dynamic-update-slice_fusion.refs_0_.refs_1_.refs_2_.refs_3_.refs_4_.refs_5_.refs_6_.refs_7_
  94.3 1.6 copy-done
  95.9 28.4 %shard_map.97 = (bf16[256,4096]{1,0:T(8,128)(2,1)}, f32[4,2,64,512]{3,2,1,0:T(8,128)}, f32[2,2,64,512]{3,2,1,0:T(8,128)}, f32[2,2,64,512]{3,2,1,0:T(8,128)}, bf16[4,3,2,64,512]{4,3,2,1,0:T(8,128)(2,1)}) custom-call(s32[32]{0:T(128)} %min.18.ids_ref, bf16[256,4096]{1,0:T(8,128)(2,1)} %bitcast.59, bf16[256,4096]{1,0:T(8,128)(2,1)} %bitcast.60, ...), custom_call_target="tpu_custom_call" | custom-call | flops 6442450944 | bytes 12582912 | tf_op jit(solution)/shard_map/pallas_call | solution.py:151
  124.3 1.1 convert_element_type.35
  125.6 3.4 %scatter_fusion = bf16[8,2,2,64,512]{4,3,2,1,0:T(8,128)(2,1)S(1)} fusion(bf16[8,2,2,64,512]{4,3,2,1,0:T(8,128)(2,1)S(1)} %broadcast_in_dim.117, s32[12]{0:T(128)S(1)} %fusion.36, bf16[12,2,64,512]{3,2,1,0:T(8,128)(2,1)} %bitcast.62), kind=kCustom, calls=%fused_computation.1 | custom fusion | bytes 4718688 | tf_op jit(solution)/shard_map/scatter | solution.py:284
  129.0 1.7 pad_maximum_fusion.1
  130.7 4.8 %all-to-all-start.2 = ((bf16[8,288,512]{2,1,0:T(8,128)(2,1)}), bf16[8,288,512]{2,1,0:T(8,128)(2,1)S(1)}, u32[]{:S(2)}, u32[]{:S(2)}) async-start(bf16[8,288,512]{2,1,0:T(8,128)(2,1)} %pad_maximum_fusion.1), calls=%async_computation.2 | async-start | bytes 4718592 | tf_op jit(solution)/shard_map/all_to_all | solution.py:288
  136.0 1.3 collective-permute-start.3
  137.3 4.0 %collective-permute-start.4 = (bf16[1,2,64,512]{3,2,1,0:T(8,128)(2,1)S(1)}, bf16[1,2,64,512]{3,2,1,0:T(8,128)(2,1)S(1)}, u32[]{:S(2)}, u32[]{:S(2)}) collective-permute-start(bf16[1,2,64,512]{3,2,1,0:T(8,128)(2,1)S(1)} %get-tuple-element.51), channel_id=1, source_target_pairs={{0,1},{1,2},{2,3},{3,4},{4,5},{5,6},{6,7},{8,9},{9,10},{10,11},{11... | collective-permute-start | bytes 393224 | tf_op jit(solution)/shard_map/ppermute | solution.py:282
  141.3 2.6 %collective-permute-start.2 = (bf16[256,4096]{1,0:T(8,128)(2,1)}, bf16[256,4096]{1,0:T(8,128)(2,1)}, u32[]{:S(2)}, u32[]{:S(2)}) collective-permute-start(bf16[256,4096]{1,0:T(8,128)(2,1)} %get-tuple-element.32), channel_id=1, source_target_pairs={{8,0},{16,8},{24,16},{0,24},{9,1},{17,9},{25,17},{1,25},{10,2},{18... | collective-permute-start | bytes 6291464 | tf_op jit(solution)/shard_map/ppermute | solution.py:37
  143.9 43.6 %all-to-all-done.2 = bf16[8,288,512]{2,1,0:T(8,128)(2,1)S(1)} async-done(((bf16[8,288,512]{2,1,0:T(8,128)(2,1)}), bf16[8,288,512]{2,1,0:T(8,128)(2,1)S(1)}, u32[]{:S(2)}, u32[]{:S(2)}) %all-to-all-start.2) | async-done | bytes 2359328 | tf_op jit(solution)/shard_map/all_to_all | solution.py:288
  187.5 0.9 broadcast_in_dim.118
  188.3 5.7 %all-to-all-start.3 = ((f32[8,32,512]{2,1,0:T(8,128)}), f32[8,32,512]{2,1,0:T(8,128)S(1)}, u32[]{:S(2)}, u32[]{:S(2)}) async-start(f32[8,32,512]{2,1,0:T(8,128)} %broadcast_in_dim.118), calls=%async_computation.3 | async-start | bytes 1048576 | tf_op jit(solution)/shard_map/all_to_all | solution.py:297
  194.8 1.3 fusion
  196.6 10.7 %all-to-all-done.3 = f32[8,32,512]{2,1,0:T(8,128)S(1)} async-done(((f32[8,32,512]{2,1,0:T(8,128)}), f32[8,32,512]{2,1,0:T(8,128)S(1)}, u32[]{:S(2)}, u32[]{:S(2)}) %all-to-all-start.3) | async-done | bytes 524320 | tf_op jit(solution)/shard_map/all_to_all | solution.py:297
  207.3 1.6 fusion.5
  209.4 2.2 collective-permute-start.5
  211.7 8.0 %collective-permute-done.5 = bf16[256,1024]{1,0:T(8,128)(2,1)S(1)} collective-permute-done((bf16[256,1024]{1,0:T(8,128)(2,1)S(1)}, bf16[256,1024]{1,0:T(8,128)(2,1)S(1)}, u32[]{:S(2)}, u32[]{:S(2)}) %collective-permute-start.5) | collective-permute-done | bytes 524320 | tf_op jit(solution)/shard_map/ppermute | solution.py:37
  219.7 0.8 slice_bitcast_fusion
  220.5 3.1 %copy.97 = bf16[1,256,4096]{2,1,0:T(8,128)(2,1)} copy(bf16[1,256,4096]{2,1,0:T(8,128)(2,1)} %bitcast.14) | data formatting | bytes 4194304
  (80 shorter events, 6.7 us)
Async XLA Ops:
  9.0 7.1 %copy-start.5 = (s32[16]{0:T(128)}, s32[16]{0:T(128)S(1)}, u32[]{:S(2)}) copy-start(s32[16]{0:T(128)S(1)} %reshape.674) | copy-start | bytes 196
  19.4 11.8 %copy-start.4 = (s32[1,32,3]{1,0,2:T(1,128)S(1)}, s32[1,32,3]{1,0,2:T(1,128)}, u32[]{:S(2)}) copy-start(s32[1,32,3]{1,0,2:T(1,128)} %param.15) | copy-start | bytes 1156
  19.4 12.0 %copy-start.7 = (s32[1,2]{1,0:T(1,128)S(1)}, s32[1,2]{1,0:T(1,128)}, u32[]{:S(2)}) copy-start(s32[1,2]{1,0:T(1,128)} %param.16) | copy-start | bytes 28
  19.4 12.8 %copy-start.9 = (s32[1,8]{1,0:T(1,128)S(1)}, s32[1,8]{1,0:T(1,128)}, u32[]{:S(2)}) copy-start(s32[1,8]{1,0:T(1,128)} %param.17) | copy-start | bytes 100
  19.4 59.6 %all-to-all-start = ((bf16[8,288,512]{2,1,0:T(8,128)(2,1)}), bf16[8,288,512]{2,1,0:T(8,128)(2,1)}, u32[]{:S(2)}, u32[]{:S(2)}) async-start(bf16[8,288,512]{2,1,0:T(8,128)(2,1)} %pad_maximum_fusion), calls=%async_computation | async-start | bytes 4718592 | tf_op jit(solution)/shard_map/all_to_all | solution.py:245
  25.9 61.4 %collective-permute-start = (bf16[1,2,64,512]{3,2,1,0:T(8,128)(2,1)}, bf16[1,2,64,512]{3,2,1,0:T(8,128)(2,1)}, u32[]{:S(2)}, u32[]{:S(2)}) collective-permute-start(bf16[1,2,64,512]{3,2,1,0:T(8,128)(2,1)} %get-tuple-element.48), channel_id=1, source_target_pairs={{0,1},{1,2},{2,3},{3,4},{4,5},{5,6},{6,7},{8,9},{9,10},{10,11},{11... | collective-permute-start | bytes 393224 | tf_op jit(solution)/shard_map/ppermute | solution.py:226
  29.9 58.3 %collective-permute-start.1 = (bf16[1,2,64,512]{3,2,1,0:T(8,128)(2,1)}, bf16[1,2,64,512]{3,2,1,0:T(8,128)(2,1)S(1)}, u32[]{:S(2)}, u32[]{:S(2)}) collective-permute-start(bf16[1,2,64,512]{3,2,1,0:T(8,128)(2,1)} %get-tuple-element.49), channel_id=1, source_target_pairs={{1,0},{2,1},{3,2},{4,3},{5,4},{6,5},{7,6},{9,8},{10,9},{11,10},{12... | collective-permute-start | bytes 393224 | tf_op jit(solution)/shard_map/ppermute | solution.py:227
  44.9 40.5 %copy-start.3 = (s32[4,8]{1,0:T(4,128)S(1)}, s32[4,8]{1,0:T(4,128)}, u32[]{:S(2)}) copy-start(s32[4,8]{1,0:T(4,128)} %concatenate.46) | copy-start | bytes 388
  80.7 11.8 %all-to-all-start.1 = ((bf16[8,32,512]{2,1,0:T(8,128)(2,1)}), bf16[8,32,512]{2,1,0:T(8,128)(2,1)S(1)}, u32[]{:S(2)}, u32[]{:S(2)}) async-start(bf16[8,32,512]{2,1,0:T(8,128)(2,1)} %broadcast_in_dim.113), calls=%async_computation.1 | async-start | bytes 524288 | tf_op jit(solution)/shard_map/all_to_all | solution.py:250
  94.3 1.6 copy-start
  130.7 5.2 %copy-start.8 = (s32[1,2]{1,0:T(1,128)S(1)}, s32[1,2]{1,0:T(1,128)}, u32[]{:S(2)}) copy-start(s32[1,2]{1,0:T(1,128)} %param.16) | copy-start | bytes 28
  130.7 5.2 %copy-start.2 = (f32[2,2,64,512]{3,2,1,0:T(8,128)S(1)}, f32[2,2,64,512]{3,2,1,0:T(8,128)}, u32[]{:S(2)}) copy-start(f32[2,2,64,512]{3,2,1,0:T(8,128)} %get-tuple-element.36) | copy-start | bytes 1572868
  130.7 56.8 %all-to-all-start.2 = ((bf16[8,288,512]{2,1,0:T(8,128)(2,1)}), bf16[8,288,512]{2,1,0:T(8,128)(2,1)S(1)}, u32[]{:S(2)}, u32[]{:S(2)}) async-start(bf16[8,288,512]{2,1,0:T(8,128)(2,1)} %pad_maximum_fusion.1), calls=%async_computation.2 | async-start | bytes 4718592 | tf_op jit(solution)/shard_map/all_to_all | solution.py:288
  136.0 60.5 %collective-permute-start.3 = (bf16[1,2,64,512]{3,2,1,0:T(8,128)(2,1)S(1)}, bf16[1,2,64,512]{3,2,1,0:T(8,128)(2,1)S(1)}, u32[]{:S(2)}, u32[]{:S(2)}) collective-permute-start(bf16[1,2,64,512]{3,2,1,0:T(8,128)(2,1)S(1)} %get-tuple-element.52), channel_id=1, source_target_pairs={{1,0},{2,1},{3,2},{4,3},{5,4},{6,5},{7,6},{9,8},{10,9},{11,10},{12... | collective-permute-start | bytes 393224 | tf_op jit(solution)/shard_map/ppermute | solution.py:281
  137.3 59.3 %collective-permute-start.4 = (bf16[1,2,64,512]{3,2,1,0:T(8,128)(2,1)S(1)}, bf16[1,2,64,512]{3,2,1,0:T(8,128)(2,1)S(1)}, u32[]{:S(2)}, u32[]{:S(2)}) collective-permute-start(bf16[1,2,64,512]{3,2,1,0:T(8,128)(2,1)S(1)} %get-tuple-element.51), channel_id=1, source_target_pairs={{0,1},{1,2},{2,3},{3,4},{4,5},{5,6},{6,7},{8,9},{9,10},{10,11},{11... | collective-permute-start | bytes 393224 | tf_op jit(solution)/shard_map/ppermute | solution.py:282
  141.3 70.4 %collective-permute-start.2 = (bf16[256,4096]{1,0:T(8,128)(2,1)}, bf16[256,4096]{1,0:T(8,128)(2,1)}, u32[]{:S(2)}, u32[]{:S(2)}) collective-permute-start(bf16[256,4096]{1,0:T(8,128)(2,1)} %get-tuple-element.32), channel_id=1, source_target_pairs={{8,0},{16,8},{24,16},{0,24},{9,1},{17,9},{25,17},{1,25},{10,2},{18... | collective-permute-start | bytes 6291464 | tf_op jit(solution)/shard_map/ppermute | solution.py:37
  188.3 19.0 %all-to-all-start.3 = ((f32[8,32,512]{2,1,0:T(8,128)}), f32[8,32,512]{2,1,0:T(8,128)S(1)}, u32[]{:S(2)}, u32[]{:S(2)}) async-start(f32[8,32,512]{2,1,0:T(8,128)} %broadcast_in_dim.118), calls=%async_computation.3 | async-start | bytes 1048576 | tf_op jit(solution)/shard_map/all_to_all | solution.py:297
  194.1 0.7 copy-start.6
  194.3 1.7 copy-start.1
  209.4 10.2 %collective-permute-start.5 = (bf16[256,1024]{1,0:T(8,128)(2,1)S(1)}, bf16[256,1024]{1,0:T(8,128)(2,1)S(1)}, u32[]{:S(2)}, u32[]{:S(2)}) collective-permute-start(bf16[256,1024]{1,0:T(8,128)(2,1)S(1)} %pad_maximum_fusion.3), channel_id=1, source_target_pairs={{8,0},{16,8},{24,16},{0,24},{9,1},{17,9},{25,17},{1,25},{10,2},{18... | collective-permute-start | bytes 1572872 | tf_op jit(solution)/shard_map/ppermute | solution.py:37

commit v10 on v9

--- a/solution.py
+++ b/solution.py
@@ -55,8 +55,8 @@
         [query[:, g * HDIM : (g + 1) * HDIM] for g in range(group)], axis=0
     )
     grad_rows = jnp.concatenate([grad[:, g * HDIM : (g + 1) * HDIM] for g in range(group)], axis=0)
-    key_rows = jnp.concatenate([tile_refs[t][0] for t in range(ntiles)], axis=0)
-    value_rows = jnp.concatenate([tile_refs[t][1] for t in range(ntiles)], axis=0)
+    key_rows = jnp.concatenate([tile_refs[t][:block_len] for t in range(ntiles)], axis=0)
+    value_rows = jnp.concatenate([tile_refs[t][block_len:] for t in range(ntiles)], axis=0)
     live = live_ref[...] > 0.5
     contract_last = (((1,), (1,)), ((), ()))
     contract_first = (((0,), (0,)), ((), ()))
@@ -120,21 +120,31 @@
     rand_ref[...] = terms[near:].astype(rand_ref.dtype)
 
 
-def block_backward(query_rows, grad_rows, all_blocks, tile_ids, key_live):
+def block_backward(query_rows, grad_rows, window, global_tiles, received, random_ids, key_live):
     shard_tokens, qwidth = query_rows.shape
-    _, _, block_len, kwidth = all_blocks.shape
-    nblocks, ntiles = tile_ids.shape
+    kwidth = window.shape[-1]
+    nblocks = window.shape[0] - 2
+    block_len = window.shape[1] // 2
+    near = 3 + GLOB
+    nrand = random_ids.shape[0] // (2 * nblocks)
+    ntiles = near + nrand
     heads_kv = kwidth // HDIM
     group_width = qwidth // heads_kv
-    near = 3 + GLOB
-    nrand = ntiles - near
+    pair_rows = 2 * block_len
     live = key_live.reshape(nblocks, ntiles * block_len, 1).astype(jnp.float32)
     row_spec = pl.BlockSpec((block_len, group_width), lambda h, b, ids: (b, h))
     tile_specs = [
+        pl.BlockSpec((None, pair_rows, HDIM), lambda h, b, ids, t=t: (b + t, 0, h)) for t in range(3)
+    ]
+    tile_specs += [
+        pl.BlockSpec((None, pair_rows, HDIM), lambda h, b, ids, g=g: (g, 0, h)) for g in range(GLOB)
+    ]
+    tile_specs += [
         pl.BlockSpec(
-            (None, 2, block_len, HDIM), lambda h, b, ids, t=t: (ids[b * ntiles + t], 0, 0, h)
+            (None, pair_rows, HDIM),
+            lambda h, b, ids, r=r: (ids[(b * nrand + r) * 2], ids[(b * nrand + r) * 2 + 1], h),
         )
-        for t in range(ntiles)
+        for r in range(nrand)
     ]
     live_spec = pl.BlockSpec((None, ntiles * block_len, 1), lambda h, b, ids: (b, 0, 0))
     own_spec = pl.BlockSpec((nblocks, 2, block_len, HDIM), lambda h, b, ids: (0, 0, 0, h))
@@ -166,7 +176,15 @@
             transcendentals=nblocks * qwidth // HDIM * block_len * ntiles * block_len,
             bytes_accessed=shard_tokens * qwidth * 6 + nblocks * ntiles * block_len * kwidth * 6,
         ),
-    )(tile_ids.reshape(-1), query_rows, grad_rows, *([all_blocks] * ntiles), live)
+    )(
+        random_ids,
+        query_rows,
+        grad_rows,
+        *([window] * 3),
+        *([global_tiles] * GLOB),
+        *([received] * nrand),
+        live,
+    )
     return outs
 
 
@@ -225,46 +243,37 @@
     down = [(j, i) for i, j in up]
     edge_before = lax.ppermute(own_blocks[query_blocks - 1 :], "seq", up)
     edge_after = lax.ppermute(own_blocks[:1], "seq", down)
-    global_mine = [
-        jnp.where(
-            global_ids[g] // query_blocks == this_shard,
-            lax.dynamic_index_in_dim(own_blocks, global_ids[g] % query_blocks, 0, keepdims=True),
-            jnp.zeros((), own_blocks.dtype),
-        )
-        for g in range(GLOB)
-    ]
     requests = random_table.reshape(shards, query_blocks * RAND)
     plan = request_plan(requests, this_shard, query_blocks)
     serve_block, slot_used, owner_mine, rank_mine = plan
     capacity = serve_block.shape[1]
     block_rows = 2 * BLK
-    served = jnp.take(own_blocks, serve_block.reshape(-1), axis=0).reshape(
-        shards, capacity * block_rows, kwidth
-    )
-    global_chunks = jnp.concatenate(global_mine, axis=0).reshape(shards, -1, kwidth)
-    received = lax.all_to_all(
-        jnp.concatenate([served, global_chunks], axis=1), "seq", 0, 0, tiled=True
-    )
-    random_tiles = received[:, : capacity * block_rows].reshape(shards * capacity, 2, BLK, kwidth)
+    nb = query_blocks
+    own_rows = jnp.concatenate(
+        [own_blocks.reshape(nb * block_rows, kwidth), jnp.zeros((1, kwidth), own_blocks.dtype)]
+    )
+    row_range = jnp.arange(block_rows, dtype=jnp.int32)
+    served_idx = (serve_block[:, :, None] * block_rows + row_range).reshape(shards, -1)
+    global_owned = global_ids // query_blocks == this_shard
+    global_idx = jnp.where(
+        global_owned[:, None], (global_ids % query_blocks)[:, None] * block_rows + row_range, nb * block_rows
+    ).reshape(shards, -1)
+    payload_idx = jnp.concatenate([served_idx, global_idx], axis=1)
+    payload = jnp.take(own_rows, payload_idx.reshape(-1), axis=0, mode="clip").reshape(
+        shards, -1, kwidth
+    )
+    received = lax.all_to_all(payload, "seq", 0, 0, tiled=True)
     global_piece = jnp.sum(received[:, capacity * block_rows :], axis=0, dtype=own_blocks.dtype)
     global_tiles = lax.all_to_all(
         jnp.broadcast_to(global_piece[None], (shards,) + global_piece.shape), "seq", 0, 0, tiled=True
-    ).reshape(GLOB, 2, BLK, kwidth)
-    received = random_tiles
-    sources = jnp.concatenate([own_blocks, edge_before, edge_after, global_tiles, received], axis=0)
-    nb = query_blocks
+    ).reshape(GLOB, block_rows, kwidth)
+    window = jnp.concatenate([edge_before, own_blocks, edge_after], axis=0).reshape(
+        nb + 2, block_rows, kwidth
+    )
     block_range = jnp.arange(nb, dtype=jnp.int32)
-    source_ids = jnp.concatenate(
-        [
-            jnp.where(block_range == 0, nb, block_range - 1)[:, None],
-            block_range[:, None],
-            jnp.where(block_range == nb - 1, nb + 1, block_range + 1)[:, None],
-            jnp.broadcast_to(nb + 2 + jnp.arange(GLOB, dtype=jnp.int32)[None, :], (nb, GLOB)),
-            (nb + 2 + GLOB + owner_mine * capacity + rank_mine).reshape(nb, RAND),
-        ],
-        axis=1,
-    )
-    source_ids = jnp.clip(source_ids, 0, sources.shape[0] - 1)
+    random_ids = jnp.stack(
+        [owner_mine, jnp.clip(rank_mine, 0, capacity - 1)], axis=1
+    ).reshape(-1)
     random_three = random_table.reshape(shards, query_blocks, RAND)
     base_ids = this_shard * query_blocks + block_range
     window_ids = base_ids[:, None] + jnp.arange(-1, 2, dtype=jnp.int32)[None, :]
@@ -274,7 +283,7 @@
     )
     key_live = token_live(tile_ids, pad_sizes, query_blocks, shard_tokens, total_blocks)
     query_grad, local_sum, edge_terms, global_part, random_part = block_backward(
-        query_rows, grad_rows, sources, source_ids, key_live
+        query_rows, grad_rows, window, global_tiles, received, random_ids, key_live
     )
     handed_query = from_behind(query_grad, "section", -1)
     edge_low = edge_terms.astype(jnp.bfloat16)
@@ -294,9 +303,10 @@
     )
     random_back = returned[:, : capacity * block_rows].reshape(shards * capacity, 2, BLK, kwidth)
     global_sum = jnp.sum(returned[:, capacity * block_rows :].astype(jnp.float32), axis=0)
+    global_sum = global_sum.astype(jnp.bfloat16)
     global_total = lax.all_to_all(
         jnp.broadcast_to(global_sum[None], (shards,) + global_sum.shape), "seq", 0, 0, tiled=True
-    ).reshape(GLOB, 2, BLK, kwidth)
+    ).reshape(GLOB, 2, BLK, kwidth).astype(jnp.float32)
     onehot = (
         slot_used.reshape(-1)[None, :]
         & (serve_block.reshape(-1)[None, :] == block_range[:, None])

time: 225 us -> 209 us (0.929)
  local copies, waits for them, and re-layouts: 36.1 us -> 24.1 us
  waiting for transfers between devices: 94.7 us -> 105 us
  other arithmetic: 18.2 us -> 10.8 us
  between operations: 6.21 us -> 0.98 us
    all_to_all x1, waiting for transfers between devices: 31.3 us -> 42.7 us  [body(): received = lax.all_to_all(payload, 'seq', 0, 0, tiled=True)]
    all_to_all x1, waiting for transfers between devices: 10.7 us -> 4.98 us  [body(): lax.all_to_all(jnp.broadcast_to(global_sum[None], (shards,) + global_sum....]
    gather x1, local copies, waits for them, and re-layouts: 3.04 us -> 7.52 us  [body(): jnp.take(own_rows, payload_idx.reshape(-1), axis=0, mode='clip')]
    slice x2 -> x0, local copies, waits for them, and re-layouts: 4.36 us -> none  [the longest x1 3.05 us: body(): received[:, :capacity * block_rows]]
    all_to_all x1, waiting for transfers between devices: 1.22 us -> 5.36 us  [body(): lax.all_to_all(jnp.broadcast_to(global_piece[None], (shards,) + global_pi...]
    select_n x5 -> x1, other arithmetic: 4.2 us -> 0.07 us  [body(): jnp.where(global_owned[:, None], (global_ids % query_blocks)[:, None] * b...]
    add x4, local copies, waits for them, and re-layouts: 4.73 us -> 1.16 us  [token_live(): (safe_ids % query_blocks)[..., None] * BLK]
    concatenate x2 -> x1, local copies, waits for them, and re-layouts: 3.12 us -> 0.04 us  [body(): jnp.concatenate([own_blocks.reshape(nb * block_rows, kwidth), jnp.zeros((...]
  transfers between devices with their start and end apart: 10 -> 10, of which waited for: 5 -> 5; matrix products, arithmetic and copies ran while one was open for 13% -> 7% of each run, Pallas kernels for 0% -> 0%
where the time goes in v10:
time: 209 us; the launch traced here: 208 us
  waiting for transfers between devices  105 us (50%)
  starting transfers between devices  36.4 us (17%)
  Pallas kernels  28.3 us (14%)
  local copies, waits for them, and re-layouts  24.1 us (12%)
  other arithmetic  10.8 us (5%)
    all_to_all x1, waiting for transfers between devices, body(): lax.all_to_all(jnp.concatenate([holder.reshape(shards, capacity * block_r...  44.4 us
    all_to_all x1, waiting for transfers between devices, body(): received = lax.all_to_all(payload, 'seq', 0, 0, tiled=True)  42.7 us
    pallas_call x1, Pallas kernels, block_backward(): pl.pallas_call(attention_kernel, grid_spec=grid_spec, out_shape=[jax.Shap...  28.3 us
    ppermute x2, waiting for transfers between devices, from_behind(): return lax.ppermute(block, axis, route)  7.99 us
    gather x1, local copies, waits for them, and re-layouts, body(): jnp.take(own_rows, payload_idx.reshape(-1), axis=0, mode='clip')  7.52 us
    all_to_all x1, starting transfers between devices, body(): received = lax.all_to_all(payload, 'seq', 0, 0, tiled=True)  6.5 us
    all_to_all x1, starting transfers between devices, body(): lax.all_to_all(jnp.broadcast_to(global_sum[None], (shards,) + global_sum....  5.6 us
    ppermute x2, starting transfers between devices, from_behind(): return lax.ppermute(block, axis, route)  5.5 us
  transfers between devices with their start and end apart: 10, of which 5 were waited for; matrix products, arithmetic and copies ran while one was open for 7% of the time, Pallas kernels for 0%

profile of v10, /device:TPU:1, one launch (start us, length us, event | category | flops | bytes accessed | tf_op | source)
XLA Modules:
  0.0 207.9 jit_solution(13967157248115963305)
XLA Ops:
  0.7 0.7 broadcast_multiply_fusion.1
  1.3 0.7 fusion.31
  2.0 0.8 copy.63
  3.3 0.3 convert_reduce_fusion
  3.7 0.2 select_reduce_fusion.1
  4.2 1.1 pad_maximum_fusion.2
  5.3 7.5 %gather_fusion = bf16[2304,512]{1,0:T(8,128)(2,1)} fusion(bf16[513,512]{1,0:T(8,128)(2,1)S(1)} %concatenate.44, s32[3072]{0:T(1024)S(1)} %pad_clamp_fusion), kind=kCustom, calls=%fused_computation | custom fusion | bytes 4727808 | tf_op jit(solution)/shard_map/jit(_take)/gather | solution.py:262
  12.9 6.5 %all-to-all-start = ((bf16[8,288,512]{2,1,0:T(8,128)(2,1)}), bf16[8,288,512]{2,1,0:T(8,128)(2,1)}, u32[]{:S(2)}, u32[]{:S(2)}) async-start(bf16[8,288,512]{2,1,0:T(8,128)(2,1)} %bitcast.12), calls=%async_computation | async-start | bytes 4718592 | tf_op jit(solution)/shard_map/all_to_all | solution.py:265
  19.4 3.4 %collective-permute-start = (bf16[1,2,64,512]{3,2,1,0:T(8,128)(2,1)S(1)}, bf16[1,2,64,512]{3,2,1,0:T(8,128)(2,1)S(1)}, u32[]{:S(2)}, u32[]{:S(2)}) collective-permute-start(bf16[1,2,64,512]{3,2,1,0:T(8,128)(2,1)S(1)} %get-tuple-element.49), channel_id=1, source_target_pairs={{0,1},{1,2},{2,3},{3,4},{4,5},{5,6},{6,7},{8,9},{9,10},{10,11},{11... | collective-permute-start | bytes 393224 | tf_op jit(solution)/shard_map/ppermute | solution.py:244
  22.8 1.3 collective-permute-start.1
  24.7 1.1 and.190
  26.0 1.0 add.257
  27.0 0.2 select_reduce_fusion
  27.3 1.0 lt.108
  28.3 0.2 dynamic-slice_reduce_fusion
  28.5 1.3 fusion.4.refs_8_
  29.8 42.7 %all-to-all-done.refs_5_.refs_6_.refs_7_ = bf16[8,288,512]{2,1,0:T(8,128)(2,1)} async-done(((bf16[8,288,512]{2,1,0:T(8,128)(2,1)}), bf16[8,288,512]{2,1,0:T(8,128)(2,1)}, u32[]{:S(2)}, u32[]{:S(2)}) %all-to-all-start) | async-done | bytes 2359328 | tf_op jit(solution)/shard_map/all_to_all | solution.py:265
  72.5 1.0 slice_reduce_fusion.1
  73.5 0.7 broadcast_in_dim.59
  74.2 4.7 %all-to-all-start.1 = ((bf16[8,32,512]{2,1,0:T(8,128)(2,1)}), bf16[8,32,512]{2,1,0:T(8,128)(2,1)S(1)}, u32[]{:S(2)}, u32[]{:S(2)}) async-start(bf16[8,32,512]{2,1,0:T(8,128)(2,1)} %broadcast_in_dim.59), calls=%async_computation.1 | async-start | bytes 524288 | tf_op jit(solution)/shard_map/all_to_all | solution.py:267
  79.0 0.6 reshape.619.ids_ref
  79.6 1.0 pad_maximum_fusion.1
  80.6 5.4 %all-to-all-done.1 = bf16[8,32,512]{2,1,0:T(8,128)(2,1)S(1)} async-done(((bf16[8,32,512]{2,1,0:T(8,128)(2,1)}), bf16[8,32,512]{2,1,0:T(8,128)(2,1)S(1)}, u32[]{:S(2)}, u32[]{:S(2)}) %all-to-all-start.1) | async-done | bytes 262176 | tf_op jit(solution)/shard_map/all_to_all | solution.py:267
  86.0 0.7 copy-done.4
  86.7 28.3 %shard_map.94 = (bf16[256,4096]{1,0:T(8,128)(2,1)}, f32[4,2,64,512]{3,2,1,0:T(8,128)}, f32[2,2,64,512]{3,2,1,0:T(8,128)}, f32[2,2,64,512]{3,2,1,0:T(8,128)}, bf16[4,3,2,64,512]{4,3,2,1,0:T(8,128)(2,1)}) custom-call(s32[24]{0:T(128)} %reshape.619.ids_ref, bf16[256,4096]{1,0:T(8,128)(2,1)} %bitcast.86, bf16[256,4096]{1,0:T(8,128)(2,1)} %bitcast.87, ...), custom_call_target="tpu_custom_call" | custom-call | flops 6442450944 | bytes 12582912 | tf_op jit(solution)/shard_map/pallas_call | solution.py:161
  115.0 1.1 convert_element_type.35
  116.1 0.2 broadcast_in_dim.63
  116.3 3.4 %scatter_fusion = bf16[8,2,2,64,512]{4,3,2,1,0:T(8,128)(2,1)S(1)} fusion(bf16[8,2,2,64,512]{4,3,2,1,0:T(8,128)(2,1)S(1)} %broadcast_in_dim.63, s32[12]{0:T(128)S(1)} %get-tuple-element.37, bf16[12,2,64,512]{3,2,1,0:T(8,128)(2,1)} %bitcast.73), kind=kCustom, calls=%fused_computation.1 | custom fusion | bytes 4718688 | tf_op jit(solution)/shard_map/scatter | solution.py:293
  119.7 1.7 pad_maximum_fusion
  121.4 4.8 %all-to-all-start.2 = ((bf16[8,288,512]{2,1,0:T(8,128)(2,1)}), bf16[8,288,512]{2,1,0:T(8,128)(2,1)S(1)}, u32[]{:S(2)}, u32[]{:S(2)}) async-start(bf16[8,288,512]{2,1,0:T(8,128)(2,1)} %pad_maximum_fusion), calls=%async_computation.2 | async-start | bytes 4718592 | tf_op jit(solution)/shard_map/all_to_all | solution.py:297
  126.3 0.1 fusion.12
  126.4 0.1 copy.75
  126.8 3.4 %collective-permute-start.4 = (bf16[1,2,64,512]{3,2,1,0:T(8,128)(2,1)S(1)}, bf16[1,2,64,512]{3,2,1,0:T(8,128)(2,1)S(1)}, u32[]{:S(2)}, u32[]{:S(2)}) collective-permute-start(bf16[1,2,64,512]{3,2,1,0:T(8,128)(2,1)S(1)} %get-tuple-element.51), channel_id=1, source_target_pairs={{0,1},{1,2},{2,3},{3,4},{4,5},{5,6},{6,7},{8,9},{9,10},{10,11},{11... | collective-permute-start | bytes 393224 | tf_op jit(solution)/shard_map/ppermute | solution.py:291
  130.2 1.3 collective-permute-start.3
  131.5 2.4 %collective-permute-start.2 = (bf16[256,4096]{1,0:T(8,128)(2,1)}, bf16[256,4096]{1,0:T(8,128)(2,1)}, u32[]{:S(2)}, u32[]{:S(2)}) collective-permute-start(bf16[256,4096]{1,0:T(8,128)(2,1)} %get-tuple-element.32), channel_id=1, source_target_pairs={{8,0},{16,8},{24,16},{0,24},{9,1},{17,9},{25,17},{1,25},{10,2},{18... | collective-permute-start | bytes 6291464 | tf_op jit(solution)/shard_map/ppermute | solution.py:37
  133.9 44.4 %all-to-all-done.2 = bf16[8,288,512]{2,1,0:T(8,128)(2,1)S(1)} async-done(((bf16[8,288,512]{2,1,0:T(8,128)(2,1)}), bf16[8,288,512]{2,1,0:T(8,128)(2,1)S(1)}, u32[]{:S(2)}, u32[]{:S(2)}) %all-to-all-start.2) | async-done | bytes 2359328 | tf_op jit(solution)/shard_map/all_to_all | solution.py:297
  178.3 0.7 broadcast_in_dim.106
  179.1 5.6 %all-to-all-start.3 = ((bf16[8,32,512]{2,1,0:T(8,128)(2,1)}), bf16[8,32,512]{2,1,0:T(8,128)(2,1)S(1)}, u32[]{:S(2)}, u32[]{:S(2)}) async-start(bf16[8,32,512]{2,1,0:T(8,128)(2,1)} %broadcast_in_dim.106), calls=%async_computation.3 | async-start | bytes 524288 | tf_op jit(solution)/shard_map/all_to_all | solution.py:307
  184.7 0.2 slice.111
  184.9 1.3 fusion
  186.2 0.4 copy_add_fusion.1
  186.8 5.0 %all-to-all-done.3 = bf16[8,32,512]{2,1,0:T(8,128)(2,1)S(1)} async-done(((bf16[8,32,512]{2,1,0:T(8,128)(2,1)}), bf16[8,32,512]{2,1,0:T(8,128)(2,1)S(1)}, u32[]{:S(2)}, u32[]{:S(2)}) %all-to-all-start.3) | async-done | bytes 262176 | tf_op jit(solution)/shard_map/all_to_all | solution.py:307
  191.8 0.6 fusion.7
  192.4 0.4 fusion.2
  192.9 3.1 %collective-permute-start.5 = (bf16[256,1024]{1,0:T(8,128)(2,1)S(1)}, bf16[256,1024]{1,0:T(8,128)(2,1)S(1)}, u32[]{:S(2)}, u32[]{:S(2)}) collective-permute-start(bf16[256,1024]{1,0:T(8,128)(2,1)S(1)} %pad_maximum_fusion.3), channel_id=1, source_target_pairs={{8,0},{16,8},{24,16},{0,24},{9,1},{17,9},{25,17},{1,25},{10,2},{18... | collective-permute-start | bytes 1572872 | tf_op jit(solution)/shard_map/ppermute | solution.py:37
  195.9 8.0 %collective-permute-done.5 = bf16[256,1024]{1,0:T(8,128)(2,1)S(1)} collective-permute-done((bf16[256,1024]{1,0:T(8,128)(2,1)S(1)}, bf16[256,1024]{1,0:T(8,128)(2,1)S(1)}, u32[]{:S(2)}, u32[]{:S(2)}) %collective-permute-start.5) | collective-permute-done | bytes 524320 | tf_op jit(solution)/shard_map/ppermute | solution.py:37
  203.9 0.8 slice_bitcast_fusion
  204.7 3.1 %copy.97 = bf16[1,256,4096]{2,1,0:T(8,128)(2,1)} copy(bf16[1,256,4096]{2,1,0:T(8,128)(2,1)} %bitcast.16) | data formatting | bytes 4194304
  (73 shorter events, 2.5 us)
Async XLA Ops:
  12.9 6.5 %copy-start = (bf16[1,256,512]{2,1,0:T(8,128)(2,1)S(1)}, bf16[1,256,512]{2,1,0:T(8,128)(2,1)}, u32[]{:S(2)}) copy-start(bf16[1,256,512]{2,1,0:T(8,128)(2,1)} %param.12) | copy-start | bytes 786436
  12.9 6.5 %copy-start.1 = (bf16[1,256,512]{2,1,0:T(8,128)(2,1)S(1)}, bf16[1,256,512]{2,1,0:T(8,128)(2,1)}, u32[]{:S(2)}) copy-start(bf16[1,256,512]{2,1,0:T(8,128)(2,1)} %param.13) | copy-start | bytes 786436
  12.9 11.2 %copy-start.5 = (s32[1,32,3]{1,0,2:T(1,128)S(1)}, s32[1,32,3]{1,0,2:T(1,128)}, u32[]{:S(2)}) copy-start(s32[1,32,3]{1,0,2:T(1,128)} %param.15) | copy-start | bytes 1156
  12.9 11.3 %copy-start.7 = (s32[1,2]{1,0:T(1,128)S(1)}, s32[1,2]{1,0:T(1,128)}, u32[]{:S(2)}) copy-start(s32[1,2]{1,0:T(1,128)} %param.16) | copy-start | bytes 28
  12.9 59.6 %all-to-all-start = ((bf16[8,288,512]{2,1,0:T(8,128)(2,1)}), bf16[8,288,512]{2,1,0:T(8,128)(2,1)}, u32[]{:S(2)}, u32[]{:S(2)}) async-start(bf16[8,288,512]{2,1,0:T(8,128)(2,1)} %bitcast.12), calls=%async_computation | async-start | bytes 4718592 | tf_op jit(solution)/shard_map/all_to_all | solution.py:265
  19.4 7.6 %copy-start.6 = (s32[1,8]{1,0:T(1,128)S(1)}, s32[1,8]{1,0:T(1,128)}, u32[]{:S(2)}) copy-start(s32[1,8]{1,0:T(1,128)} %param.17) | copy-start | bytes 100
  19.4 60.2 %collective-permute-start = (bf16[1,2,64,512]{3,2,1,0:T(8,128)(2,1)S(1)}, bf16[1,2,64,512]{3,2,1,0:T(8,128)(2,1)S(1)}, u32[]{:S(2)}, u32[]{:S(2)}) collective-permute-start(bf16[1,2,64,512]{3,2,1,0:T(8,128)(2,1)S(1)} %get-tuple-element.49), channel_id=1, source_target_pairs={{0,1},{1,2},{2,3},{3,4},{4,5},{5,6},{6,7},{8,9},{9,10},{10,11},{11... | collective-permute-start | bytes 393224 | tf_op jit(solution)/shard_map/ppermute | solution.py:244
  22.8 56.8 %collective-permute-start.1 = (bf16[1,2,64,512]{3,2,1,0:T(8,128)(2,1)S(1)}, bf16[1,2,64,512]{3,2,1,0:T(8,128)(2,1)S(1)}, u32[]{:S(2)}, u32[]{:S(2)}) collective-permute-start(bf16[1,2,64,512]{3,2,1,0:T(8,128)(2,1)S(1)} %get-tuple-element.50), channel_id=1, source_target_pairs={{1,0},{2,1},{3,2},{4,3},{5,4},{6,5},{7,6},{9,8},{10,9},{11,10},{12... | collective-permute-start | bytes 393224 | tf_op jit(solution)/shard_map/ppermute | solution.py:245
  74.2 11.8 %all-to-all-start.1 = ((bf16[8,32,512]{2,1,0:T(8,128)(2,1)}), bf16[8,32,512]{2,1,0:T(8,128)(2,1)S(1)}, u32[]{:S(2)}, u32[]{:S(2)}) async-start(bf16[8,32,512]{2,1,0:T(8,128)(2,1)} %broadcast_in_dim.59), calls=%async_computation.1 | async-start | bytes 524288 | tf_op jit(solution)/shard_map/all_to_all | solution.py:267
  86.0 0.7 copy-start.4
  121.4 5.3 %copy-start.3 = (f32[2,2,64,512]{3,2,1,0:T(8,128)S(1)}, f32[2,2,64,512]{3,2,1,0:T(8,128)}, u32[]{:S(2)}) copy-start(f32[2,2,64,512]{3,2,1,0:T(8,128)} %get-tuple-element.36) | copy-start | bytes 1572868
  121.4 56.9 %all-to-all-start.2 = ((bf16[8,288,512]{2,1,0:T(8,128)(2,1)}), bf16[8,288,512]{2,1,0:T(8,128)(2,1)S(1)}, u32[]{:S(2)}, u32[]{:S(2)}) async-start(bf16[8,288,512]{2,1,0:T(8,128)(2,1)} %pad_maximum_fusion), calls=%async_computation.2 | async-start | bytes 4718592 | tf_op jit(solution)/shard_map/all_to_all | solution.py:297
  126.8 59.9 %collective-permute-start.4 = (bf16[1,2,64,512]{3,2,1,0:T(8,128)(2,1)S(1)}, bf16[1,2,64,512]{3,2,1,0:T(8,128)(2,1)S(1)}, u32[]{:S(2)}, u32[]{:S(2)}) collective-permute-start(bf16[1,2,64,512]{3,2,1,0:T(8,128)(2,1)S(1)} %get-tuple-element.51), channel_id=1, source_target_pairs={{0,1},{1,2},{2,3},{3,4},{4,5},{5,6},{6,7},{8,9},{9,10},{10,11},{11... | collective-permute-start | bytes 393224 | tf_op jit(solution)/shard_map/ppermute | solution.py:291
  130.2 56.5 %collective-permute-start.3 = (bf16[1,2,64,512]{3,2,1,0:T(8,128)(2,1)S(1)}, bf16[1,2,64,512]{3,2,1,0:T(8,128)(2,1)S(1)}, u32[]{:S(2)}, u32[]{:S(2)}) collective-permute-start(bf16[1,2,64,512]{3,2,1,0:T(8,128)(2,1)S(1)} %get-tuple-element.52), channel_id=1, source_target_pairs={{1,0},{2,1},{3,2},{4,3},{5,4},{6,5},{7,6},{9,8},{10,9},{11,10},{12... | collective-permute-start | bytes 393224 | tf_op jit(solution)/shard_map/ppermute | solution.py:290
  131.5 64.5 %collective-permute-start.2 = (bf16[256,4096]{1,0:T(8,128)(2,1)}, bf16[256,4096]{1,0:T(8,128)(2,1)}, u32[]{:S(2)}, u32[]{:S(2)}) collective-permute-start(bf16[256,4096]{1,0:T(8,128)(2,1)} %get-tuple-element.32), channel_id=1, source_target_pairs={{8,0},{16,8},{24,16},{0,24},{9,1},{17,9},{25,17},{1,25},{10,2},{18... | collective-permute-start | bytes 6291464 | tf_op jit(solution)/shard_map/ppermute | solution.py:37
  179.1 12.7 %all-to-all-start.3 = ((bf16[8,32,512]{2,1,0:T(8,128)(2,1)}), bf16[8,32,512]{2,1,0:T(8,128)(2,1)S(1)}, u32[]{:S(2)}, u32[]{:S(2)}) async-start(bf16[8,32,512]{2,1,0:T(8,128)(2,1)} %broadcast_in_dim.106), calls=%async_computation.3 | async-start | bytes 524288 | tf_op jit(solution)/shard_map/all_to_all | solution.py:307
  184.9 1.3 copy-start.2
  192.9 11.0 %collective-permute-start.5 = (bf16[256,1024]{1,0:T(8,128)(2,1)S(1)}, bf16[256,1024]{1,0:T(8,128)(2,1)S(1)}, u32[]{:S(2)}, u32[]{:S(2)}) collective-permute-start(bf16[256,1024]{1,0:T(8,128)(2,1)S(1)} %pad_maximum_fusion.3), channel_id=1, source_target_pairs={{8,0},{16,8},{24,16},{0,24},{9,1},{17,9},{25,17},{1,25},{10,2},{18... | collective-permute-start | bytes 1572872 | tf_op jit(solution)/shard_map/ppermute | solution.py:37

commit v11 on v10

--- a/solution.py
+++ b/solution.py
@@ -249,17 +249,24 @@
     capacity = serve_block.shape[1]
     block_rows = 2 * BLK
     nb = query_blocks
-    own_rows = jnp.concatenate(
-        [own_blocks.reshape(nb * block_rows, kwidth), jnp.zeros((1, kwidth), own_blocks.dtype)]
-    )
-    row_range = jnp.arange(block_rows, dtype=jnp.int32)
-    served_idx = (serve_block[:, :, None] * block_rows + row_range).reshape(shards, -1)
+    unit_rows = GLOB * block_rows // shards
+    unit_span = block_rows // unit_rows
+    own_units = jnp.concatenate(
+        [
+            own_blocks.reshape(nb * unit_span, unit_rows, kwidth),
+            jnp.zeros((1, unit_rows, kwidth), own_blocks.dtype),
+        ]
+    )
+    unit_range = jnp.arange(unit_span, dtype=jnp.int32)
+    served_idx = (serve_block[:, :, None] * unit_span + unit_range).reshape(shards, -1)
     global_owned = global_ids // query_blocks == this_shard
     global_idx = jnp.where(
-        global_owned[:, None], (global_ids % query_blocks)[:, None] * block_rows + row_range, nb * block_rows
+        global_owned[:, None],
+        (global_ids % query_blocks)[:, None] * unit_span + unit_range,
+        nb * unit_span,
     ).reshape(shards, -1)
     payload_idx = jnp.concatenate([served_idx, global_idx], axis=1)
-    payload = jnp.take(own_rows, payload_idx.reshape(-1), axis=0, mode="clip").reshape(
+    payload = jnp.take(own_units, payload_idx.reshape(-1), axis=0, mode="clip").reshape(
         shards, -1, kwidth
     )
     received = lax.all_to_all(payload, "seq", 0, 0, tiled=True)

time: 209 us -> 203 us (0.971)
  local copies, waits for them, and re-layouts: 24.1 us -> 18.7 us
    gather x1, local copies, waits for them, and re-layouts: 7.52 us -> 2.31 us  [body(): jnp.take(own_units, payload_idx.reshape(-1), axis=0, mode='clip')]
    unnamed x19 -> x18, local copies, waits for them, and re-layouts: 4.69 us -> 4.62 us
where the time goes in v11:
time: 203 us
  waiting for transfers between devices  105 us (52%)
  starting transfers between devices  36.4 us (18%)
  Pallas kernels  28.3 us (14%)
  local copies, waits for them, and re-layouts  18.7 us (9%)
  other arithmetic  10.8 us (5%)
    all_to_all x1, waiting for transfers between devices, body(): lax.all_to_all(jnp.concatenate([holder.reshape(shards, capacity * block_r...  44.4 us
    all_to_all x1, waiting for transfers between devices, body(): received = lax.all_to_all(payload, 'seq', 0, 0, tiled=True)  42.7 us
    pallas_call x1, Pallas kernels, block_backward(): pl.pallas_call(attention_kernel, grid_spec=grid_spec, out_shape=[jax.Shap...  28.3 us
    ppermute x2, waiting for transfers between devices, from_behind(): return lax.ppermute(block, axis, route)  7.99 us
    all_to_all x1, starting transfers between devices, body(): received = lax.all_to_all(payload, 'seq', 0, 0, tiled=True)  6.5 us
    all_to_all x1, starting transfers between devices, body(): lax.all_to_all(jnp.broadcast_to(global_sum[None], (shards,) + global_sum....  5.6 us
    ppermute x2, starting transfers between devices, from_behind(): return lax.ppermute(block, axis, route)  5.51 us
    all_to_all x1, waiting for transfers between devices, body(): lax.all_to_all(jnp.broadcast_to(global_piece[None], (shards,) + global_pi...  5.36 us
  transfers between devices with their start and end apart: 10, of which 5 were waited for; matrix products, arithmetic and copies ran while one was open for 7% of the time, Pallas kernels for 0%

profile of v11, /device:TPU:1, one launch (start us, length us, event | category | flops | bytes accessed | tf_op | source)
XLA Modules:
  0.0 202.5 jit_solution(15278560056348313501)
XLA Ops:
  0.7 0.7 broadcast_multiply_fusion.1
  1.3 0.7 fusion.31
  2.0 0.8 copy.67
  3.2 0.3 convert_reduce_fusion
  3.6 0.2 select_reduce_fusion.1
  4.0 1.1 pad_maximum_fusion.2
  5.2 2.3 %gather_fusion = bf16[72,32,512]{2,1,0:T(8,128)(2,1)} fusion(bf16[17,32,512]{2,1,0:T(8,128)(2,1)S(1)} %concatenate.44, s32[1024]{0:T(1024)S(1)} %pad_clamp_fusion), kind=kCustom, calls=%fused_computation | custom fusion | bytes 4718880 | tf_op jit(solution)/shard_map/jit(_take)/gather | solution.py:269
  7.5 6.5 %all-to-all-start = ((bf16[8,288,512]{2,1,0:T(8,128)(2,1)}), bf16[8,288,512]{2,1,0:T(8,128)(2,1)}, u32[]{:S(2)}, u32[]{:S(2)}) async-start(bf16[8,288,512]{2,1,0:T(8,128)(2,1)} %bitcast.11), calls=%async_computation | async-start | bytes 4718592 | tf_op jit(solution)/shard_map/all_to_all | solution.py:272
  14.1 3.4 %collective-permute-start = (bf16[1,2,64,512]{3,2,1,0:T(8,128)(2,1)S(1)}, bf16[1,2,64,512]{3,2,1,0:T(8,128)(2,1)S(1)}, u32[]{:S(2)}, u32[]{:S(2)}) collective-permute-start(bf16[1,2,64,512]{3,2,1,0:T(8,128)(2,1)S(1)} %get-tuple-element.49), channel_id=1, source_target_pairs={{0,1},{1,2},{2,3},{3,4},{4,5},{5,6},{6,7},{8,9},{9,10},{10,11},{11... | collective-permute-start | bytes 393224 | tf_op jit(solution)/shard_map/ppermute | solution.py:244
  17.4 1.3 collective-permute-start.1
  19.4 1.1 and.190
  20.6 1.0 add.248
  21.6 0.2 select_reduce_fusion
  21.9 1.0 lt.108
  23.0 0.2 dynamic-slice_reduce_fusion
  23.1 1.3 fusion.4.refs_8_
  24.4 42.7 %all-to-all-done.refs_5_.refs_6_.refs_7_ = bf16[8,288,512]{2,1,0:T(8,128)(2,1)} async-done(((bf16[8,288,512]{2,1,0:T(8,128)(2,1)}), bf16[8,288,512]{2,1,0:T(8,128)(2,1)}, u32[]{:S(2)}, u32[]{:S(2)}) %all-to-all-start) | async-done | bytes 2359328 | tf_op jit(solution)/shard_map/all_to_all | solution.py:272
  67.1 1.0 slice_reduce_fusion.1
  68.1 0.7 broadcast_in_dim.53
  68.8 4.7 %all-to-all-start.1 = ((bf16[8,32,512]{2,1,0:T(8,128)(2,1)}), bf16[8,32,512]{2,1,0:T(8,128)(2,1)S(1)}, u32[]{:S(2)}, u32[]{:S(2)}) async-start(bf16[8,32,512]{2,1,0:T(8,128)(2,1)} %broadcast_in_dim.53), calls=%async_computation.1 | async-start | bytes 524288 | tf_op jit(solution)/shard_map/all_to_all | solution.py:274
  73.6 0.6 reshape.651.ids_ref
  74.2 1.0 pad_maximum_fusion.1
  75.3 5.4 %all-to-all-done.1 = bf16[8,32,512]{2,1,0:T(8,128)(2,1)S(1)} async-done(((bf16[8,32,512]{2,1,0:T(8,128)(2,1)}), bf16[8,32,512]{2,1,0:T(8,128)(2,1)S(1)}, u32[]{:S(2)}, u32[]{:S(2)}) %all-to-all-start.1) | async-done | bytes 262176 | tf_op jit(solution)/shard_map/all_to_all | solution.py:274
  80.6 0.7 copy-done.4
  81.3 28.3 %shard_map.94 = (bf16[256,4096]{1,0:T(8,128)(2,1)}, f32[4,2,64,512]{3,2,1,0:T(8,128)}, f32[2,2,64,512]{3,2,1,0:T(8,128)}, f32[2,2,64,512]{3,2,1,0:T(8,128)}, bf16[4,3,2,64,512]{4,3,2,1,0:T(8,128)(2,1)}) custom-call(s32[24]{0:T(128)} %reshape.651.ids_ref, bf16[256,4096]{1,0:T(8,128)(2,1)} %bitcast.80, bf16[256,4096]{1,0:T(8,128)(2,1)} %bitcast.81, ...), custom_call_target="tpu_custom_call" | custom-call | flops 6442450944 | bytes 12582912 | tf_op jit(solution)/shard_map/pallas_call | solution.py:161
  109.6 1.1 convert_element_type.35
  110.7 0.2 broadcast_in_dim.57
  111.0 3.4 %scatter_fusion = bf16[8,2,2,64,512]{4,3,2,1,0:T(8,128)(2,1)S(1)} fusion(bf16[8,2,2,64,512]{4,3,2,1,0:T(8,128)(2,1)S(1)} %broadcast_in_dim.57, s32[12]{0:T(128)S(1)} %get-tuple-element.37, bf16[12,2,64,512]{3,2,1,0:T(8,128)(2,1)} %bitcast.67), kind=kCustom, calls=%fused_computation.1 | custom fusion | bytes 4718688 | tf_op jit(solution)/shard_map/scatter | solution.py:300
  114.3 1.7 pad_maximum_fusion
  116.0 4.8 %all-to-all-start.2 = ((bf16[8,288,512]{2,1,0:T(8,128)(2,1)}), bf16[8,288,512]{2,1,0:T(8,128)(2,1)S(1)}, u32[]{:S(2)}, u32[]{:S(2)}) async-start(bf16[8,288,512]{2,1,0:T(8,128)(2,1)} %pad_maximum_fusion), calls=%async_computation.2 | async-start | bytes 4718592 | tf_op jit(solution)/shard_map/all_to_all | solution.py:304
  120.9 0.1 fusion.12
  121.1 0.1 copy.79
  121.4 3.4 %collective-permute-start.4 = (bf16[1,2,64,512]{3,2,1,0:T(8,128)(2,1)S(1)}, bf16[1,2,64,512]{3,2,1,0:T(8,128)(2,1)S(1)}, u32[]{:S(2)}, u32[]{:S(2)}) collective-permute-start(bf16[1,2,64,512]{3,2,1,0:T(8,128)(2,1)S(1)} %get-tuple-element.51), channel_id=1, source_target_pairs={{0,1},{1,2},{2,3},{3,4},{4,5},{5,6},{6,7},{8,9},{9,10},{10,11},{11... | collective-permute-start | bytes 393224 | tf_op jit(solution)/shard_map/ppermute | solution.py:298
  124.8 1.3 collective-permute-start.3
  126.1 2.5 %collective-permute-start.2 = (bf16[256,4096]{1,0:T(8,128)(2,1)}, bf16[256,4096]{1,0:T(8,128)(2,1)}, u32[]{:S(2)}, u32[]{:S(2)}) collective-permute-start(bf16[256,4096]{1,0:T(8,128)(2,1)} %get-tuple-element.32), channel_id=1, source_target_pairs={{8,0},{16,8},{24,16},{0,24},{9,1},{17,9},{25,17},{1,25},{10,2},{18... | collective-permute-start | bytes 6291464 | tf_op jit(solution)/shard_map/ppermute | solution.py:37
  128.6 44.4 %all-to-all-done.2 = bf16[8,288,512]{2,1,0:T(8,128)(2,1)S(1)} async-done(((bf16[8,288,512]{2,1,0:T(8,128)(2,1)}), bf16[8,288,512]{2,1,0:T(8,128)(2,1)S(1)}, u32[]{:S(2)}, u32[]{:S(2)}) %all-to-all-start.2) | async-done | bytes 2359328 | tf_op jit(solution)/shard_map/all_to_all | solution.py:304
  173.0 0.7 broadcast_in_dim.58
  173.7 5.6 %all-to-all-start.3 = ((bf16[8,32,512]{2,1,0:T(8,128)(2,1)}), bf16[8,32,512]{2,1,0:T(8,128)(2,1)S(1)}, u32[]{:S(2)}, u32[]{:S(2)}) async-start(bf16[8,32,512]{2,1,0:T(8,128)(2,1)} %broadcast_in_dim.58), calls=%async_computation.3 | async-start | bytes 524288 | tf_op jit(solution)/shard_map/all_to_all | solution.py:314
  179.3 0.2 slice.111
  179.5 1.3 fusion
  180.8 0.4 copy_add_fusion.1
  181.4 5.0 %all-to-all-done.3 = bf16[8,32,512]{2,1,0:T(8,128)(2,1)S(1)} async-done(((bf16[8,32,512]{2,1,0:T(8,128)(2,1)}), bf16[8,32,512]{2,1,0:T(8,128)(2,1)S(1)}, u32[]{:S(2)}, u32[]{:S(2)}) %all-to-all-start.3) | async-done | bytes 262176 | tf_op jit(solution)/shard_map/all_to_all | solution.py:314
  186.4 0.6 fusion.7
  187.0 0.4 fusion.2
  187.5 3.1 %collective-permute-start.5 = (bf16[256,1024]{1,0:T(8,128)(2,1)S(1)}, bf16[256,1024]{1,0:T(8,128)(2,1)S(1)}, u32[]{:S(2)}, u32[]{:S(2)}) collective-permute-start(bf16[256,1024]{1,0:T(8,128)(2,1)S(1)} %pad_maximum_fusion.3), channel_id=1, source_target_pairs={{8,0},{16,8},{24,16},{0,24},{9,1},{17,9},{25,17},{1,25},{10,2},{18... | collective-permute-start | bytes 1572872 | tf_op jit(solution)/shard_map/ppermute | solution.py:37
  190.6 8.0 %collective-permute-done.5 = bf16[256,1024]{1,0:T(8,128)(2,1)S(1)} collective-permute-done((bf16[256,1024]{1,0:T(8,128)(2,1)S(1)}, bf16[256,1024]{1,0:T(8,128)(2,1)S(1)}, u32[]{:S(2)}, u32[]{:S(2)}) %collective-permute-start.5) | collective-permute-done | bytes 524320 | tf_op jit(solution)/shard_map/ppermute | solution.py:37
  198.6 0.8 slice_bitcast_fusion
  199.4 3.1 %copy.99 = bf16[1,256,4096]{2,1,0:T(8,128)(2,1)} copy(bf16[1,256,4096]{2,1,0:T(8,128)(2,1)} %bitcast.15) | data formatting | bytes 4194304
  (69 shorter events, 2.3 us)
Async XLA Ops:
  7.5 6.5 %copy-start = (bf16[1,256,512]{2,1,0:T(8,128)(2,1)S(1)}, bf16[1,256,512]{2,1,0:T(8,128)(2,1)}, u32[]{:S(2)}) copy-start(bf16[1,256,512]{2,1,0:T(8,128)(2,1)} %param.12) | copy-start | bytes 786436
  7.5 6.5 %copy-start.1 = (bf16[1,256,512]{2,1,0:T(8,128)(2,1)S(1)}, bf16[1,256,512]{2,1,0:T(8,128)(2,1)}, u32[]{:S(2)}) copy-start(bf16[1,256,512]{2,1,0:T(8,128)(2,1)} %param.13) | copy-start | bytes 786436
  7.5 11.2 %copy-start.5 = (s32[1,32,3]{1,0,2:T(1,128)S(1)}, s32[1,32,3]{1,0,2:T(1,128)}, u32[]{:S(2)}) copy-start(s32[1,32,3]{1,0,2:T(1,128)} %param.15) | copy-start | bytes 1156
  7.5 11.3 %copy-start.7 = (s32[1,2]{1,0:T(1,128)S(1)}, s32[1,2]{1,0:T(1,128)}, u32[]{:S(2)}) copy-start(s32[1,2]{1,0:T(1,128)} %param.16) | copy-start | bytes 28
  7.5 59.6 %all-to-all-start = ((bf16[8,288,512]{2,1,0:T(8,128)(2,1)}), bf16[8,288,512]{2,1,0:T(8,128)(2,1)}, u32[]{:S(2)}, u32[]{:S(2)}) async-start(bf16[8,288,512]{2,1,0:T(8,128)(2,1)} %bitcast.11), calls=%async_computation | async-start | bytes 4718592 | tf_op jit(solution)/shard_map/all_to_all | solution.py:272
  14.0 7.6 %copy-start.6 = (s32[1,8]{1,0:T(1,128)S(1)}, s32[1,8]{1,0:T(1,128)}, u32[]{:S(2)}) copy-start(s32[1,8]{1,0:T(1,128)} %param.17) | copy-start | bytes 100
  14.1 60.2 %collective-permute-start = (bf16[1,2,64,512]{3,2,1,0:T(8,128)(2,1)S(1)}, bf16[1,2,64,512]{3,2,1,0:T(8,128)(2,1)S(1)}, u32[]{:S(2)}, u32[]{:S(2)}) collective-permute-start(bf16[1,2,64,512]{3,2,1,0:T(8,128)(2,1)S(1)} %get-tuple-element.49), channel_id=1, source_target_pairs={{0,1},{1,2},{2,3},{3,4},{4,5},{5,6},{6,7},{8,9},{9,10},{10,11},{11... | collective-permute-start | bytes 393224 | tf_op jit(solution)/shard_map/ppermute | solution.py:244
  17.4 56.8 %collective-permute-start.1 = (bf16[1,2,64,512]{3,2,1,0:T(8,128)(2,1)S(1)}, bf16[1,2,64,512]{3,2,1,0:T(8,128)(2,1)S(1)}, u32[]{:S(2)}, u32[]{:S(2)}) collective-permute-start(bf16[1,2,64,512]{3,2,1,0:T(8,128)(2,1)S(1)} %get-tuple-element.50), channel_id=1, source_target_pairs={{1,0},{2,1},{3,2},{4,3},{5,4},{6,5},{7,6},{9,8},{10,9},{11,10},{12... | collective-permute-start | bytes 393224 | tf_op jit(solution)/shard_map/ppermute | solution.py:245
  68.8 11.8 %all-to-all-start.1 = ((bf16[8,32,512]{2,1,0:T(8,128)(2,1)}), bf16[8,32,512]{2,1,0:T(8,128)(2,1)S(1)}, u32[]{:S(2)}, u32[]{:S(2)}) async-start(bf16[8,32,512]{2,1,0:T(8,128)(2,1)} %broadcast_in_dim.53), calls=%async_computation.1 | async-start | bytes 524288 | tf_op jit(solution)/shard_map/all_to_all | solution.py:274
  80.6 0.7 copy-start.4
  116.0 5.3 %copy-start.3 = (f32[2,2,64,512]{3,2,1,0:T(8,128)S(1)}, f32[2,2,64,512]{3,2,1,0:T(8,128)}, u32[]{:S(2)}) copy-start(f32[2,2,64,512]{3,2,1,0:T(8,128)} %get-tuple-element.36) | copy-start | bytes 1572868
  116.0 56.9 %all-to-all-start.2 = ((bf16[8,288,512]{2,1,0:T(8,128)(2,1)}), bf16[8,288,512]{2,1,0:T(8,128)(2,1)S(1)}, u32[]{:S(2)}, u32[]{:S(2)}) async-start(bf16[8,288,512]{2,1,0:T(8,128)(2,1)} %pad_maximum_fusion), calls=%async_computation.2 | async-start | bytes 4718592 | tf_op jit(solution)/shard_map/all_to_all | solution.py:304
  121.4 59.9 %collective-permute-start.4 = (bf16[1,2,64,512]{3,2,1,0:T(8,128)(2,1)S(1)}, bf16[1,2,64,512]{3,2,1,0:T(8,128)(2,1)S(1)}, u32[]{:S(2)}, u32[]{:S(2)}) collective-permute-start(bf16[1,2,64,512]{3,2,1,0:T(8,128)(2,1)S(1)} %get-tuple-element.51), channel_id=1, source_target_pairs={{0,1},{1,2},{2,3},{3,4},{4,5},{5,6},{6,7},{8,9},{9,10},{10,11},{11... | collective-permute-start | bytes 393224 | tf_op jit(solution)/shard_map/ppermute | solution.py:298
  124.8 56.5 %collective-permute-start.3 = (bf16[1,2,64,512]{3,2,1,0:T(8,128)(2,1)S(1)}, bf16[1,2,64,512]{3,2,1,0:T(8,128)(2,1)S(1)}, u32[]{:S(2)}, u32[]{:S(2)}) collective-permute-start(bf16[1,2,64,512]{3,2,1,0:T(8,128)(2,1)S(1)} %get-tuple-element.52), channel_id=1, source_target_pairs={{1,0},{2,1},{3,2},{4,3},{5,4},{6,5},{7,6},{9,8},{10,9},{11,10},{12... | collective-permute-start | bytes 393224 | tf_op jit(solution)/shard_map/ppermute | solution.py:297
  126.1 64.5 %collective-permute-start.2 = (bf16[256,4096]{1,0:T(8,128)(2,1)}, bf16[256,4096]{1,0:T(8,128)(2,1)}, u32[]{:S(2)}, u32[]{:S(2)}) collective-permute-start(bf16[256,4096]{1,0:T(8,128)(2,1)} %get-tuple-element.32), channel_id=1, source_target_pairs={{8,0},{16,8},{24,16},{0,24},{9,1},{17,9},{25,17},{1,25},{10,2},{18... | collective-permute-start | bytes 6291464 | tf_op jit(solution)/shard_map/ppermute | solution.py:37
  173.7 12.7 %all-to-all-start.3 = ((bf16[8,32,512]{2,1,0:T(8,128)(2,1)}), bf16[8,32,512]{2,1,0:T(8,128)(2,1)S(1)}, u32[]{:S(2)}, u32[]{:S(2)}) async-start(bf16[8,32,512]{2,1,0:T(8,128)(2,1)} %broadcast_in_dim.58), calls=%async_computation.3 | async-start | bytes 524288 | tf_op jit(solution)/shard_map/all_to_all | solution.py:314
  179.5 1.3 copy-start.2
  187.5 11.0 %collective-permute-start.5 = (bf16[256,1024]{1,0:T(8,128)(2,1)S(1)}, bf16[256,1024]{1,0:T(8,128)(2,1)S(1)}, u32[]{:S(2)}, u32[]{:S(2)}) collective-permute-start(bf16[256,1024]{1,0:T(8,128)(2,1)S(1)} %pad_maximum_fusion.3), channel_id=1, source_target_pairs={{8,0},{16,8},{24,16},{0,24},{9,1},{17,9},{25,17},{1,25},{10,2},{18... | collective-permute-start | bytes 1572872 | tf_op jit(solution)/shard_map/ppermute | solution.py:37

commit v12 on v11

--- a/solution.py
+++ b/solution.py
@@ -296,13 +296,30 @@
     edge_low = edge_terms.astype(jnp.bfloat16)
     from_after = lax.ppermute(edge_low[:1], "seq", down)
     from_before = lax.ppermute(edge_low[1:], "seq", up)
-    holder = jnp.zeros((shards, capacity, 2, BLK, kwidth), random_part.dtype)
-    holder = holder.at[owner_mine, rank_mine].set(
-        random_part.reshape(query_blocks * RAND, 2, BLK, kwidth)
-    )
-    global_low = global_part.astype(jnp.bfloat16).reshape(shards, -1, kwidth)
+    ntile = query_blocks * RAND
+    global_low = global_part.astype(jnp.bfloat16).reshape(shards, unit_rows, kwidth)
+    term_units = jnp.concatenate(
+        [
+            random_part.reshape(ntile * unit_span, unit_rows, kwidth),
+            global_low,
+            jnp.zeros((1, unit_rows, kwidth), random_part.dtype),
+        ]
+    )
+    tile_range = jnp.arange(ntile, dtype=jnp.int32)
+    slot_match = (owner_mine[None, None, :] == jnp.arange(shards, dtype=jnp.int32)[:, None, None]) & (
+        rank_mine[None, None, :] == jnp.arange(capacity, dtype=jnp.int32)[None, :, None]
+    )
+    slot_tile = jnp.sum(jnp.where(slot_match, tile_range, 0), axis=2)
+    slot_idx = jnp.where(
+        jnp.any(slot_match, axis=2)[:, :, None],
+        slot_tile[:, :, None] * unit_span + unit_range,
+        ntile * unit_span + shards,
+    ).reshape(shards, -1)
+    back_idx = jnp.concatenate(
+        [slot_idx, ntile * unit_span + jnp.arange(shards, dtype=jnp.int32)[:, None]], axis=1
+    )
     returned = lax.all_to_all(
-        jnp.concatenate([holder.reshape(shards, capacity * block_rows, kwidth), global_low], axis=1),
+        jnp.take(term_units, back_idx.reshape(-1), axis=0, mode="clip").reshape(shards, -1, kwidth),
         "seq",
         0,
         0,

time: 203 us -> 204 us (level)
  other arithmetic: 10.8 us -> 14.3 us
    scatter x1 -> x0, local copies, waits for them, and re-layouts: 3.38 us -> none  [body(): holder.at[owner_mine, rank_mine]]
    all_to_all x1, waiting for transfers between devices: 5.36 us -> 2.49 us  [body(): lax.all_to_all(jnp.broadcast_to(global_piece[None], (shards,) + global_pi...]
    gather x0 -> x1, local copies, waits for them, and re-layouts: none -> 2.31 us  [body(): jnp.take(term_units, back_idx.reshape(-1), axis=0, mode='clip')]
    unnamed x18 -> x28, local copies, waits for them, and re-layouts: 4.62 us -> 4.64 us
  transfers between devices with their start and end apart: 10 -> 10, of which waited for: 5 -> 5; matrix products, arithmetic and copies ran while one was open for 7% -> 8% of each run, Pallas kernels for 0% -> 0%
where the time goes in v12:
time: 204 us; the launch traced here: 203 us
  waiting for transfers between devices  103 us (50%)
  starting transfers between devices  36.4 us (18%)
  Pallas kernels  28.3 us (14%)
  local copies, waits for them, and re-layouts  18.6 us (9%)
  other arithmetic  14.3 us (7%)
    all_to_all x1, waiting for transfers between devices, body(): lax.all_to_all(jnp.take(term_units, back_idx.reshape(-1), axis=0, mode='c...  44.4 us
    all_to_all x1, waiting for transfers between devices, body(): received = lax.all_to_all(payload, 'seq', 0, 0, tiled=True)  42.9 us
    pallas_call x1, Pallas kernels, block_backward(): pl.pallas_call(attention_kernel, grid_spec=grid_spec, out_shape=[jax.Shap...  28.3 us
    ppermute x2, waiting for transfers between devices, from_behind(): return lax.ppermute(block, axis, route)  7.99 us
    all_to_all x1, starting transfers between devices, body(): received = lax.all_to_all(payload, 'seq', 0, 0, tiled=True)  6.5 us
    all_to_all x1, starting transfers between devices, body(): lax.all_to_all(jnp.broadcast_to(global_sum[None], (shards,) + global_sum....  5.6 us
    ppermute x2, starting transfers between devices, from_behind(): return lax.ppermute(block, axis, route)  5.51 us
    all_to_all x1, waiting for transfers between devices, body(): lax.all_to_all(jnp.broadcast_to(global_sum[None], (shards,) + global_sum....  4.97 us
  transfers between devices with their start and end apart: 10, of which 5 were waited for; matrix products, arithmetic and copies ran while one was open for 8% of the time, Pallas kernels for 0%

profile of v12, /device:TPU:1, one launch (start us, length us, event | category | flops | bytes accessed | tf_op | source)
XLA Modules:
  0.0 203.4 jit_solution(379990702478573896)
XLA Ops:
  0.7 1.1 broadcast_multiply_fusion.2
  1.8 0.7 fusion.29
  2.5 0.8 copy.73
  3.4 0.6 fusion.30
  4.0 0.3 convert_reduce_fusion
  4.4 0.8 dynamic-slice_reduce_fusion
  6.2 1.1 pad_maximum_fusion.1
  7.4 2.3 %gather_fusion = bf16[72,32,512]{2,1,0:T(8,128)(2,1)} fusion(bf16[17,32,512]{2,1,0:T(8,128)(2,1)S(1)} %concatenate.44, s32[1024]{0:T(1024)S(1)} %pad_clamp_fusion.1), kind=kCustom, calls=%fused_computation | custom fusion | bytes 4718880 | tf_op jit(solution)/shard_map/jit(_take)/gather | solution.py:269
  9.7 6.5 %all-to-all-start = ((bf16[8,288,512]{2,1,0:T(8,128)(2,1)}), bf16[8,288,512]{2,1,0:T(8,128)(2,1)}, u32[]{:S(2)}, u32[]{:S(2)}) async-start(bf16[8,288,512]{2,1,0:T(8,128)(2,1)} %bitcast.11), calls=%async_computation | async-start | bytes 4718592 | tf_op jit(solution)/shard_map/all_to_all | solution.py:272
  16.2 0.7 fusion.9
  16.9 3.4 %collective-permute-start = (bf16[1,2,64,512]{3,2,1,0:T(8,128)(2,1)}, bf16[1,2,64,512]{3,2,1,0:T(8,128)(2,1)S(1)}, u32[]{:S(2)}, u32[]{:S(2)}) collective-permute-start(bf16[1,2,64,512]{3,2,1,0:T(8,128)(2,1)} %get-tuple-element.49), channel_id=1, source_target_pairs={{0,1},{1,2},{2,3},{3,4},{4,5},{5,6},{6,7},{8,9},{9,10},{10,11},{11... | collective-permute-start | bytes 393224 | tf_op jit(solution)/shard_map/ppermute | solution.py:244
  20.3 1.3 collective-permute-start.1
  21.7 0.7 add.249
  22.8 1.1 and.202
  24.0 1.0 add.261
  25.0 0.2 select_reduce_fusion
  25.3 1.0 lt.86
  26.4 42.9 %all-to-all-done.refs_5_.refs_6_.refs_7_ = bf16[8,288,512]{2,1,0:T(8,128)(2,1)} async-done(((bf16[8,288,512]{2,1,0:T(8,128)(2,1)}), bf16[8,288,512]{2,1,0:T(8,128)(2,1)}, u32[]{:S(2)}, u32[]{:S(2)}) %all-to-all-start) | async-done | bytes 2359328 | tf_op jit(solution)/shard_map/all_to_all | solution.py:272
  69.3 1.0 slice_reduce_fusion.1
  70.3 0.7 broadcast_in_dim.75
  71.0 4.7 %all-to-all-start.1 = ((bf16[8,32,512]{2,1,0:T(8,128)(2,1)}), bf16[8,32,512]{2,1,0:T(8,128)(2,1)S(1)}, u32[]{:S(2)}, u32[]{:S(2)}) async-start(bf16[8,32,512]{2,1,0:T(8,128)(2,1)} %broadcast_in_dim.75), calls=%async_computation.1 | async-start | bytes 524288 | tf_op jit(solution)/shard_map/all_to_all | solution.py:274
  75.7 1.9 fusion.4.refs_8_
  77.6 0.7 pad_add_fusion.3
  78.4 0.6 reshape.666.ids_ref
  79.3 1.0 pad_maximum_fusion
  80.3 2.5 %all-to-all-done.1 = bf16[8,32,512]{2,1,0:T(8,128)(2,1)S(1)} async-done(((bf16[8,32,512]{2,1,0:T(8,128)(2,1)}), bf16[8,32,512]{2,1,0:T(8,128)(2,1)S(1)}, u32[]{:S(2)}, u32[]{:S(2)}) %all-to-all-start.1) | async-done | bytes 262176 | tf_op jit(solution)/shard_map/all_to_all | solution.py:274
  82.8 0.7 copy-done.4
  83.5 28.3 %shard_map.94 = (bf16[256,4096]{1,0:T(8,128)(2,1)}, f32[4,2,64,512]{3,2,1,0:T(8,128)}, f32[2,2,64,512]{3,2,1,0:T(8,128)}, f32[2,2,64,512]{3,2,1,0:T(8,128)}, bf16[4,3,2,64,512]{4,3,2,1,0:T(8,128)(2,1)}) custom-call(s32[24]{0:T(128)} %reshape.666.ids_ref, bf16[256,4096]{1,0:T(8,128)(2,1)} %bitcast.80, bf16[256,4096]{1,0:T(8,128)(2,1)} %bitcast.81, ...), custom_call_target="tpu_custom_call" | custom-call | flops 6442450944 | bytes 12582912 | tf_op jit(solution)/shard_map/pallas_call | solution.py:161
  111.8 1.1 convert_element_type.35
  112.9 1.6 maximum_maximum_fusion
  114.5 2.3 %gather_fusion.1 = bf16[72,32,512]{2,1,0:T(8,128)(2,1)} fusion(bf16[57,32,512]{2,1,0:T(8,128)(2,1)S(1)} %maximum_maximum_fusion, s32[1024]{0:T(1024)S(1)} %pad_clamp_fusion), kind=kCustom, calls=%fused_computation.1 | custom fusion | bytes 4718880 | tf_op jit(solution)/shard_map/jit(_take)/gather | solution.py:322
  116.9 4.8 %all-to-all-start.2 = ((bf16[8,288,512]{2,1,0:T(8,128)(2,1)}), bf16[8,288,512]{2,1,0:T(8,128)(2,1)S(1)}, u32[]{:S(2)}, u32[]{:S(2)}) async-start(bf16[8,288,512]{2,1,0:T(8,128)(2,1)} %bitcast.55), calls=%async_computation.2 | async-start | bytes 4718592 | tf_op jit(solution)/shard_map/all_to_all | solution.py:321
  122.3 3.4 %collective-permute-start.4 = (bf16[1,2,64,512]{3,2,1,0:T(8,128)(2,1)S(1)}, bf16[1,2,64,512]{3,2,1,0:T(8,128)(2,1)S(1)}, u32[]{:S(2)}, u32[]{:S(2)}) collective-permute-start(bf16[1,2,64,512]{3,2,1,0:T(8,128)(2,1)S(1)} %get-tuple-element.51), channel_id=1, source_target_pairs={{0,1},{1,2},{2,3},{3,4},{4,5},{5,6},{6,7},{8,9},{9,10},{10,11},{11... | collective-permute-start | bytes 393224 | tf_op jit(solution)/shard_map/ppermute | solution.py:298
  125.6 1.3 collective-permute-start.3
  126.9 2.4 %collective-permute-start.2 = (bf16[256,4096]{1,0:T(8,128)(2,1)}, bf16[256,4096]{1,0:T(8,128)(2,1)}, u32[]{:S(2)}, u32[]{:S(2)}) collective-permute-start(bf16[256,4096]{1,0:T(8,128)(2,1)} %get-tuple-element.32), channel_id=1, source_target_pairs={{8,0},{16,8},{24,16},{0,24},{9,1},{17,9},{25,17},{1,25},{10,2},{18... | collective-permute-start | bytes 6291464 | tf_op jit(solution)/shard_map/ppermute | solution.py:37
  129.4 44.4 %all-to-all-done.2 = bf16[8,288,512]{2,1,0:T(8,128)(2,1)S(1)} async-done(((bf16[8,288,512]{2,1,0:T(8,128)(2,1)}), bf16[8,288,512]{2,1,0:T(8,128)(2,1)S(1)}, u32[]{:S(2)}, u32[]{:S(2)}) %all-to-all-start.2) | async-done | bytes 2359328 | tf_op jit(solution)/shard_map/all_to_all | solution.py:321
  173.8 0.7 broadcast_in_dim.130
  174.5 5.6 %all-to-all-start.3 = ((bf16[8,32,512]{2,1,0:T(8,128)(2,1)}), bf16[8,32,512]{2,1,0:T(8,128)(2,1)S(1)}, u32[]{:S(2)}, u32[]{:S(2)}) async-start(bf16[8,32,512]{2,1,0:T(8,128)(2,1)} %broadcast_in_dim.130), calls=%async_computation.3 | async-start | bytes 524288 | tf_op jit(solution)/shard_map/all_to_all | solution.py:331
  180.1 0.2 slice.111
  180.4 1.3 fusion
  181.7 0.4 copy_add_fusion.1
  182.3 5.0 %all-to-all-done.3 = bf16[8,32,512]{2,1,0:T(8,128)(2,1)S(1)} async-done(((bf16[8,32,512]{2,1,0:T(8,128)(2,1)}), bf16[8,32,512]{2,1,0:T(8,128)(2,1)S(1)}, u32[]{:S(2)}, u32[]{:S(2)}) %all-to-all-start.3) | async-done | bytes 262176 | tf_op jit(solution)/shard_map/all_to_all | solution.py:331
  187.2 0.6 fusion.7
  187.8 0.4 fusion.2
  188.4 3.1 %collective-permute-start.5 = (bf16[256,1024]{1,0:T(8,128)(2,1)S(1)}, bf16[256,1024]{1,0:T(8,128)(2,1)S(1)}, u32[]{:S(2)}, u32[]{:S(2)}) collective-permute-start(bf16[256,1024]{1,0:T(8,128)(2,1)S(1)} %pad_maximum_fusion.2), channel_id=1, source_target_pairs={{8,0},{16,8},{24,16},{0,24},{9,1},{17,9},{25,17},{1,25},{10,2},{18... | collective-permute-start | bytes 1572872 | tf_op jit(solution)/shard_map/ppermute | solution.py:37
  191.4 8.0 %collective-permute-done.5 = bf16[256,1024]{1,0:T(8,128)(2,1)S(1)} collective-permute-done((bf16[256,1024]{1,0:T(8,128)(2,1)S(1)}, bf16[256,1024]{1,0:T(8,128)(2,1)S(1)}, u32[]{:S(2)}, u32[]{:S(2)}) %collective-permute-start.5) | collective-permute-done | bytes 524320 | tf_op jit(solution)/shard_map/ppermute | solution.py:37
  199.4 0.8 slice_bitcast_fusion
  200.2 3.1 %copy.105 = bf16[1,256,4096]{2,1,0:T(8,128)(2,1)} copy(bf16[1,256,4096]{2,1,0:T(8,128)(2,1)} %bitcast.15) | data formatting | bytes 4194304
  (90 shorter events, 3.2 us)
Async XLA Ops:
  2.5 4.8 %copy-start.8 = (pred[2]{0:T(512)(128)(4,1)}, pred[2]{0:T(512)(128)(4,1)S(1)}, u32[]{:S(2)}) copy-start(pred[2]{0:T(512)(128)(4,1)S(1)} %fusion.29) | copy-start | bytes 10
  3.3 2.7 %copy-start.5 = (pred[8,12]{1,0:T(8,128)(4,1)}, pred[8,12]{1,0:T(8,128)(4,1)S(1)}, u32[]{:S(2)}) copy-start(pred[8,12]{1,0:T(8,128)(4,1)S(1)} %get-tuple-element.41) | copy-start | bytes 292
  9.7 6.5 %copy-start = (bf16[1,256,512]{2,1,0:T(8,128)(2,1)S(1)}, bf16[1,256,512]{2,1,0:T(8,128)(2,1)}, u32[]{:S(2)}) copy-start(bf16[1,256,512]{2,1,0:T(8,128)(2,1)} %param.12) | copy-start | bytes 786436
  9.7 6.5 %copy-start.1 = (bf16[1,256,512]{2,1,0:T(8,128)(2,1)S(1)}, bf16[1,256,512]{2,1,0:T(8,128)(2,1)}, u32[]{:S(2)}) copy-start(bf16[1,256,512]{2,1,0:T(8,128)(2,1)} %param.13) | copy-start | bytes 786436
  9.7 11.9 %copy-start.7 = (s32[1,32,3]{1,0,2:T(1,128)S(1)}, s32[1,32,3]{1,0,2:T(1,128)}, u32[]{:S(2)}) copy-start(s32[1,32,3]{1,0,2:T(1,128)} %param.15) | copy-start | bytes 1156
  9.7 11.9 %copy-start.12 = (s32[1,2]{1,0:T(1,128)S(1)}, s32[1,2]{1,0:T(1,128)}, u32[]{:S(2)}) copy-start(s32[1,2]{1,0:T(1,128)} %param.16) | copy-start | bytes 28
  9.7 59.6 %all-to-all-start = ((bf16[8,288,512]{2,1,0:T(8,128)(2,1)}), bf16[8,288,512]{2,1,0:T(8,128)(2,1)}, u32[]{:S(2)}, u32[]{:S(2)}) async-start(bf16[8,288,512]{2,1,0:T(8,128)(2,1)} %bitcast.11), calls=%async_computation | async-start | bytes 4718592 | tf_op jit(solution)/shard_map/all_to_all | solution.py:272
  16.2 8.8 %copy-start.11 = (s32[1,8]{1,0:T(1,128)S(1)}, s32[1,8]{1,0:T(1,128)}, u32[]{:S(2)}) copy-start(s32[1,8]{1,0:T(1,128)} %param.17) | copy-start | bytes 100
  16.9 62.4 %collective-permute-start = (bf16[1,2,64,512]{3,2,1,0:T(8,128)(2,1)}, bf16[1,2,64,512]{3,2,1,0:T(8,128)(2,1)S(1)}, u32[]{:S(2)}, u32[]{:S(2)}) collective-permute-start(bf16[1,2,64,512]{3,2,1,0:T(8,128)(2,1)} %get-tuple-element.49), channel_id=1, source_target_pairs={{0,1},{1,2},{2,3},{3,4},{4,5},{5,6},{6,7},{8,9},{9,10},{10,11},{11... | collective-permute-start | bytes 393224 | tf_op jit(solution)/shard_map/ppermute | solution.py:244
  20.3 59.0 %collective-permute-start.1 = (bf16[1,2,64,512]{3,2,1,0:T(8,128)(2,1)S(1)}, bf16[1,2,64,512]{3,2,1,0:T(8,128)(2,1)S(1)}, u32[]{:S(2)}, u32[]{:S(2)}) collective-permute-start(bf16[1,2,64,512]{3,2,1,0:T(8,128)(2,1)S(1)} %get-tuple-element.50), channel_id=1, source_target_pairs={{1,0},{2,1},{3,2},{4,3},{5,4},{6,5},{7,6},{9,8},{10,9},{11,10},{12... | collective-permute-start | bytes 393224 | tf_op jit(solution)/shard_map/ppermute | solution.py:245
  71.0 11.8 %all-to-all-start.1 = ((bf16[8,32,512]{2,1,0:T(8,128)(2,1)}), bf16[8,32,512]{2,1,0:T(8,128)(2,1)S(1)}, u32[]{:S(2)}, u32[]{:S(2)}) async-start(bf16[8,32,512]{2,1,0:T(8,128)(2,1)} %broadcast_in_dim.75), calls=%async_computation.1 | async-start | bytes 524288 | tf_op jit(solution)/shard_map/all_to_all | solution.py:274
  82.8 0.7 copy-start.4
  116.9 4.9 %copy-start.6 = (pred[8,12]{1,0:T(8,128)(4,1)S(1)}, pred[8,12]{1,0:T(8,128)(4,1)}, u32[]{:S(2)}) copy-start(pred[8,12]{1,0:T(8,128)(4,1)} %copy-done.5) | copy-start | bytes 292
  116.9 5.3 %copy-start.3 = (f32[2,2,64,512]{3,2,1,0:T(8,128)S(1)}, f32[2,2,64,512]{3,2,1,0:T(8,128)}, u32[]{:S(2)}) copy-start(f32[2,2,64,512]{3,2,1,0:T(8,128)} %get-tuple-element.36) | copy-start | bytes 1572868
  116.9 56.9 %all-to-all-start.2 = ((bf16[8,288,512]{2,1,0:T(8,128)(2,1)}), bf16[8,288,512]{2,1,0:T(8,128)(2,1)S(1)}, u32[]{:S(2)}, u32[]{:S(2)}) async-start(bf16[8,288,512]{2,1,0:T(8,128)(2,1)} %bitcast.55), calls=%async_computation.2 | async-start | bytes 4718592 | tf_op jit(solution)/shard_map/all_to_all | solution.py:321
  122.3 59.9 %collective-permute-start.4 = (bf16[1,2,64,512]{3,2,1,0:T(8,128)(2,1)S(1)}, bf16[1,2,64,512]{3,2,1,0:T(8,128)(2,1)S(1)}, u32[]{:S(2)}, u32[]{:S(2)}) collective-permute-start(bf16[1,2,64,512]{3,2,1,0:T(8,128)(2,1)S(1)} %get-tuple-element.51), channel_id=1, source_target_pairs={{0,1},{1,2},{2,3},{3,4},{4,5},{5,6},{6,7},{8,9},{9,10},{10,11},{11... | collective-permute-start | bytes 393224 | tf_op jit(solution)/shard_map/ppermute | solution.py:298
  125.6 56.5 %collective-permute-start.3 = (bf16[1,2,64,512]{3,2,1,0:T(8,128)(2,1)S(1)}, bf16[1,2,64,512]{3,2,1,0:T(8,128)(2,1)S(1)}, u32[]{:S(2)}, u32[]{:S(2)}) collective-permute-start(bf16[1,2,64,512]{3,2,1,0:T(8,128)(2,1)S(1)} %get-tuple-element.52), channel_id=1, source_target_pairs={{1,0},{2,1},{3,2},{4,3},{5,4},{6,5},{7,6},{9,8},{10,9},{11,10},{12... | collective-permute-start | bytes 393224 | tf_op jit(solution)/shard_map/ppermute | solution.py:297
  126.9 64.5 %collective-permute-start.2 = (bf16[256,4096]{1,0:T(8,128)(2,1)}, bf16[256,4096]{1,0:T(8,128)(2,1)}, u32[]{:S(2)}, u32[]{:S(2)}) collective-permute-start(bf16[256,4096]{1,0:T(8,128)(2,1)} %get-tuple-element.32), channel_id=1, source_target_pairs={{8,0},{16,8},{24,16},{0,24},{9,1},{17,9},{25,17},{1,25},{10,2},{18... | collective-permute-start | bytes 6291464 | tf_op jit(solution)/shard_map/ppermute | solution.py:37
  174.5 12.7 %all-to-all-start.3 = ((bf16[8,32,512]{2,1,0:T(8,128)(2,1)}), bf16[8,32,512]{2,1,0:T(8,128)(2,1)S(1)}, u32[]{:S(2)}, u32[]{:S(2)}) async-start(bf16[8,32,512]{2,1,0:T(8,128)(2,1)} %broadcast_in_dim.130), calls=%async_computation.3 | async-start | bytes 524288 | tf_op jit(solution)/shard_map/all_to_all | solution.py:331
  180.4 1.3 copy-start.2
  181.7 5.6 %copy-start.9 = (pred[2]{0:T(512)(128)(4,1)S(1)}, pred[2]{0:T(512)(128)(4,1)}, u32[]{:S(2)}) copy-start(pred[2]{0:T(512)(128)(4,1)} %copy-done.8) | copy-start | bytes 10
  181.7 5.6 %copy-start.10 = (s32[2]{0:T(128)S(1)}, s32[2]{0:T(128)}, u32[]{:S(2)}) copy-start(s32[2]{0:T(128)} %get-tuple-element.44) | copy-start | bytes 28
  188.4 11.0 %collective-permute-start.5 = (bf16[256,1024]{1,0:T(8,128)(2,1)S(1)}, bf16[256,1024]{1,0:T(8,128)(2,1)S(1)}, u32[]{:S(2)}, u32[]{:S(2)}) collective-permute-start(bf16[256,1024]{1,0:T(8,128)(2,1)S(1)} %pad_maximum_fusion.2), channel_id=1, source_target_pairs={{8,0},{16,8},{24,16},{0,24},{9,1},{17,9},{25,17},{1,25},{10,2},{18... | collective-permute-start | bytes 1572872 | tf_op jit(solution)/shard_map/ppermute | solution.py:37

commit v13 on v12

--- a/solution.py
+++ b/solution.py
@@ -35,6 +35,23 @@
     devices = range(lax.axis_size(axis))
     route = [((i - distance) % len(devices), i) for i in devices]
     return lax.ppermute(block, axis, route)
+
+
+def copy_kernel(src_ref, dst_ref):
+    dst_ref[...] = src_ref[...]
+
+
+def fresh_copy(array):
+    rows, width = array.shape[-2:]
+    spec = pl.BlockSpec((None, rows, width), lambda i: (0, 0, 0))
+    return pl.pallas_call(
+        copy_kernel,
+        grid=(1,),
+        in_specs=[spec],
+        out_specs=spec,
+        out_shape=jax.ShapeDtypeStruct(array.shape, array.dtype),
+        cost_estimate=pl.CostEstimate(flops=0, transcendentals=0, bytes_accessed=2 * array.size * array.dtype.itemsize),
+    )(array)
 
 
 def attention_kernel(ids_ref, q_ref, g_ref, *refs):
@@ -292,7 +309,7 @@
     query_grad, local_sum, edge_terms, global_part, random_part = block_backward(
         query_rows, grad_rows, window, global_tiles, received, random_ids, key_live
     )
-    handed_query = from_behind(query_grad, "section", -1)
+    handed_query = from_behind(query_grad[None], "section", -1)
     edge_low = edge_terms.astype(jnp.bfloat16)
     from_after = lax.ppermute(edge_low[:1], "seq", down)
     from_before = lax.ppermute(edge_low[1:], "seq", up)
@@ -354,9 +371,10 @@
         ],
         axis=-1,
     )
+    handed_query, kv_grad = lax.optimization_barrier((fresh_copy(handed_query), kv_grad))
     handed_kv = from_behind(kv_grad, "section", -1)
     return (
-        handed_query[None],
+        handed_query,
         handed_kv[None, :, :kwidth],
         handed_kv[None, :, kwidth:],
     )

time: 204 us -> 201 us (0.985)
  local copies, waits for them, and re-layouts: 18.6 us -> 15.5 us
  Pallas kernels: 28.3 us -> 31.4 us
  waiting for transfers between devices: 103 us -> 100 us
    all_to_all x1, waiting for transfers between devices: 44.4 us -> 21.7 us  [body(): lax.all_to_all(jnp.take(term_units, back_idx.reshape(-1), axis=0, mode='c...]
    ppermute x2, waiting for transfers between devices: 7.99 us -> 28 us  [from_behind(): return lax.ppermute(block, axis, route)]
    unnamed x28 -> x27, local copies, waits for them, and re-layouts: 4.64 us -> 1.51 us
    pallas_call x0 -> x1, Pallas kernels: none -> 3.04 us  [fresh_copy(): pl.pallas_call(copy_kernel, grid=(1,), in_specs=[spec], out_specs=spec, o...]
  transfers between devices with their start and end apart: 10 -> 10, of which waited for: 5 -> 6; matrix products, arithmetic and copies ran while one was open for 8% -> 8% of each run, Pallas kernels for 0% -> 2%
where the time goes in v13:
time: 201 us; the launch traced here: 200 us
  waiting for transfers between devices  100 us (50%)
  starting transfers between devices  36.1 us (18%)
  Pallas kernels  31.4 us (16%)
  local copies, waits for them, and re-layouts  15.5 us (8%)
  other arithmetic  14.3 us (7%)
    all_to_all x1, waiting for transfers between devices, body(): received = lax.all_to_all(payload, 'seq', 0, 0, tiled=True)  42.9 us
    pallas_call x1, Pallas kernels, block_backward(): pl.pallas_call(attention_kernel, grid_spec=grid_spec, out_shape=[jax.Shap...  28.3 us
    ppermute x2, waiting for transfers between devices, from_behind(): return lax.ppermute(block, axis, route)  28 us
    all_to_all x1, waiting for transfers between devices, body(): lax.all_to_all(jnp.take(term_units, back_idx.reshape(-1), axis=0, mode='c...  21.7 us
    all_to_all x1, starting transfers between devices, body(): received = lax.all_to_all(payload, 'seq', 0, 0, tiled=True)  6.5 us
    all_to_all x1, starting transfers between devices, body(): lax.all_to_all(jnp.broadcast_to(global_sum[None], (shards,) + global_sum....  5.6 us
    ppermute x2, starting transfers between devices, from_behind(): return lax.ppermute(block, axis, route)  5.05 us
    all_to_all x1, waiting for transfers between devices, body(): lax.all_to_all(jnp.broadcast_to(global_sum[None], (shards,) + global_sum....  4.97 us
  transfers between devices with their start and end apart: 10, of which 6 were waited for; matrix products, arithmetic and copies ran while one was open for 8% of the time, Pallas kernels for 2%

profile of v13, /device:TPU:1, one launch (start us, length us, event | category | flops | bytes accessed | tf_op | source)
XLA Modules:
  0.0 200.2 jit_solution(8122728766618847768)
XLA Ops:
  0.7 1.1 broadcast_multiply_fusion.2
  1.8 0.7 fusion.29
  2.5 0.8 copy.73
  3.4 0.6 fusion.30
  4.0 0.3 convert_reduce_fusion
  4.4 0.8 dynamic-slice_reduce_fusion
  6.2 1.1 pad_maximum_fusion.1
  7.4 2.3 %gather_fusion = bf16[72,32,512]{2,1,0:T(8,128)(2,1)} fusion(bf16[17,32,512]{2,1,0:T(8,128)(2,1)S(1)} %concatenate.44, s32[1024]{0:T(1024)S(1)} %pad_clamp_fusion.1), kind=kCustom, calls=%fused_computation | custom fusion | bytes 4718880 | tf_op jit(solution)/shard_map/jit(_take)/gather | solution.py:286
  9.7 6.5 %all-to-all-start = ((bf16[8,288,512]{2,1,0:T(8,128)(2,1)}), bf16[8,288,512]{2,1,0:T(8,128)(2,1)}, u32[]{:S(2)}, u32[]{:S(2)}) async-start(bf16[8,288,512]{2,1,0:T(8,128)(2,1)} %bitcast.11), calls=%async_computation | async-start | bytes 4718592 | tf_op jit(solution)/shard_map/all_to_all | solution.py:289
  16.2 0.7 fusion.9
  16.9 3.4 %collective-permute-start = (bf16[1,2,64,512]{3,2,1,0:T(8,128)(2,1)}, bf16[1,2,64,512]{3,2,1,0:T(8,128)(2,1)S(1)}, u32[]{:S(2)}, u32[]{:S(2)}) collective-permute-start(bf16[1,2,64,512]{3,2,1,0:T(8,128)(2,1)} %get-tuple-element.53), channel_id=1, source_target_pairs={{0,1},{1,2},{2,3},{3,4},{4,5},{5,6},{6,7},{8,9},{9,10},{10,11},{11... | collective-permute-start | bytes 393224 | tf_op jit(solution)/shard_map/ppermute | solution.py:261
  20.3 1.3 collective-permute-start.1
  21.7 0.7 add.249
  22.8 1.1 and.202
  24.0 1.0 add.261
  25.3 1.0 lt.86
  26.4 42.9 %all-to-all-done.refs_5_.refs_6_.refs_7_ = bf16[8,288,512]{2,1,0:T(8,128)(2,1)} async-done(((bf16[8,288,512]{2,1,0:T(8,128)(2,1)}), bf16[8,288,512]{2,1,0:T(8,128)(2,1)}, u32[]{:S(2)}, u32[]{:S(2)}) %all-to-all-start) | async-done | bytes 2359328 | tf_op jit(solution)/shard_map/all_to_all | solution.py:289
  69.3 1.0 slice_reduce_fusion.1
  70.3 0.7 broadcast_in_dim.75
  71.0 4.7 %all-to-all-start.1 = ((bf16[8,32,512]{2,1,0:T(8,128)(2,1)}), bf16[8,32,512]{2,1,0:T(8,128)(2,1)S(1)}, u32[]{:S(2)}, u32[]{:S(2)}) async-start(bf16[8,32,512]{2,1,0:T(8,128)(2,1)} %broadcast_in_dim.75), calls=%async_computation.1 | async-start | bytes 524288 | tf_op jit(solution)/shard_map/all_to_all | solution.py:291
  75.7 1.9 fusion.4.refs_8_
  77.6 0.7 pad_add_fusion.3
  78.4 0.6 reshape.666.ids_ref
  79.3 1.0 pad_maximum_fusion
  80.3 2.5 %all-to-all-done.1 = bf16[8,32,512]{2,1,0:T(8,128)(2,1)S(1)} async-done(((bf16[8,32,512]{2,1,0:T(8,128)(2,1)}), bf16[8,32,512]{2,1,0:T(8,128)(2,1)S(1)}, u32[]{:S(2)}, u32[]{:S(2)}) %all-to-all-start.1) | async-done | bytes 262176 | tf_op jit(solution)/shard_map/all_to_all | solution.py:291
  82.8 0.7 copy-done.4
  83.5 28.3 %shard_map.94 = (bf16[256,4096]{1,0:T(8,128)(2,1)}, f32[4,2,64,512]{3,2,1,0:T(8,128)}, f32[2,2,64,512]{3,2,1,0:T(8,128)}, f32[2,2,64,512]{3,2,1,0:T(8,128)}, bf16[4,3,2,64,512]{4,3,2,1,0:T(8,128)(2,1)}) custom-call(s32[24]{0:T(128)} %reshape.666.ids_ref, bf16[256,4096]{1,0:T(8,128)(2,1)} %bitcast.80, bf16[256,4096]{1,0:T(8,128)(2,1)} %bitcast.81, ...), custom_call_target="tpu_custom_call" | custom-call | flops 6442450944 | bytes 12582912 | tf_op jit(solution)/shard_map/pallas_call | solution.py:178
  111.8 1.1 convert_element_type.35
  112.9 1.6 maximum_maximum_fusion
  114.5 2.3 %gather_fusion.1 = bf16[72,32,512]{2,1,0:T(8,128)(2,1)} fusion(bf16[57,32,512]{2,1,0:T(8,128)(2,1)S(1)} %maximum_maximum_fusion, s32[1024]{0:T(1024)S(1)} %pad_clamp_fusion), kind=kCustom, calls=%fused_computation.1 | custom fusion | bytes 4718880 | tf_op jit(solution)/shard_map/jit(_take)/gather | solution.py:339
  116.9 4.8 %all-to-all-start.2 = ((bf16[8,288,512]{2,1,0:T(8,128)(2,1)}), bf16[8,288,512]{2,1,0:T(8,128)(2,1)S(1)}, u32[]{:S(2)}, u32[]{:S(2)}) async-start(bf16[8,288,512]{2,1,0:T(8,128)(2,1)} %bitcast.55), calls=%async_computation.2 | async-start | bytes 4718592 | tf_op jit(solution)/shard_map/all_to_all | solution.py:338
  121.7 2.0 collective-permute-start.2
  124.3 3.5 %collective-permute-start.4 = (bf16[1,2,64,512]{3,2,1,0:T(8,128)(2,1)S(1)}, bf16[1,2,64,512]{3,2,1,0:T(8,128)(2,1)S(1)}, u32[]{:S(2)}, u32[]{:S(2)}) collective-permute-start(bf16[1,2,64,512]{3,2,1,0:T(8,128)(2,1)S(1)} %get-tuple-element.55), channel_id=1, source_target_pairs={{0,1},{1,2},{2,3},{3,4},{4,5},{5,6},{6,7},{8,9},{9,10},{10,11},{11... | collective-permute-start | bytes 393224 | tf_op jit(solution)/shard_map/ppermute | solution.py:315
  127.8 1.3 collective-permute-start.3
  129.1 20.0 %collective-permute-done.2.src_ref = bf16[1,256,4096]{2,1,0:T(8,128)(2,1)} collective-permute-done((bf16[1,256,4096]{2,1,0:T(8,128)(2,1)}, bf16[1,256,4096]{2,1,0:T(8,128)(2,1)}, u32[]{:S(2)}, u32[]{:S(2)}) %collective-permute-start.2) | collective-permute-done | bytes 2097184 | tf_op jit(solution)/shard_map/ppermute | solution.py:37
  149.0 3.0 %shard_map.95 = bf16[1,256,4096]{2,1,0:T(8,128)(2,1)} custom-call(bf16[1,256,4096]{2,1,0:T(8,128)(2,1)} %collective-permute-done.2.src_ref), custom_call_target="tpu_custom_call" | custom-call | bytes 4194304 | tf_op jit(solution)/shard_map/pallas_call | solution.py:47
  152.1 21.7 %all-to-all-done.2 = bf16[8,288,512]{2,1,0:T(8,128)(2,1)S(1)} async-done(((bf16[8,288,512]{2,1,0:T(8,128)(2,1)}), bf16[8,288,512]{2,1,0:T(8,128)(2,1)S(1)}, u32[]{:S(2)}, u32[]{:S(2)}) %all-to-all-start.2) | async-done | bytes 2359328 | tf_op jit(solution)/shard_map/all_to_all | solution.py:338
  173.8 0.7 broadcast_in_dim.130
  174.5 5.6 %all-to-all-start.3 = ((bf16[8,32,512]{2,1,0:T(8,128)(2,1)}), bf16[8,32,512]{2,1,0:T(8,128)(2,1)S(1)}, u32[]{:S(2)}, u32[]{:S(2)}) async-start(bf16[8,32,512]{2,1,0:T(8,128)(2,1)} %broadcast_in_dim.130), calls=%async_computation.3 | async-start | bytes 524288 | tf_op jit(solution)/shard_map/all_to_all | solution.py:348
  180.1 0.2 slice.111
  180.4 1.3 fusion
  181.7 0.4 copy_add_fusion.1
  182.3 5.0 %all-to-all-done.3 = bf16[8,32,512]{2,1,0:T(8,128)(2,1)S(1)} async-done(((bf16[8,32,512]{2,1,0:T(8,128)(2,1)}), bf16[8,32,512]{2,1,0:T(8,128)(2,1)S(1)}, u32[]{:S(2)}, u32[]{:S(2)}) %all-to-all-start.3) | async-done | bytes 262176 | tf_op jit(solution)/shard_map/all_to_all | solution.py:348
  187.2 0.6 fusion.7
  187.8 0.4 fusion.2
  188.4 3.1 %collective-permute-start.5 = (bf16[256,1024]{1,0:T(8,128)(2,1)S(1)}, bf16[256,1024]{1,0:T(8,128)(2,1)S(1)}, u32[]{:S(2)}, u32[]{:S(2)}) collective-permute-start(bf16[256,1024]{1,0:T(8,128)(2,1)S(1)} %pad_maximum_fusion.2), channel_id=1, source_target_pairs={{8,0},{16,8},{24,16},{0,24},{9,1},{17,9},{25,17},{1,25},{10,2},{18... | collective-permute-start | bytes 1572872 | tf_op jit(solution)/shard_map/ppermute | solution.py:37
  191.4 8.0 %collective-permute-done.5 = bf16[256,1024]{1,0:T(8,128)(2,1)S(1)} collective-permute-done((bf16[256,1024]{1,0:T(8,128)(2,1)S(1)}, bf16[256,1024]{1,0:T(8,128)(2,1)S(1)}, u32[]{:S(2)}, u32[]{:S(2)}) %collective-permute-start.5) | collective-permute-done | bytes 524320 | tf_op jit(solution)/shard_map/ppermute | solution.py:37
  199.4 0.8 slice_bitcast_fusion
  (90 shorter events, 3.4 us)
Async XLA Ops:
  2.5 4.8 %copy-start.8 = (pred[2]{0:T(512)(128)(4,1)}, pred[2]{0:T(512)(128)(4,1)S(1)}, u32[]{:S(2)}) copy-start(pred[2]{0:T(512)(128)(4,1)S(1)} %fusion.29) | copy-start | bytes 10
  3.3 2.7 %copy-start.5 = (pred[8,12]{1,0:T(8,128)(4,1)}, pred[8,12]{1,0:T(8,128)(4,1)S(1)}, u32[]{:S(2)}) copy-start(pred[8,12]{1,0:T(8,128)(4,1)S(1)} %get-tuple-element.45) | copy-start | bytes 292
  9.7 6.5 %copy-start = (bf16[1,256,512]{2,1,0:T(8,128)(2,1)S(1)}, bf16[1,256,512]{2,1,0:T(8,128)(2,1)}, u32[]{:S(2)}) copy-start(bf16[1,256,512]{2,1,0:T(8,128)(2,1)} %param.12) | copy-start | bytes 786436
  9.7 6.5 %copy-start.1 = (bf16[1,256,512]{2,1,0:T(8,128)(2,1)S(1)}, bf16[1,256,512]{2,1,0:T(8,128)(2,1)}, u32[]{:S(2)}) copy-start(bf16[1,256,512]{2,1,0:T(8,128)(2,1)} %param.13) | copy-start | bytes 786436
  9.7 11.9 %copy-start.7 = (s32[1,32,3]{1,0,2:T(1,128)S(1)}, s32[1,32,3]{1,0,2:T(1,128)}, u32[]{:S(2)}) copy-start(s32[1,32,3]{1,0,2:T(1,128)} %param.15) | copy-start | bytes 1156
  9.7 11.9 %copy-start.12 = (s32[1,2]{1,0:T(1,128)S(1)}, s32[1,2]{1,0:T(1,128)}, u32[]{:S(2)}) copy-start(s32[1,2]{1,0:T(1,128)} %param.16) | copy-start | bytes 28
  9.7 59.6 %all-to-all-start = ((bf16[8,288,512]{2,1,0:T(8,128)(2,1)}), bf16[8,288,512]{2,1,0:T(8,128)(2,1)}, u32[]{:S(2)}, u32[]{:S(2)}) async-start(bf16[8,288,512]{2,1,0:T(8,128)(2,1)} %bitcast.11), calls=%async_computation | async-start | bytes 4718592 | tf_op jit(solution)/shard_map/all_to_all | solution.py:289
  16.2 8.8 %copy-start.11 = (s32[1,8]{1,0:T(1,128)S(1)}, s32[1,8]{1,0:T(1,128)}, u32[]{:S(2)}) copy-start(s32[1,8]{1,0:T(1,128)} %param.17) | copy-start | bytes 100
  16.9 62.4 %collective-permute-start = (bf16[1,2,64,512]{3,2,1,0:T(8,128)(2,1)}, bf16[1,2,64,512]{3,2,1,0:T(8,128)(2,1)S(1)}, u32[]{:S(2)}, u32[]{:S(2)}) collective-permute-start(bf16[1,2,64,512]{3,2,1,0:T(8,128)(2,1)} %get-tuple-element.53), channel_id=1, source_target_pairs={{0,1},{1,2},{2,3},{3,4},{4,5},{5,6},{6,7},{8,9},{9,10},{10,11},{11... | collective-permute-start | bytes 393224 | tf_op jit(solution)/shard_map/ppermute | solution.py:261
  20.3 59.0 %collective-permute-start.1 = (bf16[1,2,64,512]{3,2,1,0:T(8,128)(2,1)S(1)}, bf16[1,2,64,512]{3,2,1,0:T(8,128)(2,1)S(1)}, u32[]{:S(2)}, u32[]{:S(2)}) collective-permute-start(bf16[1,2,64,512]{3,2,1,0:T(8,128)(2,1)S(1)} %get-tuple-element.54), channel_id=1, source_target_pairs={{1,0},{2,1},{3,2},{4,3},{5,4},{6,5},{7,6},{9,8},{10,9},{11,10},{12... | collective-permute-start | bytes 393224 | tf_op jit(solution)/shard_map/ppermute | solution.py:262
  71.0 11.8 %all-to-all-start.1 = ((bf16[8,32,512]{2,1,0:T(8,128)(2,1)}), bf16[8,32,512]{2,1,0:T(8,128)(2,1)S(1)}, u32[]{:S(2)}, u32[]{:S(2)}) async-start(bf16[8,32,512]{2,1,0:T(8,128)(2,1)} %broadcast_in_dim.75), calls=%async_computation.1 | async-start | bytes 524288 | tf_op jit(solution)/shard_map/all_to_all | solution.py:291
  82.8 0.7 copy-start.4
  116.9 6.9 %copy-start.6 = (pred[8,12]{1,0:T(8,128)(4,1)S(1)}, pred[8,12]{1,0:T(8,128)(4,1)}, u32[]{:S(2)}) copy-start(pred[8,12]{1,0:T(8,128)(4,1)} %copy-done.5) | copy-start | bytes 292
  116.9 7.3 %copy-start.3 = (f32[2,2,64,512]{3,2,1,0:T(8,128)S(1)}, f32[2,2,64,512]{3,2,1,0:T(8,128)}, u32[]{:S(2)}) copy-start(f32[2,2,64,512]{3,2,1,0:T(8,128)} %get-tuple-element.38) | copy-start | bytes 1572868
  116.9 56.9 %all-to-all-start.2 = ((bf16[8,288,512]{2,1,0:T(8,128)(2,1)}), bf16[8,288,512]{2,1,0:T(8,128)(2,1)S(1)}, u32[]{:S(2)}, u32[]{:S(2)}) async-start(bf16[8,288,512]{2,1,0:T(8,128)(2,1)} %bitcast.55), calls=%async_computation.2 | async-start | bytes 4718592 | tf_op jit(solution)/shard_map/all_to_all | solution.py:338
  121.7 27.3 %collective-permute-start.2 = (bf16[1,256,4096]{2,1,0:T(8,128)(2,1)}, bf16[1,256,4096]{2,1,0:T(8,128)(2,1)}, u32[]{:S(2)}, u32[]{:S(2)}) collective-permute-start(bf16[1,256,4096]{2,1,0:T(8,128)(2,1)} %bitcast.82), channel_id=1, source_target_pairs={{8,0},{16,8},{24,16},{0,24},{9,1},{17,9},{25,17},{1,25},{10,2},{18... | collective-permute-start | bytes 6291464 | tf_op jit(solution)/shard_map/ppermute | solution.py:37
  124.3 57.9 %collective-permute-start.4 = (bf16[1,2,64,512]{3,2,1,0:T(8,128)(2,1)S(1)}, bf16[1,2,64,512]{3,2,1,0:T(8,128)(2,1)S(1)}, u32[]{:S(2)}, u32[]{:S(2)}) collective-permute-start(bf16[1,2,64,512]{3,2,1,0:T(8,128)(2,1)S(1)} %get-tuple-element.55), channel_id=1, source_target_pairs={{0,1},{1,2},{2,3},{3,4},{4,5},{5,6},{6,7},{8,9},{9,10},{10,11},{11... | collective-permute-start | bytes 393224 | tf_op jit(solution)/shard_map/ppermute | solution.py:315
  127.8 54.4 %collective-permute-start.3 = (bf16[1,2,64,512]{3,2,1,0:T(8,128)(2,1)S(1)}, bf16[1,2,64,512]{3,2,1,0:T(8,128)(2,1)S(1)}, u32[]{:S(2)}, u32[]{:S(2)}) collective-permute-start(bf16[1,2,64,512]{3,2,1,0:T(8,128)(2,1)S(1)} %get-tuple-element.56), channel_id=1, source_target_pairs={{1,0},{2,1},{3,2},{4,3},{5,4},{6,5},{7,6},{9,8},{10,9},{11,10},{12... | collective-permute-start | bytes 393224 | tf_op jit(solution)/shard_map/ppermute | solution.py:314
  174.5 12.7 %all-to-all-start.3 = ((bf16[8,32,512]{2,1,0:T(8,128)(2,1)}), bf16[8,32,512]{2,1,0:T(8,128)(2,1)S(1)}, u32[]{:S(2)}, u32[]{:S(2)}) async-start(bf16[8,32,512]{2,1,0:T(8,128)(2,1)} %broadcast_in_dim.130), calls=%async_computation.3 | async-start | bytes 524288 | tf_op jit(solution)/shard_map/all_to_all | solution.py:348
  180.4 1.3 copy-start.2
  181.7 5.6 %copy-start.9 = (pred[2]{0:T(512)(128)(4,1)S(1)}, pred[2]{0:T(512)(128)(4,1)}, u32[]{:S(2)}) copy-start(pred[2]{0:T(512)(128)(4,1)} %copy-done.8) | copy-start | bytes 10
  181.7 5.6 %copy-start.10 = (s32[2]{0:T(128)S(1)}, s32[2]{0:T(128)}, u32[]{:S(2)}) copy-start(s32[2]{0:T(128)} %get-tuple-element.48) | copy-start | bytes 28
  188.4 11.0 %collective-permute-start.5 = (bf16[256,1024]{1,0:T(8,128)(2,1)S(1)}, bf16[256,1024]{1,0:T(8,128)(2,1)S(1)}, u32[]{:S(2)}, u32[]{:S(2)}) collective-permute-start(bf16[256,1024]{1,0:T(8,128)(2,1)S(1)} %pad_maximum_fusion.2), channel_id=1, source_target_pairs={{8,0},{16,8},{24,16},{0,24},{9,1},{17,9},{25,17},{1,25},{10,2},{18... | collective-permute-start | bytes 1572872 | tf_op jit(solution)/shard_map/ppermute | solution.py:37

commit v14 on v13

--- a/solution.py
+++ b/solution.py
@@ -35,6 +35,27 @@
     devices = range(lax.axis_size(axis))
     route = [((i - distance) % len(devices), i) for i in devices]
     return lax.ppermute(block, axis, route)
+
+
+def chunk_sum(chunks, axis):
+    devices = lax.axis_size(axis)
+    me = lax.axis_index(axis)
+    total = lax.dynamic_index_in_dim(chunks, me, 0, keepdims=False)
+    for d in range(1, devices):
+        send = lax.dynamic_index_in_dim(chunks, (me + d) % devices, 0, keepdims=False)
+        total = total + lax.ppermute(send, axis, [(i, (i + d) % devices) for i in range(devices)])
+    return total
+
+
+def chunk_gather(piece, axis):
+    devices = lax.axis_size(axis)
+    me = lax.axis_index(axis)
+    stacked = [piece] + [
+        lax.ppermute(piece, axis, [(i, (i + d) % devices) for i in range(devices)])
+        for d in range(1, devices)
+    ]
+    order = (me - jnp.arange(devices, dtype=jnp.int32)) % devices
+    return jnp.take(jnp.stack(stacked), order, axis=0, mode="clip")
 
 
 def copy_kernel(src_ref, dst_ref):
@@ -268,29 +289,22 @@
     nb = query_blocks
     unit_rows = GLOB * block_rows // shards
     unit_span = block_rows // unit_rows
-    own_units = jnp.concatenate(
-        [
-            own_blocks.reshape(nb * unit_span, unit_rows, kwidth),
-            jnp.zeros((1, unit_rows, kwidth), own_blocks.dtype),
-        ]
-    )
     unit_range = jnp.arange(unit_span, dtype=jnp.int32)
-    served_idx = (serve_block[:, :, None] * unit_span + unit_range).reshape(shards, -1)
-    global_owned = global_ids // query_blocks == this_shard
-    global_idx = jnp.where(
-        global_owned[:, None],
-        (global_ids % query_blocks)[:, None] * unit_span + unit_range,
-        nb * unit_span,
-    ).reshape(shards, -1)
-    payload_idx = jnp.concatenate([served_idx, global_idx], axis=1)
-    payload = jnp.take(own_units, payload_idx.reshape(-1), axis=0, mode="clip").reshape(
-        shards, -1, kwidth
-    )
-    received = lax.all_to_all(payload, "seq", 0, 0, tiled=True)
-    global_piece = jnp.sum(received[:, capacity * block_rows :], axis=0, dtype=own_blocks.dtype)
-    global_tiles = lax.all_to_all(
-        jnp.broadcast_to(global_piece[None], (shards,) + global_piece.shape), "seq", 0, 0, tiled=True
-    ).reshape(GLOB, block_rows, kwidth)
+    served = jnp.take(own_blocks, serve_block.reshape(-1), axis=0, mode="clip").reshape(
+        shards, capacity * block_rows, kwidth
+    )
+    global_mine = [
+        jnp.where(
+            global_ids[g] // query_blocks == this_shard,
+            lax.dynamic_index_in_dim(own_blocks, global_ids[g] % query_blocks, 0, keepdims=True),
+            jnp.zeros((), own_blocks.dtype),
+        )
+        for g in range(GLOB)
+    ]
+    global_chunks = jnp.concatenate(global_mine, axis=0).reshape(shards, unit_rows, kwidth)
+    received = lax.all_to_all(served, "seq", 0, 0, tiled=True)
+    global_piece = chunk_sum(global_chunks, "seq")
+    global_tiles = chunk_gather(global_piece, "seq").reshape(GLOB, block_rows, kwidth)
     window = jnp.concatenate([edge_before, own_blocks, edge_after], axis=0).reshape(
         nb + 2, block_rows, kwidth
     )
@@ -314,11 +328,10 @@
     from_after = lax.ppermute(edge_low[:1], "seq", down)
     from_before = lax.ppermute(edge_low[1:], "seq", up)
     ntile = query_blocks * RAND
-    global_low = global_part.astype(jnp.bfloat16).reshape(shards, unit_rows, kwidth)
+    global_chunks_back = global_part.reshape(shards, unit_rows, kwidth)
     term_units = jnp.concatenate(
         [
             random_part.reshape(ntile * unit_span, unit_rows, kwidth),
-            global_low,
             jnp.zeros((1, unit_rows, kwidth), random_part.dtype),
         ]
     )
@@ -327,27 +340,21 @@
         rank_mine[None, None, :] == jnp.arange(capacity, dtype=jnp.int32)[None, :, None]
     )
     slot_tile = jnp.sum(jnp.where(slot_match, tile_range, 0), axis=2)
-    slot_idx = jnp.where(
+    back_idx = jnp.where(
         jnp.any(slot_match, axis=2)[:, :, None],
         slot_tile[:, :, None] * unit_span + unit_range,
-        ntile * unit_span + shards,
-    ).reshape(shards, -1)
-    back_idx = jnp.concatenate(
-        [slot_idx, ntile * unit_span + jnp.arange(shards, dtype=jnp.int32)[:, None]], axis=1
-    )
+        ntile * unit_span,
+    ).reshape(-1)
     returned = lax.all_to_all(
-        jnp.take(term_units, back_idx.reshape(-1), axis=0, mode="clip").reshape(shards, -1, kwidth),
+        jnp.take(term_units, back_idx, axis=0, mode="clip").reshape(shards, -1, kwidth),
         "seq",
         0,
         0,
         tiled=True,
     )
-    random_back = returned[:, : capacity * block_rows].reshape(shards * capacity, 2, BLK, kwidth)
-    global_sum = jnp.sum(returned[:, capacity * block_rows :].astype(jnp.float32), axis=0)
-    global_sum = global_sum.astype(jnp.bfloat16)
-    global_total = lax.all_to_all(
-        jnp.broadcast_to(global_sum[None], (shards,) + global_sum.shape), "seq", 0, 0, tiled=True
-    ).reshape(GLOB, 2, BLK, kwidth).astype(jnp.float32)
+    global_sum = chunk_sum(global_chunks_back, "seq")
+    global_total = chunk_gather(global_sum, "seq").reshape(GLOB, 2, BLK, kwidth)
+    random_back = returned.reshape(shards * capacity, 2, BLK, kwidth)
     onehot = (
         slot_used.reshape(-1)[None, :]
         & (serve_block.reshape(-1)[None, :] == block_range[:, None])

time: 201 us -> 261 us (1.30)
  starting transfers between devices: 36.1 us -> 78.4 us
  waiting for transfers between devices: 100 us -> 109 us
  between operations: 1.02 us -> 6.51 us
  local copies, waits for them, and re-layouts: 15.5 us -> 20.8 us
  other arithmetic: 14.3 us -> 9.83 us
    ppermute x0 -> x28, waiting for transfers between devices: none -> 101 us  [the longest x14 59.8 us: chunk_sum(): lax.ppermute(send, axis, [(i, (i + d) % devices) for i in range(devices)])]
    all_to_all x4 -> x2, waiting for transfers between devices: 72.1 us -> 0.01 us  [the longest x1 0.01 us: body(): received = lax.all_to_all(served, 'seq', 0, 0, tiled=True)]
    ppermute x0 -> x28, starting transfers between devices: none -> 51 us  [the longest x14 39.4 us: chunk_sum(): lax.ppermute(send, axis, [(i, (i + d) % devices) for i in range(devices)])]
    ppermute x2, waiting for transfers between devices: 28 us -> 7.99 us  [from_behind(): return lax.ppermute(block, axis, route)]
    all_to_all x4 -> x2, starting transfers between devices: 21.6 us -> 8.58 us  [the longest x1 4.48 us: body(): received = lax.all_to_all(served, 'seq', 0, 0, tiled=True)]
    ppermute x2, starting transfers between devices: 5.05 us -> 11 us  [from_behind(): return lax.ppermute(block, axis, route)]
    gather x2 -> x4, local copies, waits for them, and re-layouts: 4.62 us -> 6.68 us  [the longest x2 2.63 us: chunk_gather(): return jnp.take(jnp.stack(stacked), order, axis=0, mode='clip')]
  transfers between devices with their start and end apart: 10 -> 36, of which waited for: 6 -> 13; matrix products, arithmetic and copies ran while one was open for 8% -> 10% of each run, Pallas kernels for 2% -> 1%
where the time goes in v14:
time: 261 us; the launch traced here: 259 us
  waiting for transfers between devices  109 us (42%)
  starting transfers between devices  78.4 us (30%)
  Pallas kernels  30.8 us (12%)
  local copies, waits for them, and re-layouts  20.8 us (8%)
  other arithmetic  9.83 us (4%)
  between operations  6.51 us (2%)
  matrix products  3.87 us (1%)
    ppermute x14, waiting for transfers between devices, chunk_sum(): lax.ppermute(send, axis, [(i, (i + d) % devices) for i in range(devices)])  59.8 us
    ppermute x14, waiting for transfers between devices, chunk_gather(): lax.ppermute(piece, axis, [(i, (i + d) % devices) for i in range(devices)])  41.3 us
    ppermute x14, starting transfers between devices, chunk_sum(): lax.ppermute(send, axis, [(i, (i + d) % devices) for i in range(devices)])  39.4 us
    pallas_call x1, Pallas kernels, block_backward(): pl.pallas_call(attention_kernel, grid_spec=grid_spec, out_shape=[jax.Shap...  27.8 us
    ppermute x14, starting transfers between devices, chunk_gather(): lax.ppermute(piece, axis, [(i, (i + d) % devices) for i in range(devices)])  11.6 us
    ppermute x2, starting transfers between devices, from_behind(): return lax.ppermute(block, axis, route)  11 us
    ppermute x2, waiting for transfers between devices, from_behind(): return lax.ppermute(block, axis, route)  7.99 us
  transfers between devices with their start and end apart: 36, of which 13 were waited for; matrix products, arithmetic and copies ran while one was open for 10% of the time, Pallas kernels for 1%

profile of v14, /device:TPU:1, one launch (start us, length us, event | category | flops | bytes accessed | tf_op | source)
XLA Modules:
  0.0 259.3 jit_solution(16428712921264125673)
XLA Ops:
  0.8 1.3 fusion.54
  9.2 2.0 collective-permute-start.2
  11.2 3.1 %collective-permute-start.8 = (bf16[32,512]{1,0:T(8,128)(2,1)}, bf16[32,512]{1,0:T(8,128)(2,1)S(1)}, u32[]{:S(2)}, u32[]{:S(2)}) collective-permute-start(bf16[32,512]{1,0:T(8,128)(2,1)} %get-tuple-element.69), channel_id=1, source_target_pairs={{0,7},{1,0},{2,1},{3,2},{4,3},{5,4},{6,5},{7,6},{8,15},{9,8},{10,9... | collective-permute-start | bytes 98312 | tf_op jit(solution)/shard_map/ppermute | solution.py:46
  14.3 1.4 collective-permute-start.7
  15.7 2.4 collective-permute-start.5
  20.5 2.0 gather_fusion.1
  22.5 4.5 %all-to-all-start = ((bf16[8,256,512]{2,1,0:T(8,128)(2,1)}), bf16[8,256,512]{2,1,0:T(8,128)(2,1)}, u32[]{:S(2)}, u32[]{:S(2)}) async-start(bf16[8,256,512]{2,1,0:T(8,128)(2,1)} %bitcast.29), calls=%async_computation | async-start | bytes 4194304 | tf_op jit(solution)/shard_map/all_to_all | solution.py:305
  28.5 1.1 and.277
  32.2 1.3 fusion.4.refs_8_
  33.6 2.3 collective-permute-start.4
  35.9 1.2 collective-permute-start.3
  37.1 3.1 %collective-permute-start = (bf16[1,2,64,512]{3,2,1,0:T(8,128)(2,1)S(1)}, bf16[1,2,64,512]{3,2,1,0:T(8,128)(2,1)S(1)}, u32[]{:S(2)}, u32[]{:S(2)}) collective-permute-start(bf16[1,2,64,512]{3,2,1,0:T(8,128)(2,1)S(1)} %get-tuple-element.63), channel_id=1, source_target_pairs={{0,1},{1,2},{2,3},{3,4},{4,5},{5,6},{6,7},{8,9},{9,10},{10,11},{11... | collective-permute-start | bytes 393224 | tf_op jit(solution)/shard_map/ppermute | solution.py:282
  40.2 1.3 collective-permute-start.1
  41.5 36.8 %collective-permute-done.4 = bf16[32,512]{1,0:T(8,128)(2,1)S(1)} collective-permute-done((bf16[32,512]{1,0:T(8,128)(2,1)}, bf16[32,512]{1,0:T(8,128)(2,1)S(1)}, u32[]{:S(2)}, u32[]{:S(2)}) %collective-permute-start.4) | collective-permute-done | bytes 32800 | tf_op jit(solution)/shard_map/ppermute | solution.py:46
  80.7 1.2 collective-permute-start.13
  81.9 2.9 %collective-permute-done.9 = bf16[32,512]{1,0:T(8,128)(2,1)S(1)} collective-permute-done((bf16[32,512]{1,0:T(8,128)(2,1)S(1)}, bf16[32,512]{1,0:T(8,128)(2,1)S(1)}, u32[]{:S(2)}, u32[]{:S(2)}) %collective-permute-start.9) | collective-permute-done | bytes 32800 | tf_op jit(solution)/shard_map/ppermute | solution.py:54
  84.8 4.6 %collective-permute-done.10 = bf16[32,512]{1,0:T(8,128)(2,1)S(1)} collective-permute-done((bf16[32,512]{1,0:T(8,128)(2,1)S(1)}, bf16[32,512]{1,0:T(8,128)(2,1)S(1)}, u32[]{:S(2)}, u32[]{:S(2)}) %collective-permute-start.10) | collective-permute-done | bytes 32800 | tf_op jit(solution)/shard_map/ppermute | solution.py:54
  89.3 4.6 %collective-permute-done.11 = bf16[32,512]{1,0:T(8,128)(2,1)S(1)} collective-permute-done((bf16[32,512]{1,0:T(8,128)(2,1)S(1)}, bf16[32,512]{1,0:T(8,128)(2,1)S(1)}, u32[]{:S(2)}, u32[]{:S(2)}) %collective-permute-start.11) | collective-permute-done | bytes 32800 | tf_op jit(solution)/shard_map/ppermute | solution.py:54
  94.0 3.6 %collective-permute-done.12 = bf16[32,512]{1,0:T(8,128)(2,1)S(1)} collective-permute-done((bf16[32,512]{1,0:T(8,128)(2,1)S(1)}, bf16[32,512]{1,0:T(8,128)(2,1)S(1)}, u32[]{:S(2)}, u32[]{:S(2)}) %collective-permute-start.12) | collective-permute-done | bytes 32800 | tf_op jit(solution)/shard_map/ppermute | solution.py:54
  97.6 2.7 %collective-permute-done.15 = bf16[32,512]{1,0:T(8,128)(2,1)S(1)} collective-permute-done((bf16[32,512]{1,0:T(8,128)(2,1)S(1)}, bf16[32,512]{1,0:T(8,128)(2,1)S(1)}, u32[]{:S(2)}, u32[]{:S(2)}) %collective-permute-start.15) | collective-permute-done | bytes 32800 | tf_op jit(solution)/shard_map/ppermute | solution.py:54
  100.3 1.3 gather_fusion
  102.6 27.8 %shard_map.97 = (bf16[256,4096]{1,0:T(8,128)(2,1)}, f32[4,2,64,512]{3,2,1,0:T(8,128)}, f32[2,2,64,512]{3,2,1,0:T(8,128)}, f32[2,2,64,512]{3,2,1,0:T(8,128)}, bf16[4,3,2,64,512]{4,3,2,1,0:T(8,128)(2,1)}) custom-call(s32[24]{0:T(128)} %reshape.678.ids_ref, bf16[256,4096]{1,0:T(8,128)(2,1)} %bitcast.169, bf16[256,4096]{1,0:T(8,128)(2,1)} %bitcast.170, ...), custom_call_target="tpu_custom_call" | custom-call | flops 6442450944 | bytes 12582912 | tf_op jit(solution)/shard_map/pallas_call | solution.py:199
  130.4 1.5 concatenate.42
  131.9 2.0 gather_fusion.2
  134.0 4.1 %all-to-all-start.1 = ((bf16[8,256,512]{2,1,0:T(8,128)(2,1)}), bf16[8,256,512]{2,1,0:T(8,128)(2,1)S(1)}, u32[]{:S(2)}, u32[]{:S(2)}) async-start(bf16[8,256,512]{2,1,0:T(8,128)(2,1)} %bitcast.145), calls=%async_computation.1 | async-start | bytes 4194304 | tf_op jit(solution)/shard_map/all_to_all | solution.py:348
  139.3 1.5 collective-permute-start.19
  140.7 2.7 %collective-permute-start.25 = (f32[32,512]{1,0:T(8,128)S(1)}, f32[32,512]{1,0:T(8,128)S(1)}, u32[]{:S(2)}, u32[]{:S(2)}) collective-permute-start(f32[32,512]{1,0:T(8,128)S(1)} %get-tuple-element.56), channel_id=1, source_target_pairs={{0,7},{1,0},{2,1},{3,2},{4,3},{5,4},{6,5},{7,6},{8,15},{9,8},{10,9... | collective-permute-start | bytes 196616 | tf_op jit(solution)/shard_map/ppermute | solution.py:46
  144.0 1.5 collective-permute-start.24
  145.4 2.4 collective-permute-start.22
  147.8 23.0 %collective-permute-done.19 = f32[32,512]{1,0:T(8,128)S(1)} collective-permute-done((f32[32,512]{1,0:T(8,128)S(1)}, f32[32,512]{1,0:T(8,128)S(1)}, u32[]{:S(2)}, u32[]{:S(2)}) %collective-permute-start.19) | collective-permute-done | bytes 65568 | tf_op jit(solution)/shard_map/ppermute | solution.py:46
  170.8 19.0 %collective-permute-start.21 = (f32[32,512]{1,0:T(8,128)}, f32[32,512]{1,0:T(8,128)S(1)}, u32[]{:S(2)}, u32[]{:S(2)}) collective-permute-start(f32[32,512]{1,0:T(8,128)} %get-tuple-element.60), channel_id=1, source_target_pairs={{0,3},{1,4},{2,5},{3,6},{4,7},{5,0},{6,1},{7,2},{8,11},{9,12},{10,... | collective-permute-start | bytes 196616 | tf_op jit(solution)/shard_map/ppermute | solution.py:46
  190.5 1.3 copy.77
  192.5 5.1 %collective-permute-start.16 = (bf16[1,256,4096]{2,1,0:T(8,128)(2,1)}, bf16[1,256,4096]{2,1,0:T(8,128)(2,1)}, u32[]{:S(2)}, u32[]{:S(2)}) collective-permute-start(bf16[1,256,4096]{2,1,0:T(8,128)(2,1)} %bitcast.171), channel_id=1, source_target_pairs={{8,0},{16,8},{24,16},{0,24},{9,1},{17,9},{25,17},{1,25},{10,2},{18... | collective-permute-start | bytes 6291464 | tf_op jit(solution)/shard_map/ppermute | solution.py:37
  198.5 3.2 %collective-permute-start.26 = (f32[32,512]{1,0:T(8,128)S(1)}, f32[32,512]{1,0:T(8,128)S(1)}, u32[]{:S(2)}, u32[]{:S(2)}) collective-permute-start(f32[32,512]{1,0:T(8,128)S(1)} %get-tuple-element.44), channel_id=1, source_target_pairs={{0,1},{1,2},{2,3},{3,4},{4,5},{5,6},{6,7},{7,0},{8,9},{9,10},{10,1... | collective-permute-start | bytes 196616 | tf_op jit(solution)/shard_map/ppermute | solution.py:54
  202.4 2.2 collective-permute-start.18
  204.6 1.3 collective-permute-start.17
  205.9 6.3 %collective-permute-start.31 = (f32[32,512]{1,0:T(8,128)S(1)}, f32[32,512]{1,0:T(8,128)S(1)}, u32[]{:S(2)}, u32[]{:S(2)}) collective-permute-start(f32[32,512]{1,0:T(8,128)S(1)} %get-tuple-element.44), channel_id=1, source_target_pairs={{0,6},{1,7},{2,0},{3,1},{4,2},{5,3},{6,4},{7,5},{8,14},{9,15},{10,... | collective-permute-start | bytes 196616 | tf_op jit(solution)/shard_map/ppermute | solution.py:54
  212.2 5.6 %collective-permute-done.27 = f32[32,512]{1,0:T(8,128)S(1)} collective-permute-done((f32[32,512]{1,0:T(8,128)S(1)}, f32[32,512]{1,0:T(8,128)S(1)}, u32[]{:S(2)}, u32[]{:S(2)}) %collective-permute-start.27) | collective-permute-done | bytes 65568 | tf_op jit(solution)/shard_map/ppermute | solution.py:54
  217.8 5.6 %collective-permute-done.28 = f32[32,512]{1,0:T(8,128)S(1)} collective-permute-done((f32[32,512]{1,0:T(8,128)S(1)}, f32[32,512]{1,0:T(8,128)S(1)}, u32[]{:S(2)}, u32[]{:S(2)}) %collective-permute-start.28) | collective-permute-done | bytes 65568 | tf_op jit(solution)/shard_map/ppermute | solution.py:54
  223.4 4.0 %collective-permute-done.29 = f32[32,512]{1,0:T(8,128)S(1)} collective-permute-done((f32[32,512]{1,0:T(8,128)S(1)}, f32[32,512]{1,0:T(8,128)S(1)}, u32[]{:S(2)}, u32[]{:S(2)}) %collective-permute-start.29) | collective-permute-done | bytes 65568 | tf_op jit(solution)/shard_map/ppermute | solution.py:54
  227.4 4.7 %collective-permute-done.30 = f32[32,512]{1,0:T(8,128)S(1)} collective-permute-done((f32[32,512]{1,0:T(8,128)S(1)}, f32[32,512]{1,0:T(8,128)S(1)}, u32[]{:S(2)}, u32[]{:S(2)}) %collective-permute-start.30) | collective-permute-done | bytes 65568 | tf_op jit(solution)/shard_map/ppermute | solution.py:54
  232.1 3.1 %collective-permute-done.32 = f32[32,512]{1,0:T(8,128)S(1)} collective-permute-done((f32[32,512]{1,0:T(8,128)S(1)}, f32[32,512]{1,0:T(8,128)S(1)}, u32[]{:S(2)}, u32[]{:S(2)}) %collective-permute-start.32) | collective-permute-done | bytes 65568 | tf_op jit(solution)/shard_map/ppermute | solution.py:54
  235.2 1.4 gather_fusion.3
  236.6 2.6 fusion.5
  239.2 3.0 %shard_map.98 = bf16[1,256,4096]{2,1,0:T(8,128)(2,1)} custom-call(bf16[1,256,4096]{2,1,0:T(8,128)(2,1)} %collective-permute-done.16.src_ref), custom_call_target="tpu_custom_call" | custom-call | bytes 4194304 | tf_op jit(solution)/shard_map/pallas_call | solution.py:68
  242.3 1.3 fusion
  244.6 5.9 %collective-permute-start.33 = (bf16[256,1024]{1,0:T(8,128)(2,1)S(1)}, bf16[256,1024]{1,0:T(8,128)(2,1)S(1)}, u32[]{:S(2)}, u32[]{:S(2)}) collective-permute-start(bf16[256,1024]{1,0:T(8,128)(2,1)S(1)} %pad_maximum_fusion.2), channel_id=1, source_target_pairs={{8,0},{16,8},{24,16},{0,24},{9,1},{17,9},{25,17},{1,25},{10,2},{18... | collective-permute-start | bytes 1572872 | tf_op jit(solution)/shard_map/ppermute | solution.py:37
  250.5 8.0 %collective-permute-done.33 = bf16[256,1024]{1,0:T(8,128)(2,1)S(1)} collective-permute-done((bf16[256,1024]{1,0:T(8,128)(2,1)S(1)}, bf16[256,1024]{1,0:T(8,128)(2,1)S(1)}, u32[]{:S(2)}, u32[]{:S(2)}) %collective-permute-start.33) | collective-permute-done | bytes 524320 | tf_op jit(solution)/shard_map/ppermute | solution.py:37
  (146 shorter events, 18.5 us)
Async XLA Ops:
  0.6 19.5 %copy-start.1 = (bf16[1,256,512]{2,1,0:T(8,128)(2,1)S(1)}, bf16[1,256,512]{2,1,0:T(8,128)(2,1)}, u32[]{:S(2)}) copy-start(bf16[1,256,512]{2,1,0:T(8,128)(2,1)} %param.13) | copy-start | bytes 786436
  0.6 19.5 %copy-start = (bf16[1,256,512]{2,1,0:T(8,128)(2,1)S(1)}, bf16[1,256,512]{2,1,0:T(8,128)(2,1)}, u32[]{:S(2)}) copy-start(bf16[1,256,512]{2,1,0:T(8,128)(2,1)} %param.12) | copy-start | bytes 786436
  0.7 17.5 %copy-start.5 = (s32[1,32,3]{1,0,2:T(1,128)S(1)}, s32[1,32,3]{1,0,2:T(1,128)}, u32[]{:S(2)}) copy-start(s32[1,32,3]{1,0,2:T(1,128)} %param.15) | copy-start | bytes 1156
  9.2 24.4 %collective-permute-start.2 = (bf16[32,512]{1,0:T(8,128)(2,1)}, bf16[32,512]{1,0:T(8,128)(2,1)S(1)}, u32[]{:S(2)}, u32[]{:S(2)}) collective-permute-start(bf16[32,512]{1,0:T(8,128)(2,1)} %get-tuple-element.68), channel_id=1, source_target_pairs={{0,1},{1,2},{2,3},{3,4},{4,5},{5,6},{6,7},{7,0},{8,9},{9,10},{10,1... | collective-permute-start | bytes 98312 | tf_op jit(solution)/shard_map/ppermute | solution.py:46
  11.2 24.6 %collective-permute-start.8 = (bf16[32,512]{1,0:T(8,128)(2,1)}, bf16[32,512]{1,0:T(8,128)(2,1)S(1)}, u32[]{:S(2)}, u32[]{:S(2)}) collective-permute-start(bf16[32,512]{1,0:T(8,128)(2,1)} %get-tuple-element.69), channel_id=1, source_target_pairs={{0,7},{1,0},{2,1},{3,2},{4,3},{5,4},{6,5},{7,6},{8,15},{9,8},{10,9... | collective-permute-start | bytes 98312 | tf_op jit(solution)/shard_map/ppermute | solution.py:46
  14.3 22.8 %collective-permute-start.7 = (bf16[32,512]{1,0:T(8,128)(2,1)}, bf16[32,512]{1,0:T(8,128)(2,1)}, u32[]{:S(2)}, u32[]{:S(2)}) collective-permute-start(bf16[32,512]{1,0:T(8,128)(2,1)} %get-tuple-element.70), channel_id=1, source_target_pairs={{0,6},{1,7},{2,0},{3,1},{4,2},{5,3},{6,4},{7,5},{8,14},{9,15},{10,... | collective-permute-start | bytes 98312 | tf_op jit(solution)/shard_map/ppermute | solution.py:46
  15.7 24.5 %collective-permute-start.6 = (bf16[32,512]{1,0:T(8,128)(2,1)}, bf16[32,512]{1,0:T(8,128)(2,1)}, u32[]{:S(2)}, u32[]{:S(2)}) collective-permute-start(bf16[32,512]{1,0:T(8,128)(2,1)} %get-tuple-element.71), channel_id=1, source_target_pairs={{0,5},{1,6},{2,7},{3,0},{4,1},{5,2},{6,3},{7,4},{8,13},{9,14},{10,... | collective-permute-start | bytes 98312 | tf_op jit(solution)/shard_map/ppermute | solution.py:46
  15.7 25.8 %collective-permute-start.5 = (bf16[32,512]{1,0:T(8,128)(2,1)}, bf16[32,512]{1,0:T(8,128)(2,1)}, u32[]{:S(2)}, u32[]{:S(2)}) collective-permute-start(bf16[32,512]{1,0:T(8,128)(2,1)} %get-tuple-element.72), channel_id=1, source_target_pairs={{0,4},{1,5},{2,6},{3,7},{4,0},{5,1},{6,2},{7,3},{8,12},{9,13},{10,... | collective-permute-start | bytes 98312 | tf_op jit(solution)/shard_map/ppermute | solution.py:46
  22.5 4.7 %copy-start.6 = (s32[1,2]{1,0:T(1,128)S(1)}, s32[1,2]{1,0:T(1,128)}, u32[]{:S(2)}) copy-start(s32[1,2]{1,0:T(1,128)} %param.16) | copy-start | bytes 28
  22.5 8.2 %copy-start.12 = (s32[1,8]{1,0:T(1,128)S(1)}, s32[1,8]{1,0:T(1,128)}, u32[]{:S(2)}) copy-start(s32[1,8]{1,0:T(1,128)} %param.17) | copy-start | bytes 100
  22.5 80.1 %all-to-all-start = ((bf16[8,256,512]{2,1,0:T(8,128)(2,1)}), bf16[8,256,512]{2,1,0:T(8,128)(2,1)}, u32[]{:S(2)}, u32[]{:S(2)}) async-start(bf16[8,256,512]{2,1,0:T(8,128)(2,1)} %bitcast.29), calls=%async_computation | async-start | bytes 4194304 | tf_op jit(solution)/shard_map/all_to_all | solution.py:305
  28.3 3.9 %copy-start.10 = (pred[8,2]{1,0:T(8,128)(4,1)S(1)}, pred[8,2]{1,0:T(8,128)(4,1)}, u32[]{:S(2)}) copy-start(pred[8,2]{1,0:T(8,128)(4,1)} %copy.78) | copy-start | bytes 52
  32.1 47.1 %copy-start.8 = (s32[12]{0:T(128)S(1)}, s32[12]{0:T(128)}, u32[]{:S(2)}) copy-start(s32[12]{0:T(128)} %get-tuple-element.42) | copy-start | bytes 148
  32.1 47.1 %copy-start.9 = (s32[12,1]{0,1:T(1,128)S(1)}, s32[12,1]{0,1:T(1,128)}, u32[]{:S(2)}) copy-start(s32[12,1]{0,1:T(1,128)} %get-tuple-element.76) | copy-start | bytes 148
  33.6 44.7 %collective-permute-start.4 = (bf16[32,512]{1,0:T(8,128)(2,1)}, bf16[32,512]{1,0:T(8,128)(2,1)S(1)}, u32[]{:S(2)}, u32[]{:S(2)}) collective-permute-start(bf16[32,512]{1,0:T(8,128)(2,1)} %get-tuple-element.73), channel_id=1, source_target_pairs={{0,3},{1,4},{2,5},{3,6},{4,7},{5,0},{6,1},{7,2},{8,11},{9,12},{10,... | collective-permute-start | bytes 98312 | tf_op jit(solution)/shard_map/ppermute | solution.py:46
  35.9 42.4 %collective-permute-start.3 = (bf16[32,512]{1,0:T(8,128)(2,1)S(1)}, bf16[32,512]{1,0:T(8,128)(2,1)S(1)}, u32[]{:S(2)}, u32[]{:S(2)}) collective-permute-start(bf16[32,512]{1,0:T(8,128)(2,1)S(1)} %get-tuple-element.74), channel_id=1, source_target_pairs={{0,2},{1,3},{2,4},{3,5},{4,6},{5,7},{6,0},{7,1},{8,10},{9,11},{10,... | collective-permute-start | bytes 98312 | tf_op jit(solution)/shard_map/ppermute | solution.py:46
  37.1 64.5 %collective-permute-start = (bf16[1,2,64,512]{3,2,1,0:T(8,128)(2,1)S(1)}, bf16[1,2,64,512]{3,2,1,0:T(8,128)(2,1)S(1)}, u32[]{:S(2)}, u32[]{:S(2)}) collective-permute-start(bf16[1,2,64,512]{3,2,1,0:T(8,128)(2,1)S(1)} %get-tuple-element.63), channel_id=1, source_target_pairs={{0,1},{1,2},{2,3},{3,4},{4,5},{5,6},{6,7},{8,9},{9,10},{10,11},{11... | collective-permute-start | bytes 393224 | tf_op jit(solution)/shard_map/ppermute | solution.py:282
  40.2 61.4 %collective-permute-start.1 = (bf16[1,2,64,512]{3,2,1,0:T(8,128)(2,1)S(1)}, bf16[1,2,64,512]{3,2,1,0:T(8,128)(2,1)S(1)}, u32[]{:S(2)}, u32[]{:S(2)}) collective-permute-start(bf16[1,2,64,512]{3,2,1,0:T(8,128)(2,1)S(1)} %get-tuple-element.64), channel_id=1, source_target_pairs={{1,0},{2,1},{3,2},{4,3},{5,4},{6,5},{7,6},{9,8},{10,9},{11,10},{12... | collective-permute-start | bytes 393224 | tf_op jit(solution)/shard_map/ppermute | solution.py:283
  79.1 5.6 %collective-permute-start.9 = (bf16[32,512]{1,0:T(8,128)(2,1)S(1)}, bf16[32,512]{1,0:T(8,128)(2,1)S(1)}, u32[]{:S(2)}, u32[]{:S(2)}) collective-permute-start(bf16[32,512]{1,0:T(8,128)(2,1)S(1)} %get-tuple-element.50), channel_id=1, source_target_pairs={{0,1},{1,2},{2,3},{3,4},{4,5},{5,6},{6,7},{7,0},{8,9},{9,10},{10,1... | collective-permute-start | bytes 98312 | tf_op jit(solution)/shard_map/ppermute | solution.py:54
  79.9 17.6 %collective-permute-start.14 = (bf16[32,512]{1,0:T(8,128)(2,1)S(1)}, bf16[32,512]{1,0:T(8,128)(2,1)S(1)}, u32[]{:S(2)}, u32[]{:S(2)}) collective-permute-start(bf16[32,512]{1,0:T(8,128)(2,1)S(1)} %get-tuple-element.50), channel_id=1, source_target_pairs={{0,6},{1,7},{2,0},{3,1},{4,2},{5,3},{6,4},{7,5},{8,14},{9,15},{10,... | collective-permute-start | bytes 98312 | tf_op jit(solution)/shard_map/ppermute | solution.py:54
  80.7 16.8 %collective-permute-start.13 = (bf16[32,512]{1,0:T(8,128)(2,1)S(1)}, bf16[32,512]{1,0:T(8,128)(2,1)S(1)}, u32[]{:S(2)}, u32[]{:S(2)}) collective-permute-start(bf16[32,512]{1,0:T(8,128)(2,1)S(1)} %get-tuple-element.50), channel_id=1, source_target_pairs={{0,5},{1,6},{2,7},{3,0},{4,1},{5,2},{6,3},{7,4},{8,13},{9,14},{10,... | collective-permute-start | bytes 98312 | tf_op jit(solution)/shard_map/ppermute | solution.py:54
  84.8 4.6 %collective-permute-start.10 = (bf16[32,512]{1,0:T(8,128)(2,1)S(1)}, bf16[32,512]{1,0:T(8,128)(2,1)S(1)}, u32[]{:S(2)}, u32[]{:S(2)}) collective-permute-start(bf16[32,512]{1,0:T(8,128)(2,1)S(1)} %get-tuple-element.50), channel_id=1, source_target_pairs={{0,2},{1,3},{2,4},{3,5},{4,6},{5,7},{6,0},{7,1},{8,10},{9,11},{10,... | collective-permute-start | bytes 98312 | tf_op jit(solution)/shard_map/ppermute | solution.py:54
  89.3 4.6 %collective-permute-start.11 = (bf16[32,512]{1,0:T(8,128)(2,1)S(1)}, bf16[32,512]{1,0:T(8,128)(2,1)S(1)}, u32[]{:S(2)}, u32[]{:S(2)}) collective-permute-start(bf16[32,512]{1,0:T(8,128)(2,1)S(1)} %get-tuple-element.50), channel_id=1, source_target_pairs={{0,3},{1,4},{2,5},{3,6},{4,7},{5,0},{6,1},{7,2},{8,11},{9,12},{10,... | collective-permute-start | bytes 98312 | tf_op jit(solution)/shard_map/ppermute | solution.py:54
  93.9 3.7 %collective-permute-start.12 = (bf16[32,512]{1,0:T(8,128)(2,1)S(1)}, bf16[32,512]{1,0:T(8,128)(2,1)S(1)}, u32[]{:S(2)}, u32[]{:S(2)}) collective-permute-start(bf16[32,512]{1,0:T(8,128)(2,1)S(1)} %get-tuple-element.50), channel_id=1, source_target_pairs={{0,4},{1,5},{2,6},{3,7},{4,0},{5,1},{6,2},{7,3},{8,12},{9,13},{10,... | collective-permute-start | bytes 98312 | tf_op jit(solution)/shard_map/ppermute | solution.py:54
  97.5 2.8 %collective-permute-start.15 = (bf16[32,512]{1,0:T(8,128)(2,1)S(1)}, bf16[32,512]{1,0:T(8,128)(2,1)S(1)}, u32[]{:S(2)}, u32[]{:S(2)}) collective-permute-start(bf16[32,512]{1,0:T(8,128)(2,1)S(1)} %get-tuple-element.50), channel_id=1, source_target_pairs={{0,7},{1,0},{2,1},{3,2},{4,3},{5,4},{6,5},{7,6},{8,15},{9,8},{10,9... | collective-permute-start | bytes 98312 | tf_op jit(solution)/shard_map/ppermute | solution.py:54
  134.0 4.1 %copy-start.7 = (s32[1,2]{1,0:T(1,128)S(1)}, s32[1,2]{1,0:T(1,128)}, u32[]{:S(2)}) copy-start(s32[1,2]{1,0:T(1,128)} %param.16) | copy-start | bytes 28
  134.0 4.6 %copy-start.4 = (f32[2,2,64,512]{3,2,1,0:T(8,128)S(1)}, f32[2,2,64,512]{3,2,1,0:T(8,128)}, u32[]{:S(2)}) copy-start(f32[2,2,64,512]{3,2,1,0:T(8,128)} %get-tuple-element.38) | copy-start | bytes 1572868
  134.0 58.5 %copy-start.3 = (f32[2,2,64,512]{3,2,1,0:T(8,128)S(1)}, f32[2,2,64,512]{3,2,1,0:T(8,128)}, u32[]{:S(2)}) copy-start(f32[2,2,64,512]{3,2,1,0:T(8,128)} %get-tuple-element.37) | copy-start | bytes 1572868
  134.0 108.3 %all-to-all-start.1 = ((bf16[8,256,512]{2,1,0:T(8,128)(2,1)}), bf16[8,256,512]{2,1,0:T(8,128)(2,1)S(1)}, u32[]{:S(2)}, u32[]{:S(2)}) async-start(bf16[8,256,512]{2,1,0:T(8,128)(2,1)} %bitcast.145), calls=%async_computation.1 | async-start | bytes 4194304 | tf_op jit(solution)/shard_map/all_to_all | solution.py:348
  139.3 31.5 %collective-permute-start.19 = (f32[32,512]{1,0:T(8,128)S(1)}, f32[32,512]{1,0:T(8,128)S(1)}, u32[]{:S(2)}, u32[]{:S(2)}) collective-permute-start(f32[32,512]{1,0:T(8,128)S(1)} %get-tuple-element.55), channel_id=1, source_target_pairs={{0,1},{1,2},{2,3},{3,4},{4,5},{5,6},{6,7},{7,0},{8,9},{9,10},{10,1... | collective-permute-start | bytes 196616 | tf_op jit(solution)/shard_map/ppermute | solution.py:46
  140.7 49.1 %collective-permute-start.25 = (f32[32,512]{1,0:T(8,128)S(1)}, f32[32,512]{1,0:T(8,128)S(1)}, u32[]{:S(2)}, u32[]{:S(2)}) collective-permute-start(f32[32,512]{1,0:T(8,128)S(1)} %get-tuple-element.56), channel_id=1, source_target_pairs={{0,7},{1,0},{2,1},{3,2},{4,3},{5,4},{6,5},{7,6},{8,15},{9,8},{10,9... | collective-permute-start | bytes 196616 | tf_op jit(solution)/shard_map/ppermute | solution.py:46
  144.0 48.5 %collective-permute-start.24 = (f32[32,512]{1,0:T(8,128)}, f32[32,512]{1,0:T(8,128)S(1)}, u32[]{:S(2)}, u32[]{:S(2)}) collective-permute-start(f32[32,512]{1,0:T(8,128)} %get-tuple-element.57), channel_id=1, source_target_pairs={{0,6},{1,7},{2,0},{3,1},{4,2},{5,3},{6,4},{7,5},{8,14},{9,15},{10,... | collective-permute-start | bytes 196616 | tf_op jit(solution)/shard_map/ppermute | solution.py:46
  145.4 52.2 %collective-permute-start.23 = (f32[32,512]{1,0:T(8,128)}, f32[32,512]{1,0:T(8,128)S(1)}, u32[]{:S(2)}, u32[]{:S(2)}) collective-permute-start(f32[32,512]{1,0:T(8,128)} %get-tuple-element.58), channel_id=1, source_target_pairs={{0,5},{1,6},{2,7},{3,0},{4,1},{5,2},{6,3},{7,4},{8,13},{9,14},{10,... | collective-permute-start | bytes 196616 | tf_op jit(solution)/shard_map/ppermute | solution.py:46
  145.4 52.2 %collective-permute-start.22 = (f32[32,512]{1,0:T(8,128)}, f32[32,512]{1,0:T(8,128)S(1)}, u32[]{:S(2)}, u32[]{:S(2)}) collective-permute-start(f32[32,512]{1,0:T(8,128)} %get-tuple-element.59), channel_id=1, source_target_pairs={{0,4},{1,5},{2,6},{3,7},{4,0},{5,1},{6,2},{7,3},{8,12},{9,13},{10,... | collective-permute-start | bytes 196616 | tf_op jit(solution)/shard_map/ppermute | solution.py:46
  170.8 26.9 %collective-permute-start.21 = (f32[32,512]{1,0:T(8,128)}, f32[32,512]{1,0:T(8,128)S(1)}, u32[]{:S(2)}, u32[]{:S(2)}) collective-permute-start(f32[32,512]{1,0:T(8,128)} %get-tuple-element.60), channel_id=1, source_target_pairs={{0,3},{1,4},{2,5},{3,6},{4,7},{5,0},{6,1},{7,2},{8,11},{9,12},{10,... | collective-permute-start | bytes 196616 | tf_op jit(solution)/shard_map/ppermute | solution.py:46
  189.8 7.8 %collective-permute-start.20 = (f32[32,512]{1,0:T(8,128)}, f32[32,512]{1,0:T(8,128)}, u32[]{:S(2)}, u32[]{:S(2)}) collective-permute-start(f32[32,512]{1,0:T(8,128)} %get-tuple-element.61), channel_id=1, source_target_pairs={{0,2},{1,3},{2,4},{3,5},{4,6},{5,7},{6,0},{7,1},{8,10},{9,11},{10,... | collective-permute-start | bytes 196616 | tf_op jit(solution)/shard_map/ppermute | solution.py:46
  190.5 46.1 %copy-start.11 = (pred[2]{0:T(512)(128)(4,1)S(1)}, pred[2]{0:T(512)(128)(4,1)}, u32[]{:S(2)}) copy-start(pred[2]{0:T(512)(128)(4,1)} %fusion.47) | copy-start | bytes 10
  192.5 46.7 %collective-permute-start.16 = (bf16[1,256,4096]{2,1,0:T(8,128)(2,1)}, bf16[1,256,4096]{2,1,0:T(8,128)(2,1)}, u32[]{:S(2)}, u32[]{:S(2)}) collective-permute-start(bf16[1,256,4096]{2,1,0:T(8,128)(2,1)} %bitcast.171), channel_id=1, source_target_pairs={{8,0},{16,8},{24,16},{0,24},{9,1},{17,9},{25,17},{1,25},{10,2},{18... | collective-permute-start | bytes 6291464 | tf_op jit(solution)/shard_map/ppermute | solution.py:37
  198.5 13.6 %collective-permute-start.26 = (f32[32,512]{1,0:T(8,128)S(1)}, f32[32,512]{1,0:T(8,128)S(1)}, u32[]{:S(2)}, u32[]{:S(2)}) collective-permute-start(f32[32,512]{1,0:T(8,128)S(1)} %get-tuple-element.44), channel_id=1, source_target_pairs={{0,1},{1,2},{2,3},{3,4},{4,5},{5,6},{6,7},{7,0},{8,9},{9,10},{10,1... | collective-permute-start | bytes 196616 | tf_op jit(solution)/shard_map/ppermute | solution.py:54
  202.4 41.6 %collective-permute-start.18 = (bf16[1,2,64,512]{3,2,1,0:T(8,128)(2,1)S(1)}, bf16[1,2,64,512]{3,2,1,0:T(8,128)(2,1)S(1)}, u32[]{:S(2)}, u32[]{:S(2)}) collective-permute-start(bf16[1,2,64,512]{3,2,1,0:T(8,128)(2,1)S(1)} %get-tuple-element.66), channel_id=1, source_target_pairs={{0,1},{1,2},{2,3},{3,4},{4,5},{5,6},{6,7},{8,9},{9,10},{10,11},{11... | collective-permute-start | bytes 393224 | tf_op jit(solution)/shard_map/ppermute | solution.py:329
  204.6 39.4 %collective-permute-start.17 = (bf16[1,2,64,512]{3,2,1,0:T(8,128)(2,1)}, bf16[1,2,64,512]{3,2,1,0:T(8,128)(2,1)S(1)}, u32[]{:S(2)}, u32[]{:S(2)}) collective-permute-start(bf16[1,2,64,512]{3,2,1,0:T(8,128)(2,1)} %get-tuple-element.67), channel_id=1, source_target_pairs={{1,0},{2,1},{3,2},{4,3},{5,4},{6,5},{7,6},{9,8},{10,9},{11,10},{12... | collective-permute-start | bytes 393224 | tf_op jit(solution)/shard_map/ppermute | solution.py:328
  205.9 26.3 %collective-permute-start.31 = (f32[32,512]{1,0:T(8,128)S(1)}, f32[32,512]{1,0:T(8,128)S(1)}, u32[]{:S(2)}, u32[]{:S(2)}) collective-permute-start(f32[32,512]{1,0:T(8,128)S(1)} %get-tuple-element.44), channel_id=1, source_target_pairs={{0,6},{1,7},{2,0},{3,1},{4,2},{5,3},{6,4},{7,5},{8,14},{9,15},{10,... | collective-permute-start | bytes 196616 | tf_op jit(solution)/shard_map/ppermute | solution.py:54
  212.2 5.6 %collective-permute-start.27 = (f32[32,512]{1,0:T(8,128)S(1)}, f32[32,512]{1,0:T(8,128)S(1)}, u32[]{:S(2)}, u32[]{:S(2)}) collective-permute-start(f32[32,512]{1,0:T(8,128)S(1)} %get-tuple-element.44), channel_id=1, source_target_pairs={{0,2},{1,3},{2,4},{3,5},{4,6},{5,7},{6,0},{7,1},{8,10},{9,11},{10,... | collective-permute-start | bytes 196616 | tf_op jit(solution)/shard_map/ppermute | solution.py:54
  217.8 5.6 %collective-permute-start.28 = (f32[32,512]{1,0:T(8,128)S(1)}, f32[32,512]{1,0:T(8,128)S(1)}, u32[]{:S(2)}, u32[]{:S(2)}) collective-permute-start(f32[32,512]{1,0:T(8,128)S(1)} %get-tuple-element.44), channel_id=1, source_target_pairs={{0,3},{1,4},{2,5},{3,6},{4,7},{5,0},{6,1},{7,2},{8,11},{9,12},{10,... | collective-permute-start | bytes 196616 | tf_op jit(solution)/shard_map/ppermute | solution.py:54
  223.4 4.0 %collective-permute-start.29 = (f32[32,512]{1,0:T(8,128)S(1)}, f32[32,512]{1,0:T(8,128)S(1)}, u32[]{:S(2)}, u32[]{:S(2)}) collective-permute-start(f32[32,512]{1,0:T(8,128)S(1)} %get-tuple-element.44), channel_id=1, source_target_pairs={{0,4},{1,5},{2,6},{3,7},{4,0},{5,1},{6,2},{7,3},{8,12},{9,13},{10,... | collective-permute-start | bytes 196616 | tf_op jit(solution)/shard_map/ppermute | solution.py:54
  227.4 4.7 %collective-permute-start.30 = (f32[32,512]{1,0:T(8,128)S(1)}, f32[32,512]{1,0:T(8,128)S(1)}, u32[]{:S(2)}, u32[]{:S(2)}) collective-permute-start(f32[32,512]{1,0:T(8,128)S(1)} %get-tuple-element.44), channel_id=1, source_target_pairs={{0,5},{1,6},{2,7},{3,0},{4,1},{5,2},{6,3},{7,4},{8,13},{9,14},{10,... | collective-permute-start | bytes 196616 | tf_op jit(solution)/shard_map/ppermute | solution.py:54
  232.1 3.1 %collective-permute-start.32 = (f32[32,512]{1,0:T(8,128)S(1)}, f32[32,512]{1,0:T(8,128)S(1)}, u32[]{:S(2)}, u32[]{:S(2)}) collective-permute-start(f32[32,512]{1,0:T(8,128)S(1)} %get-tuple-element.44), channel_id=1, source_target_pairs={{0,7},{1,0},{2,1},{3,2},{4,3},{5,4},{6,5},{7,6},{8,15},{9,8},{10,9... | collective-permute-start | bytes 196616 | tf_op jit(solution)/shard_map/ppermute | solution.py:54
  244.6 13.8 %collective-permute-start.33 = (bf16[256,1024]{1,0:T(8,128)(2,1)S(1)}, bf16[256,1024]{1,0:T(8,128)(2,1)S(1)}, u32[]{:S(2)}, u32[]{:S(2)}) collective-permute-start(bf16[256,1024]{1,0:T(8,128)(2,1)S(1)} %pad_maximum_fusion.2), channel_id=1, source_target_pairs={{8,0},{16,8},{24,16},{0,24},{9,1},{17,9},{25,17},{1,25},{10,2},{18... | collective-permute-start | bytes 1572872 | tf_op jit(solution)/shard_map/ppermute | solution.py:37
  (1 other events, 1.3 us)

commit v15 on v13

--- a/solution.py
+++ b/solution.py
@@ -56,10 +56,10 @@
 
 def attention_kernel(ids_ref, q_ref, g_ref, *refs):
     del ids_ref
-    ntiles = len(refs) - 6
+    ntiles = len(refs) - 7
     tile_refs = refs[:ntiles]
     live_ref = refs[ntiles]
-    dq_ref, own_ref, edge_ref, glob_ref, rand_ref = refs[ntiles + 1 :]
+    dq_ref, own_ref, edge_ref, glob_out, rand_ref, glob_ref = refs[ntiles + 1 :]
     nblocks = own_ref.shape[0]
     block_len, width = q_ref.shape
     group = width // HDIM
@@ -115,7 +115,7 @@
     def _():
         own_ref[...] = jnp.zeros_like(own_ref)
         glob_ref[...] = jnp.zeros_like(glob_ref)
-        edge_ref[0] = terms[0]
+        edge_ref[0] = terms[0].astype(edge_ref.dtype)
 
     @pl.when(b > 0)
     def _():
@@ -131,9 +131,13 @@
 
     @pl.when(b == nblocks - 1)
     def _():
-        edge_ref[1] = terms[2]
+        edge_ref[1] = terms[2].astype(edge_ref.dtype)
 
     glob_ref[...] = glob_ref[...] + terms[3:near]
+
+    @pl.when(b == nblocks - 1)
+    def _():
+        glob_out[...] = glob_ref[...].astype(glob_out.dtype)
     rand_ref[...] = terms[near:].astype(rand_ref.dtype)
 
 
@@ -174,6 +178,7 @@
         grid=(heads_kv, nblocks),
         in_specs=[row_spec, row_spec, *tile_specs, live_spec],
         out_specs=[row_spec, own_spec, edge_spec, glob_spec, rand_spec],
+        scratch_shapes=[pltpu.VMEM((GLOB, 2, block_len, HDIM), jnp.float32)],
     )
     outs = pl.pallas_call(
         attention_kernel,
@@ -181,8 +186,8 @@
         out_shape=[
             jax.ShapeDtypeStruct((shard_tokens, qwidth), jnp.bfloat16),
             jax.ShapeDtypeStruct((nblocks, 2, block_len, kwidth), jnp.float32),
-            jax.ShapeDtypeStruct((2, 2, block_len, kwidth), jnp.float32),
-            jax.ShapeDtypeStruct((GLOB, 2, block_len, kwidth), jnp.float32),
+            jax.ShapeDtypeStruct((2, 2, block_len, kwidth), jnp.bfloat16),
+            jax.ShapeDtypeStruct((GLOB, 2, block_len, kwidth), jnp.bfloat16),
             jax.ShapeDtypeStruct((nblocks, nrand, 2, block_len, kwidth), jnp.bfloat16),
         ],
         compiler_params=pltpu.CompilerParams(

time: 201 us -> 200 us (level)
  transfers between devices with their start and end apart: 10 -> 10, of which waited for: 6 -> 6; matrix products, arithmetic and copies ran while one was open for 8% -> 7% of each run, Pallas kernels for 2% -> 2%
where the time goes in v15:
time: 200 us; the launch traced here: 199 us
  waiting for transfers between devices  100 us (50%)
  starting transfers between devices  36.1 us (18%)
  Pallas kernels  31.5 us (16%)
  local copies, waits for them, and re-layouts  15.5 us (8%)
  other arithmetic  13.4 us (7%)
    all_to_all x1, waiting for transfers between devices, body(): received = lax.all_to_all(payload, 'seq', 0, 0, tiled=True)  42.9 us
    pallas_call x1, Pallas kernels, block_backward(): pl.pallas_call(attention_kernel, grid_spec=grid_spec, out_shape=[jax.Shap...  28.4 us
    ppermute x2, waiting for transfers between devices, from_behind(): return lax.ppermute(block, axis, route)  28 us
    all_to_all x1, waiting for transfers between devices, body(): lax.all_to_all(jnp.take(term_units, back_idx.reshape(-1), axis=0, mode='c...  21.7 us
    all_to_all x1, starting transfers between devices, body(): received = lax.all_to_all(payload, 'seq', 0, 0, tiled=True)  6.5 us
    all_to_all x1, starting transfers between devices, body(): lax.all_to_all(jnp.broadcast_to(global_sum[None], (shards,) + global_sum....  5.6 us
    ppermute x2, starting transfers between devices, from_behind(): return lax.ppermute(block, axis, route)  5.04 us
    all_to_all x1, waiting for transfers between devices, body(): lax.all_to_all(jnp.broadcast_to(global_sum[None], (shards,) + global_sum....  5.03 us
  transfers between devices with their start and end apart: 10, of which 6 were waited for; matrix products, arithmetic and copies ran while one was open for 7% of the time, Pallas kernels for 2%

profile of v15, /device:TPU:1, one launch (start us, length us, event | category | flops | bytes accessed | tf_op | source)
XLA Modules:
  0.0 199.5 jit_solution(11477044050890775059)
XLA Ops:
  0.7 1.3 broadcast_multiply_fusion.2
  1.9 0.7 fusion.29
  2.6 0.8 copy.73
  3.5 0.5 fusion.30
  4.1 0.3 convert_reduce_fusion
  4.4 0.8 dynamic-slice_reduce_fusion
  6.3 1.1 pad_maximum_fusion.1
  7.4 2.3 %gather_fusion = bf16[72,32,512]{2,1,0:T(8,128)(2,1)} fusion(bf16[17,32,512]{2,1,0:T(8,128)(2,1)S(1)} %concatenate.44, s32[1024]{0:T(1024)S(1)} %pad_clamp_fusion.1), kind=kCustom, calls=%fused_computation | custom fusion | bytes 4718880 | tf_op jit(solution)/shard_map/jit(_take)/gather | solution.py:291
  9.8 6.5 %all-to-all-start = ((bf16[8,288,512]{2,1,0:T(8,128)(2,1)}), bf16[8,288,512]{2,1,0:T(8,128)(2,1)}, u32[]{:S(2)}, u32[]{:S(2)}) async-start(bf16[8,288,512]{2,1,0:T(8,128)(2,1)} %bitcast.11), calls=%async_computation | async-start | bytes 4718592 | tf_op jit(solution)/shard_map/all_to_all | solution.py:294
  16.3 0.7 fusion.9
  17.0 3.4 %collective-permute-start = (bf16[1,2,64,512]{3,2,1,0:T(8,128)(2,1)}, bf16[1,2,64,512]{3,2,1,0:T(8,128)(2,1)S(1)}, u32[]{:S(2)}, u32[]{:S(2)}) collective-permute-start(bf16[1,2,64,512]{3,2,1,0:T(8,128)(2,1)} %get-tuple-element.53), channel_id=1, source_target_pairs={{0,1},{1,2},{2,3},{3,4},{4,5},{5,6},{6,7},{8,9},{9,10},{10,11},{11... | collective-permute-start | bytes 393224 | tf_op jit(solution)/shard_map/ppermute | solution.py:266
  20.3 1.3 collective-permute-start.1
  21.8 0.7 add.249
  22.8 1.1 and.202
  24.1 1.0 add.261
  25.1 0.2 select_reduce_fusion
  25.4 1.0 lt.86
  26.4 42.9 %all-to-all-done.refs_5_.refs_6_.refs_7_ = bf16[8,288,512]{2,1,0:T(8,128)(2,1)} async-done(((bf16[8,288,512]{2,1,0:T(8,128)(2,1)}), bf16[8,288,512]{2,1,0:T(8,128)(2,1)}, u32[]{:S(2)}, u32[]{:S(2)}) %all-to-all-start) | async-done | bytes 2359328 | tf_op jit(solution)/shard_map/all_to_all | solution.py:294
  69.4 1.0 slice_reduce_fusion.1
  70.4 0.7 broadcast_in_dim.75
  71.1 4.7 %all-to-all-start.1 = ((bf16[8,32,512]{2,1,0:T(8,128)(2,1)}), bf16[8,32,512]{2,1,0:T(8,128)(2,1)S(1)}, u32[]{:S(2)}, u32[]{:S(2)}) async-start(bf16[8,32,512]{2,1,0:T(8,128)(2,1)} %broadcast_in_dim.75), calls=%async_computation.1 | async-start | bytes 524288 | tf_op jit(solution)/shard_map/all_to_all | solution.py:296
  75.8 1.9 fusion.4.refs_8_
  77.7 0.7 pad_add_fusion.3
  78.4 0.6 reshape.666.ids_ref
  79.3 1.0 pad_maximum_fusion
  80.3 2.5 %all-to-all-done.1 = bf16[8,32,512]{2,1,0:T(8,128)(2,1)S(1)} async-done(((bf16[8,32,512]{2,1,0:T(8,128)(2,1)}), bf16[8,32,512]{2,1,0:T(8,128)(2,1)S(1)}, u32[]{:S(2)}, u32[]{:S(2)}) %all-to-all-start.1) | async-done | bytes 262176 | tf_op jit(solution)/shard_map/all_to_all | solution.py:296
  82.9 0.7 copy-done.3
  83.6 28.4 %shard_map.94 = (bf16[256,4096]{1,0:T(8,128)(2,1)}, f32[4,2,64,512]{3,2,1,0:T(8,128)}, bf16[2,2,64,512]{3,2,1,0:T(8,128)(2,1)}, bf16[2,2,64,512]{3,2,1,0:T(8,128)(2,1)}, bf16[4,3,2,64,512]{4,3,2,1,0:T(8,128)(2,1)}) custom-call(s32[24]{0:T(128)} %reshape.666.ids_ref, bf16[256,4096]{1,0:T(8,128)(2,1)} %bitcast.80, bf16[256,4096]{1,0:T(8,128)(2,1)} %bitcast.81, ...), custom_call_target="tpu_custom_call" | custom-call | flops 6442450944 | bytes 12582912 | tf_op jit(solution)/shard_map/pallas_call | solution.py:183
  112.0 1.7 maximum_maximum_fusion
  113.8 2.3 %gather_fusion.1 = bf16[72,32,512]{2,1,0:T(8,128)(2,1)} fusion(bf16[57,32,512]{2,1,0:T(8,128)(2,1)S(1)} %maximum_maximum_fusion, s32[1024]{0:T(1024)S(1)} %pad_clamp_fusion), kind=kCustom, calls=%fused_computation.1 | custom fusion | bytes 4718880 | tf_op jit(solution)/shard_map/jit(_take)/gather | solution.py:344
  116.1 4.8 %all-to-all-start.2 = ((bf16[8,288,512]{2,1,0:T(8,128)(2,1)}), bf16[8,288,512]{2,1,0:T(8,128)(2,1)S(1)}, u32[]{:S(2)}, u32[]{:S(2)}) async-start(bf16[8,288,512]{2,1,0:T(8,128)(2,1)} %bitcast.55), calls=%async_computation.2 | async-start | bytes 4718592 | tf_op jit(solution)/shard_map/all_to_all | solution.py:343
  120.9 2.0 collective-permute-start.2
  123.4 3.5 %collective-permute-start.4 = (bf16[1,2,64,512]{3,2,1,0:T(8,128)(2,1)S(1)}, bf16[1,2,64,512]{3,2,1,0:T(8,128)(2,1)S(1)}, u32[]{:S(2)}, u32[]{:S(2)}) collective-permute-start(bf16[1,2,64,512]{3,2,1,0:T(8,128)(2,1)S(1)} %get-tuple-element.55), channel_id=1, source_target_pairs={{0,1},{1,2},{2,3},{3,4},{4,5},{5,6},{6,7},{8,9},{9,10},{10,11},{11... | collective-permute-start | bytes 393224 | tf_op jit(solution)/shard_map/ppermute | solution.py:320
  126.9 1.3 collective-permute-start.3
  128.2 20.0 %collective-permute-done.2.src_ref = bf16[1,256,4096]{2,1,0:T(8,128)(2,1)} collective-permute-done((bf16[1,256,4096]{2,1,0:T(8,128)(2,1)}, bf16[1,256,4096]{2,1,0:T(8,128)(2,1)}, u32[]{:S(2)}, u32[]{:S(2)}) %collective-permute-start.2) | collective-permute-done | bytes 2097184 | tf_op jit(solution)/shard_map/ppermute | solution.py:37
  148.2 3.0 %shard_map.95 = bf16[1,256,4096]{2,1,0:T(8,128)(2,1)} custom-call(bf16[1,256,4096]{2,1,0:T(8,128)(2,1)} %collective-permute-done.2.src_ref), custom_call_target="tpu_custom_call" | custom-call | bytes 4194304 | tf_op jit(solution)/shard_map/pallas_call | solution.py:47
  151.3 21.7 %all-to-all-done.2 = bf16[8,288,512]{2,1,0:T(8,128)(2,1)S(1)} async-done(((bf16[8,288,512]{2,1,0:T(8,128)(2,1)}), bf16[8,288,512]{2,1,0:T(8,128)(2,1)S(1)}, u32[]{:S(2)}, u32[]{:S(2)}) %all-to-all-start.2) | async-done | bytes 2359328 | tf_op jit(solution)/shard_map/all_to_all | solution.py:343
  173.0 0.7 broadcast_in_dim.130
  173.7 5.6 %all-to-all-start.3 = ((bf16[8,32,512]{2,1,0:T(8,128)(2,1)}), bf16[8,32,512]{2,1,0:T(8,128)(2,1)S(1)}, u32[]{:S(2)}, u32[]{:S(2)}) async-start(bf16[8,32,512]{2,1,0:T(8,128)(2,1)} %broadcast_in_dim.130), calls=%async_computation.3 | async-start | bytes 524288 | tf_op jit(solution)/shard_map/all_to_all | solution.py:353
  179.3 0.2 slice.111
  179.6 1.3 fusion
  180.9 0.4 copy_add_fusion.1
  181.4 5.0 %all-to-all-done.3 = bf16[8,32,512]{2,1,0:T(8,128)(2,1)S(1)} async-done(((bf16[8,32,512]{2,1,0:T(8,128)(2,1)}), bf16[8,32,512]{2,1,0:T(8,128)(2,1)S(1)}, u32[]{:S(2)}, u32[]{:S(2)}) %all-to-all-start.3) | async-done | bytes 262176 | tf_op jit(solution)/shard_map/all_to_all | solution.py:353
  186.4 0.6 fusion.7
  187.0 0.5 fusion.2
  187.6 3.1 %collective-permute-start.5 = (bf16[256,1024]{1,0:T(8,128)(2,1)S(1)}, bf16[256,1024]{1,0:T(8,128)(2,1)S(1)}, u32[]{:S(2)}, u32[]{:S(2)}) collective-permute-start(bf16[256,1024]{1,0:T(8,128)(2,1)S(1)} %pad_maximum_fusion.2), channel_id=1, source_target_pairs={{8,0},{16,8},{24,16},{0,24},{9,1},{17,9},{25,17},{1,25},{10,2},{18... | collective-permute-start | bytes 1572872 | tf_op jit(solution)/shard_map/ppermute | solution.py:37
  190.7 8.0 %collective-permute-done.5 = bf16[256,1024]{1,0:T(8,128)(2,1)S(1)} collective-permute-done((bf16[256,1024]{1,0:T(8,128)(2,1)S(1)}, bf16[256,1024]{1,0:T(8,128)(2,1)S(1)}, u32[]{:S(2)}, u32[]{:S(2)}) %collective-permute-start.5) | collective-permute-done | bytes 524320 | tf_op jit(solution)/shard_map/ppermute | solution.py:37
  198.7 0.8 slice_bitcast_fusion
  (88 shorter events, 3.2 us)
Async XLA Ops:
  2.6 4.8 %copy-start.8 = (pred[2]{0:T(512)(128)(4,1)}, pred[2]{0:T(512)(128)(4,1)S(1)}, u32[]{:S(2)}) copy-start(pred[2]{0:T(512)(128)(4,1)S(1)} %fusion.29) | copy-start | bytes 10
  3.5 2.7 %copy-start.5 = (pred[8,12]{1,0:T(8,128)(4,1)}, pred[8,12]{1,0:T(8,128)(4,1)S(1)}, u32[]{:S(2)}) copy-start(pred[8,12]{1,0:T(8,128)(4,1)S(1)} %get-tuple-element.45) | copy-start | bytes 292
  9.8 6.5 %copy-start = (bf16[1,256,512]{2,1,0:T(8,128)(2,1)S(1)}, bf16[1,256,512]{2,1,0:T(8,128)(2,1)}, u32[]{:S(2)}) copy-start(bf16[1,256,512]{2,1,0:T(8,128)(2,1)} %param.12) | copy-start | bytes 786436
  9.8 6.5 %copy-start.1 = (bf16[1,256,512]{2,1,0:T(8,128)(2,1)S(1)}, bf16[1,256,512]{2,1,0:T(8,128)(2,1)}, u32[]{:S(2)}) copy-start(bf16[1,256,512]{2,1,0:T(8,128)(2,1)} %param.13) | copy-start | bytes 786436
  9.8 11.9 %copy-start.7 = (s32[1,32,3]{1,0,2:T(1,128)S(1)}, s32[1,32,3]{1,0,2:T(1,128)}, u32[]{:S(2)}) copy-start(s32[1,32,3]{1,0,2:T(1,128)} %param.15) | copy-start | bytes 1156
  9.8 11.9 %copy-start.12 = (s32[1,2]{1,0:T(1,128)S(1)}, s32[1,2]{1,0:T(1,128)}, u32[]{:S(2)}) copy-start(s32[1,2]{1,0:T(1,128)} %param.16) | copy-start | bytes 28
  9.8 59.6 %all-to-all-start = ((bf16[8,288,512]{2,1,0:T(8,128)(2,1)}), bf16[8,288,512]{2,1,0:T(8,128)(2,1)}, u32[]{:S(2)}, u32[]{:S(2)}) async-start(bf16[8,288,512]{2,1,0:T(8,128)(2,1)} %bitcast.11), calls=%async_computation | async-start | bytes 4718592 | tf_op jit(solution)/shard_map/all_to_all | solution.py:294
  16.3 8.8 %copy-start.11 = (s32[1,8]{1,0:T(1,128)S(1)}, s32[1,8]{1,0:T(1,128)}, u32[]{:S(2)}) copy-start(s32[1,8]{1,0:T(1,128)} %param.17) | copy-start | bytes 100
  17.0 62.3 %collective-permute-start = (bf16[1,2,64,512]{3,2,1,0:T(8,128)(2,1)}, bf16[1,2,64,512]{3,2,1,0:T(8,128)(2,1)S(1)}, u32[]{:S(2)}, u32[]{:S(2)}) collective-permute-start(bf16[1,2,64,512]{3,2,1,0:T(8,128)(2,1)} %get-tuple-element.53), channel_id=1, source_target_pairs={{0,1},{1,2},{2,3},{3,4},{4,5},{5,6},{6,7},{8,9},{9,10},{10,11},{11... | collective-permute-start | bytes 393224 | tf_op jit(solution)/shard_map/ppermute | solution.py:266
  20.3 59.0 %collective-permute-start.1 = (bf16[1,2,64,512]{3,2,1,0:T(8,128)(2,1)S(1)}, bf16[1,2,64,512]{3,2,1,0:T(8,128)(2,1)S(1)}, u32[]{:S(2)}, u32[]{:S(2)}) collective-permute-start(bf16[1,2,64,512]{3,2,1,0:T(8,128)(2,1)S(1)} %get-tuple-element.54), channel_id=1, source_target_pairs={{1,0},{2,1},{3,2},{4,3},{5,4},{6,5},{7,6},{9,8},{10,9},{11,10},{12... | collective-permute-start | bytes 393224 | tf_op jit(solution)/shard_map/ppermute | solution.py:267
  71.1 11.8 %all-to-all-start.1 = ((bf16[8,32,512]{2,1,0:T(8,128)(2,1)}), bf16[8,32,512]{2,1,0:T(8,128)(2,1)S(1)}, u32[]{:S(2)}, u32[]{:S(2)}) async-start(bf16[8,32,512]{2,1,0:T(8,128)(2,1)} %broadcast_in_dim.75), calls=%async_computation.1 | async-start | bytes 524288 | tf_op jit(solution)/shard_map/all_to_all | solution.py:296
  82.9 0.7 copy-start.3
  116.0 6.9 %copy-start.6 = (pred[8,12]{1,0:T(8,128)(4,1)S(1)}, pred[8,12]{1,0:T(8,128)(4,1)}, u32[]{:S(2)}) copy-start(pred[8,12]{1,0:T(8,128)(4,1)} %copy-done.5) | copy-start | bytes 292
  116.1 7.3 %copy-start.4 = (bf16[2,2,64,512]{3,2,1,0:T(8,128)(2,1)S(1)}, bf16[2,2,64,512]{3,2,1,0:T(8,128)(2,1)}, u32[]{:S(2)}) copy-start(bf16[2,2,64,512]{3,2,1,0:T(8,128)(2,1)} %get-tuple-element.38) | copy-start | bytes 786436
  116.1 56.9 %all-to-all-start.2 = ((bf16[8,288,512]{2,1,0:T(8,128)(2,1)}), bf16[8,288,512]{2,1,0:T(8,128)(2,1)S(1)}, u32[]{:S(2)}, u32[]{:S(2)}) async-start(bf16[8,288,512]{2,1,0:T(8,128)(2,1)} %bitcast.55), calls=%async_computation.2 | async-start | bytes 4718592 | tf_op jit(solution)/shard_map/all_to_all | solution.py:343
  120.9 27.3 %collective-permute-start.2 = (bf16[1,256,4096]{2,1,0:T(8,128)(2,1)}, bf16[1,256,4096]{2,1,0:T(8,128)(2,1)}, u32[]{:S(2)}, u32[]{:S(2)}) collective-permute-start(bf16[1,256,4096]{2,1,0:T(8,128)(2,1)} %bitcast.82), channel_id=1, source_target_pairs={{8,0},{16,8},{24,16},{0,24},{9,1},{17,9},{25,17},{1,25},{10,2},{18... | collective-permute-start | bytes 6291464 | tf_op jit(solution)/shard_map/ppermute | solution.py:37
  123.4 57.9 %collective-permute-start.4 = (bf16[1,2,64,512]{3,2,1,0:T(8,128)(2,1)S(1)}, bf16[1,2,64,512]{3,2,1,0:T(8,128)(2,1)S(1)}, u32[]{:S(2)}, u32[]{:S(2)}) collective-permute-start(bf16[1,2,64,512]{3,2,1,0:T(8,128)(2,1)S(1)} %get-tuple-element.55), channel_id=1, source_target_pairs={{0,1},{1,2},{2,3},{3,4},{4,5},{5,6},{6,7},{8,9},{9,10},{10,11},{11... | collective-permute-start | bytes 393224 | tf_op jit(solution)/shard_map/ppermute | solution.py:320
  126.9 54.3 %collective-permute-start.3 = (bf16[1,2,64,512]{3,2,1,0:T(8,128)(2,1)S(1)}, bf16[1,2,64,512]{3,2,1,0:T(8,128)(2,1)S(1)}, u32[]{:S(2)}, u32[]{:S(2)}) collective-permute-start(bf16[1,2,64,512]{3,2,1,0:T(8,128)(2,1)S(1)} %get-tuple-element.56), channel_id=1, source_target_pairs={{1,0},{2,1},{3,2},{4,3},{5,4},{6,5},{7,6},{9,8},{10,9},{11,10},{12... | collective-permute-start | bytes 393224 | tf_op jit(solution)/shard_map/ppermute | solution.py:319
  173.7 12.7 %all-to-all-start.3 = ((bf16[8,32,512]{2,1,0:T(8,128)(2,1)}), bf16[8,32,512]{2,1,0:T(8,128)(2,1)S(1)}, u32[]{:S(2)}, u32[]{:S(2)}) async-start(bf16[8,32,512]{2,1,0:T(8,128)(2,1)} %broadcast_in_dim.130), calls=%async_computation.3 | async-start | bytes 524288 | tf_op jit(solution)/shard_map/all_to_all | solution.py:353
  179.5 1.3 copy-start.2
  180.9 5.6 %copy-start.9 = (pred[2]{0:T(512)(128)(4,1)S(1)}, pred[2]{0:T(512)(128)(4,1)}, u32[]{:S(2)}) copy-start(pred[2]{0:T(512)(128)(4,1)} %copy-done.8) | copy-start | bytes 10
  180.9 5.6 %copy-start.10 = (s32[2]{0:T(128)S(1)}, s32[2]{0:T(128)}, u32[]{:S(2)}) copy-start(s32[2]{0:T(128)} %get-tuple-element.48) | copy-start | bytes 28
  187.6 11.0 %collective-permute-start.5 = (bf16[256,1024]{1,0:T(8,128)(2,1)S(1)}, bf16[256,1024]{1,0:T(8,128)(2,1)S(1)}, u32[]{:S(2)}, u32[]{:S(2)}) collective-permute-start(bf16[256,1024]{1,0:T(8,128)(2,1)S(1)} %pad_maximum_fusion.2), channel_id=1, source_target_pairs={{8,0},{16,8},{24,16},{0,24},{9,1},{17,9},{25,17},{1,25},{10,2},{18... | collective-permute-start | bytes 1572872 | tf_op jit(solution)/shard_map/ppermute | solution.py:37

commit v16 on v15

--- a/solution.py
+++ b/solution.py
@@ -369,19 +369,13 @@
     kv_sum = kv_sum + jnp.einsum(
         "gq,gxsk->qxsk", global_pick, global_total, precision=lax.Precision.HIGHEST
     )
-    kv_grad = jnp.concatenate(
-        [
-            kv_sum[:, 0].reshape(shard_tokens, kwidth).astype(jnp.bfloat16),
-            kv_sum[:, 1].reshape(shard_tokens, kwidth).astype(jnp.bfloat16),
-        ],
-        axis=-1,
-    )
+    kv_grad = kv_sum.astype(jnp.bfloat16)
     handed_query, kv_grad = lax.optimization_barrier((fresh_copy(handed_query), kv_grad))
     handed_kv = from_behind(kv_grad, "section", -1)
     return (
         handed_query,
-        handed_kv[None, :, :kwidth],
-        handed_kv[None, :, kwidth:],
+        handed_kv[:, 0].reshape(1, shard_tokens, kwidth),
+        handed_kv[:, 1].reshape(1, shard_tokens, kwidth),
     )
 
 

time: 200 us -> 200 us (level)
  transfers between devices with their start and end apart: 10 -> 10, of which waited for: 6 -> 6; matrix products, arithmetic and copies ran while one was open for 7% -> 8% of each run, Pallas kernels for 2% -> 2%
where the time goes in v16:
time: 200 us; the launch traced here: 199 us
  waiting for transfers between devices  100 us (50%)
  starting transfers between devices  36.1 us (18%)
  Pallas kernels  31.5 us (16%)
  local copies, waits for them, and re-layouts  15.5 us (8%)
  other arithmetic  13.3 us (7%)
    all_to_all x1, waiting for transfers between devices, body(): received = lax.all_to_all(payload, 'seq', 0, 0, tiled=True)  42.9 us
    pallas_call x1, Pallas kernels, block_backward(): pl.pallas_call(attention_kernel, grid_spec=grid_spec, out_shape=[jax.Shap...  28.4 us
    ppermute x2, waiting for transfers between devices, from_behind(): return lax.ppermute(block, axis, route)  28 us
    all_to_all x1, waiting for transfers between devices, body(): lax.all_to_all(jnp.take(term_units, back_idx.reshape(-1), axis=0, mode='c...  21.7 us
    all_to_all x1, starting transfers between devices, body(): received = lax.all_to_all(payload, 'seq', 0, 0, tiled=True)  6.5 us
    all_to_all x1, starting transfers between devices, body(): lax.all_to_all(jnp.broadcast_to(global_sum[None], (shards,) + global_sum....  5.6 us
    ppermute x2, starting transfers between devices, from_behind(): return lax.ppermute(block, axis, route)  5.05 us
    all_to_all x1, waiting for transfers between devices, body(): lax.all_to_all(jnp.broadcast_to(global_sum[None], (shards,) + global_sum....  4.97 us
  transfers between devices with their start and end apart: 10, of which 6 were waited for; matrix products, arithmetic and copies ran while one was open for 8% of the time, Pallas kernels for 2%

profile of v16, /device:TPU:1, one launch (start us, length us, event | category | flops | bytes accessed | tf_op | source)
XLA Modules:
  0.0 199.3 jit_solution(5011278492095257304)
XLA Ops:
  0.7 1.2 broadcast_multiply_fusion.2
  1.8 0.7 fusion.29
  2.5 0.8 copy.73
  3.5 0.6 fusion.30
  4.0 0.3 convert_reduce_fusion
  4.4 0.8 dynamic-slice_reduce_fusion
  6.2 1.1 pad_maximum_fusion.1
  7.4 2.3 %gather_fusion = bf16[72,32,512]{2,1,0:T(8,128)(2,1)} fusion(bf16[17,32,512]{2,1,0:T(8,128)(2,1)S(1)} %concatenate.41, s32[1024]{0:T(1024)S(1)} %pad_clamp_fusion.1), kind=kCustom, calls=%fused_computation | custom fusion | bytes 4718880 | tf_op jit(solution)/shard_map/jit(_take)/gather | solution.py:291
  9.7 6.5 %all-to-all-start = ((bf16[8,288,512]{2,1,0:T(8,128)(2,1)}), bf16[8,288,512]{2,1,0:T(8,128)(2,1)}, u32[]{:S(2)}, u32[]{:S(2)}) async-start(bf16[8,288,512]{2,1,0:T(8,128)(2,1)} %bitcast.11), calls=%async_computation | async-start | bytes 4718592 | tf_op jit(solution)/shard_map/all_to_all | solution.py:294
  16.3 0.7 fusion.9
  16.9 3.4 %collective-permute-start = (bf16[1,2,64,512]{3,2,1,0:T(8,128)(2,1)}, bf16[1,2,64,512]{3,2,1,0:T(8,128)(2,1)S(1)}, u32[]{:S(2)}, u32[]{:S(2)}) collective-permute-start(bf16[1,2,64,512]{3,2,1,0:T(8,128)(2,1)} %get-tuple-element.51), channel_id=1, source_target_pairs={{0,1},{1,2},{2,3},{3,4},{4,5},{5,6},{6,7},{8,9},{9,10},{10,11},{11... | collective-permute-start | bytes 393224 | tf_op jit(solution)/shard_map/ppermute | solution.py:266
  20.3 1.3 collective-permute-start.1
  21.7 0.7 add.249
  22.8 1.1 and.202
  24.0 1.0 add.261
  25.1 0.2 select_reduce_fusion
  25.4 1.0 lt.86
  26.4 42.9 %all-to-all-done.refs_5_.refs_6_.refs_7_ = bf16[8,288,512]{2,1,0:T(8,128)(2,1)} async-done(((bf16[8,288,512]{2,1,0:T(8,128)(2,1)}), bf16[8,288,512]{2,1,0:T(8,128)(2,1)}, u32[]{:S(2)}, u32[]{:S(2)}) %all-to-all-start) | async-done | bytes 2359328 | tf_op jit(solution)/shard_map/all_to_all | solution.py:294
  69.3 1.0 slice_reduce_fusion.1
  70.3 0.7 broadcast_in_dim.66
  71.0 4.7 %all-to-all-start.1 = ((bf16[8,32,512]{2,1,0:T(8,128)(2,1)}), bf16[8,32,512]{2,1,0:T(8,128)(2,1)S(1)}, u32[]{:S(2)}, u32[]{:S(2)}) async-start(bf16[8,32,512]{2,1,0:T(8,128)(2,1)} %broadcast_in_dim.66), calls=%async_computation.1 | async-start | bytes 524288 | tf_op jit(solution)/shard_map/all_to_all | solution.py:296
  75.7 1.9 fusion.4.refs_8_
  77.7 0.7 pad_add_fusion.3
  78.4 0.7 reshape.664.ids_ref
  79.3 1.0 pad_maximum_fusion
  80.4 2.5 %all-to-all-done.1 = bf16[8,32,512]{2,1,0:T(8,128)(2,1)S(1)} async-done(((bf16[8,32,512]{2,1,0:T(8,128)(2,1)}), bf16[8,32,512]{2,1,0:T(8,128)(2,1)S(1)}, u32[]{:S(2)}, u32[]{:S(2)}) %all-to-all-start.1) | async-done | bytes 262176 | tf_op jit(solution)/shard_map/all_to_all | solution.py:296
  82.8 0.7 copy-done.3
  83.5 28.4 %shard_map.94 = (bf16[256,4096]{1,0:T(8,128)(2,1)}, f32[4,2,64,512]{3,2,1,0:T(8,128)}, bf16[2,2,64,512]{3,2,1,0:T(8,128)(2,1)}, bf16[2,2,64,512]{3,2,1,0:T(8,128)(2,1)}, bf16[4,3,2,64,512]{4,3,2,1,0:T(8,128)(2,1)}) custom-call(s32[24]{0:T(128)} %reshape.664.ids_ref, bf16[256,4096]{1,0:T(8,128)(2,1)} %bitcast.76, bf16[256,4096]{1,0:T(8,128)(2,1)} %bitcast.77, ...), custom_call_target="tpu_custom_call" | custom-call | flops 6442450944 | bytes 12582912 | tf_op jit(solution)/shard_map/pallas_call | solution.py:183
  112.0 1.7 maximum_maximum_fusion
  113.7 2.3 %gather_fusion.1 = bf16[72,32,512]{2,1,0:T(8,128)(2,1)} fusion(bf16[57,32,512]{2,1,0:T(8,128)(2,1)S(1)} %maximum_maximum_fusion, s32[1024]{0:T(1024)S(1)} %pad_clamp_fusion), kind=kCustom, calls=%fused_computation.1 | custom fusion | bytes 4718880 | tf_op jit(solution)/shard_map/jit(_take)/gather | solution.py:344
  116.0 4.8 %all-to-all-start.2 = ((bf16[8,288,512]{2,1,0:T(8,128)(2,1)}), bf16[8,288,512]{2,1,0:T(8,128)(2,1)S(1)}, u32[]{:S(2)}, u32[]{:S(2)}) async-start(bf16[8,288,512]{2,1,0:T(8,128)(2,1)} %bitcast.51), calls=%async_computation.2 | async-start | bytes 4718592 | tf_op jit(solution)/shard_map/all_to_all | solution.py:343
  120.8 2.0 collective-permute-start.2
  123.4 3.5 %collective-permute-start.4 = (bf16[1,2,64,512]{3,2,1,0:T(8,128)(2,1)S(1)}, bf16[1,2,64,512]{3,2,1,0:T(8,128)(2,1)S(1)}, u32[]{:S(2)}, u32[]{:S(2)}) collective-permute-start(bf16[1,2,64,512]{3,2,1,0:T(8,128)(2,1)S(1)} %get-tuple-element.53), channel_id=1, source_target_pairs={{0,1},{1,2},{2,3},{3,4},{4,5},{5,6},{6,7},{8,9},{9,10},{10,11},{11... | collective-permute-start | bytes 393224 | tf_op jit(solution)/shard_map/ppermute | solution.py:320
  126.9 1.3 collective-permute-start.3
  128.2 20.0 %collective-permute-done.2.src_ref = bf16[1,256,4096]{2,1,0:T(8,128)(2,1)} collective-permute-done((bf16[1,256,4096]{2,1,0:T(8,128)(2,1)}, bf16[1,256,4096]{2,1,0:T(8,128)(2,1)}, u32[]{:S(2)}, u32[]{:S(2)}) %collective-permute-start.2) | collective-permute-done | bytes 2097184 | tf_op jit(solution)/shard_map/ppermute | solution.py:37
  148.2 3.0 %shard_map.95 = bf16[1,256,4096]{2,1,0:T(8,128)(2,1)} custom-call(bf16[1,256,4096]{2,1,0:T(8,128)(2,1)} %collective-permute-done.2.src_ref), custom_call_target="tpu_custom_call" | custom-call | bytes 4194304 | tf_op jit(solution)/shard_map/pallas_call | solution.py:47
  151.2 21.7 %all-to-all-done.2 = bf16[8,288,512]{2,1,0:T(8,128)(2,1)S(1)} async-done(((bf16[8,288,512]{2,1,0:T(8,128)(2,1)}), bf16[8,288,512]{2,1,0:T(8,128)(2,1)S(1)}, u32[]{:S(2)}, u32[]{:S(2)}) %all-to-all-start.2) | async-done | bytes 2359328 | tf_op jit(solution)/shard_map/all_to_all | solution.py:343
  173.0 0.7 broadcast_in_dim.124
  173.7 5.6 %all-to-all-start.3 = ((bf16[8,32,512]{2,1,0:T(8,128)(2,1)}), bf16[8,32,512]{2,1,0:T(8,128)(2,1)S(1)}, u32[]{:S(2)}, u32[]{:S(2)}) async-start(bf16[8,32,512]{2,1,0:T(8,128)(2,1)} %broadcast_in_dim.124), calls=%async_computation.3 | async-start | bytes 524288 | tf_op jit(solution)/shard_map/all_to_all | solution.py:353
  179.3 0.2 slice.101
  179.5 1.3 fusion
  180.8 0.4 copy_add_fusion.1
  181.4 5.0 %all-to-all-done.3 = bf16[8,32,512]{2,1,0:T(8,128)(2,1)S(1)} async-done(((bf16[8,32,512]{2,1,0:T(8,128)(2,1)}), bf16[8,32,512]{2,1,0:T(8,128)(2,1)S(1)}, u32[]{:S(2)}, u32[]{:S(2)}) %all-to-all-start.3) | async-done | bytes 262176 | tf_op jit(solution)/shard_map/all_to_all | solution.py:353
  186.4 0.6 fusion.7
  187.0 0.4 fusion.2
  187.4 3.1 %collective-permute-start.5 = (bf16[4,2,64,512]{3,2,1,0:T(8,128)(2,1)S(1)}, bf16[4,2,64,512]{3,2,1,0:T(8,128)(2,1)S(1)}, u32[]{:S(2)}, u32[]{:S(2)}) collective-permute-start(bf16[4,2,64,512]{3,2,1,0:T(8,128)(2,1)S(1)} %fusion.2), channel_id=1, source_target_pairs={{8,0},{16,8},{24,16},{0,24},{9,1},{17,9},{25,17},{1,25},{10,2},{18... | collective-permute-start | bytes 1572872 | tf_op jit(solution)/shard_map/ppermute | solution.py:37
  190.4 8.0 %collective-permute-done.5 = bf16[4,2,64,512]{3,2,1,0:T(8,128)(2,1)S(1)} collective-permute-done((bf16[4,2,64,512]{3,2,1,0:T(8,128)(2,1)S(1)}, bf16[4,2,64,512]{3,2,1,0:T(8,128)(2,1)S(1)}, u32[]{:S(2)}, u32[]{:S(2)}) %collective-permute-start.5) | collective-permute-done | bytes 524320 | tf_op jit(solution)/shard_map/ppermute | solution.py:37
  198.4 0.8 fusion.32
  (86 shorter events, 3.1 us)
Async XLA Ops:
  2.5 4.8 %copy-start.8 = (pred[2]{0:T(512)(128)(4,1)}, pred[2]{0:T(512)(128)(4,1)S(1)}, u32[]{:S(2)}) copy-start(pred[2]{0:T(512)(128)(4,1)S(1)} %fusion.29) | copy-start | bytes 10
  3.4 2.7 %copy-start.5 = (pred[8,12]{1,0:T(8,128)(4,1)}, pred[8,12]{1,0:T(8,128)(4,1)S(1)}, u32[]{:S(2)}) copy-start(pred[8,12]{1,0:T(8,128)(4,1)S(1)} %get-tuple-element.45) | copy-start | bytes 292
  9.7 6.5 %copy-start = (bf16[1,256,512]{2,1,0:T(8,128)(2,1)S(1)}, bf16[1,256,512]{2,1,0:T(8,128)(2,1)}, u32[]{:S(2)}) copy-start(bf16[1,256,512]{2,1,0:T(8,128)(2,1)} %param.12) | copy-start | bytes 786436
  9.7 6.5 %copy-start.1 = (bf16[1,256,512]{2,1,0:T(8,128)(2,1)S(1)}, bf16[1,256,512]{2,1,0:T(8,128)(2,1)}, u32[]{:S(2)}) copy-start(bf16[1,256,512]{2,1,0:T(8,128)(2,1)} %param.13) | copy-start | bytes 786436
  9.7 11.9 %copy-start.7 = (s32[1,32,3]{1,0,2:T(1,128)S(1)}, s32[1,32,3]{1,0,2:T(1,128)}, u32[]{:S(2)}) copy-start(s32[1,32,3]{1,0,2:T(1,128)} %param.15) | copy-start | bytes 1156
  9.7 11.9 %copy-start.12 = (s32[1,2]{1,0:T(1,128)S(1)}, s32[1,2]{1,0:T(1,128)}, u32[]{:S(2)}) copy-start(s32[1,2]{1,0:T(1,128)} %param.16) | copy-start | bytes 28
  9.7 59.6 %all-to-all-start = ((bf16[8,288,512]{2,1,0:T(8,128)(2,1)}), bf16[8,288,512]{2,1,0:T(8,128)(2,1)}, u32[]{:S(2)}, u32[]{:S(2)}) async-start(bf16[8,288,512]{2,1,0:T(8,128)(2,1)} %bitcast.11), calls=%async_computation | async-start | bytes 4718592 | tf_op jit(solution)/shard_map/all_to_all | solution.py:294
  16.2 8.8 %copy-start.11 = (s32[1,8]{1,0:T(1,128)S(1)}, s32[1,8]{1,0:T(1,128)}, u32[]{:S(2)}) copy-start(s32[1,8]{1,0:T(1,128)} %param.17) | copy-start | bytes 100
  16.9 62.4 %collective-permute-start = (bf16[1,2,64,512]{3,2,1,0:T(8,128)(2,1)}, bf16[1,2,64,512]{3,2,1,0:T(8,128)(2,1)S(1)}, u32[]{:S(2)}, u32[]{:S(2)}) collective-permute-start(bf16[1,2,64,512]{3,2,1,0:T(8,128)(2,1)} %get-tuple-element.51), channel_id=1, source_target_pairs={{0,1},{1,2},{2,3},{3,4},{4,5},{5,6},{6,7},{8,9},{9,10},{10,11},{11... | collective-permute-start | bytes 393224 | tf_op jit(solution)/shard_map/ppermute | solution.py:266
  20.3 59.0 %collective-permute-start.1 = (bf16[1,2,64,512]{3,2,1,0:T(8,128)(2,1)S(1)}, bf16[1,2,64,512]{3,2,1,0:T(8,128)(2,1)S(1)}, u32[]{:S(2)}, u32[]{:S(2)}) collective-permute-start(bf16[1,2,64,512]{3,2,1,0:T(8,128)(2,1)S(1)} %get-tuple-element.52), channel_id=1, source_target_pairs={{1,0},{2,1},{3,2},{4,3},{5,4},{6,5},{7,6},{9,8},{10,9},{11,10},{12... | collective-permute-start | bytes 393224 | tf_op jit(solution)/shard_map/ppermute | solution.py:267
  71.0 11.8 %all-to-all-start.1 = ((bf16[8,32,512]{2,1,0:T(8,128)(2,1)}), bf16[8,32,512]{2,1,0:T(8,128)(2,1)S(1)}, u32[]{:S(2)}, u32[]{:S(2)}) async-start(bf16[8,32,512]{2,1,0:T(8,128)(2,1)} %broadcast_in_dim.66), calls=%async_computation.1 | async-start | bytes 524288 | tf_op jit(solution)/shard_map/all_to_all | solution.py:296
  82.8 0.7 copy-start.3
  116.0 6.9 %copy-start.6 = (pred[8,12]{1,0:T(8,128)(4,1)S(1)}, pred[8,12]{1,0:T(8,128)(4,1)}, u32[]{:S(2)}) copy-start(pred[8,12]{1,0:T(8,128)(4,1)} %copy-done.5) | copy-start | bytes 292
  116.0 7.3 %copy-start.4 = (bf16[2,2,64,512]{3,2,1,0:T(8,128)(2,1)S(1)}, bf16[2,2,64,512]{3,2,1,0:T(8,128)(2,1)}, u32[]{:S(2)}) copy-start(bf16[2,2,64,512]{3,2,1,0:T(8,128)(2,1)} %get-tuple-element.38) | copy-start | bytes 786436
  116.0 56.9 %all-to-all-start.2 = ((bf16[8,288,512]{2,1,0:T(8,128)(2,1)}), bf16[8,288,512]{2,1,0:T(8,128)(2,1)S(1)}, u32[]{:S(2)}, u32[]{:S(2)}) async-start(bf16[8,288,512]{2,1,0:T(8,128)(2,1)} %bitcast.51), calls=%async_computation.2 | async-start | bytes 4718592 | tf_op jit(solution)/shard_map/all_to_all | solution.py:343
  120.8 27.3 %collective-permute-start.2 = (bf16[1,256,4096]{2,1,0:T(8,128)(2,1)}, bf16[1,256,4096]{2,1,0:T(8,128)(2,1)}, u32[]{:S(2)}, u32[]{:S(2)}) collective-permute-start(bf16[1,256,4096]{2,1,0:T(8,128)(2,1)} %bitcast.78), channel_id=1, source_target_pairs={{8,0},{16,8},{24,16},{0,24},{9,1},{17,9},{25,17},{1,25},{10,2},{18... | collective-permute-start | bytes 6291464 | tf_op jit(solution)/shard_map/ppermute | solution.py:37
  123.4 58.0 %collective-permute-start.4 = (bf16[1,2,64,512]{3,2,1,0:T(8,128)(2,1)S(1)}, bf16[1,2,64,512]{3,2,1,0:T(8,128)(2,1)S(1)}, u32[]{:S(2)}, u32[]{:S(2)}) collective-permute-start(bf16[1,2,64,512]{3,2,1,0:T(8,128)(2,1)S(1)} %get-tuple-element.53), channel_id=1, source_target_pairs={{0,1},{1,2},{2,3},{3,4},{4,5},{5,6},{6,7},{8,9},{9,10},{10,11},{11... | collective-permute-start | bytes 393224 | tf_op jit(solution)/shard_map/ppermute | solution.py:320
  126.9 54.4 %collective-permute-start.3 = (bf16[1,2,64,512]{3,2,1,0:T(8,128)(2,1)S(1)}, bf16[1,2,64,512]{3,2,1,0:T(8,128)(2,1)S(1)}, u32[]{:S(2)}, u32[]{:S(2)}) collective-permute-start(bf16[1,2,64,512]{3,2,1,0:T(8,128)(2,1)S(1)} %get-tuple-element.54), channel_id=1, source_target_pairs={{1,0},{2,1},{3,2},{4,3},{5,4},{6,5},{7,6},{9,8},{10,9},{11,10},{12... | collective-permute-start | bytes 393224 | tf_op jit(solution)/shard_map/ppermute | solution.py:319
  173.7 12.7 %all-to-all-start.3 = ((bf16[8,32,512]{2,1,0:T(8,128)(2,1)}), bf16[8,32,512]{2,1,0:T(8,128)(2,1)S(1)}, u32[]{:S(2)}, u32[]{:S(2)}) async-start(bf16[8,32,512]{2,1,0:T(8,128)(2,1)} %broadcast_in_dim.124), calls=%async_computation.3 | async-start | bytes 524288 | tf_op jit(solution)/shard_map/all_to_all | solution.py:353
  179.5 1.3 copy-start.2
  180.8 5.6 %copy-start.9 = (pred[2]{0:T(512)(128)(4,1)S(1)}, pred[2]{0:T(512)(128)(4,1)}, u32[]{:S(2)}) copy-start(pred[2]{0:T(512)(128)(4,1)} %copy-done.8) | copy-start | bytes 10
  180.8 5.6 %copy-start.10 = (s32[2]{0:T(128)S(1)}, s32[2]{0:T(128)}, u32[]{:S(2)}) copy-start(s32[2]{0:T(128)} %get-tuple-element.48) | copy-start | bytes 28
  187.4 11.1 %collective-permute-start.5 = (bf16[4,2,64,512]{3,2,1,0:T(8,128)(2,1)S(1)}, bf16[4,2,64,512]{3,2,1,0:T(8,128)(2,1)S(1)}, u32[]{:S(2)}, u32[]{:S(2)}) collective-permute-start(bf16[4,2,64,512]{3,2,1,0:T(8,128)(2,1)S(1)} %fusion.2), channel_id=1, source_target_pairs={{8,0},{16,8},{24,16},{0,24},{9,1},{17,9},{25,17},{1,25},{10,2},{18... | collective-permute-start | bytes 1572872 | tf_op jit(solution)/shard_map/ppermute | solution.py:37
